TPU v7x, 256 devices: a whole 4x4x8 slice. The times are simulated.
256 devices in a mesh: row: 8 (over y, core), col: 32 (over x, z).
Axes of the slice: x: 4, y: 4, z: 8, core: 2. Of those that a mesh axis runs over, the one named last changes fastest.
Arguments:
- density: float32 [512, 1024, 128], P('row', 'col'), may hold values from 0 to 40, as said below
Outputs:
- coarse: float32 [512, 1024, 128], P('row', 'col')
- moments: float32 [3, 4, 2, 4], replicated
Inputs may be any that keep to these rules, and one draw needn't show every extreme that they name: Positive density.
All inputs are finite; a program needn't handle non-finite values.
Results may differ from a plain program's by a relative error of at most 0.0003.
Values sent between devices are 32-bit elements; how exact they have to be, the bound alone decides.
No kernel may reach another device: no remote copies, remote signals or barrier semaphores. Data moves between devices by JAX's collectives and lax.ppermute only.
A program may use at most 64 MiB of HBM per device.

v0:
```python
import jax
import jax.numpy as jnp
from jax import lax
from jax.sharding import PartitionSpec as P

SUB = 256


SPLINE_TAPS = (0.0625, 0.25, 0.375, 0.25, 0.0625)
SPACINGS = (4, 8, 16)
EPSILON = 1e-06


def padded_2(block, sides, width):
    for axis, dim in sides:
        count = lax.axis_size(axis)
        forward = [(i, i + 1) for i in range(count - 1)]
        forward.append((count - 1, 0))
        backward = [(target, source) for source, target in forward]
        low = lax.ppermute(
            lax.slice_in_dim(block, block.shape[dim] - width, None, axis=dim), axis, forward
        )
        high = lax.ppermute(lax.slice_in_dim(block, 0, width, axis=dim), axis, backward)
        block = jnp.concatenate([low, block, high], axis=dim)
    return block


def holed_pass(padded, spacing, axis_number, length_out):
    summed = SPLINE_TAPS[0] * lax.slice_in_dim(padded, 0, length_out, axis=axis_number)
    for tap_index in (1, 2, 3, 4):
        portion = lax.slice_in_dim(
            padded, tap_index * spacing, tap_index * spacing + length_out, axis=axis_number
        )
        summed = summed + SPLINE_TAPS[tap_index] * portion
    return summed


def depth_pass(values_in, spacing):
    summed = SPLINE_TAPS[2] * values_in
    for tap_index in (0, 1, 3, 4):
        summed = summed + SPLINE_TAPS[tap_index] * jnp.roll(
            values_in, -(tap_index - 2) * spacing, axis=2
        )
    return summed


def moment_planes(detail):
    square = detail * detail
    return jnp.stack(
        [
            jnp.sum(jnp.abs(detail), axis=2),
            jnp.sum(square, axis=2),
            jnp.sum(square * detail, axis=2),
            jnp.sum(square * square, axis=2),
        ]
    )


def finish_table(table, planes):
    means = table / jnp.float32(SUB * SUB * planes)
    second = means[:, 1]
    third = means[:, 2] / (second + EPSILON) ** 1.5
    fourth = means[:, 3] / (second + EPSILON) ** 2
    return jnp.stack([means[:, 0], second, third, fourth], axis=1)


def per_device(density):
    size_x, size_y, planes = density.shape
    plane_list = []
    current = density
    for spacing in SPACINGS:
        padded = padded_2(current, (("row", 0), ("col", 1)), 2 * spacing)
        along_x = holed_pass(padded, spacing, 0, size_x)
        along_y = holed_pass(along_x, spacing, 1, size_y)
        smoother = depth_pass(along_y, spacing)
        plane_list.append(moment_planes(current - smoother))
        current = smoother
    planes_all = jnp.stack(plane_list)
    count_x = lax.axis_size("row") * size_x // SUB
    count_y = lax.axis_size("col") * size_y // SUB
    rows_global = lax.axis_index("row") * size_x + jnp.arange(size_x, dtype=jnp.int32)
    cols_global = lax.axis_index("col") * size_y + jnp.arange(size_y, dtype=jnp.int32)
    onehot_x = (
        (rows_global // SUB)[:, None] == jnp.arange(count_x, dtype=jnp.int32)[None, :]
    ).astype(jnp.float32)
    onehot_y = (
        (cols_global // SUB)[:, None] == jnp.arange(count_y, dtype=jnp.int32)[None, :]
    ).astype(jnp.float32)
    partial_table = jnp.einsum(
        "xa,skxy,yb->skab", onehot_x, planes_all, onehot_y, precision=lax.Precision.HIGHEST
    )
    table = lax.psum(partial_table, ("row", "col"))
    return (current, finish_table(table, planes))


def solution(mesh):
    placed = (P("row", "col", None),)
    return jax.shard_map(
        per_device,
        mesh=mesh,
        in_specs=placed,
        out_specs=(P("row", "col", None), P()),
        check_vma=False,
    )
```

profile of v0, /device:TPU:8, one launch (start us, length us, event | category | flops | bytes accessed | tf_op | source)
XLA Modules:
  0.0 214.3 jit_solution(4838625982686023832)
XLA Ops:
  0.6 1.0 fusion.79
  1.6 1.7 collective-permute-start.1
  3.4 2.6 %collective-permute-done = f32[8,32,128]{2,1,0:T(8,128)S(1)} collective-permute-done((f32[8,32,128]{2,1,0:T(8,128)S(1)}, f32[8,32,128]{2,1,0:T(8,128)S(1)}, u32[]{:S(2)}, u32[]{:S(2)}) %collective-permute-start) | collective-permute-done | bytes 131104 | tf_op jit(solution)/shard_map/ppermute | solution.py:20
  6.0 1.3 constant_dynamic-update-slice_fusion.1
  7.4 2.0 collective-permute-start.2
  9.4 6.2 %collective-permute-start.3 = (f32[80,8,128]{2,1,0:T(8,128)S(1)}, f32[80,8,128]{2,1,0:T(8,128)S(1)}, u32[]{:S(2)}, u32[]{:S(2)}) collective-permute-start(f32[80,8,128]{2,1,0:T(8,128)S(1)} %get-tuple-element.25), channel_id=1, source_target_pairs={{1,0},{2,1},{3,2},{4,3},{5,4},{6,5},{7,6},{8,7},{9,8},{10,9},{11,1... | collective-permute-start | bytes 983048 | tf_op jit(solution)/shard_map/ppermute | solution.py:23
  15.6 8.1 %collective-permute-done.2 = f32[80,8,128]{2,1,0:T(8,128)S(1)} collective-permute-done((f32[80,8,128]{2,1,0:T(8,128)S(1)}, f32[80,8,128]{2,1,0:T(8,128)S(1)}, u32[]{:S(2)}, u32[]{:S(2)}) %collective-permute-start.2) | collective-permute-done | bytes 327712 | tf_op jit(solution)/shard_map/ppermute | solution.py:20
  23.9 0.4 fusion.8
  24.3 0.4 fusion.26
  26.2 0.9 copy-done
  27.1 1.5 fusion.57
  28.6 1.7 collective-permute-start.5
  30.4 4.1 %collective-permute-done.4 = f32[16,32,128]{2,1,0:T(8,128)S(1)} collective-permute-done((f32[16,32,128]{2,1,0:T(8,128)S(1)}, f32[16,32,128]{2,1,0:T(8,128)S(1)}, u32[]{:S(2)}, u32[]{:S(2)}) %collective-permute-start.4) | collective-permute-done | bytes 262176 | tf_op jit(solution)/shard_map/ppermute | solution.py:20
  34.8 5.3 %collective-permute-start.7 = (f32[96,16,128]{2,1,0:T(8,128)S(1)}, f32[96,16,128]{2,1,0:T(8,128)S(1)}, u32[]{:S(2)}, u32[]{:S(2)}) collective-permute-start(f32[96,16,128]{2,1,0:T(8,128)S(1)} %get-tuple-element.23), channel_id=1, source_target_pairs={{1,0},{2,1},{3,2},{4,3},{5,4},{6,5},{7,6},{8,7},{9,8},{10,9},{11,1... | collective-permute-start | bytes 2359304 | tf_op jit(solution)/shard_map/ppermute | solution.py:23
  40.1 17.9 %collective-permute-done.6 = f32[96,16,128]{2,1,0:T(8,128)S(1)} collective-permute-done((f32[96,16,128]{2,1,0:T(8,128)S(1)}, f32[96,16,128]{2,1,0:T(8,128)S(1)}, u32[]{:S(2)}, u32[]{:S(2)}) %collective-permute-start.6) | collective-permute-done | bytes 786464 | tf_op jit(solution)/shard_map/ppermute | solution.py:20
  58.0 0.4 pad_maximum_fusion.1
  58.4 0.6 fusion.4
  60.8 1.5 fusion.59
  62.7 1.4 collective-permute-start.9
  64.1 6.9 %collective-permute-done.8 = f32[32,32,128]{2,1,0:T(8,128)S(1)} collective-permute-done((f32[32,32,128]{2,1,0:T(8,128)S(1)}, f32[32,32,128]{2,1,0:T(8,128)S(1)}, u32[]{:S(2)}, u32[]{:S(2)}) %collective-permute-start.8) | collective-permute-done | bytes 524320 | tf_op jit(solution)/shard_map/ppermute | solution.py:20
  71.0 1.6 pad_maximum_fusion.2
  72.7 5.6 %collective-permute-start.11 = (f32[128,32,128]{2,1,0:T(8,128)}, f32[128,32,128]{2,1,0:T(8,128)}, u32[]{:S(2)}, u32[]{:S(2)}) collective-permute-start(f32[128,32,128]{2,1,0:T(8,128)} %pad_maximum_fusion.2), channel_id=1, source_target_pairs={{1,0},{2,1},{3,2},{4,3},{5,4},{6,5},{7,6},{8,7},{9,8},{10,9},{11,1... | collective-permute-start | bytes 6291464 | tf_op jit(solution)/shard_map/ppermute | solution.py:23
  78.3 1.2 abs_reduce_fusion.2
  79.5 1.2 abs_reduce_fusion.1
  80.6 44.0 %collective-permute-done.10 = f32[128,32,128]{2,1,0:T(8,128)} collective-permute-done((f32[128,32,128]{2,1,0:T(8,128)}, f32[128,32,128]{2,1,0:T(8,128)}, u32[]{:S(2)}, u32[]{:S(2)}) %collective-permute-start.10) | collective-permute-done | bytes 2097184 | tf_op jit(solution)/shard_map/ppermute | solution.py:20
  124.6 5.2 %pad_maximum_fusion = f32[128,96,128]{2,1,0:T(8,128)S(1)} fusion(f32[128,32,128]{2,1,0:T(8,128)} %collective-permute-done.11, f32[32,32,128]{2,1,0:T(8,128)S(1)} %copy-done.4, f32[64,32,128]{2,1,0:T(8,128)S(1)} %get-tuple-element.19, f32[32,32,128]{2,1,0:T(8,128)S(1)} %copy-done.2, f32[128,32,128]{2,1,0:T(8,128)} %collective-permute-done.10), kind=kLoop, calls=%fused_computation | loop fusion | flops 6291456 | bytes 12582912 | tf_op jit(solution)/shard_map/concatenate | solution.py:24
  129.8 1.8 fusion
  131.6 0.4 fusion.18
  133.5 2.6 %fusion.61 = (f32[64,32,128]{2,1,0:T(8,128)S(1)}, f32[64,32,128]{2,1,0:T(8,128)}) fusion(f32[64,32,128]{2,1,0:T(8,128)S(1)} %get-tuple-element.19, f32[64,32,32]{2,1,0:T(8,128)S(1)} %get-tuple-element.27, f32[64,32,96]{2,1,0:T(8,128)S(1)} %get-tuple-element.29, f32[64,32,16]{2,1,0:T(8,128)S(1)} %get-tuple-element.31, ...), kind=kLoop, calls=%fused_computation.137 | loop fusion | flops 6029312 | bytes 12582912 | tf_op jit(solution)/shard_map/sub | solution.py:76
  136.2 1.2 abs_reduce_fusion
  137.8 75.8 %psum.7 = f32[3,4,2,4]{3,1,2,0:T(4,128)S(1)} all-reduce(f32[3,4,2,4]{3,1,2,0:T(4,128)S(1)} %fusion.51), channel_id=1, replica_groups=mesh['row'=8,'col'=32] {'row','col'}, use_global_device_ids=true, to_apply=%region_12.13 | all-reduce | flops 96 | bytes 768 | tf_op jit(solution)/shard_map/psum | solution.py:92
  213.7 0.6 copy.3
  (51 shorter events, 6.4 us)
Async XLA Ops:
  1.6 4.4 %collective-permute-start = (f32[8,32,128]{2,1,0:T(8,128)S(1)}, f32[8,32,128]{2,1,0:T(8,128)S(1)}, u32[]{:S(2)}, u32[]{:S(2)}) collective-permute-start(f32[8,32,128]{2,1,0:T(8,128)S(1)} %get-tuple-element.55), channel_id=1, source_target_pairs={{0,32},{32,64},{64,96},{96,128},{128,160},{160,192},{192,224},{224... | collective-permute-start | bytes 393224 | tf_op jit(solution)/shard_map/ppermute | solution.py:20
  1.6 5.7 %collective-permute-start.1 = (f32[8,32,128]{2,1,0:T(8,128)S(1)}, f32[8,32,128]{2,1,0:T(8,128)S(1)}, u32[]{:S(2)}, u32[]{:S(2)}) collective-permute-start(f32[8,32,128]{2,1,0:T(8,128)S(1)} %get-tuple-element.54), channel_id=1, source_target_pairs={{32,0},{64,32},{96,64},{128,96},{160,128},{192,160},{224,192},{0,2... | collective-permute-start | bytes 393224 | tf_op jit(solution)/shard_map/ppermute | solution.py:23
  7.4 16.4 %collective-permute-start.2 = (f32[80,8,128]{2,1,0:T(8,128)S(1)}, f32[80,8,128]{2,1,0:T(8,128)S(1)}, u32[]{:S(2)}, u32[]{:S(2)}) collective-permute-start(f32[80,8,128]{2,1,0:T(8,128)S(1)} %get-tuple-element.24), channel_id=1, source_target_pairs={{0,1},{1,2},{2,3},{3,4},{4,5},{5,6},{6,7},{7,8},{8,9},{9,10},{10,1... | collective-permute-start | bytes 983048 | tf_op jit(solution)/shard_map/ppermute | solution.py:20
  9.4 14.4 %collective-permute-start.3 = (f32[80,8,128]{2,1,0:T(8,128)S(1)}, f32[80,8,128]{2,1,0:T(8,128)S(1)}, u32[]{:S(2)}, u32[]{:S(2)}) collective-permute-start(f32[80,8,128]{2,1,0:T(8,128)S(1)} %get-tuple-element.25), channel_id=1, source_target_pairs={{1,0},{2,1},{3,2},{4,3},{5,4},{6,5},{7,6},{8,7},{9,8},{10,9},{11,1... | collective-permute-start | bytes 983048 | tf_op jit(solution)/shard_map/ppermute | solution.py:23
  25.9 1.2 copy-start
  28.6 5.8 %collective-permute-start.4 = (f32[16,32,128]{2,1,0:T(8,128)S(1)}, f32[16,32,128]{2,1,0:T(8,128)S(1)}, u32[]{:S(2)}, u32[]{:S(2)}) collective-permute-start(f32[16,32,128]{2,1,0:T(8,128)S(1)} %get-tuple-element.44), channel_id=1, source_target_pairs={{0,32},{32,64},{64,96},{96,128},{128,160},{160,192},{192,224},{224... | collective-permute-start | bytes 786440 | tf_op jit(solution)/shard_map/ppermute | solution.py:20
  28.6 5.8 %collective-permute-start.5 = (f32[16,32,128]{2,1,0:T(8,128)S(1)}, f32[16,32,128]{2,1,0:T(8,128)S(1)}, u32[]{:S(2)}, u32[]{:S(2)}) collective-permute-start(f32[16,32,128]{2,1,0:T(8,128)S(1)} %get-tuple-element.45), channel_id=1, source_target_pairs={{32,0},{64,32},{96,64},{128,96},{160,128},{192,160},{224,192},{0,2... | collective-permute-start | bytes 786440 | tf_op jit(solution)/shard_map/ppermute | solution.py:23
  34.7 23.3 %collective-permute-start.6 = (f32[96,16,128]{2,1,0:T(8,128)S(1)}, f32[96,16,128]{2,1,0:T(8,128)S(1)}, u32[]{:S(2)}, u32[]{:S(2)}) collective-permute-start(f32[96,16,128]{2,1,0:T(8,128)S(1)} %get-tuple-element.22), channel_id=1, source_target_pairs={{0,1},{1,2},{2,3},{3,4},{4,5},{5,6},{6,7},{7,8},{8,9},{9,10},{10,1... | collective-permute-start | bytes 2359304 | tf_op jit(solution)/shard_map/ppermute | solution.py:20
  34.8 23.2 %collective-permute-start.7 = (f32[96,16,128]{2,1,0:T(8,128)S(1)}, f32[96,16,128]{2,1,0:T(8,128)S(1)}, u32[]{:S(2)}, u32[]{:S(2)}) collective-permute-start(f32[96,16,128]{2,1,0:T(8,128)S(1)} %get-tuple-element.23), channel_id=1, source_target_pairs={{1,0},{2,1},{3,2},{4,3},{5,4},{6,5},{7,6},{8,7},{9,8},{10,9},{11,1... | collective-permute-start | bytes 2359304 | tf_op jit(solution)/shard_map/ppermute | solution.py:23
  62.4 8.6 %collective-permute-start.8 = (f32[32,32,128]{2,1,0:T(8,128)S(1)}, f32[32,32,128]{2,1,0:T(8,128)S(1)}, u32[]{:S(2)}, u32[]{:S(2)}) collective-permute-start(f32[32,32,128]{2,1,0:T(8,128)S(1)} %get-tuple-element.34), channel_id=1, source_target_pairs={{0,32},{32,64},{64,96},{96,128},{128,160},{160,192},{192,224},{224... | collective-permute-start | bytes 1572872 | tf_op jit(solution)/shard_map/ppermute | solution.py:20
  62.7 8.3 %collective-permute-start.9 = (f32[32,32,128]{2,1,0:T(8,128)S(1)}, f32[32,32,128]{2,1,0:T(8,128)S(1)}, u32[]{:S(2)}, u32[]{:S(2)}) collective-permute-start(f32[32,32,128]{2,1,0:T(8,128)S(1)} %get-tuple-element.35), channel_id=1, source_target_pairs={{32,0},{64,32},{96,64},{128,96},{160,128},{192,160},{224,192},{0,2... | collective-permute-start | bytes 1572872 | tf_op jit(solution)/shard_map/ppermute | solution.py:23
  71.0 1.6 copy-start.1
  71.0 1.6 copy-start.3
  72.7 51.9 %collective-permute-start.10 = (f32[128,32,128]{2,1,0:T(8,128)}, f32[128,32,128]{2,1,0:T(8,128)}, u32[]{:S(2)}, u32[]{:S(2)}) collective-permute-start(f32[128,32,128]{2,1,0:T(8,128)} %pad_maximum_fusion.2), channel_id=1, source_target_pairs={{0,1},{1,2},{2,3},{3,4},{4,5},{5,6},{6,7},{7,8},{8,9},{9,10},{10,1... | collective-permute-start | bytes 6291464 | tf_op jit(solution)/shard_map/ppermute | solution.py:20
  72.7 51.9 %collective-permute-start.11 = (f32[128,32,128]{2,1,0:T(8,128)}, f32[128,32,128]{2,1,0:T(8,128)}, u32[]{:S(2)}, u32[]{:S(2)}) collective-permute-start(f32[128,32,128]{2,1,0:T(8,128)} %pad_maximum_fusion.2), channel_id=1, source_target_pairs={{1,0},{2,1},{3,2},{4,3},{5,4},{6,5},{7,6},{8,7},{9,8},{10,9},{11,1... | collective-permute-start | bytes 6291464 | tf_op jit(solution)/shard_map/ppermute | solution.py:23
  79.4 45.2 %copy-start.2 = (f32[32,32,128]{2,1,0:T(8,128)S(1)}, f32[32,32,128]{2,1,0:T(8,128)}, u32[]{:S(2)}) copy-start(f32[32,32,128]{2,1,0:T(8,128)} %copy-done.1) | copy-start | bytes 1572868
  79.4 45.2 %copy-start.4 = (f32[32,32,128]{2,1,0:T(8,128)S(1)}, f32[32,32,128]{2,1,0:T(8,128)}, u32[]{:S(2)}) copy-start(f32[32,32,128]{2,1,0:T(8,128)} %copy-done.3) | copy-start | bytes 1572868
where the time goes:
time: 217 us; the launch traced here: 214 us
  waiting for transfers between devices  83.6 us (39%)
  blocking collectives  75.8 us (35%)
  starting transfers between devices  24.5 us (11%)
  other arithmetic  20.5 us (9%)
  local copies, waits for them, and re-layouts  8.47 us (4%)
    ppermute x6, waiting for transfers between devices, padded_2(): lax.ppermute(lax.slice_in_dim(block, block.shape[dim] - width, None, axis...  83.5 us
    psum x1, blocking collectives, per_device(): table = lax.psum(partial_table, ('row', 'col'))  75.8 us
    ppermute x6, starting transfers between devices, padded_2(): lax.ppermute(lax.slice_in_dim(block, 0, width, axis=dim), axis, backward)  22 us
    concatenate x5, other arithmetic, padded_2(): block = jnp.concatenate([low, block, high], axis=dim)  7.45 us
    sub x3, other arithmetic, per_device(): plane_list.append(moment_planes(current - smoother))  5.62 us
    slice x12, local copies, waits for them, and re-layouts, depth_pass(): jnp.roll(values_in, -(tap_index - 2) * spacing, axis=2)  4.39 us
  transfers between devices with their start and end apart: 12, of which 6 were waited for; matrix products, arithmetic and copies ran while one was open for 2% of the time, Pallas kernels for 0%

commit v1 on v0

v1 whole, which is shorter than its diff:
```python
import jax
import jax.numpy as jnp
from jax import lax
from jax.sharding import PartitionSpec as P

SUB = 256


SPLINE_TAPS = (0.0625, 0.25, 0.375, 0.25, 0.0625)
SPACINGS = (4, 8, 16)
EPSILON = 1e-06


def ring_pairs(count):
    forward = [(i, (i + 1) % count) for i in range(count)]
    backward = [(target, source) for source, target in forward]
    return forward, backward


def padded_1(block, axis, dim, width):
    count = lax.axis_size(axis)
    assert width <= block.shape[dim]
    forward, backward = ring_pairs(count)
    low = lax.ppermute(
        lax.slice_in_dim(block, block.shape[dim] - width, None, axis=dim), axis, forward
    )
    high = lax.ppermute(lax.slice_in_dim(block, 0, width, axis=dim), axis, backward)
    return jnp.concatenate([low, block, high], axis=dim)


def holed_pass(padded, spacing, axis_number, length_out):
    summed = SPLINE_TAPS[0] * lax.slice_in_dim(padded, 0, length_out, axis=axis_number)
    for tap_index in (1, 2, 3, 4):
        portion = lax.slice_in_dim(
            padded, tap_index * spacing, tap_index * spacing + length_out, axis=axis_number
        )
        summed = summed + SPLINE_TAPS[tap_index] * portion
    return summed


def depth_pass(values_in, spacing):
    summed = SPLINE_TAPS[2] * values_in
    for tap_index in (0, 1, 3, 4):
        summed = summed + SPLINE_TAPS[tap_index] * jnp.roll(
            values_in, -(tap_index - 2) * spacing, axis=2
        )
    return summed


def moment_sums(detail):
    square = detail * detail
    return jnp.stack(
        [
            jnp.sum(jnp.abs(detail)),
            jnp.sum(square),
            jnp.sum(square * detail),
            jnp.sum(square * square),
        ]
    )


def finish_table(table, planes):
    means = table / jnp.float32(SUB * SUB * planes)
    second = means[:, 1]
    third = means[:, 2] / (second + EPSILON) ** 1.5
    fourth = means[:, 3] / (second + EPSILON) ** 2
    return jnp.stack([means[:, 0], second, third, fourth], axis=1)


def butterfly_sum(table, axes):
    for axis in axes:
        count = lax.axis_size(axis)
        assert count & (count - 1) == 0
        step = 1
        while step < count:
            pairs = [(i, i ^ step) for i in range(count)]
            table = table + lax.ppermute(table, axis, pairs)
            step *= 2
    return table


def per_device(density):
    size_x, size_y, planes = density.shape
    assert SUB % size_x == 0 and SUB % size_y == 0
    sums = []
    current = density
    for spacing in SPACINGS:
        padded_x = padded_1(current, "row", 0, 2 * spacing)
        along_x = holed_pass(padded_x, spacing, 0, size_x)
        padded_y = padded_1(along_x, "col", 1, 2 * spacing)
        along_y = holed_pass(padded_y, spacing, 1, size_y)
        smoother = depth_pass(along_y, spacing)
        sums.append(moment_sums(current - smoother))
        current = smoother
    partial = jnp.stack(sums)
    count_x = lax.axis_size("row") * size_x // SUB
    count_y = lax.axis_size("col") * size_y // SUB
    block_x = lax.axis_index("row") * size_x // SUB
    block_y = lax.axis_index("col") * size_y // SUB
    onehot_x = (jnp.arange(count_x, dtype=jnp.int32) == block_x).astype(jnp.float32)
    onehot_y = (jnp.arange(count_y, dtype=jnp.int32) == block_y).astype(jnp.float32)
    partial_table = (
        partial[:, :, None, None] * onehot_x[None, None, :, None] * onehot_y[None, None, None, :]
    )
    table = butterfly_sum(partial_table, ("row", "col"))
    return (current, finish_table(table, planes))


def solution(mesh):
    placed = (P("row", "col", None),)
    return jax.shard_map(
        per_device,
        mesh=mesh,
        in_specs=placed,
        out_specs=(P("row", "col", None), P()),
        check_vma=False,
    )
```

time: 217 us -> 146 us (0.67); the launches traced: 214 us -> 146 us
  blocking collectives: 75.8 us -> 0 us
  waiting for transfers between devices: 83.6 us -> 86.9 us
  starting transfers between devices: 24.5 us -> 27.8 us
    psum x1 -> x0, blocking collectives: 75.8 us -> none  [per_device(): table = lax.psum(partial_table, ('row', 'col'))]
    another operation x2 -> x3, other arithmetic: 0.04 us -> 7.59 us  [per_device(): partial = jnp.stack(sums)]
    concatenate x5 -> x0, other arithmetic: 7.45 us -> none  [padded_2(): block = jnp.concatenate([low, block, high], axis=dim)]
    ppermute x12 -> x20, waiting for transfers between devices: 83.6 us -> 86.9 us  [the longest x6 38.3 us: padded_1(): lax.ppermute(lax.slice_in_dim(block, block.shape[dim] - width, None, axis...]
    ppermute x12 -> x20, starting transfers between devices: 24.5 us -> 27.8 us  [the longest x6 22 us: padded_1(): lax.ppermute(lax.slice_in_dim(block, 0, width, axis=dim), axis, backward)]
    unnamed x13 -> x3, local copies, waits for them, and re-layouts: 2.82 us -> 0.02 us
  transfers between devices with their start and end apart: 12 -> 20, of which waited for: 6 -> 15; matrix products, arithmetic and copies ran while one was open for 2% -> 6% of each run, Pallas kernels for 0% -> 0%
where the time goes in v1:
time: 146 us
  waiting for transfers between devices  86.9 us (60%)
  starting transfers between devices  27.8 us (19%)
  other arithmetic  22.6 us (15%)
  local copies, waits for them, and re-layouts  7.25 us (5%)
    ppermute x6, waiting for transfers between devices, padded_1(): lax.ppermute(lax.slice_in_dim(block, block.shape[dim] - width, None, axis...  38.3 us
    ppermute x8, waiting for transfers between devices, butterfly_sum(): table = table + lax.ppermute(table, axis, pairs)  32.2 us
    ppermute x6, starting transfers between devices, padded_1(): lax.ppermute(lax.slice_in_dim(block, 0, width, axis=dim), axis, backward)  22 us
    ppermute x6, waiting for transfers between devices, padded_1(): lax.ppermute(lax.slice_in_dim(block, 0, width, axis=dim), axis, backward)  16.4 us
    another operation x3, other arithmetic, per_device(): partial = jnp.stack(sums)  7.59 us
    add x6, other arithmetic, holed_pass(): summed = summed + SPLINE_TAPS[tap_index] * portion  6.02 us
    sub x3, other arithmetic, per_device(): sums.append(moment_sums(current - smoother))  4.89 us
    slice x12, local copies, waits for them, and re-layouts, depth_pass(): jnp.roll(values_in, -(tap_index - 2) * spacing, axis=2)  4.45 us
  transfers between devices with their start and end apart: 20, of which 15 were waited for; matrix products, arithmetic and copies ran while one was open for 6% of the time, Pallas kernels for 0%

profile of v1, /device:TPU:8, one launch (start us, length us, event | category | flops | bytes accessed | tf_op | source)
XLA Modules:
  0.0 145.6 jit_solution(7019828529462913057)
XLA Ops:
  1.6 1.7 %collective-permute-start.1 = (f32[8,32,128]{2,1,0:T(8,128)S(1)}, f32[8,32,128]{2,1,0:T(8,128)S(1)}, u32[]{:S(2)}, u32[]{:S(2)}) collective-permute-start(f32[8,32,128]{2,1,0:T(8,128)S(1)} %get-tuple-element.55), channel_id=1, source_target_pairs={{32,0},{64,32},{96,64},{128,96},{160,128},{192,160},{224,192},{0,2... | collective-permute-start | bytes 393224 | tf_op jit(solution)/shard_map/ppermute | solution.py:27
  3.4 2.6 %collective-permute-done = f32[8,32,128]{2,1,0:T(8,128)S(1)} collective-permute-done((f32[8,32,128]{2,1,0:T(8,128)S(1)}, f32[8,32,128]{2,1,0:T(8,128)S(1)}, u32[]{:S(2)}, u32[]{:S(2)}) %collective-permute-start) | collective-permute-done | bytes 131104 | tf_op jit(solution)/shard_map/ppermute | solution.py:24
  6.1 1.6 %constant_dynamic-update-slice_fusion = (f32[72,32,128]{2,1,0:T(8,128)S(1)}, f32[72,32,128]{2,1,0:T(8,128)S(1)}) fusion(f32[72,32,128]{2,1,0:T(8,128)S(1)} %constant_dynamic-update-slice_fusion.1, f32[64,32,128]{2,1,0:T(8,128)} %param.1), kind=kLoop, calls=%fused_computation.124 | loop fusion | bytes 3145728 | tf_op jit(solution)/shard_map/concatenate | solution.py:28
  8.1 2.0 %collective-permute-start.2 = (f32[64,8,128]{2,1,0:T(8,128)S(1)}, f32[64,8,128]{2,1,0:T(8,128)S(1)}, u32[]{:S(2)}, u32[]{:S(2)}) collective-permute-start(f32[64,8,128]{2,1,0:T(8,128)S(1)} %get-tuple-element.50), channel_id=1, source_target_pairs={{0,1},{1,2},{2,3},{3,4},{4,5},{5,6},{6,7},{7,8},{8,9},{9,10},{10,1... | collective-permute-start | bytes 786440 | tf_op jit(solution)/shard_map/ppermute | solution.py:24
  10.1 6.2 %collective-permute-start.3 = (f32[64,8,128]{2,1,0:T(8,128)S(1)}, f32[64,8,128]{2,1,0:T(8,128)S(1)}, u32[]{:S(2)}, u32[]{:S(2)}) collective-permute-start(f32[64,8,128]{2,1,0:T(8,128)S(1)} %get-tuple-element.51), channel_id=1, source_target_pairs={{1,0},{2,1},{3,2},{4,3},{5,4},{6,5},{7,6},{8,7},{9,8},{10,9},{11,1... | collective-permute-start | bytes 786440 | tf_op jit(solution)/shard_map/ppermute | solution.py:27
  16.3 6.5 %collective-permute-done.2 = f32[64,8,128]{2,1,0:T(8,128)S(1)} collective-permute-done((f32[64,8,128]{2,1,0:T(8,128)S(1)}, f32[64,8,128]{2,1,0:T(8,128)S(1)}, u32[]{:S(2)}, u32[]{:S(2)}) %collective-permute-start.2) | collective-permute-done | bytes 262176 | tf_op jit(solution)/shard_map/ppermute | solution.py:24
  24.8 1.3 fusion.69
  26.2 1.7 %collective-permute-start.5 = (f32[16,32,128]{2,1,0:T(8,128)S(1)}, f32[16,32,128]{2,1,0:T(8,128)S(1)}, u32[]{:S(2)}, u32[]{:S(2)}) collective-permute-start(f32[16,32,128]{2,1,0:T(8,128)S(1)} %get-tuple-element.41), channel_id=1, source_target_pairs={{32,0},{64,32},{96,64},{128,96},{160,128},{192,160},{224,192},{0,2... | collective-permute-start | bytes 786440 | tf_op jit(solution)/shard_map/ppermute | solution.py:27
  27.9 4.1 %collective-permute-done.4 = f32[16,32,128]{2,1,0:T(8,128)S(1)} collective-permute-done((f32[16,32,128]{2,1,0:T(8,128)S(1)}, f32[16,32,128]{2,1,0:T(8,128)S(1)}, u32[]{:S(2)}, u32[]{:S(2)}) %collective-permute-start.4) | collective-permute-done | bytes 262176 | tf_op jit(solution)/shard_map/ppermute | solution.py:24
  32.4 5.3 %collective-permute-start.7 = (f32[64,16,128]{2,1,0:T(8,128)S(1)}, f32[64,16,128]{2,1,0:T(8,128)S(1)}, u32[]{:S(2)}, u32[]{:S(2)}) collective-permute-start(f32[64,16,128]{2,1,0:T(8,128)S(1)} %get-tuple-element.39), channel_id=1, source_target_pairs={{1,0},{2,1},{3,2},{4,3},{5,4},{6,5},{7,6},{8,7},{9,8},{10,9},{11,1... | collective-permute-start | bytes 1572872 | tf_op jit(solution)/shard_map/ppermute | solution.py:27
  37.8 12.3 %collective-permute-done.6 = f32[64,16,128]{2,1,0:T(8,128)S(1)} collective-permute-done((f32[64,16,128]{2,1,0:T(8,128)S(1)}, f32[64,16,128]{2,1,0:T(8,128)S(1)}, u32[]{:S(2)}, u32[]{:S(2)}) %collective-permute-start.6) | collective-permute-done | bytes 524320 | tf_op jit(solution)/shard_map/ppermute | solution.py:24
  51.9 1.3 fusion.71
  53.6 1.4 collective-permute-start.9
  55.0 6.9 %collective-permute-done.8 = f32[32,32,128]{2,1,0:T(8,128)S(1)} collective-permute-done((f32[32,32,128]{2,1,0:T(8,128)S(1)}, f32[32,32,128]{2,1,0:T(8,128)S(1)}, u32[]{:S(2)}, u32[]{:S(2)}) %collective-permute-start.8) | collective-permute-done | bytes 524320 | tf_op jit(solution)/shard_map/ppermute | solution.py:24
  61.9 1.4 fusion.25
  63.2 5.5 %collective-permute-start.11 = (f32[64,32,128]{2,1,0:T(8,128)}, f32[64,32,128]{2,1,0:T(8,128)}, u32[]{:S(2)}, u32[]{:S(2)}) collective-permute-start(f32[64,32,128]{2,1,0:T(8,128)} %fusion.25), channel_id=1, source_target_pairs={{1,0},{2,1},{3,2},{4,3},{5,4},{6,5},{7,6},{8,7},{9,8},{10,9},{11,1... | collective-permute-start | bytes 3145736 | tf_op jit(solution)/shard_map/ppermute | solution.py:27
  69.8 1.1 abs_reduce_fusion.1
  70.9 5.0 %maximum_bitcast_fusion = (f32[1,4]{1,0:T(1,128)S(1)}, f32[1,4]{1,0:T(1,128)S(1)}) fusion(f32[1]{0:T(128)} %bitcast.3, f32[1]{0:T(128)} %bitcast.2, f32[1]{0:T(128)} %bitcast.1, f32[1]{0:T(128)} %bitcast, f32[1]{0:T(128)} %bitcast.8, f32[1]{0:T(128)} %bitcast.7, f32[1]{0:T(128)} %bitcast.6, f32[1]{0:T(128)} %bitcast.5), kind=kLoop, calls=%fused_computation.136 | loop fusion | flops 24 | bytes 64 | tf_op jit(solution)/shard_map/stack | solution.py:95
  76.0 16.4 %collective-permute-done.11 = f32[64,32,128]{2,1,0:T(8,128)} collective-permute-done((f32[64,32,128]{2,1,0:T(8,128)}, f32[64,32,128]{2,1,0:T(8,128)}, u32[]{:S(2)}, u32[]{:S(2)}) %collective-permute-start.11) | collective-permute-done | bytes 1048608 | tf_op jit(solution)/shard_map/ppermute | solution.py:27
  92.4 6.1 %collective-permute-done.10 = f32[64,32,128]{2,1,0:T(8,128)} collective-permute-done((f32[64,32,128]{2,1,0:T(8,128)}, f32[64,32,128]{2,1,0:T(8,128)}, u32[]{:S(2)}, u32[]{:S(2)}) %collective-permute-start.10) | collective-permute-done | bytes 1048608 | tf_op jit(solution)/shard_map/ppermute | solution.py:24
  98.4 3.2 %fusion.40 = f32[64,32,128]{2,1,0:T(8,128)S(1)} fusion(f32[64,32,128]{2,1,0:T(8,128)} %collective-permute-done.11, f32[64,32,128]{2,1,0:T(8,128)} %fusion.25, f32[64,32,128]{2,1,0:T(8,128)} %collective-permute-done.10), kind=kLoop, calls=%fused_computation.66 | loop fusion | flops 2883584 | bytes 4194304 | tf_op jit(solution)/shard_map/add | solution.py:37
  103.1 2.3 %fusion.73 = (f32[64,32,128]{2,1,0:T(8,128)S(1)}, f32[64,32,128]{2,1,0:T(8,128)}) fusion(f32[64,32,128]{2,1,0:T(8,128)S(1)} %get-tuple-element.17, f32[64,32,32]{2,1,0:T(8,128)S(1)} %get-tuple-element.21, f32[64,32,96]{2,1,0:T(8,128)S(1)} %get-tuple-element.23, f32[64,32,16]{2,1,0:T(8,128)S(1)} %get-tuple-element.25, ...), kind=kLoop, calls=%fused_computation.142 | loop fusion | flops 3670016 | bytes 8388608 | tf_op jit(solution)/shard_map/sub | solution.py:93
  106.4 2.5 %maximum_bitcast_fusion.2 = f32[1,4]{1,0:T(1,128)S(1)} fusion(f32[1]{0:T(128)} %bitcast.13, f32[1]{0:T(128)} %bitcast.12, f32[1]{0:T(128)} %bitcast.11, f32[1]{0:T(128)} %bitcast.10), kind=kLoop, calls=%fused_computation.138 | loop fusion | flops 12 | bytes 32 | tf_op jit(solution)/shard_map/stack | solution.py:95
  110.5 1.3 collective-permute-start.13
  111.8 2.5 %collective-permute-done.13 = f32[3,4,2,4]{3,2,1,0:T(2,128)S(1)} collective-permute-done((f32[3,4,2,4]{3,2,1,0:T(2,128)S(1)}, f32[3,4,2,4]{3,2,1,0:T(2,128)S(1)}, u32[]{:S(2)}, u32[]{:S(2)}) %collective-permute-start.13) | collective-permute-done | bytes 416 | tf_op jit(solution)/shard_map/ppermute | solution.py:77
  114.3 1.4 collective-permute-start.14
  115.8 3.9 %collective-permute-done.14 = f32[3,4,2,4]{3,2,1,0:T(2,128)S(1)} collective-permute-done((f32[3,4,2,4]{3,2,1,0:T(2,128)S(1)}, f32[3,4,2,4]{3,2,1,0:T(2,128)S(1)}, u32[]{:S(2)}, u32[]{:S(2)}) %collective-permute-start.14) | collective-permute-done | bytes 416 | tf_op jit(solution)/shard_map/ppermute | solution.py:77
  119.7 3.7 %collective-permute-done.15 = f32[3,4,2,4]{3,2,1,0:T(2,128)S(1)} collective-permute-done((f32[3,4,2,4]{3,2,1,0:T(2,128)S(1)}, f32[3,4,2,4]{3,2,1,0:T(2,128)S(1)}, u32[]{:S(2)}, u32[]{:S(2)}) %collective-permute-start.15) | collective-permute-done | bytes 416 | tf_op jit(solution)/shard_map/ppermute | solution.py:77
  123.5 4.6 %collective-permute-done.16 = f32[3,4,2,4]{3,2,1,0:T(2,128)S(1)} collective-permute-done((f32[3,4,2,4]{3,2,1,0:T(2,128)S(1)}, f32[3,4,2,4]{3,2,1,0:T(2,128)S(1)}, u32[]{:S(2)}, u32[]{:S(2)}) %collective-permute-start.16) | collective-permute-done | bytes 416 | tf_op jit(solution)/shard_map/ppermute | solution.py:77
  128.2 7.6 %collective-permute-done.17 = f32[3,4,2,4]{3,2,1,0:T(2,128)S(1)} collective-permute-done((f32[3,4,2,4]{3,2,1,0:T(2,128)S(1)}, f32[3,4,2,4]{3,2,1,0:T(2,128)S(1)}, u32[]{:S(2)}, u32[]{:S(2)}) %collective-permute-start.17) | collective-permute-done | bytes 416 | tf_op jit(solution)/shard_map/ppermute | solution.py:77
  135.9 3.7 %collective-permute-done.18 = f32[3,4,2,4]{3,2,1,0:T(2,128)S(1)} collective-permute-done((f32[3,4,2,4]{3,2,1,0:T(2,128)S(1)}, f32[3,4,2,4]{3,2,1,0:T(2,128)S(1)}, u32[]{:S(2)}, u32[]{:S(2)}) %collective-permute-start.18) | collective-permute-done | bytes 416 | tf_op jit(solution)/shard_map/ppermute | solution.py:77
  139.7 5.2 %collective-permute-done.19 = f32[3,4,2,4]{3,2,1,0:T(2,128)S(1)} collective-permute-done((f32[3,4,2,4]{3,2,1,0:T(2,128)S(1)}, f32[3,4,2,4]{3,2,1,0:T(2,128)S(1)}, u32[]{:S(2)}, u32[]{:S(2)}) %collective-permute-start.19) | collective-permute-done | bytes 416 | tf_op jit(solution)/shard_map/ppermute | solution.py:77
  (60 shorter events, 12.4 us)
Async XLA Ops:
  1.6 4.4 %collective-permute-start = (f32[8,32,128]{2,1,0:T(8,128)S(1)}, f32[8,32,128]{2,1,0:T(8,128)S(1)}, u32[]{:S(2)}, u32[]{:S(2)}) collective-permute-start(f32[8,32,128]{2,1,0:T(8,128)S(1)} %get-tuple-element.54), channel_id=1, source_target_pairs={{0,32},{32,64},{64,96},{96,128},{128,160},{160,192},{192,224},{224... | collective-permute-start | bytes 393224 | tf_op jit(solution)/shard_map/ppermute | solution.py:24
  1.6 6.0 %collective-permute-start.1 = (f32[8,32,128]{2,1,0:T(8,128)S(1)}, f32[8,32,128]{2,1,0:T(8,128)S(1)}, u32[]{:S(2)}, u32[]{:S(2)}) collective-permute-start(f32[8,32,128]{2,1,0:T(8,128)S(1)} %get-tuple-element.55), channel_id=1, source_target_pairs={{32,0},{64,32},{96,64},{128,96},{160,128},{192,160},{224,192},{0,2... | collective-permute-start | bytes 393224 | tf_op jit(solution)/shard_map/ppermute | solution.py:27
  6.0 1.6 %copy-start = (f32[64,32,128]{2,1,0:T(8,128)S(1)}, f32[64,32,128]{2,1,0:T(8,128)}, u32[]{:S(2)}) copy-start(f32[64,32,128]{2,1,0:T(8,128)} %param.1) | copy-start | bytes 3145732
  8.1 14.7 %collective-permute-start.2 = (f32[64,8,128]{2,1,0:T(8,128)S(1)}, f32[64,8,128]{2,1,0:T(8,128)S(1)}, u32[]{:S(2)}, u32[]{:S(2)}) collective-permute-start(f32[64,8,128]{2,1,0:T(8,128)S(1)} %get-tuple-element.50), channel_id=1, source_target_pairs={{0,1},{1,2},{2,3},{3,4},{4,5},{5,6},{6,7},{7,8},{8,9},{9,10},{10,1... | collective-permute-start | bytes 786440 | tf_op jit(solution)/shard_map/ppermute | solution.py:24
  10.1 12.7 %collective-permute-start.3 = (f32[64,8,128]{2,1,0:T(8,128)S(1)}, f32[64,8,128]{2,1,0:T(8,128)S(1)}, u32[]{:S(2)}, u32[]{:S(2)}) collective-permute-start(f32[64,8,128]{2,1,0:T(8,128)S(1)} %get-tuple-element.51), channel_id=1, source_target_pairs={{1,0},{2,1},{3,2},{4,3},{5,4},{6,5},{7,6},{8,7},{9,8},{10,9},{11,1... | collective-permute-start | bytes 786440 | tf_op jit(solution)/shard_map/ppermute | solution.py:27
  26.2 5.8 %collective-permute-start.4 = (f32[16,32,128]{2,1,0:T(8,128)S(1)}, f32[16,32,128]{2,1,0:T(8,128)S(1)}, u32[]{:S(2)}, u32[]{:S(2)}) collective-permute-start(f32[16,32,128]{2,1,0:T(8,128)S(1)} %get-tuple-element.40), channel_id=1, source_target_pairs={{0,32},{32,64},{64,96},{96,128},{128,160},{160,192},{192,224},{224... | collective-permute-start | bytes 786440 | tf_op jit(solution)/shard_map/ppermute | solution.py:24
  26.2 5.8 %collective-permute-start.5 = (f32[16,32,128]{2,1,0:T(8,128)S(1)}, f32[16,32,128]{2,1,0:T(8,128)S(1)}, u32[]{:S(2)}, u32[]{:S(2)}) collective-permute-start(f32[16,32,128]{2,1,0:T(8,128)S(1)} %get-tuple-element.41), channel_id=1, source_target_pairs={{32,0},{64,32},{96,64},{128,96},{160,128},{192,160},{224,192},{0,2... | collective-permute-start | bytes 786440 | tf_op jit(solution)/shard_map/ppermute | solution.py:27
  32.4 17.7 %collective-permute-start.6 = (f32[64,16,128]{2,1,0:T(8,128)S(1)}, f32[64,16,128]{2,1,0:T(8,128)S(1)}, u32[]{:S(2)}, u32[]{:S(2)}) collective-permute-start(f32[64,16,128]{2,1,0:T(8,128)S(1)} %get-tuple-element.38), channel_id=1, source_target_pairs={{0,1},{1,2},{2,3},{3,4},{4,5},{5,6},{6,7},{7,8},{8,9},{9,10},{10,1... | collective-permute-start | bytes 1572872 | tf_op jit(solution)/shard_map/ppermute | solution.py:24
  32.4 17.6 %collective-permute-start.7 = (f32[64,16,128]{2,1,0:T(8,128)S(1)}, f32[64,16,128]{2,1,0:T(8,128)S(1)}, u32[]{:S(2)}, u32[]{:S(2)}) collective-permute-start(f32[64,16,128]{2,1,0:T(8,128)S(1)} %get-tuple-element.39), channel_id=1, source_target_pairs={{1,0},{2,1},{3,2},{4,3},{5,4},{6,5},{7,6},{8,7},{9,8},{10,9},{11,1... | collective-permute-start | bytes 1572872 | tf_op jit(solution)/shard_map/ppermute | solution.py:27
  53.3 8.6 %collective-permute-start.8 = (f32[32,32,128]{2,1,0:T(8,128)S(1)}, f32[32,32,128]{2,1,0:T(8,128)S(1)}, u32[]{:S(2)}, u32[]{:S(2)}) collective-permute-start(f32[32,32,128]{2,1,0:T(8,128)S(1)} %get-tuple-element.28), channel_id=1, source_target_pairs={{0,32},{32,64},{64,96},{96,128},{128,160},{160,192},{192,224},{224... | collective-permute-start | bytes 1572872 | tf_op jit(solution)/shard_map/ppermute | solution.py:24
  53.6 8.3 %collective-permute-start.9 = (f32[32,32,128]{2,1,0:T(8,128)S(1)}, f32[32,32,128]{2,1,0:T(8,128)S(1)}, u32[]{:S(2)}, u32[]{:S(2)}) collective-permute-start(f32[32,32,128]{2,1,0:T(8,128)S(1)} %get-tuple-element.29), channel_id=1, source_target_pairs={{32,0},{64,32},{96,64},{128,96},{160,128},{192,160},{224,192},{0,2... | collective-permute-start | bytes 1572872 | tf_op jit(solution)/shard_map/ppermute | solution.py:27
  63.2 29.1 %collective-permute-start.11 = (f32[64,32,128]{2,1,0:T(8,128)}, f32[64,32,128]{2,1,0:T(8,128)}, u32[]{:S(2)}, u32[]{:S(2)}) collective-permute-start(f32[64,32,128]{2,1,0:T(8,128)} %fusion.25), channel_id=1, source_target_pairs={{1,0},{2,1},{3,2},{4,3},{5,4},{6,5},{7,6},{8,7},{9,8},{10,9},{11,1... | collective-permute-start | bytes 3145736 | tf_op jit(solution)/shard_map/ppermute | solution.py:27
  68.8 29.7 %collective-permute-start.10 = (f32[64,32,128]{2,1,0:T(8,128)}, f32[64,32,128]{2,1,0:T(8,128)}, u32[]{:S(2)}, u32[]{:S(2)}) collective-permute-start(f32[64,32,128]{2,1,0:T(8,128)} %fusion.25), channel_id=1, source_target_pairs={{0,1},{1,2},{2,3},{3,4},{4,5},{5,6},{6,7},{7,8},{8,9},{9,10},{10,1... | collective-permute-start | bytes 3145736 | tf_op jit(solution)/shard_map/ppermute | solution.py:24
  109.1 1.3 collective-permute-start.12
  110.5 3.8 %collective-permute-start.13 = (f32[3,4,2,4]{3,2,1,0:T(2,128)S(1)}, f32[3,4,2,4]{3,2,1,0:T(2,128)S(1)}, u32[]{:S(2)}, u32[]{:S(2)}) collective-permute-start(f32[3,4,2,4]{3,2,1,0:T(2,128)S(1)} %fusion.68), channel_id=1, source_target_pairs={{0,64},{32,96},{64,0},{96,32},{128,192},{160,224},{192,128},{224,1... | collective-permute-start | bytes 1160 | tf_op jit(solution)/shard_map/ppermute | solution.py:77
  114.3 5.3 %collective-permute-start.14 = (f32[3,4,2,4]{3,2,1,0:T(2,128)S(1)}, f32[3,4,2,4]{3,2,1,0:T(2,128)S(1)}, u32[]{:S(2)}, u32[]{:S(2)}) collective-permute-start(f32[3,4,2,4]{3,2,1,0:T(2,128)S(1)} %fusion.92), channel_id=1, source_target_pairs={{0,128},{32,160},{64,192},{96,224},{128,0},{160,32},{192,64},{224,... | collective-permute-start | bytes 1160 | tf_op jit(solution)/shard_map/ppermute | solution.py:77
  119.6 3.8 %collective-permute-start.15 = (f32[3,4,2,4]{3,2,1,0:T(2,128)S(1)}, f32[3,4,2,4]{3,2,1,0:T(2,128)S(1)}, u32[]{:S(2)}, u32[]{:S(2)}) collective-permute-start(f32[3,4,2,4]{3,2,1,0:T(2,128)S(1)} %add.178), channel_id=1, source_target_pairs={{0,1},{1,0},{2,3},{3,2},{4,5},{5,4},{6,7},{7,6},{8,9},{9,8},{10,11... | collective-permute-start | bytes 1160 | tf_op jit(solution)/shard_map/ppermute | solution.py:77
  123.4 4.7 %collective-permute-start.16 = (f32[3,4,2,4]{3,2,1,0:T(2,128)S(1)}, f32[3,4,2,4]{3,2,1,0:T(2,128)S(1)}, u32[]{:S(2)}, u32[]{:S(2)}) collective-permute-start(f32[3,4,2,4]{3,2,1,0:T(2,128)S(1)} %add.179), channel_id=1, source_target_pairs={{0,2},{1,3},{2,0},{3,1},{4,6},{5,7},{6,4},{7,5},{8,10},{9,11},{10,... | collective-permute-start | bytes 1160 | tf_op jit(solution)/shard_map/ppermute | solution.py:77
  128.1 7.7 %collective-permute-start.17 = (f32[3,4,2,4]{3,2,1,0:T(2,128)S(1)}, f32[3,4,2,4]{3,2,1,0:T(2,128)S(1)}, u32[]{:S(2)}, u32[]{:S(2)}) collective-permute-start(f32[3,4,2,4]{3,2,1,0:T(2,128)S(1)} %add.180), channel_id=1, source_target_pairs={{0,4},{1,5},{2,6},{3,7},{4,0},{5,1},{6,2},{7,3},{8,12},{9,13},{10,... | collective-permute-start | bytes 1160 | tf_op jit(solution)/shard_map/ppermute | solution.py:77
  135.8 3.8 %collective-permute-start.18 = (f32[3,4,2,4]{3,2,1,0:T(2,128)S(1)}, f32[3,4,2,4]{3,2,1,0:T(2,128)S(1)}, u32[]{:S(2)}, u32[]{:S(2)}) collective-permute-start(f32[3,4,2,4]{3,2,1,0:T(2,128)S(1)} %add.181), channel_id=1, source_target_pairs={{0,8},{1,9},{2,10},{3,11},{4,12},{5,13},{6,14},{7,15},{8,0},{9,1},... | collective-permute-start | bytes 1160 | tf_op jit(solution)/shard_map/ppermute | solution.py:77
  139.6 5.3 %collective-permute-start.19 = (f32[3,4,2,4]{3,2,1,0:T(2,128)S(1)}, f32[3,4,2,4]{3,2,1,0:T(2,128)S(1)}, u32[]{:S(2)}, u32[]{:S(2)}) collective-permute-start(f32[3,4,2,4]{3,2,1,0:T(2,128)S(1)} %add.182), channel_id=1, source_target_pairs={{0,16},{1,17},{2,18},{3,19},{4,20},{5,21},{6,22},{7,23},{8,24},{9,... | collective-permute-start | bytes 1160 | tf_op jit(solution)/shard_map/ppermute | solution.py:77

commit v2 on v1

--- a/solution.py
+++ b/solution.py
@@ -49,14 +49,8 @@
 
 def moment_sums(detail):
     square = detail * detail
-    return jnp.stack(
-        [
-            jnp.sum(jnp.abs(detail)),
-            jnp.sum(square),
-            jnp.sum(square * detail),
-            jnp.sum(square * square),
-        ]
-    )
+    powers = jnp.stack([jnp.abs(detail), square, square * detail, square * square])
+    return jnp.sum(powers.reshape(4, -1), axis=1)
 
 
 def finish_table(table, planes):
@@ -67,16 +61,13 @@
     return jnp.stack([means[:, 0], second, third, fourth], axis=1)
 
 
-def butterfly_sum(table, axes):
+def gather_partials(partial, axes):
+    count = 1
     for axis in axes:
-        count = lax.axis_size(axis)
-        assert count & (count - 1) == 0
-        step = 1
-        while step < count:
-            pairs = [(i, i ^ step) for i in range(count)]
-            table = table + lax.ppermute(table, axis, pairs)
-            step *= 2
-    return table
+        count *= lax.axis_size(axis)
+    flat = partial.reshape(1, -1)
+    sent = jnp.broadcast_to(flat, (count, flat.shape[1]))
+    return lax.all_to_all(sent, axes, 0, 0, tiled=True)
 
 
 def per_device(density):
@@ -95,14 +86,11 @@
     partial = jnp.stack(sums)
     count_x = lax.axis_size("row") * size_x // SUB
     count_y = lax.axis_size("col") * size_y // SUB
-    block_x = lax.axis_index("row") * size_x // SUB
-    block_y = lax.axis_index("col") * size_y // SUB
-    onehot_x = (jnp.arange(count_x, dtype=jnp.int32) == block_x).astype(jnp.float32)
-    onehot_y = (jnp.arange(count_y, dtype=jnp.int32) == block_y).astype(jnp.float32)
-    partial_table = (
-        partial[:, :, None, None] * onehot_x[None, None, :, None] * onehot_y[None, None, None, :]
-    )
-    table = butterfly_sum(partial_table, ("row", "col"))
+    gathered = gather_partials(partial, ("row", "col"))
+    per_x = SUB // size_x
+    per_y = SUB // size_y
+    grouped = gathered.reshape(count_x, per_x, count_y, per_y, len(SPACINGS), 4)
+    table = jnp.transpose(jnp.sum(grouped, axis=(1, 3)), (2, 3, 0, 1))
     return (current, finish_table(table, planes))
 
 

time: 146 us -> 126 us (0.86); the launches traced: 146 us -> 124 us
  waiting for transfers between devices: 86.9 us -> 46.5 us
  blocking collectives: 0 us -> 22.1 us
  starting transfers between devices: 27.8 us -> 24.8 us
    ppermute x8 -> x0, waiting for transfers between devices: 32.2 us -> none  [butterfly_sum(): table = table + lax.ppermute(table, axis, pairs)]
    all_to_all x0 -> x1, blocking collectives: none -> 22.1 us  [gather_partials(): return lax.all_to_all(sent, axes, 0, 0, tiled=True)]
    ppermute x6, waiting for transfers between devices: 16.4 us -> 0.02 us  [padded_1(): lax.ppermute(lax.slice_in_dim(block, 0, width, axis=dim), axis, backward)]
    reduce_sum x3 -> x4, other arithmetic: 3.13 us -> 12.7 us  [the longest x3 12.6 us: moment_sums(): return jnp.sum(powers.reshape(4, -1), axis=1)]
    ppermute x6, waiting for transfers between devices: 38.3 us -> 46.5 us  [padded_1(): lax.ppermute(lax.slice_in_dim(block, block.shape[dim] - width, None, axis...]
    another operation x3 -> x1, other arithmetic: 7.59 us -> 0.01 us  [per_device(): partial = jnp.stack(sums)]
    abs x0 -> x3, other arithmetic: none -> 5.06 us  [moment_sums(): jnp.abs(detail)]
    sub x3 -> x0, other arithmetic: 4.89 us -> none  [per_device(): sums.append(moment_sums(current - smoother))]
  transfers between devices with their start and end apart: 20 -> 12, of which waited for: 15 -> 6; matrix products, arithmetic and copies ran while one was open for 6% -> 9% of each run, Pallas kernels for 0% -> 0%
where the time goes in v2:
time: 126 us; the launch traced here: 124 us
  waiting for transfers between devices  46.5 us (37%)
  starting transfers between devices  24.8 us (20%)
  blocking collectives  22.1 us (18%)
  other arithmetic  21.9 us (17%)
  local copies, waits for them, and re-layouts  7.75 us (6%)
    ppermute x6, waiting for transfers between devices, padded_1(): lax.ppermute(lax.slice_in_dim(block, block.shape[dim] - width, None, axis...  46.5 us
    all_to_all x1, blocking collectives, gather_partials(): return lax.all_to_all(sent, axes, 0, 0, tiled=True)  22.1 us
    ppermute x6, starting transfers between devices, padded_1(): lax.ppermute(lax.slice_in_dim(block, 0, width, axis=dim), axis, backward)  22.1 us
    reduce_sum x3, other arithmetic, moment_sums(): return jnp.sum(powers.reshape(4, -1), axis=1)  12.6 us
    abs x3, other arithmetic, moment_sums(): jnp.abs(detail)  5.06 us
    slice x12, local copies, waits for them, and re-layouts, depth_pass(): jnp.roll(values_in, -(tap_index - 2) * spacing, axis=2)  4.45 us
    ppermute x6, starting transfers between devices, padded_1(): lax.ppermute(lax.slice_in_dim(block, block.shape[dim] - width, None, axis...  2.72 us
  transfers between devices with their start and end apart: 12, of which 6 were waited for; matrix products, arithmetic and copies ran while one was open for 9% of the time, Pallas kernels for 0%

profile of v2, /device:TPU:8, one launch (start us, length us, event | category | flops | bytes accessed | tf_op | source)
XLA Modules:
  0.0 123.9 jit_solution(3622781618294092105)
XLA Ops:
  0.6 1.0 fusion.84
  1.6 1.7 %collective-permute-start.1 = (f32[8,32,128]{2,1,0:T(8,128)S(1)}, f32[8,32,128]{2,1,0:T(8,128)S(1)}, u32[]{:S(2)}, u32[]{:S(2)}) collective-permute-start(f32[8,32,128]{2,1,0:T(8,128)S(1)} %get-tuple-element.55), channel_id=1, source_target_pairs={{32,0},{64,32},{96,64},{128,96},{160,128},{192,160},{224,192},{0,2... | collective-permute-start | bytes 393224 | tf_op jit(solution)/shard_map/ppermute | solution.py:27
  3.4 2.6 %collective-permute-done = f32[8,32,128]{2,1,0:T(8,128)S(1)} collective-permute-done((f32[8,32,128]{2,1,0:T(8,128)S(1)}, f32[8,32,128]{2,1,0:T(8,128)S(1)}, u32[]{:S(2)}, u32[]{:S(2)}) %collective-permute-start) | collective-permute-done | bytes 131104 | tf_op jit(solution)/shard_map/ppermute | solution.py:24
  6.1 1.6 %constant_dynamic-update-slice_fusion = (f32[72,32,128]{2,1,0:T(8,128)S(1)}, f32[72,32,128]{2,1,0:T(8,128)S(1)}) fusion(f32[72,32,128]{2,1,0:T(8,128)S(1)} %constant_dynamic-update-slice_fusion.1, f32[64,32,128]{2,1,0:T(8,128)} %param.1), kind=kLoop, calls=%fused_computation.115 | loop fusion | bytes 3145728 | tf_op jit(solution)/shard_map/concatenate | solution.py:28
  7.7 0.4 fusion.46
  8.1 2.0 %collective-permute-start.2 = (f32[64,8,128]{2,1,0:T(8,128)S(1)}, f32[64,8,128]{2,1,0:T(8,128)S(1)}, u32[]{:S(2)}, u32[]{:S(2)}) collective-permute-start(f32[64,8,128]{2,1,0:T(8,128)S(1)} %get-tuple-element.50), channel_id=1, source_target_pairs={{0,1},{1,2},{2,3},{3,4},{4,5},{5,6},{6,7},{7,8},{8,9},{9,10},{10,1... | collective-permute-start | bytes 786440 | tf_op jit(solution)/shard_map/ppermute | solution.py:24
  10.1 6.2 %collective-permute-start.3 = (f32[64,8,128]{2,1,0:T(8,128)S(1)}, f32[64,8,128]{2,1,0:T(8,128)S(1)}, u32[]{:S(2)}, u32[]{:S(2)}) collective-permute-start(f32[64,8,128]{2,1,0:T(8,128)S(1)} %get-tuple-element.51), channel_id=1, source_target_pairs={{1,0},{2,1},{3,2},{4,3},{5,4},{6,5},{7,6},{8,7},{9,8},{10,9},{11,1... | collective-permute-start | bytes 786440 | tf_op jit(solution)/shard_map/ppermute | solution.py:27
  16.3 6.5 %collective-permute-done.2 = f32[64,8,128]{2,1,0:T(8,128)S(1)} collective-permute-done((f32[64,8,128]{2,1,0:T(8,128)S(1)}, f32[64,8,128]{2,1,0:T(8,128)S(1)}, u32[]{:S(2)}, u32[]{:S(2)}) %collective-permute-start.2) | collective-permute-done | bytes 262176 | tf_op jit(solution)/shard_map/ppermute | solution.py:24
  22.8 0.5 fusion.11
  24.8 1.4 %fusion.62 = (f32[64,32,128]{2,1,0:T(8,128)S(1)}, f32[64,32,128]{2,1,0:T(8,128)S(1)}, f32[64,32,128]{2,1,0:T(8,128)S(1)}) fusion(f32[64,32,128]{2,1,0:T(8,128)S(1)} %copy-done, f32[64,32,8]{2,1,0:T(8,128)S(1)} %get-tuple-element.43, f32[64,32,120]{2,1,0:T(8,128)S(1)} %get-tuple-element.45, f32[64,32,4]{2,1,0:T(8,128)S(1)} %get-tuple-element.47, ...), kind=kLoop, calls=%fused_computation.123 | loop fusion | flops 3932160 | bytes 9437184 | tf_op jit(solution)/shard_map/abs | solution.py:52
  26.3 1.7 %collective-permute-start.5 = (f32[16,32,128]{2,1,0:T(8,128)S(1)}, f32[16,32,128]{2,1,0:T(8,128)S(1)}, u32[]{:S(2)}, u32[]{:S(2)}) collective-permute-start(f32[16,32,128]{2,1,0:T(8,128)S(1)} %get-tuple-element.41), channel_id=1, source_target_pairs={{32,0},{64,32},{96,64},{128,96},{160,128},{192,160},{224,192},{0,2... | collective-permute-start | bytes 786440 | tf_op jit(solution)/shard_map/ppermute | solution.py:27
  28.0 4.1 %collective-permute-done.4 = f32[16,32,128]{2,1,0:T(8,128)S(1)} collective-permute-done((f32[16,32,128]{2,1,0:T(8,128)S(1)}, f32[16,32,128]{2,1,0:T(8,128)S(1)}, u32[]{:S(2)}, u32[]{:S(2)}) %collective-permute-start.4) | collective-permute-done | bytes 262176 | tf_op jit(solution)/shard_map/ppermute | solution.py:24
  32.5 5.3 %collective-permute-start.7 = (f32[64,16,128]{2,1,0:T(8,128)S(1)}, f32[64,16,128]{2,1,0:T(8,128)S(1)}, u32[]{:S(2)}, u32[]{:S(2)}) collective-permute-start(f32[64,16,128]{2,1,0:T(8,128)S(1)} %get-tuple-element.39), channel_id=1, source_target_pairs={{1,0},{2,1},{3,2},{4,3},{5,4},{6,5},{7,6},{8,7},{9,8},{10,9},{11,1... | collective-permute-start | bytes 1572872 | tf_op jit(solution)/shard_map/ppermute | solution.py:27
  37.9 12.3 %collective-permute-done.6 = f32[64,16,128]{2,1,0:T(8,128)S(1)} collective-permute-done((f32[64,16,128]{2,1,0:T(8,128)S(1)}, f32[64,16,128]{2,1,0:T(8,128)S(1)}, u32[]{:S(2)}, u32[]{:S(2)}) %collective-permute-start.6) | collective-permute-done | bytes 524320 | tf_op jit(solution)/shard_map/ppermute | solution.py:24
  52.0 1.4 %fusion.64 = (f32[64,32,128]{2,1,0:T(8,128)S(1)}, f32[64,32,128]{2,1,0:T(8,128)S(1)}, f32[64,32,128]{2,1,0:T(8,128)S(1)}) fusion(f32[64,32,128]{2,1,0:T(8,128)S(1)} %get-tuple-element.4, f32[64,32,16]{2,1,0:T(8,128)S(1)} %get-tuple-element.31, f32[64,32,112]{2,1,0:T(8,128)S(1)} %get-tuple-element.33, f32[64,32,8]{2,1,0:T(8,128)S(1)} %get-tuple-element.35, ...), kind=kLoop, calls=%fused_computation.124 | loop fusion | flops 3932160 | bytes 9437184 | tf_op jit(solution)/shard_map/abs | solution.py:52
  53.8 1.4 %collective-permute-start.9 = (f32[32,32,128]{2,1,0:T(8,128)S(1)}, f32[32,32,128]{2,1,0:T(8,128)S(1)}, u32[]{:S(2)}, u32[]{:S(2)}) collective-permute-start(f32[32,32,128]{2,1,0:T(8,128)S(1)} %get-tuple-element.29), channel_id=1, source_target_pairs={{32,0},{64,32},{96,64},{128,96},{160,128},{192,160},{224,192},{0,2... | collective-permute-start | bytes 1572872 | tf_op jit(solution)/shard_map/ppermute | solution.py:27
  55.2 0.4 multiply_multiply_fusion.5
  55.6 6.5 %collective-permute-done.8 = f32[32,32,128]{2,1,0:T(8,128)S(1)} collective-permute-done((f32[32,32,128]{2,1,0:T(8,128)S(1)}, f32[32,32,128]{2,1,0:T(8,128)S(1)}, u32[]{:S(2)}, u32[]{:S(2)}) %collective-permute-start.8) | collective-permute-done | bytes 524320 | tf_op jit(solution)/shard_map/ppermute | solution.py:24
  62.1 0.4 fusion.19
  62.7 5.6 %collective-permute-start.11 = (f32[64,32,128]{2,1,0:T(8,128)S(1)}, f32[64,32,128]{2,1,0:T(8,128)S(1)}, u32[]{:S(2)}, u32[]{:S(2)}) collective-permute-start(f32[64,32,128]{2,1,0:T(8,128)S(1)} %fusion.19), channel_id=1, source_target_pairs={{1,0},{2,1},{3,2},{4,3},{5,4},{6,5},{7,6},{8,7},{9,8},{10,9},{11,1... | collective-permute-start | bytes 3145736 | tf_op jit(solution)/shard_map/ppermute | solution.py:27
  68.3 4.2 %maximum_reduce_fusion = f32[4]{0:T(128)S(1)} fusion(f32[1,262144]{1,0:T(1,128)S(1)} %bitcast.21, f32[1,262144]{1,0:T(1,128)S(1)} %bitcast.19, f32[1,262144]{1,0:T(1,128)S(1)} %bitcast.20, f32[1,262144]{1,0:T(1,128)S(1)} %bitcast.28), kind=kLoop, calls=%fused_computation | loop fusion | flops 4194300 | bytes 4194320 | tf_op jit(solution)/shard_map/reduce_sum | solution.py:53
  72.5 0.4 multiply_multiply_fusion.3
  72.9 4.2 %maximum_reduce_fusion.1 = f32[4]{0:T(128)S(1)} fusion(f32[1,262144]{1,0:T(1,128)S(1)} %bitcast.24, f32[1,262144]{1,0:T(1,128)S(1)} %bitcast.22, f32[1,262144]{1,0:T(1,128)S(1)} %bitcast.23, f32[1,262144]{1,0:T(1,128)S(1)} %bitcast.29), kind=kLoop, calls=%fused_computation.1 | loop fusion | flops 4194300 | bytes 4194320 | tf_op jit(solution)/shard_map/reduce_sum | solution.py:53
  77.1 14.6 %collective-permute-done.10 = f32[64,32,128]{2,1,0:T(8,128)S(1)} collective-permute-done((f32[64,32,128]{2,1,0:T(8,128)S(1)}, f32[64,32,128]{2,1,0:T(8,128)S(1)}, u32[]{:S(2)}, u32[]{:S(2)}) %collective-permute-start.10) | collective-permute-done | bytes 1048608 | tf_op jit(solution)/shard_map/ppermute | solution.py:24
  91.7 0.4 fusion.34
  92.5 0.4 fusion.69
  92.9 0.4 fusion.70
  93.6 2.3 %fusion.66 = (f32[64,32,128]{2,1,0:T(8,128)S(1)}, f32[64,32,128]{2,1,0:T(8,128)S(1)}, f32[64,32,128]{2,1,0:T(8,128)}) fusion(f32[64,32,128]{2,1,0:T(8,128)S(1)} %get-tuple-element.7, f32[64,32,32]{2,1,0:T(8,128)S(1)} %get-tuple-element.21, f32[64,32,96]{2,1,0:T(8,128)S(1)} %get-tuple-element.23, f32[64,32,16]{2,1,0:T(8,128)S(1)} %get-tuple-element.25, ...), kind=kLoop, calls=%fused_computation.125 | loop fusion | flops 3932160 | bytes 9437184 | tf_op jit(solution)/shard_map/abs | solution.py:52
  95.9 0.4 multiply_multiply_fusion.1
  96.3 4.2 %maximum_reduce_fusion.2 = f32[4]{0:T(128)S(1)} fusion(f32[1,262144]{1,0:T(1,128)S(1)} %bitcast.27, f32[1,262144]{1,0:T(1,128)S(1)} %bitcast.25, f32[1,262144]{1,0:T(1,128)S(1)} %bitcast.26, f32[1,262144]{1,0:T(1,128)S(1)} %bitcast.30), kind=kLoop, calls=%fused_computation.2 | loop fusion | flops 4194300 | bytes 4194320 | tf_op jit(solution)/shard_map/reduce_sum | solution.py:53
  100.7 22.1 %all_to_all.6 = f32[256,1,12]{2,1,0:T(1,128)S(1)} all-to-all(f32[256,1,12]{2,1,0:T(1,128)S(1)} %broadcast_in_dim.8), channel_id=1, replica_groups=mesh['row'=8,'col'=32] {'row','col'}, dimensions={0} | all-to-all | bytes 24576 | tf_op jit(solution)/shard_map/all_to_all | solution.py:70
  123.3 0.6 pad_maximum_fusion.10
  (40 shorter events, 6.0 us)
Async XLA Ops:
  1.6 4.4 %collective-permute-start = (f32[8,32,128]{2,1,0:T(8,128)S(1)}, f32[8,32,128]{2,1,0:T(8,128)S(1)}, u32[]{:S(2)}, u32[]{:S(2)}) collective-permute-start(f32[8,32,128]{2,1,0:T(8,128)S(1)} %get-tuple-element.54), channel_id=1, source_target_pairs={{0,32},{32,64},{64,96},{96,128},{128,160},{160,192},{192,224},{224... | collective-permute-start | bytes 393224 | tf_op jit(solution)/shard_map/ppermute | solution.py:24
  1.6 6.0 %collective-permute-start.1 = (f32[8,32,128]{2,1,0:T(8,128)S(1)}, f32[8,32,128]{2,1,0:T(8,128)S(1)}, u32[]{:S(2)}, u32[]{:S(2)}) collective-permute-start(f32[8,32,128]{2,1,0:T(8,128)S(1)} %get-tuple-element.55), channel_id=1, source_target_pairs={{32,0},{64,32},{96,64},{128,96},{160,128},{192,160},{224,192},{0,2... | collective-permute-start | bytes 393224 | tf_op jit(solution)/shard_map/ppermute | solution.py:27
  6.0 1.6 %copy-start = (f32[64,32,128]{2,1,0:T(8,128)S(1)}, f32[64,32,128]{2,1,0:T(8,128)}, u32[]{:S(2)}) copy-start(f32[64,32,128]{2,1,0:T(8,128)} %param.1) | copy-start | bytes 3145732
  8.1 14.7 %collective-permute-start.2 = (f32[64,8,128]{2,1,0:T(8,128)S(1)}, f32[64,8,128]{2,1,0:T(8,128)S(1)}, u32[]{:S(2)}, u32[]{:S(2)}) collective-permute-start(f32[64,8,128]{2,1,0:T(8,128)S(1)} %get-tuple-element.50), channel_id=1, source_target_pairs={{0,1},{1,2},{2,3},{3,4},{4,5},{5,6},{6,7},{7,8},{8,9},{9,10},{10,1... | collective-permute-start | bytes 786440 | tf_op jit(solution)/shard_map/ppermute | solution.py:24
  10.1 12.7 %collective-permute-start.3 = (f32[64,8,128]{2,1,0:T(8,128)S(1)}, f32[64,8,128]{2,1,0:T(8,128)S(1)}, u32[]{:S(2)}, u32[]{:S(2)}) collective-permute-start(f32[64,8,128]{2,1,0:T(8,128)S(1)} %get-tuple-element.51), channel_id=1, source_target_pairs={{1,0},{2,1},{3,2},{4,3},{5,4},{6,5},{7,6},{8,7},{9,8},{10,9},{11,1... | collective-permute-start | bytes 786440 | tf_op jit(solution)/shard_map/ppermute | solution.py:27
  26.2 5.8 %collective-permute-start.4 = (f32[16,32,128]{2,1,0:T(8,128)S(1)}, f32[16,32,128]{2,1,0:T(8,128)S(1)}, u32[]{:S(2)}, u32[]{:S(2)}) collective-permute-start(f32[16,32,128]{2,1,0:T(8,128)S(1)} %get-tuple-element.40), channel_id=1, source_target_pairs={{0,32},{32,64},{64,96},{96,128},{128,160},{160,192},{192,224},{224... | collective-permute-start | bytes 786440 | tf_op jit(solution)/shard_map/ppermute | solution.py:24
  26.3 5.8 %collective-permute-start.5 = (f32[16,32,128]{2,1,0:T(8,128)S(1)}, f32[16,32,128]{2,1,0:T(8,128)S(1)}, u32[]{:S(2)}, u32[]{:S(2)}) collective-permute-start(f32[16,32,128]{2,1,0:T(8,128)S(1)} %get-tuple-element.41), channel_id=1, source_target_pairs={{32,0},{64,32},{96,64},{128,96},{160,128},{192,160},{224,192},{0,2... | collective-permute-start | bytes 786440 | tf_op jit(solution)/shard_map/ppermute | solution.py:27
  32.4 17.7 %collective-permute-start.6 = (f32[64,16,128]{2,1,0:T(8,128)S(1)}, f32[64,16,128]{2,1,0:T(8,128)S(1)}, u32[]{:S(2)}, u32[]{:S(2)}) collective-permute-start(f32[64,16,128]{2,1,0:T(8,128)S(1)} %get-tuple-element.38), channel_id=1, source_target_pairs={{0,1},{1,2},{2,3},{3,4},{4,5},{5,6},{6,7},{7,8},{8,9},{9,10},{10,1... | collective-permute-start | bytes 1572872 | tf_op jit(solution)/shard_map/ppermute | solution.py:24
  32.5 17.6 %collective-permute-start.7 = (f32[64,16,128]{2,1,0:T(8,128)S(1)}, f32[64,16,128]{2,1,0:T(8,128)S(1)}, u32[]{:S(2)}, u32[]{:S(2)}) collective-permute-start(f32[64,16,128]{2,1,0:T(8,128)S(1)} %get-tuple-element.39), channel_id=1, source_target_pairs={{1,0},{2,1},{3,2},{4,3},{5,4},{6,5},{7,6},{8,7},{9,8},{10,9},{11,1... | collective-permute-start | bytes 1572872 | tf_op jit(solution)/shard_map/ppermute | solution.py:27
  53.5 8.6 %collective-permute-start.8 = (f32[32,32,128]{2,1,0:T(8,128)S(1)}, f32[32,32,128]{2,1,0:T(8,128)S(1)}, u32[]{:S(2)}, u32[]{:S(2)}) collective-permute-start(f32[32,32,128]{2,1,0:T(8,128)S(1)} %get-tuple-element.28), channel_id=1, source_target_pairs={{0,32},{32,64},{64,96},{96,128},{128,160},{160,192},{192,224},{224... | collective-permute-start | bytes 1572872 | tf_op jit(solution)/shard_map/ppermute | solution.py:24
  53.8 8.3 %collective-permute-start.9 = (f32[32,32,128]{2,1,0:T(8,128)S(1)}, f32[32,32,128]{2,1,0:T(8,128)S(1)}, u32[]{:S(2)}, u32[]{:S(2)}) collective-permute-start(f32[32,32,128]{2,1,0:T(8,128)S(1)} %get-tuple-element.29), channel_id=1, source_target_pairs={{32,0},{64,32},{96,64},{128,96},{160,128},{192,160},{224,192},{0,2... | collective-permute-start | bytes 1572872 | tf_op jit(solution)/shard_map/ppermute | solution.py:27
  62.5 29.3 %collective-permute-start.10 = (f32[64,32,128]{2,1,0:T(8,128)S(1)}, f32[64,32,128]{2,1,0:T(8,128)S(1)}, u32[]{:S(2)}, u32[]{:S(2)}) collective-permute-start(f32[64,32,128]{2,1,0:T(8,128)S(1)} %fusion.19), channel_id=1, source_target_pairs={{0,1},{1,2},{2,3},{3,4},{4,5},{5,6},{6,7},{7,8},{8,9},{9,10},{10,1... | collective-permute-start | bytes 3145736 | tf_op jit(solution)/shard_map/ppermute | solution.py:24
  62.7 29.0 %collective-permute-start.11 = (f32[64,32,128]{2,1,0:T(8,128)S(1)}, f32[64,32,128]{2,1,0:T(8,128)S(1)}, u32[]{:S(2)}, u32[]{:S(2)}) collective-permute-start(f32[64,32,128]{2,1,0:T(8,128)S(1)} %fusion.19), channel_id=1, source_target_pairs={{1,0},{2,1},{3,2},{4,3},{5,4},{6,5},{7,6},{8,7},{9,8},{10,9},{11,1... | collective-permute-start | bytes 3145736 | tf_op jit(solution)/shard_map/ppermute | solution.py:27

commit v3 on v2

--- a/solution.py
+++ b/solution.py
@@ -1,5 +1,6 @@
 import jax
 import jax.numpy as jnp
+import numpy as np
 from jax import lax
 from jax.sharding import PartitionSpec as P
 
@@ -38,19 +39,37 @@
     return summed
 
 
+def depth_matrix(planes, spacing):
+    matrix = np.zeros((planes, planes), np.float32)
+    for tap_index in range(5):
+        for i in range(planes):
+            matrix[(i + (tap_index - 2) * spacing) % planes, i] += SPLINE_TAPS[tap_index]
+    return matrix
+
+
 def depth_pass(values_in, spacing):
-    summed = SPLINE_TAPS[2] * values_in
-    for tap_index in (0, 1, 3, 4):
-        summed = summed + SPLINE_TAPS[tap_index] * jnp.roll(
-            values_in, -(tap_index - 2) * spacing, axis=2
-        )
-    return summed
+    rows = values_in.shape[:-1]
+    planes = values_in.shape[-1]
+    flat = values_in.reshape(-1, planes)
+    summed = jnp.dot(
+        flat,
+        jnp.asarray(depth_matrix(planes, spacing)),
+        precision=lax.Precision.HIGHEST,
+        preferred_element_type=jnp.float32,
+    )
+    return summed.reshape(*rows, planes)
 
 
 def moment_sums(detail):
     square = detail * detail
-    powers = jnp.stack([jnp.abs(detail), square, square * detail, square * square])
-    return jnp.sum(powers.reshape(4, -1), axis=1)
+    return jnp.stack(
+        [
+            jnp.sum(jnp.abs(detail), axis=(0, 1)),
+            jnp.sum(square, axis=(0, 1)),
+            jnp.sum(square * detail, axis=(0, 1)),
+            jnp.sum(square * square, axis=(0, 1)),
+        ]
+    )
 
 
 def finish_table(table, planes):
@@ -83,7 +102,7 @@
         smoother = depth_pass(along_y, spacing)
         sums.append(moment_sums(current - smoother))
         current = smoother
-    partial = jnp.stack(sums)
+    partial = jnp.sum(jnp.stack(sums), axis=-1)
     count_x = lax.axis_size("row") * size_x // SUB
     count_y = lax.axis_size("col") * size_y // SUB
     gathered = gather_partials(partial, ("row", "col"))

time: 126 us -> 116 us (0.921)
  other arithmetic: 21.9 us -> 3.78 us
  waiting for transfers between devices: 46.5 us -> 61.9 us
  local copies, waits for them, and re-layouts: 7.75 us -> 3.32 us
  matrix products: 0 us -> 4.1 us
  blocking collectives: 22.1 us -> 18.1 us
  starting transfers between devices: 24.8 us -> 21.7 us
    ppermute x6, waiting for transfers between devices: 0.02 us -> 31.7 us  [padded_1(): lax.ppermute(lax.slice_in_dim(block, 0, width, axis=dim), axis, backward)]
    ppermute x6, waiting for transfers between devices: 46.5 us -> 30.3 us  [padded_1(): lax.ppermute(lax.slice_in_dim(block, block.shape[dim] - width, None, axis...]
    reduce_sum x3 -> x4, other arithmetic: 12.6 us -> 0.95 us  [the longest x3 0.86 us: moment_sums(): jnp.sum(jnp.abs(detail), axis=(0, 1))]
    abs x3 -> x0, other arithmetic: 5.06 us -> none  [moment_sums(): jnp.abs(detail)]
    slice x12 -> x0, local copies, waits for them, and re-layouts: 4.45 us -> none  [depth_pass(): jnp.roll(values_in, -(tap_index - 2) * spacing, axis=2)]
    dot_general x0 -> x3, matrix products: none -> 4.1 us  [depth_pass(): jnp.dot(flat, jnp.asarray(depth_matrix(planes, spacing)), precision=lax.P...]
    all_to_all x1, blocking collectives: 22.1 us -> 18.1 us  [gather_partials(): return lax.all_to_all(sent, axes, 0, 0, tiled=True)]
    ppermute x6, starting transfers between devices: 22.1 us -> 18.6 us  [padded_1(): lax.ppermute(lax.slice_in_dim(block, 0, width, axis=dim), axis, backward)]
  transfers between devices with their start and end apart: 12 -> 12, of which waited for: 6 -> 9; matrix products, arithmetic and copies ran while one was open for 9% -> 2% of each run, Pallas kernels for 0% -> 0%
where the time goes in v3:
time: 116 us; the launch traced here: 114 us
  waiting for transfers between devices  61.9 us (53%)
  starting transfers between devices  21.7 us (19%)
  blocking collectives  18.1 us (16%)
  matrix products  4.1 us (4%)
  other arithmetic  3.78 us (3%)
  local copies, waits for them, and re-layouts  3.32 us (3%)
    ppermute x6, waiting for transfers between devices, padded_1(): lax.ppermute(lax.slice_in_dim(block, 0, width, axis=dim), axis, backward)  31.7 us
    ppermute x6, waiting for transfers between devices, padded_1(): lax.ppermute(lax.slice_in_dim(block, block.shape[dim] - width, None, axis...  30.3 us
    ppermute x6, starting transfers between devices, padded_1(): lax.ppermute(lax.slice_in_dim(block, 0, width, axis=dim), axis, backward)  18.6 us
    all_to_all x1, blocking collectives, gather_partials(): return lax.all_to_all(sent, axes, 0, 0, tiled=True)  18.1 us
    dot_general x3, matrix products, depth_pass(): jnp.dot(flat, jnp.asarray(depth_matrix(planes, spacing)), precision=lax.P...  4.1 us
    ppermute x6, starting transfers between devices, padded_1(): lax.ppermute(lax.slice_in_dim(block, block.shape[dim] - width, None, axis...  3.09 us
  transfers between devices with their start and end apart: 12, of which 9 were waited for; matrix products, arithmetic and copies ran while one was open for 2% of the time, Pallas kernels for 0%

profile of v3, /device:TPU:8, one launch (start us, length us, event | category | flops | bytes accessed | tf_op | source)
XLA Modules:
  0.0 113.8 jit_solution(8949996860376947619)
XLA Ops:
  0.6 1.0 fusion.76
  1.6 1.7 %collective-permute-start.1 = (f32[8,32,128]{2,1,0:T(8,128)S(1)}, f32[8,32,128]{2,1,0:T(8,128)S(1)}, u32[]{:S(2)}, u32[]{:S(2)}) collective-permute-start(f32[8,32,128]{2,1,0:T(8,128)S(1)} %get-tuple-element.27), channel_id=1, source_target_pairs={{32,0},{64,32},{96,64},{128,96},{160,128},{192,160},{224,192},{0,2... | collective-permute-start | bytes 393224 | tf_op jit(solution)/shard_map/ppermute | solution.py:28
  3.4 2.6 %collective-permute-done = f32[8,32,128]{2,1,0:T(8,128)S(1)} collective-permute-done((f32[8,32,128]{2,1,0:T(8,128)S(1)}, f32[8,32,128]{2,1,0:T(8,128)S(1)}, u32[]{:S(2)}, u32[]{:S(2)}) %collective-permute-start) | collective-permute-done | bytes 131104 | tf_op jit(solution)/shard_map/ppermute | solution.py:25
  6.1 1.6 %constant_dynamic-update-slice_fusion = (f32[72,32,128]{2,1,0:T(8,128)S(1)}, f32[72,32,128]{2,1,0:T(8,128)S(1)}) fusion(f32[72,32,128]{2,1,0:T(8,128)S(1)} %constant_dynamic-update-slice_fusion.1, f32[64,32,128]{2,1,0:T(8,128)} %param.4), kind=kLoop, calls=%fused_computation.109 | loop fusion | bytes 3145728 | tf_op jit(solution)/shard_map/concatenate | solution.py:29
  7.7 0.4 fusion.57
  8.1 2.0 %collective-permute-start.2 = (f32[64,8,128]{2,1,0:T(8,128)S(1)}, f32[64,8,128]{2,1,0:T(8,128)S(1)}, u32[]{:S(2)}, u32[]{:S(2)}) collective-permute-start(f32[64,8,128]{2,1,0:T(8,128)S(1)} %get-tuple-element.22), channel_id=1, source_target_pairs={{0,1},{1,2},{2,3},{3,4},{4,5},{5,6},{6,7},{7,8},{8,9},{9,10},{10,1... | collective-permute-start | bytes 786440 | tf_op jit(solution)/shard_map/ppermute | solution.py:25
  10.1 6.2 %collective-permute-start.3 = (f32[64,8,128]{2,1,0:T(8,128)S(1)}, f32[64,8,128]{2,1,0:T(8,128)S(1)}, u32[]{:S(2)}, u32[]{:S(2)}) collective-permute-start(f32[64,8,128]{2,1,0:T(8,128)S(1)} %get-tuple-element.23), channel_id=1, source_target_pairs={{1,0},{2,1},{3,2},{4,3},{5,4},{6,5},{7,6},{8,7},{9,8},{10,9},{11,1... | collective-permute-start | bytes 786440 | tf_op jit(solution)/shard_map/ppermute | solution.py:28
  16.3 6.4 %collective-permute-done.2 = f32[64,8,128]{2,1,0:T(8,128)S(1)} collective-permute-done((f32[64,8,128]{2,1,0:T(8,128)S(1)}, f32[64,8,128]{2,1,0:T(8,128)S(1)}, u32[]{:S(2)}, u32[]{:S(2)}) %collective-permute-start.2) | collective-permute-done | bytes 262176 | tf_op jit(solution)/shard_map/ppermute | solution.py:25
  22.8 0.5 fusion.11
  23.3 1.0 fusion.79
  24.4 0.5 collective-permute-start.4
  24.9 3.4 %collective-permute-done.5 = f32[16,32,128]{2,1,0:T(8,128)S(1)} collective-permute-done((f32[16,32,128]{2,1,0:T(8,128)S(1)}, f32[16,32,128]{2,1,0:T(8,128)S(1)}, u32[]{:S(2)}, u32[]{:S(2)}) %collective-permute-start.5) | collective-permute-done | bytes 262176 | tf_op jit(solution)/shard_map/ppermute | solution.py:28
  28.3 1.9 %collective-permute-done.4 = f32[16,32,128]{2,1,0:T(8,128)S(1)} collective-permute-done((f32[16,32,128]{2,1,0:T(8,128)S(1)}, f32[16,32,128]{2,1,0:T(8,128)S(1)}, u32[]{:S(2)}, u32[]{:S(2)}) %collective-permute-start.4) | collective-permute-done | bytes 262176 | tf_op jit(solution)/shard_map/ppermute | solution.py:25
  30.2 0.4 fusion.71
  30.8 5.3 %collective-permute-start.7 = (f32[64,16,128]{2,1,0:T(8,128)S(1)}, f32[64,16,128]{2,1,0:T(8,128)S(1)}, u32[]{:S(2)}, u32[]{:S(2)}) collective-permute-start(f32[64,16,128]{2,1,0:T(8,128)S(1)} %get-tuple-element.19), channel_id=1, source_target_pairs={{1,0},{2,1},{3,2},{4,3},{5,4},{6,5},{7,6},{8,7},{9,8},{10,9},{11,1... | collective-permute-start | bytes 1572872 | tf_op jit(solution)/shard_map/ppermute | solution.py:28
  36.1 11.8 %collective-permute-done.6 = f32[64,16,128]{2,1,0:T(8,128)S(1)} collective-permute-done((f32[64,16,128]{2,1,0:T(8,128)S(1)}, f32[64,16,128]{2,1,0:T(8,128)S(1)}, u32[]{:S(2)}, u32[]{:S(2)}) %collective-permute-start.6) | collective-permute-done | bytes 524320 | tf_op jit(solution)/shard_map/ppermute | solution.py:25
  47.9 0.4 fusion.33
  48.3 1.0 fusion.78
  49.4 0.5 collective-permute-start.8
  49.9 6.2 %collective-permute-done.9 = f32[32,32,128]{2,1,0:T(8,128)S(1)} collective-permute-done((f32[32,32,128]{2,1,0:T(8,128)S(1)}, f32[32,32,128]{2,1,0:T(8,128)S(1)}, u32[]{:S(2)}, u32[]{:S(2)}) %collective-permute-start.9) | collective-permute-done | bytes 524320 | tf_op jit(solution)/shard_map/ppermute | solution.py:28
  56.1 1.9 %collective-permute-done.8 = f32[32,32,128]{2,1,0:T(8,128)S(1)} collective-permute-done((f32[32,32,128]{2,1,0:T(8,128)S(1)}, f32[32,32,128]{2,1,0:T(8,128)S(1)}, u32[]{:S(2)}, u32[]{:S(2)}) %collective-permute-start.8) | collective-permute-done | bytes 524320 | tf_op jit(solution)/shard_map/ppermute | solution.py:25
  58.0 0.4 fusion.25
  58.4 5.2 %collective-permute-start.11 = (f32[64,32,128]{2,1,0:T(8,128)S(1)}, f32[64,32,128]{2,1,0:T(8,128)S(1)}, u32[]{:S(2)}, u32[]{:S(2)}) collective-permute-start(f32[64,32,128]{2,1,0:T(8,128)S(1)} %fusion.25), channel_id=1, source_target_pairs={{1,0},{2,1},{3,2},{4,3},{5,4},{6,5},{7,6},{8,7},{9,8},{10,9},{11,1... | collective-permute-start | bytes 3145736 | tf_op jit(solution)/shard_map/ppermute | solution.py:28
  63.7 0.3 abs_reduce_fusion.2
  63.9 0.3 abs_reduce_fusion.1
  64.3 22.1 %collective-permute-done.11 = f32[64,32,128]{2,1,0:T(8,128)S(1)} collective-permute-done((f32[64,32,128]{2,1,0:T(8,128)S(1)}, f32[64,32,128]{2,1,0:T(8,128)S(1)}, u32[]{:S(2)}, u32[]{:S(2)}) %collective-permute-start.11) | collective-permute-done | bytes 1048608 | tf_op jit(solution)/shard_map/ppermute | solution.py:28
  86.3 5.5 %collective-permute-done.10 = f32[64,32,128]{2,1,0:T(8,128)S(1)} collective-permute-done((f32[64,32,128]{2,1,0:T(8,128)S(1)}, f32[64,32,128]{2,1,0:T(8,128)S(1)}, u32[]{:S(2)}, u32[]{:S(2)}) %collective-permute-start.10) | collective-permute-done | bytes 1048608 | tf_op jit(solution)/shard_map/ppermute | solution.py:25
  91.8 2.1 %fusion.77 = (f32[64,32,128]{2,1,0:T(8,128)S(1)}, f32[64,32,128]{2,1,0:T(8,128)}) fusion(f32[64,32,128]{2,1,0:T(8,128)S(1)} %bitcast.37, f32[128,128,1]{1,0,2:T(8,128)S(1)} %copy-done.1, f32[64,32,128]{2,1,0:T(8,128)S(1)} %collective-permute-done.11, f32[64,32,128]{2,1,0:T(8,128)S(1)} %fusion.25, f32[64,32,128]{2,1,0:T(8,128)S(1)} %collective-permute-done.10), kind=kOutput, calls=%fused_computation.130 | convolution fusion | flops 405798912 | bytes 6356992 | tf_op jit(solution)/shard_map/dot_general | solution.py:54
  94.0 0.3 abs_reduce_fusion
  94.5 18.1 %all_to_all.6 = f32[256,1,12]{2,1,0:T(1,128)S(1)} all-to-all(f32[256,1,12]{2,1,0:T(1,128)S(1)} %broadcast_in_dim.8), channel_id=1, replica_groups=mesh['row'=8,'col'=32] {'row','col'}, dimensions={0} | all-to-all | bytes 24576 | tf_op jit(solution)/shard_map/all_to_all | solution.py:89
  112.7 0.3 reshape.41
  113.2 0.6 pad_maximum_fusion.10
  (32 shorter events, 0.9 us)
Async XLA Ops:
  1.6 4.4 %collective-permute-start = (f32[8,32,128]{2,1,0:T(8,128)S(1)}, f32[8,32,128]{2,1,0:T(8,128)S(1)}, u32[]{:S(2)}, u32[]{:S(2)}) collective-permute-start(f32[8,32,128]{2,1,0:T(8,128)S(1)} %get-tuple-element.26), channel_id=1, source_target_pairs={{0,32},{32,64},{64,96},{96,128},{128,160},{160,192},{192,224},{224... | collective-permute-start | bytes 393224 | tf_op jit(solution)/shard_map/ppermute | solution.py:25
  1.6 6.0 %collective-permute-start.1 = (f32[8,32,128]{2,1,0:T(8,128)S(1)}, f32[8,32,128]{2,1,0:T(8,128)S(1)}, u32[]{:S(2)}, u32[]{:S(2)}) collective-permute-start(f32[8,32,128]{2,1,0:T(8,128)S(1)} %get-tuple-element.27), channel_id=1, source_target_pairs={{32,0},{64,32},{96,64},{128,96},{160,128},{192,160},{224,192},{0,2... | collective-permute-start | bytes 393224 | tf_op jit(solution)/shard_map/ppermute | solution.py:28
  6.0 1.6 %copy-start = (f32[64,32,128]{2,1,0:T(8,128)S(1)}, f32[64,32,128]{2,1,0:T(8,128)}, u32[]{:S(2)}) copy-start(f32[64,32,128]{2,1,0:T(8,128)} %param.4) | copy-start | bytes 3145732
  8.1 14.7 %collective-permute-start.2 = (f32[64,8,128]{2,1,0:T(8,128)S(1)}, f32[64,8,128]{2,1,0:T(8,128)S(1)}, u32[]{:S(2)}, u32[]{:S(2)}) collective-permute-start(f32[64,8,128]{2,1,0:T(8,128)S(1)} %get-tuple-element.22), channel_id=1, source_target_pairs={{0,1},{1,2},{2,3},{3,4},{4,5},{5,6},{6,7},{7,8},{8,9},{9,10},{10,1... | collective-permute-start | bytes 786440 | tf_op jit(solution)/shard_map/ppermute | solution.py:25
  10.1 13.2 %copy-start.3 = (f32[128,128]{1,0:T(8,128)S(1)}, f32[128,128]{1,0:T(8,128)}, u32[]{:S(2)}) copy-start(f32[128,128]{1,0:T(8,128)} %constant.22.clone) | copy-start | bytes 196612
  10.1 12.7 %collective-permute-start.3 = (f32[64,8,128]{2,1,0:T(8,128)S(1)}, f32[64,8,128]{2,1,0:T(8,128)S(1)}, u32[]{:S(2)}, u32[]{:S(2)}) collective-permute-start(f32[64,8,128]{2,1,0:T(8,128)S(1)} %get-tuple-element.23), channel_id=1, source_target_pairs={{1,0},{2,1},{3,2},{4,3},{5,4},{6,5},{7,6},{8,7},{9,8},{10,9},{11,1... | collective-permute-start | bytes 786440 | tf_op jit(solution)/shard_map/ppermute | solution.py:28
  24.3 3.9 %collective-permute-start.5 = (f32[16,32,128]{2,1,0:T(8,128)S(1)}, f32[16,32,128]{2,1,0:T(8,128)S(1)}, u32[]{:S(2)}, u32[]{:S(2)}) collective-permute-start(f32[16,32,128]{2,1,0:T(8,128)S(1)} %bitcast.44), channel_id=1, source_target_pairs={{32,0},{64,32},{96,64},{128,96},{160,128},{192,160},{224,192},{0,2... | collective-permute-start | bytes 786440 | tf_op jit(solution)/shard_map/ppermute | solution.py:28
  24.4 5.8 %collective-permute-start.4 = (f32[16,32,128]{2,1,0:T(8,128)S(1)}, f32[16,32,128]{2,1,0:T(8,128)S(1)}, u32[]{:S(2)}, u32[]{:S(2)}) collective-permute-start(f32[16,32,128]{2,1,0:T(8,128)S(1)} %bitcast.43), channel_id=1, source_target_pairs={{0,32},{32,64},{64,96},{96,128},{128,160},{160,192},{192,224},{224... | collective-permute-start | bytes 786440 | tf_op jit(solution)/shard_map/ppermute | solution.py:25
  30.7 17.3 %collective-permute-start.6 = (f32[64,16,128]{2,1,0:T(8,128)S(1)}, f32[64,16,128]{2,1,0:T(8,128)S(1)}, u32[]{:S(2)}, u32[]{:S(2)}) collective-permute-start(f32[64,16,128]{2,1,0:T(8,128)S(1)} %get-tuple-element.18), channel_id=1, source_target_pairs={{0,1},{1,2},{2,3},{3,4},{4,5},{5,6},{6,7},{7,8},{8,9},{9,10},{10,1... | collective-permute-start | bytes 1572872 | tf_op jit(solution)/shard_map/ppermute | solution.py:25
  30.8 17.5 %copy-start.2 = (f32[128,128]{1,0:T(8,128)S(1)}, f32[128,128]{1,0:T(8,128)}, u32[]{:S(2)}) copy-start(f32[128,128]{1,0:T(8,128)} %constant.23.clone) | copy-start | bytes 196612
  30.8 17.1 %collective-permute-start.7 = (f32[64,16,128]{2,1,0:T(8,128)S(1)}, f32[64,16,128]{2,1,0:T(8,128)S(1)}, u32[]{:S(2)}, u32[]{:S(2)}) collective-permute-start(f32[64,16,128]{2,1,0:T(8,128)S(1)} %get-tuple-element.19), channel_id=1, source_target_pairs={{1,0},{2,1},{3,2},{4,3},{5,4},{6,5},{7,6},{8,7},{9,8},{10,9},{11,1... | collective-permute-start | bytes 1572872 | tf_op jit(solution)/shard_map/ppermute | solution.py:28
  49.4 6.7 %collective-permute-start.9 = (f32[32,32,128]{2,1,0:T(8,128)S(1)}, f32[32,32,128]{2,1,0:T(8,128)S(1)}, u32[]{:S(2)}, u32[]{:S(2)}) collective-permute-start(f32[32,32,128]{2,1,0:T(8,128)S(1)} %bitcast.42), channel_id=1, source_target_pairs={{32,0},{64,32},{96,64},{128,96},{160,128},{192,160},{224,192},{0,2... | collective-permute-start | bytes 1572872 | tf_op jit(solution)/shard_map/ppermute | solution.py:28
  49.4 8.6 %collective-permute-start.8 = (f32[32,32,128]{2,1,0:T(8,128)S(1)}, f32[32,32,128]{2,1,0:T(8,128)S(1)}, u32[]{:S(2)}, u32[]{:S(2)}) collective-permute-start(f32[32,32,128]{2,1,0:T(8,128)S(1)} %bitcast.41), channel_id=1, source_target_pairs={{0,32},{32,64},{64,96},{96,128},{128,160},{160,192},{192,224},{224... | collective-permute-start | bytes 1572872 | tf_op jit(solution)/shard_map/ppermute | solution.py:25
  58.4 33.4 %copy-start.1 = (f32[128,128,1]{1,0,2:T(8,128)S(1)}, f32[128,128,1]{1,0,2:T(8,128)}, u32[]{:S(2)}) copy-start(f32[128,128,1]{1,0,2:T(8,128)} %constant.25) | copy-start | bytes 196612
  58.4 27.9 %collective-permute-start.11 = (f32[64,32,128]{2,1,0:T(8,128)S(1)}, f32[64,32,128]{2,1,0:T(8,128)S(1)}, u32[]{:S(2)}, u32[]{:S(2)}) collective-permute-start(f32[64,32,128]{2,1,0:T(8,128)S(1)} %fusion.25), channel_id=1, source_target_pairs={{1,0},{2,1},{3,2},{4,3},{5,4},{6,5},{7,6},{8,7},{9,8},{10,9},{11,1... | collective-permute-start | bytes 3145736 | tf_op jit(solution)/shard_map/ppermute | solution.py:28
  63.7 28.2 %collective-permute-start.10 = (f32[64,32,128]{2,1,0:T(8,128)S(1)}, f32[64,32,128]{2,1,0:T(8,128)S(1)}, u32[]{:S(2)}, u32[]{:S(2)}) collective-permute-start(f32[64,32,128]{2,1,0:T(8,128)S(1)} %fusion.25), channel_id=1, source_target_pairs={{0,1},{1,2},{2,3},{3,4},{4,5},{5,6},{6,7},{7,8},{8,9},{9,10},{10,1... | collective-permute-start | bytes 3145736 | tf_op jit(solution)/shard_map/ppermute | solution.py:25

commit v4 on v3

--- a/solution.py
+++ b/solution.py
@@ -10,6 +10,7 @@
 SPLINE_TAPS = (0.0625, 0.25, 0.375, 0.25, 0.0625)
 SPACINGS = (4, 8, 16)
 EPSILON = 1e-06
+ONE_ROUND = (4,)
 
 
 def ring_pairs(count):
@@ -27,6 +28,47 @@
     )
     high = lax.ppermute(lax.slice_in_dim(block, 0, width, axis=dim), axis, backward)
     return jnp.concatenate([low, block, high], axis=dim)
+
+
+def padded_both(block, width):
+    rows = lax.axis_size("row")
+    cols = lax.axis_size("col")
+    size_x, size_y = block.shape[0], block.shape[1]
+    assert width <= size_x and width <= size_y
+
+    def shifted(piece, dr, dc):
+        if dc == 0:
+            return lax.ppermute(piece, "row", [(i, (i + dr) % rows) for i in range(rows)])
+        if dr == 0:
+            return lax.ppermute(piece, "col", [(i, (i + dc) % cols) for i in range(cols)])
+        pairs = [
+            (r * cols + c, ((r + dr) % rows) * cols + (c + dc) % cols)
+            for r in range(rows)
+            for c in range(cols)
+        ]
+        return lax.ppermute(piece, ("row", "col"), pairs)
+
+    top = slice(size_x - width, size_x)
+    bottom = slice(0, width)
+    right_edge = slice(size_y - width, size_y)
+    left_edge = slice(0, width)
+    full = slice(None)
+    up = shifted(block[top, full], 1, 0)
+    down = shifted(block[bottom, full], -1, 0)
+    left = shifted(block[full, right_edge], 0, 1)
+    right = shifted(block[full, left_edge], 0, -1)
+    up_left = shifted(block[top, right_edge], 1, 1)
+    up_right = shifted(block[top, left_edge], 1, -1)
+    down_left = shifted(block[bottom, right_edge], -1, 1)
+    down_right = shifted(block[bottom, left_edge], -1, -1)
+    return jnp.concatenate(
+        [
+            jnp.concatenate([up_left, up, up_right], axis=1),
+            jnp.concatenate([left, block, right], axis=1),
+            jnp.concatenate([down_left, down, down_right], axis=1),
+        ],
+        axis=0,
+    )
 
 
 def holed_pass(padded, spacing, axis_number, length_out):
@@ -95,10 +137,14 @@
     sums = []
     current = density
     for spacing in SPACINGS:
-        padded_x = padded_1(current, "row", 0, 2 * spacing)
-        along_x = holed_pass(padded_x, spacing, 0, size_x)
-        padded_y = padded_1(along_x, "col", 1, 2 * spacing)
-        along_y = holed_pass(padded_y, spacing, 1, size_y)
+        if spacing in ONE_ROUND:
+            padded = padded_both(current, 2 * spacing)
+            along_y = holed_pass(holed_pass(padded, spacing, 0, size_x), spacing, 1, size_y)
+        else:
+            padded_x = padded_1(current, "row", 0, 2 * spacing)
+            along_x = holed_pass(padded_x, spacing, 0, size_x)
+            padded_y = padded_1(along_x, "col", 1, 2 * spacing)
+            along_y = holed_pass(padded_y, spacing, 1, size_y)
         smoother = depth_pass(along_y, spacing)
         sums.append(moment_sums(current - smoother))
         current = smoother

time: 116 us -> 119 us (1.026)
  starting transfers between devices: 21.7 us -> 27.1 us
  waiting for transfers between devices: 61.9 us -> 58.1 us
    ppermute x0 -> x8, starting transfers between devices: none -> 13.4 us  [the longest x4 7.98 us: shifted(): return lax.ppermute(piece, ('row', 'col'), pairs)]
    ppermute x6 -> x4, waiting for transfers between devices: 30.3 us -> 20.8 us  [padded_1(): lax.ppermute(lax.slice_in_dim(block, block.shape[dim] - width, None, axis...]
    ppermute x6 -> x4, starting transfers between devices: 18.6 us -> 13.1 us  [padded_1(): lax.ppermute(lax.slice_in_dim(block, 0, width, axis=dim), axis, backward)]
    ppermute x0 -> x8, waiting for transfers between devices: none -> 5.15 us  [the longest x2 3.35 us: shifted(): lax.ppermute(piece, 'col', [(i, (i + dc) % cols) for i in range(cols)])]
    slice x0 -> x3, local copies, waits for them, and re-layouts: none -> 2.96 us  [the longest x1 1.16 us: padded_both(): right = shifted(block[full, left_edge], 0, -1)]
    ppermute x6 -> x4, starting transfers between devices: 3.09 us -> 0.59 us  [padded_1(): lax.ppermute(lax.slice_in_dim(block, block.shape[dim] - width, None, axis...]
    concatenate x2 -> x1, local copies, waits for them, and re-layouts: 1.57 us -> 0.02 us  [padded_both(): jnp.concatenate([left, block, right], axis=1)]
    ppermute x6 -> x4, waiting for transfers between devices: 31.7 us -> 32.1 us  [padded_1(): lax.ppermute(lax.slice_in_dim(block, 0, width, axis=dim), axis, backward)]
  transfers between devices with their start and end apart: 12 -> 16, of which waited for: 9 -> 10; matrix products, arithmetic and copies ran while one was open for 2% -> 2% of each run, Pallas kernels for 0% -> 0%
where the time goes in v4:
time: 119 us; the launch traced here: 116 us
  waiting for transfers between devices  58.1 us (49%)
  starting transfers between devices  27.1 us (23%)
  blocking collectives  18 us (15%)
  local copies, waits for them, and re-layouts  4.16 us (3%)
  matrix products  4.11 us (3%)
  other arithmetic  4.08 us (3%)
    ppermute x4, waiting for transfers between devices, padded_1(): lax.ppermute(lax.slice_in_dim(block, 0, width, axis=dim), axis, backward)  32.1 us
    ppermute x4, waiting for transfers between devices, padded_1(): lax.ppermute(lax.slice_in_dim(block, block.shape[dim] - width, None, axis...  20.8 us
    all_to_all x1, blocking collectives, gather_partials(): return lax.all_to_all(sent, axes, 0, 0, tiled=True)  18 us
    ppermute x4, starting transfers between devices, padded_1(): lax.ppermute(lax.slice_in_dim(block, 0, width, axis=dim), axis, backward)  13.1 us
    ppermute x4, starting transfers between devices, shifted(): return lax.ppermute(piece, ('row', 'col'), pairs)  7.98 us
    ppermute x2, starting transfers between devices, shifted(): lax.ppermute(piece, 'col', [(i, (i + dc) % cols) for i in range(cols)])  5.42 us
    dot_general x3, matrix products, depth_pass(): jnp.dot(flat, jnp.asarray(depth_matrix(planes, spacing)), precision=lax.P...  4.11 us
    ppermute x2, waiting for transfers between devices, shifted(): lax.ppermute(piece, 'col', [(i, (i + dc) % cols) for i in range(cols)])  3.35 us
  transfers between devices with their start and end apart: 16, of which 10 were waited for; matrix products, arithmetic and copies ran while one was open for 2% of the time, Pallas kernels for 0%

profile of v4, /device:TPU:8, one launch (start us, length us, event | category | flops | bytes accessed | tf_op | source)
XLA Modules:
  0.0 116.4 jit_solution(11423485280763683496)
XLA Ops:
  0.6 1.2 fusion.71
  1.8 2.0 %collective-permute-start.3 = (f32[64,8,128]{2,1,0:T(8,128)S(1)}, f32[64,8,128]{2,1,0:T(8,128)S(1)}, u32[]{:S(2)}, u32[]{:S(2)}) collective-permute-start(f32[64,8,128]{2,1,0:T(8,128)S(1)} %get-tuple-element.31), channel_id=1, source_target_pairs={{0,1},{1,2},{2,3},{3,4},{4,5},{5,6},{6,7},{7,8},{8,9},{9,10},{10,1... | collective-permute-start | bytes 786440 | tf_op jit(solution)/shard_map/ppermute | solution.py:43
  3.8 0.8 fusion.69
  4.6 1.2 collective-permute-start
  5.8 3.4 %collective-permute-start.5 = (f32[8,8,128]{2,1,0:T(8,128)S(1)}, f32[8,8,128]{2,1,0:T(8,128)S(1)}, u32[]{:S(2)}, u32[]{:S(2)}) collective-permute-start(f32[8,8,128]{2,1,0:T(8,128)S(1)} %get-tuple-element.25), channel_id=1, source_target_pairs={{0,225},{1,226},{2,227},{3,228},{4,229},{5,230},{6,231},{7,232},{8... | collective-permute-start | bytes 98312 | tf_op jit(solution)/shard_map/ppermute | solution.py:49
  9.1 3.4 %collective-permute-start.4 = (f32[64,8,128]{2,1,0:T(8,128)S(1)}, f32[64,8,128]{2,1,0:T(8,128)S(1)}, u32[]{:S(2)}, u32[]{:S(2)}) collective-permute-start(f32[64,8,128]{2,1,0:T(8,128)S(1)} %get-tuple-element.30), channel_id=1, source_target_pairs={{0,31},{1,0},{2,1},{3,2},{4,3},{5,4},{6,5},{7,6},{8,7},{9,8},{10,9... | collective-permute-start | bytes 786440 | tf_op jit(solution)/shard_map/ppermute | solution.py:43
  12.6 1.0 fusion.70
  13.6 3.3 %collective-permute-done.3 = f32[64,8,128]{2,1,0:T(8,128)S(1)} collective-permute-done((f32[64,8,128]{2,1,0:T(8,128)S(1)}, f32[64,8,128]{2,1,0:T(8,128)S(1)}, u32[]{:S(2)}, u32[]{:S(2)}) %collective-permute-start.3) | collective-permute-done | bytes 262176 | tf_op jit(solution)/shard_map/ppermute | solution.py:43
  17.1 1.9 %collective-permute-start.2 = (f32[8,8,128]{2,1,0:T(8,128)S(1)}, f32[8,8,128]{2,1,0:T(8,128)S(1)}, u32[]{:S(2)}, u32[]{:S(2)}) collective-permute-start(f32[8,8,128]{2,1,0:T(8,128)S(1)} %get-tuple-element.26), channel_id=1, source_target_pairs={{0,63},{1,32},{2,33},{3,34},{4,35},{5,36},{6,37},{7,38},{8,39},{9,... | collective-permute-start | bytes 98312 | tf_op jit(solution)/shard_map/ppermute | solution.py:49
  19.0 1.5 %collective-permute-start.7 = (f32[8,8,128]{2,1,0:T(8,128)S(1)}, f32[8,8,128]{2,1,0:T(8,128)S(1)}, u32[]{:S(2)}, u32[]{:S(2)}) collective-permute-start(f32[8,8,128]{2,1,0:T(8,128)S(1)} %get-tuple-element.27), channel_id=1, source_target_pairs={{0,255},{1,224},{2,225},{3,226},{4,227},{5,228},{6,229},{7,230},{8... | collective-permute-start | bytes 98312 | tf_op jit(solution)/shard_map/ppermute | solution.py:49
  20.5 0.9 collective-permute-done.2
  21.4 0.9 collective-permute-done.7
  22.6 0.5 fusion
  23.1 0.4 fusion.51
  23.9 1.0 fusion.74
  25.0 2.5 %collective-permute-start.9 = (f32[16,32,128]{2,1,0:T(8,128)S(1)}, f32[16,32,128]{2,1,0:T(8,128)S(1)}, u32[]{:S(2)}, u32[]{:S(2)}) collective-permute-start(f32[16,32,128]{2,1,0:T(8,128)S(1)} %bitcast.44), channel_id=1, source_target_pairs={{32,0},{64,32},{96,64},{128,96},{160,128},{192,160},{224,192},{0,2... | collective-permute-start | bytes 786440 | tf_op jit(solution)/shard_map/ppermute | solution.py:29
  27.5 3.9 %collective-permute-done.9 = f32[16,32,128]{2,1,0:T(8,128)S(1)} collective-permute-done((f32[16,32,128]{2,1,0:T(8,128)S(1)}, f32[16,32,128]{2,1,0:T(8,128)S(1)}, u32[]{:S(2)}, u32[]{:S(2)}) %collective-permute-start.9) | collective-permute-done | bytes 262176 | tf_op jit(solution)/shard_map/ppermute | solution.py:29
  31.4 1.9 %collective-permute-done.8 = f32[16,32,128]{2,1,0:T(8,128)S(1)} collective-permute-done((f32[16,32,128]{2,1,0:T(8,128)S(1)}, f32[16,32,128]{2,1,0:T(8,128)S(1)}, u32[]{:S(2)}, u32[]{:S(2)}) %collective-permute-start.8) | collective-permute-done | bytes 262176 | tf_op jit(solution)/shard_map/ppermute | solution.py:26
  33.3 0.4 fusion.65
  33.9 5.3 %collective-permute-start.11 = (f32[64,16,128]{2,1,0:T(8,128)S(1)}, f32[64,16,128]{2,1,0:T(8,128)S(1)}, u32[]{:S(2)}, u32[]{:S(2)}) collective-permute-start(f32[64,16,128]{2,1,0:T(8,128)S(1)} %get-tuple-element.21), channel_id=1, source_target_pairs={{1,0},{2,1},{3,2},{4,3},{5,4},{6,5},{7,6},{8,7},{9,8},{10,9},{11,1... | collective-permute-start | bytes 1572872 | tf_op jit(solution)/shard_map/ppermute | solution.py:29
  39.2 11.5 %collective-permute-done.10 = f32[64,16,128]{2,1,0:T(8,128)S(1)} collective-permute-done((f32[64,16,128]{2,1,0:T(8,128)S(1)}, f32[64,16,128]{2,1,0:T(8,128)S(1)}, u32[]{:S(2)}, u32[]{:S(2)}) %collective-permute-start.10) | collective-permute-done | bytes 524320 | tf_op jit(solution)/shard_map/ppermute | solution.py:26
  51.1 1.0 fusion.73
  52.2 0.5 collective-permute-start.12
  52.7 6.2 %collective-permute-done.13 = f32[32,32,128]{2,1,0:T(8,128)S(1)} collective-permute-done((f32[32,32,128]{2,1,0:T(8,128)S(1)}, f32[32,32,128]{2,1,0:T(8,128)S(1)}, u32[]{:S(2)}, u32[]{:S(2)}) %collective-permute-start.13) | collective-permute-done | bytes 524320 | tf_op jit(solution)/shard_map/ppermute | solution.py:29
  58.9 1.9 %collective-permute-done.12 = f32[32,32,128]{2,1,0:T(8,128)S(1)} collective-permute-done((f32[32,32,128]{2,1,0:T(8,128)S(1)}, f32[32,32,128]{2,1,0:T(8,128)S(1)}, u32[]{:S(2)}, u32[]{:S(2)}) %collective-permute-start.12) | collective-permute-done | bytes 524320 | tf_op jit(solution)/shard_map/ppermute | solution.py:26
  60.8 0.4 fusion.21
  61.2 5.2 %collective-permute-start.15 = (f32[64,32,128]{2,1,0:T(8,128)S(1)}, f32[64,32,128]{2,1,0:T(8,128)S(1)}, u32[]{:S(2)}, u32[]{:S(2)}) collective-permute-start(f32[64,32,128]{2,1,0:T(8,128)S(1)} %fusion.21), channel_id=1, source_target_pairs={{1,0},{2,1},{3,2},{4,3},{5,4},{6,5},{7,6},{8,7},{9,8},{10,9},{11,1... | collective-permute-start | bytes 3145736 | tf_op jit(solution)/shard_map/ppermute | solution.py:29
  67.0 22.0 %collective-permute-done.15 = f32[64,32,128]{2,1,0:T(8,128)S(1)} collective-permute-done((f32[64,32,128]{2,1,0:T(8,128)S(1)}, f32[64,32,128]{2,1,0:T(8,128)S(1)}, u32[]{:S(2)}, u32[]{:S(2)}) %collective-permute-start.15) | collective-permute-done | bytes 1048608 | tf_op jit(solution)/shard_map/ppermute | solution.py:29
  89.0 5.5 %collective-permute-done.14 = f32[64,32,128]{2,1,0:T(8,128)S(1)} collective-permute-done((f32[64,32,128]{2,1,0:T(8,128)S(1)}, f32[64,32,128]{2,1,0:T(8,128)S(1)}, u32[]{:S(2)}, u32[]{:S(2)}) %collective-permute-start.14) | collective-permute-done | bytes 1048608 | tf_op jit(solution)/shard_map/ppermute | solution.py:26
  94.6 2.1 %fusion.72 = (f32[64,32,128]{2,1,0:T(8,128)S(1)}, f32[64,32,128]{2,1,0:T(8,128)}) fusion(f32[64,32,128]{2,1,0:T(8,128)S(1)} %bitcast.37, f32[128,128,1]{1,0,2:T(8,128)S(1)} %copy-done.1, f32[64,32,128]{2,1,0:T(8,128)S(1)} %collective-permute-done.15, f32[64,32,128]{2,1,0:T(8,128)S(1)} %fusion.21, f32[64,32,128]{2,1,0:T(8,128)S(1)} %collective-permute-done.14), kind=kOutput, calls=%fused_computation.125 | convolution fusion | flops 405798912 | bytes 6356992 | tf_op jit(solution)/shard_map/dot_general | solution.py:96
  97.3 18.0 %all_to_all.6 = f32[256,1,12]{2,1,0:T(1,128)S(1)} all-to-all(f32[256,1,12]{2,1,0:T(1,128)S(1)} %broadcast_in_dim.8), channel_id=1, replica_groups=mesh['row'=8,'col'=32] {'row','col'}, dimensions={0} | all-to-all | bytes 24576 | tf_op jit(solution)/shard_map/all_to_all | solution.py:131
  115.8 0.6 pad_maximum_fusion.9
  (42 shorter events, 3.1 us)
Async XLA Ops:
  0.6 16.3 %copy-start = (f32[64,32,128]{2,1,0:T(8,128)S(1)}, f32[64,32,128]{2,1,0:T(8,128)}, u32[]{:S(2)}) copy-start(f32[64,32,128]{2,1,0:T(8,128)} %param.4) | copy-start | bytes 3145732
  1.8 15.1 %collective-permute-start.3 = (f32[64,8,128]{2,1,0:T(8,128)S(1)}, f32[64,8,128]{2,1,0:T(8,128)S(1)}, u32[]{:S(2)}, u32[]{:S(2)}) collective-permute-start(f32[64,8,128]{2,1,0:T(8,128)S(1)} %get-tuple-element.31), channel_id=1, source_target_pairs={{0,1},{1,2},{2,3},{3,4},{4,5},{5,6},{6,7},{7,8},{8,9},{9,10},{10,1... | collective-permute-start | bytes 786440 | tf_op jit(solution)/shard_map/ppermute | solution.py:43
  4.6 12.4 %collective-permute-start = (f32[8,8,128]{2,1,0:T(8,128)S(1)}, f32[8,8,128]{2,1,0:T(8,128)S(1)}, u32[]{:S(2)}, u32[]{:S(2)}) collective-permute-start(f32[8,8,128]{2,1,0:T(8,128)S(1)} %get-tuple-element.24), channel_id=1, source_target_pairs={{0,33},{1,34},{2,35},{3,36},{4,37},{5,38},{6,39},{7,40},{8,41},{9,... | collective-permute-start | bytes 98312 | tf_op jit(solution)/shard_map/ppermute | solution.py:49
  5.8 14.8 %collective-permute-start.5 = (f32[8,8,128]{2,1,0:T(8,128)S(1)}, f32[8,8,128]{2,1,0:T(8,128)S(1)}, u32[]{:S(2)}, u32[]{:S(2)}) collective-permute-start(f32[8,8,128]{2,1,0:T(8,128)S(1)} %get-tuple-element.25), channel_id=1, source_target_pairs={{0,225},{1,226},{2,227},{3,228},{4,229},{5,230},{6,231},{7,232},{8... | collective-permute-start | bytes 98312 | tf_op jit(solution)/shard_map/ppermute | solution.py:49
  9.1 9.8 %collective-permute-start.4 = (f32[64,8,128]{2,1,0:T(8,128)S(1)}, f32[64,8,128]{2,1,0:T(8,128)S(1)}, u32[]{:S(2)}, u32[]{:S(2)}) collective-permute-start(f32[64,8,128]{2,1,0:T(8,128)S(1)} %get-tuple-element.30), channel_id=1, source_target_pairs={{0,31},{1,0},{2,1},{3,2},{4,3},{5,4},{6,5},{7,6},{8,7},{9,8},{10,9... | collective-permute-start | bytes 786440 | tf_op jit(solution)/shard_map/ppermute | solution.py:43
  13.6 8.8 %collective-permute-start.1 = (f32[8,32,128]{2,1,0:T(8,128)S(1)}, f32[8,32,128]{2,1,0:T(8,128)S(1)}, u32[]{:S(2)}, u32[]{:S(2)}) collective-permute-start(f32[8,32,128]{2,1,0:T(8,128)S(1)} %get-tuple-element.28), channel_id=1, source_target_pairs={{0,32},{32,64},{64,96},{96,128},{128,160},{160,192},{192,224},{224... | collective-permute-start | bytes 393224 | tf_op jit(solution)/shard_map/ppermute | solution.py:41
  16.9 5.4 %collective-permute-start.6 = (f32[8,32,128]{2,1,0:T(8,128)S(1)}, f32[8,32,128]{2,1,0:T(8,128)S(1)}, u32[]{:S(2)}, u32[]{:S(2)}) collective-permute-start(f32[8,32,128]{2,1,0:T(8,128)S(1)} %get-tuple-element.29), channel_id=1, source_target_pairs={{0,224},{32,0},{64,32},{96,64},{128,96},{160,128},{192,160},{224,1... | collective-permute-start | bytes 393224 | tf_op jit(solution)/shard_map/ppermute | solution.py:41
  17.1 4.3 %collective-permute-start.2 = (f32[8,8,128]{2,1,0:T(8,128)S(1)}, f32[8,8,128]{2,1,0:T(8,128)S(1)}, u32[]{:S(2)}, u32[]{:S(2)}) collective-permute-start(f32[8,8,128]{2,1,0:T(8,128)S(1)} %get-tuple-element.26), channel_id=1, source_target_pairs={{0,63},{1,32},{2,33},{3,34},{4,35},{5,36},{6,37},{7,38},{8,39},{9,... | collective-permute-start | bytes 98312 | tf_op jit(solution)/shard_map/ppermute | solution.py:49
  19.0 3.3 %collective-permute-start.7 = (f32[8,8,128]{2,1,0:T(8,128)S(1)}, f32[8,8,128]{2,1,0:T(8,128)S(1)}, u32[]{:S(2)}, u32[]{:S(2)}) collective-permute-start(f32[8,8,128]{2,1,0:T(8,128)S(1)} %get-tuple-element.27), channel_id=1, source_target_pairs={{0,255},{1,224},{2,225},{3,226},{4,227},{5,228},{6,229},{7,230},{8... | collective-permute-start | bytes 98312 | tf_op jit(solution)/shard_map/ppermute | solution.py:49
  23.1 0.8 copy-start.3
  25.0 6.4 %collective-permute-start.9 = (f32[16,32,128]{2,1,0:T(8,128)S(1)}, f32[16,32,128]{2,1,0:T(8,128)S(1)}, u32[]{:S(2)}, u32[]{:S(2)}) collective-permute-start(f32[16,32,128]{2,1,0:T(8,128)S(1)} %bitcast.44), channel_id=1, source_target_pairs={{32,0},{64,32},{96,64},{128,96},{160,128},{192,160},{224,192},{0,2... | collective-permute-start | bytes 786440 | tf_op jit(solution)/shard_map/ppermute | solution.py:29
  27.5 5.8 %collective-permute-start.8 = (f32[16,32,128]{2,1,0:T(8,128)S(1)}, f32[16,32,128]{2,1,0:T(8,128)S(1)}, u32[]{:S(2)}, u32[]{:S(2)}) collective-permute-start(f32[16,32,128]{2,1,0:T(8,128)S(1)} %bitcast.43), channel_id=1, source_target_pairs={{0,32},{32,64},{64,96},{96,128},{128,160},{160,192},{192,224},{224... | collective-permute-start | bytes 786440 | tf_op jit(solution)/shard_map/ppermute | solution.py:26
  33.8 16.9 %collective-permute-start.10 = (f32[64,16,128]{2,1,0:T(8,128)S(1)}, f32[64,16,128]{2,1,0:T(8,128)S(1)}, u32[]{:S(2)}, u32[]{:S(2)}) collective-permute-start(f32[64,16,128]{2,1,0:T(8,128)S(1)} %get-tuple-element.20), channel_id=1, source_target_pairs={{0,1},{1,2},{2,3},{3,4},{4,5},{5,6},{6,7},{7,8},{8,9},{9,10},{10,1... | collective-permute-start | bytes 1572872 | tf_op jit(solution)/shard_map/ppermute | solution.py:26
  33.9 17.2 %copy-start.2 = (f32[128,128]{1,0:T(8,128)S(1)}, f32[128,128]{1,0:T(8,128)}, u32[]{:S(2)}) copy-start(f32[128,128]{1,0:T(8,128)} %constant.26.clone) | copy-start | bytes 196612
  33.9 16.8 %collective-permute-start.11 = (f32[64,16,128]{2,1,0:T(8,128)S(1)}, f32[64,16,128]{2,1,0:T(8,128)S(1)}, u32[]{:S(2)}, u32[]{:S(2)}) collective-permute-start(f32[64,16,128]{2,1,0:T(8,128)S(1)} %get-tuple-element.21), channel_id=1, source_target_pairs={{1,0},{2,1},{3,2},{4,3},{5,4},{6,5},{7,6},{8,7},{9,8},{10,9},{11,1... | collective-permute-start | bytes 1572872 | tf_op jit(solution)/shard_map/ppermute | solution.py:29
  52.2 6.7 %collective-permute-start.13 = (f32[32,32,128]{2,1,0:T(8,128)S(1)}, f32[32,32,128]{2,1,0:T(8,128)S(1)}, u32[]{:S(2)}, u32[]{:S(2)}) collective-permute-start(f32[32,32,128]{2,1,0:T(8,128)S(1)} %bitcast.42), channel_id=1, source_target_pairs={{32,0},{64,32},{96,64},{128,96},{160,128},{192,160},{224,192},{0,2... | collective-permute-start | bytes 1572872 | tf_op jit(solution)/shard_map/ppermute | solution.py:29
  52.2 8.6 %collective-permute-start.12 = (f32[32,32,128]{2,1,0:T(8,128)S(1)}, f32[32,32,128]{2,1,0:T(8,128)S(1)}, u32[]{:S(2)}, u32[]{:S(2)}) collective-permute-start(f32[32,32,128]{2,1,0:T(8,128)S(1)} %bitcast.41), channel_id=1, source_target_pairs={{0,32},{32,64},{64,96},{96,128},{128,160},{160,192},{192,224},{224... | collective-permute-start | bytes 1572872 | tf_op jit(solution)/shard_map/ppermute | solution.py:26
  61.2 33.4 %copy-start.1 = (f32[128,128,1]{1,0,2:T(8,128)S(1)}, f32[128,128,1]{1,0,2:T(8,128)}, u32[]{:S(2)}) copy-start(f32[128,128,1]{1,0,2:T(8,128)} %constant.28) | copy-start | bytes 196612
  61.2 27.8 %collective-permute-start.15 = (f32[64,32,128]{2,1,0:T(8,128)S(1)}, f32[64,32,128]{2,1,0:T(8,128)S(1)}, u32[]{:S(2)}, u32[]{:S(2)}) collective-permute-start(f32[64,32,128]{2,1,0:T(8,128)S(1)} %fusion.21), channel_id=1, source_target_pairs={{1,0},{2,1},{3,2},{4,3},{5,4},{6,5},{7,6},{8,7},{9,8},{10,9},{11,1... | collective-permute-start | bytes 3145736 | tf_op jit(solution)/shard_map/ppermute | solution.py:29
  66.4 28.1 %collective-permute-start.14 = (f32[64,32,128]{2,1,0:T(8,128)S(1)}, f32[64,32,128]{2,1,0:T(8,128)S(1)}, u32[]{:S(2)}, u32[]{:S(2)}) collective-permute-start(f32[64,32,128]{2,1,0:T(8,128)S(1)} %fusion.21), channel_id=1, source_target_pairs={{0,1},{1,2},{2,3},{3,4},{4,5},{5,6},{6,7},{7,8},{8,9},{9,10},{10,1... | collective-permute-start | bytes 3145736 | tf_op jit(solution)/shard_map/ppermute | solution.py:26

commit v5 on v3

--- a/solution.py
+++ b/solution.py
@@ -3,6 +3,7 @@
 import numpy as np
 from jax import lax
 from jax.sharding import PartitionSpec as P
+
 
 SUB = 256
 
@@ -16,6 +17,17 @@
     forward = [(i, (i + 1) % count) for i in range(count)]
     backward = [(target, source) for source, target in forward]
     return forward, backward
+
+
+def edges_1(block, axis, dim, width):
+    count = lax.axis_size(axis)
+    assert width <= block.shape[dim]
+    forward, backward = ring_pairs(count)
+    low = lax.ppermute(
+        lax.slice_in_dim(block, block.shape[dim] - width, None, axis=dim), axis, forward
+    )
+    high = lax.ppermute(lax.slice_in_dim(block, 0, width, axis=dim), axis, backward)
+    return low, high
 
 
 def padded_1(block, axis, dim, width):
@@ -95,13 +107,23 @@
     sums = []
     current = density
     for spacing in SPACINGS:
-        padded_x = padded_1(current, "row", 0, 2 * spacing)
-        along_x = holed_pass(padded_x, spacing, 0, size_x)
-        padded_y = padded_1(along_x, "col", 1, 2 * spacing)
-        along_y = holed_pass(padded_y, spacing, 1, size_y)
-        smoother = depth_pass(along_y, spacing)
-        sums.append(moment_sums(current - smoother))
-        current = smoother
+      width = 2 * spacing
+      padded_x = padded_1(current, "row", 0, width)
+      along_x = holed_pass(padded_x, spacing, 0, size_x)
+      if size_x > 2 * width:
+          inner = holed_pass(current, spacing, 0, size_x - 2 * width)
+          inner_low, inner_high = edges_1(inner, "col", 1, width)
+          rims = jnp.concatenate([along_x[:width], along_x[size_x - width :]], axis=0)
+          rim_low, rim_high = edges_1(rims, "col", 1, width)
+          low = jnp.concatenate([rim_low[:width], inner_low, rim_low[width:]], axis=0)
+          high = jnp.concatenate([rim_high[:width], inner_high, rim_high[width:]], axis=0)
+          padded_y = jnp.concatenate([low, along_x, high], axis=1)
+      else:
+          padded_y = padded_1(along_x, "col", 1, width)
+      along_y = holed_pass(padded_y, spacing, 1, size_y)
+      smoother = depth_pass(along_y, spacing)
+      sums.append(moment_sums(current - smoother))
+      current = smoother
     partial = jnp.sum(jnp.stack(sums), axis=-1)
     count_x = lax.axis_size("row") * size_x // SUB
     count_y = lax.axis_size("col") * size_y // SUB

time: 116 us -> 119 us (1.026)
  waiting for transfers between devices: 61.9 us -> 52.9 us
  starting transfers between devices: 21.7 us -> 29.5 us
  other arithmetic: 3.78 us -> 7.18 us
  blocking collectives: 18.1 us -> 19.3 us
    ppermute x0 -> x8, starting transfers between devices: none -> 21.2 us  [the longest x4 16.2 us: edges_1(): lax.ppermute(lax.slice_in_dim(block, 0, width, axis=dim), axis, backward)]
    ppermute x6 -> x4, waiting for transfers between devices: 30.3 us -> 10 us  [padded_1(): lax.ppermute(lax.slice_in_dim(block, block.shape[dim] - width, None, axis...]
    ppermute x0 -> x8, waiting for transfers between devices: none -> 10.8 us  [the longest x4 6.59 us: edges_1(): lax.ppermute(lax.slice_in_dim(block, block.shape[dim] - width, None, axis...]
    ppermute x6 -> x4, starting transfers between devices: 18.6 us -> 7.74 us  [padded_1(): lax.ppermute(lax.slice_in_dim(block, 0, width, axis=dim), axis, backward)]
    add x4 -> x5, other arithmetic: 1.65 us -> 4.28 us  [holed_pass(): summed = summed + SPLINE_TAPS[tap_index] * portion]
    ppermute x6 -> x4, starting transfers between devices: 3.09 us -> 0.52 us  [padded_1(): lax.ppermute(lax.slice_in_dim(block, block.shape[dim] - width, None, axis...]
    concatenate x2, local copies, waits for them, and re-layouts: 1.57 us -> 0.16 us  [padded_1(): return jnp.concatenate([low, block, high], axis=dim)]
    ppermute x6 -> x4, waiting for transfers between devices: 31.7 us -> 32.1 us  [padded_1(): lax.ppermute(lax.slice_in_dim(block, 0, width, axis=dim), axis, backward)]
  transfers between devices with their start and end apart: 12 -> 16, of which waited for: 9 -> 10; matrix products, arithmetic and copies ran while one was open for 2% -> 3% of each run, Pallas kernels for 0% -> 0%
where the time goes in v5:
time: 119 us; the launch traced here: 117 us
  waiting for transfers between devices  52.9 us (44%)
  starting transfers between devices  29.5 us (25%)
  blocking collectives  19.3 us (16%)
  other arithmetic  7.18 us (6%)
  matrix products  4.14 us (3%)
  local copies, waits for them, and re-layouts  2.57 us (2%)
    ppermute x4, waiting for transfers between devices, padded_1(): lax.ppermute(lax.slice_in_dim(block, 0, width, axis=dim), axis, backward)  32.1 us
    all_to_all x1, blocking collectives, gather_partials(): return lax.all_to_all(sent, axes, 0, 0, tiled=True)  19.3 us
    ppermute x4, starting transfers between devices, edges_1(): lax.ppermute(lax.slice_in_dim(block, 0, width, axis=dim), axis, backward)  16.2 us
    ppermute x4, waiting for transfers between devices, padded_1(): lax.ppermute(lax.slice_in_dim(block, block.shape[dim] - width, None, axis...  10 us
    ppermute x4, starting transfers between devices, padded_1(): lax.ppermute(lax.slice_in_dim(block, 0, width, axis=dim), axis, backward)  7.74 us
    ppermute x4, waiting for transfers between devices, edges_1(): lax.ppermute(lax.slice_in_dim(block, block.shape[dim] - width, None, axis...  6.59 us
    ppermute x4, starting transfers between devices, edges_1(): lax.ppermute(lax.slice_in_dim(block, block.shape[dim] - width, None, axis...  5.06 us
    add x5, other arithmetic, holed_pass(): summed = summed + SPLINE_TAPS[tap_index] * portion  4.28 us
  transfers between devices with their start and end apart: 16, of which 10 were waited for; matrix products, arithmetic and copies ran while one was open for 3% of the time, Pallas kernels for 0%

profile of v5, /device:TPU:8, one launch (start us, length us, event | category | flops | bytes accessed | tf_op | source)
XLA Modules:
  0.0 116.6 jit_solution(13497829541117492780)
XLA Ops:
  0.6 1.0 fusion.69
  1.7 1.7 %collective-permute-start.1 = (f32[8,32,128]{2,1,0:T(8,128)S(1)}, f32[8,32,128]{2,1,0:T(8,128)S(1)}, u32[]{:S(2)}, u32[]{:S(2)}) collective-permute-start(f32[8,32,128]{2,1,0:T(8,128)S(1)} %get-tuple-element.31), channel_id=1, source_target_pairs={{32,0},{64,32},{96,64},{128,96},{160,128},{192,160},{224,192},{0,2... | collective-permute-start | bytes 393224 | tf_op jit(solution)/shard_map/ppermute | solution.py:40
  3.4 2.9 %multiply_add_fusion = f32[48,32,128]{2,1,0:T(8,128)S(1)} fusion(f32[64,32,128]{2,1,0:T(8,128)} %param.4), kind=kLoop, calls=%fused_computation.92 | loop fusion | flops 1769472 | bytes 4718592 | tf_op jit(solution)/shard_map/add | solution.py:50
  6.5 0.4 fusion.45
  6.9 2.0 %collective-permute-start.2 = (f32[16,8,128]{2,1,0:T(8,128)S(1)}, f32[16,8,128]{2,1,0:T(8,128)S(1)}, u32[]{:S(2)}, u32[]{:S(2)}) collective-permute-start(f32[16,8,128]{2,1,0:T(8,128)S(1)} %get-tuple-element.42), channel_id=1, source_target_pairs={{0,1},{1,2},{2,3},{3,4},{4,5},{5,6},{6,7},{7,8},{8,9},{9,10},{10,1... | collective-permute-start | bytes 196616 | tf_op jit(solution)/shard_map/ppermute | solution.py:26
  9.0 2.0 %collective-permute-start.3 = (f32[48,8,128]{2,1,0:T(8,128)S(1)}, f32[48,8,128]{2,1,0:T(8,128)S(1)}, u32[]{:S(2)}, u32[]{:S(2)}) collective-permute-start(f32[48,8,128]{2,1,0:T(8,128)S(1)} %get-tuple-element.32), channel_id=1, source_target_pairs={{0,1},{1,2},{2,3},{3,4},{4,5},{5,6},{6,7},{7,8},{8,9},{9,10},{10,1... | collective-permute-start | bytes 589832 | tf_op jit(solution)/shard_map/ppermute | solution.py:26
  11.0 4.3 %collective-permute-start.5 = (f32[48,8,128]{2,1,0:T(8,128)S(1)}, f32[48,8,128]{2,1,0:T(8,128)S(1)}, u32[]{:S(2)}, u32[]{:S(2)}) collective-permute-start(f32[48,8,128]{2,1,0:T(8,128)S(1)} %get-tuple-element.33), channel_id=1, source_target_pairs={{1,0},{2,1},{3,2},{4,3},{5,4},{6,5},{7,6},{8,7},{9,8},{10,9},{11,1... | collective-permute-start | bytes 589832 | tf_op jit(solution)/shard_map/ppermute | solution.py:29
  15.3 2.0 %collective-permute-start.4 = (f32[16,8,128]{2,1,0:T(8,128)S(1)}, f32[16,8,128]{2,1,0:T(8,128)S(1)}, u32[]{:S(2)}, u32[]{:S(2)}) collective-permute-start(f32[16,8,128]{2,1,0:T(8,128)S(1)} %get-tuple-element.43), channel_id=1, source_target_pairs={{1,0},{2,1},{3,2},{4,3},{5,4},{6,5},{7,6},{8,7},{9,8},{10,9},{11,1... | collective-permute-start | bytes 196616 | tf_op jit(solution)/shard_map/ppermute | solution.py:29
  17.5 4.2 %collective-permute-done.4 = f32[16,8,128]{2,1,0:T(8,128)S(1)} collective-permute-done((f32[16,8,128]{2,1,0:T(8,128)S(1)}, f32[16,8,128]{2,1,0:T(8,128)S(1)}, u32[]{:S(2)}, u32[]{:S(2)}) %collective-permute-start.4) | collective-permute-done | bytes 65568 | tf_op jit(solution)/shard_map/ppermute | solution.py:29
  21.9 0.4 fusion.41
  22.8 1.0 fusion.78
  23.8 0.6 collective-permute-start.7
  24.4 3.9 %collective-permute-done.7 = f32[16,32,128]{2,1,0:T(8,128)S(1)} collective-permute-done((f32[16,32,128]{2,1,0:T(8,128)S(1)}, f32[16,32,128]{2,1,0:T(8,128)S(1)}, u32[]{:S(2)}, u32[]{:S(2)}) %collective-permute-start.7) | collective-permute-done | bytes 262176 | tf_op jit(solution)/shard_map/ppermute | solution.py:40
  28.3 1.9 %collective-permute-done.6 = f32[16,32,128]{2,1,0:T(8,128)S(1)} collective-permute-done((f32[16,32,128]{2,1,0:T(8,128)S(1)}, f32[16,32,128]{2,1,0:T(8,128)S(1)}, u32[]{:S(2)}, u32[]{:S(2)}) %collective-permute-start.6) | collective-permute-done | bytes 262176 | tf_op jit(solution)/shard_map/ppermute | solution.py:37
  30.2 0.4 fusion.64
  30.7 1.0 collective-permute-start.8
  31.8 4.5 %collective-permute-start.10 = (f32[32,16,128]{2,1,0:T(8,128)S(1)}, f32[32,16,128]{2,1,0:T(8,128)S(1)}, u32[]{:S(2)}, u32[]{:S(2)}) collective-permute-start(f32[32,16,128]{2,1,0:T(8,128)S(1)} %get-tuple-element.37), channel_id=1, source_target_pairs={{1,0},{2,1},{3,2},{4,3},{5,4},{6,5},{7,6},{8,7},{9,8},{10,9},{11,1... | collective-permute-start | bytes 786440 | tf_op jit(solution)/shard_map/ppermute | solution.py:29
  36.5 5.3 %collective-permute-start.11 = (f32[32,16,128]{2,1,0:T(8,128)S(1)}, f32[32,16,128]{2,1,0:T(8,128)S(1)}, u32[]{:S(2)}, u32[]{:S(2)}) collective-permute-start(f32[32,16,128]{2,1,0:T(8,128)S(1)} %get-tuple-element.35), channel_id=1, source_target_pairs={{1,0},{2,1},{3,2},{4,3},{5,4},{6,5},{7,6},{8,7},{9,8},{10,9},{11,1... | collective-permute-start | bytes 786440 | tf_op jit(solution)/shard_map/ppermute | solution.py:29
  41.8 1.3 %collective-permute-done.8 = f32[32,16,128]{2,1,0:T(8,128)S(1)} collective-permute-done((f32[32,16,128]{2,1,0:T(8,128)S(1)}, f32[32,16,128]{2,1,0:T(8,128)S(1)}, u32[]{:S(2)}, u32[]{:S(2)}) %collective-permute-start.8) | collective-permute-done | bytes 262176 | tf_op jit(solution)/shard_map/ppermute | solution.py:26
  43.2 5.1 %collective-permute-done.9 = f32[32,16,128]{2,1,0:T(8,128)S(1)} collective-permute-done((f32[32,16,128]{2,1,0:T(8,128)S(1)}, f32[32,16,128]{2,1,0:T(8,128)S(1)}, u32[]{:S(2)}, u32[]{:S(2)}) %collective-permute-start.9) | collective-permute-done | bytes 262176 | tf_op jit(solution)/shard_map/ppermute | solution.py:26
  48.5 0.6 abs_reduce_fusion.2
  49.4 1.0 fusion.77
  50.5 0.5 collective-permute-start.12
  51.0 6.2 %collective-permute-done.13 = f32[32,32,128]{2,1,0:T(8,128)S(1)} collective-permute-done((f32[32,32,128]{2,1,0:T(8,128)S(1)}, f32[32,32,128]{2,1,0:T(8,128)S(1)}, u32[]{:S(2)}, u32[]{:S(2)}) %collective-permute-start.13) | collective-permute-done | bytes 524320 | tf_op jit(solution)/shard_map/ppermute | solution.py:40
  57.2 2.6 %collective-permute-done.12 = f32[32,32,128]{2,1,0:T(8,128)S(1)} collective-permute-done((f32[32,32,128]{2,1,0:T(8,128)S(1)}, f32[32,32,128]{2,1,0:T(8,128)S(1)}, u32[]{:S(2)}, u32[]{:S(2)}) %collective-permute-start.12) | collective-permute-done | bytes 524320 | tf_op jit(solution)/shard_map/ppermute | solution.py:37
  59.7 0.4 fusion.17
  60.1 5.4 %collective-permute-start.15 = (f32[64,32,128]{2,1,0:T(8,128)S(1)}, f32[64,32,128]{2,1,0:T(8,128)S(1)}, u32[]{:S(2)}, u32[]{:S(2)}) collective-permute-start(f32[64,32,128]{2,1,0:T(8,128)S(1)} %fusion.17), channel_id=1, source_target_pairs={{1,0},{2,1},{3,2},{4,3},{5,4},{6,5},{7,6},{8,7},{9,8},{10,9},{11,1... | collective-permute-start | bytes 3145736 | tf_op jit(solution)/shard_map/ppermute | solution.py:40
  65.9 22.0 %collective-permute-done.15 = f32[64,32,128]{2,1,0:T(8,128)S(1)} collective-permute-done((f32[64,32,128]{2,1,0:T(8,128)S(1)}, f32[64,32,128]{2,1,0:T(8,128)S(1)}, u32[]{:S(2)}, u32[]{:S(2)}) %collective-permute-start.15) | collective-permute-done | bytes 1048608 | tf_op jit(solution)/shard_map/ppermute | solution.py:40
  87.9 5.5 %collective-permute-done.14 = f32[64,32,128]{2,1,0:T(8,128)S(1)} collective-permute-done((f32[64,32,128]{2,1,0:T(8,128)S(1)}, f32[64,32,128]{2,1,0:T(8,128)S(1)}, u32[]{:S(2)}, u32[]{:S(2)}) %collective-permute-start.14) | collective-permute-done | bytes 1048608 | tf_op jit(solution)/shard_map/ppermute | solution.py:37
  93.4 2.2 %fusion.76 = (f32[64,32,128]{2,1,0:T(8,128)S(1)}, f32[64,32,128]{2,1,0:T(8,128)}) fusion(f32[64,32,128]{2,1,0:T(8,128)S(1)} %bitcast.39, f32[128,128,1]{1,0,2:T(8,128)S(1)} %copy-done.1, f32[64,32,128]{2,1,0:T(8,128)S(1)} %collective-permute-done.15, f32[64,32,128]{2,1,0:T(8,128)S(1)} %fusion.17, f32[64,32,128]{2,1,0:T(8,128)S(1)} %collective-permute-done.14), kind=kOutput, calls=%fused_computation.140 | convolution fusion | flops 405798912 | bytes 6356992 | tf_op jit(solution)/shard_map/dot_general | solution.py:66
  96.1 19.3 %all_to_all.6 = f32[256,1,12]{2,1,0:T(1,128)S(1)} all-to-all(f32[256,1,12]{2,1,0:T(1,128)S(1)} %broadcast_in_dim.8), channel_id=1, replica_groups=mesh['row'=8,'col'=32] {'row','col'}, dimensions={0} | all-to-all | bytes 24576 | tf_op jit(solution)/shard_map/all_to_all | solution.py:101
  115.9 0.6 pad_maximum_fusion.11
  (52 shorter events, 3.4 us)
Async XLA Ops:
  1.6 4.6 %collective-permute-start = (f32[8,32,128]{2,1,0:T(8,128)S(1)}, f32[8,32,128]{2,1,0:T(8,128)S(1)}, u32[]{:S(2)}, u32[]{:S(2)}) collective-permute-start(f32[8,32,128]{2,1,0:T(8,128)S(1)} %get-tuple-element.30), channel_id=1, source_target_pairs={{0,32},{32,64},{64,96},{96,128},{128,160},{160,192},{192,224},{224... | collective-permute-start | bytes 393224 | tf_op jit(solution)/shard_map/ppermute | solution.py:37
  1.6 4.6 %copy-start = (f32[64,32,128]{2,1,0:T(8,128)S(1)}, f32[64,32,128]{2,1,0:T(8,128)}, u32[]{:S(2)}) copy-start(f32[64,32,128]{2,1,0:T(8,128)} %param.4) | copy-start | bytes 3145732
  1.7 4.8 %collective-permute-start.1 = (f32[8,32,128]{2,1,0:T(8,128)S(1)}, f32[8,32,128]{2,1,0:T(8,128)S(1)}, u32[]{:S(2)}, u32[]{:S(2)}) collective-permute-start(f32[8,32,128]{2,1,0:T(8,128)S(1)} %get-tuple-element.31), channel_id=1, source_target_pairs={{32,0},{64,32},{96,64},{128,96},{160,128},{192,160},{224,192},{0,2... | collective-permute-start | bytes 393224 | tf_op jit(solution)/shard_map/ppermute | solution.py:40
  6.9 10.5 %collective-permute-start.2 = (f32[16,8,128]{2,1,0:T(8,128)S(1)}, f32[16,8,128]{2,1,0:T(8,128)S(1)}, u32[]{:S(2)}, u32[]{:S(2)}) collective-permute-start(f32[16,8,128]{2,1,0:T(8,128)S(1)} %get-tuple-element.42), channel_id=1, source_target_pairs={{0,1},{1,2},{2,3},{3,4},{4,5},{5,6},{6,7},{7,8},{8,9},{9,10},{10,1... | collective-permute-start | bytes 196616 | tf_op jit(solution)/shard_map/ppermute | solution.py:26
  9.0 12.8 %collective-permute-start.3 = (f32[48,8,128]{2,1,0:T(8,128)S(1)}, f32[48,8,128]{2,1,0:T(8,128)S(1)}, u32[]{:S(2)}, u32[]{:S(2)}) collective-permute-start(f32[48,8,128]{2,1,0:T(8,128)S(1)} %get-tuple-element.32), channel_id=1, source_target_pairs={{0,1},{1,2},{2,3},{3,4},{4,5},{5,6},{6,7},{7,8},{8,9},{9,10},{10,1... | collective-permute-start | bytes 589832 | tf_op jit(solution)/shard_map/ppermute | solution.py:26
  11.0 10.8 %collective-permute-start.5 = (f32[48,8,128]{2,1,0:T(8,128)S(1)}, f32[48,8,128]{2,1,0:T(8,128)S(1)}, u32[]{:S(2)}, u32[]{:S(2)}) collective-permute-start(f32[48,8,128]{2,1,0:T(8,128)S(1)} %get-tuple-element.33), channel_id=1, source_target_pairs={{1,0},{2,1},{3,2},{4,3},{5,4},{6,5},{7,6},{8,7},{9,8},{10,9},{11,1... | collective-permute-start | bytes 589832 | tf_op jit(solution)/shard_map/ppermute | solution.py:29
  15.3 6.4 %collective-permute-start.4 = (f32[16,8,128]{2,1,0:T(8,128)S(1)}, f32[16,8,128]{2,1,0:T(8,128)S(1)}, u32[]{:S(2)}, u32[]{:S(2)}) collective-permute-start(f32[16,8,128]{2,1,0:T(8,128)S(1)} %get-tuple-element.43), channel_id=1, source_target_pairs={{1,0},{2,1},{3,2},{4,3},{5,4},{6,5},{7,6},{8,7},{9,8},{10,9},{11,1... | collective-permute-start | bytes 196616 | tf_op jit(solution)/shard_map/ppermute | solution.py:29
  21.9 0.8 copy-start.3
  23.8 4.5 %collective-permute-start.7 = (f32[16,32,128]{2,1,0:T(8,128)S(1)}, f32[16,32,128]{2,1,0:T(8,128)S(1)}, u32[]{:S(2)}, u32[]{:S(2)}) collective-permute-start(f32[16,32,128]{2,1,0:T(8,128)S(1)} %bitcast.46), channel_id=1, source_target_pairs={{32,0},{64,32},{96,64},{128,96},{160,128},{192,160},{224,192},{0,2... | collective-permute-start | bytes 786440 | tf_op jit(solution)/shard_map/ppermute | solution.py:40
  24.4 5.8 %collective-permute-start.6 = (f32[16,32,128]{2,1,0:T(8,128)S(1)}, f32[16,32,128]{2,1,0:T(8,128)S(1)}, u32[]{:S(2)}, u32[]{:S(2)}) collective-permute-start(f32[16,32,128]{2,1,0:T(8,128)S(1)} %bitcast.45), channel_id=1, source_target_pairs={{0,32},{32,64},{64,96},{96,128},{128,160},{160,192},{192,224},{224... | collective-permute-start | bytes 786440 | tf_op jit(solution)/shard_map/ppermute | solution.py:37
  30.7 12.5 %collective-permute-start.8 = (f32[32,16,128]{2,1,0:T(8,128)S(1)}, f32[32,16,128]{2,1,0:T(8,128)S(1)}, u32[]{:S(2)}, u32[]{:S(2)}) collective-permute-start(f32[32,16,128]{2,1,0:T(8,128)S(1)} %get-tuple-element.36), channel_id=1, source_target_pairs={{0,1},{1,2},{2,3},{3,4},{4,5},{5,6},{6,7},{7,8},{8,9},{9,10},{10,1... | collective-permute-start | bytes 786440 | tf_op jit(solution)/shard_map/ppermute | solution.py:26
  31.8 11.3 %collective-permute-start.10 = (f32[32,16,128]{2,1,0:T(8,128)S(1)}, f32[32,16,128]{2,1,0:T(8,128)S(1)}, u32[]{:S(2)}, u32[]{:S(2)}) collective-permute-start(f32[32,16,128]{2,1,0:T(8,128)S(1)} %get-tuple-element.37), channel_id=1, source_target_pairs={{1,0},{2,1},{3,2},{4,3},{5,4},{6,5},{7,6},{8,7},{9,8},{10,9},{11,1... | collective-permute-start | bytes 786440 | tf_op jit(solution)/shard_map/ppermute | solution.py:29
  36.4 11.9 %collective-permute-start.9 = (f32[32,16,128]{2,1,0:T(8,128)S(1)}, f32[32,16,128]{2,1,0:T(8,128)S(1)}, u32[]{:S(2)}, u32[]{:S(2)}) collective-permute-start(f32[32,16,128]{2,1,0:T(8,128)S(1)} %get-tuple-element.34), channel_id=1, source_target_pairs={{0,1},{1,2},{2,3},{3,4},{4,5},{5,6},{6,7},{7,8},{8,9},{9,10},{10,1... | collective-permute-start | bytes 786440 | tf_op jit(solution)/shard_map/ppermute | solution.py:26
  36.5 11.8 %collective-permute-start.11 = (f32[32,16,128]{2,1,0:T(8,128)S(1)}, f32[32,16,128]{2,1,0:T(8,128)S(1)}, u32[]{:S(2)}, u32[]{:S(2)}) collective-permute-start(f32[32,16,128]{2,1,0:T(8,128)S(1)} %get-tuple-element.35), channel_id=1, source_target_pairs={{1,0},{2,1},{3,2},{4,3},{5,4},{6,5},{7,6},{8,7},{9,8},{10,9},{11,1... | collective-permute-start | bytes 786440 | tf_op jit(solution)/shard_map/ppermute | solution.py:29
  48.5 0.8 copy-start.2
  50.4 6.7 %collective-permute-start.13 = (f32[32,32,128]{2,1,0:T(8,128)S(1)}, f32[32,32,128]{2,1,0:T(8,128)S(1)}, u32[]{:S(2)}, u32[]{:S(2)}) collective-permute-start(f32[32,32,128]{2,1,0:T(8,128)S(1)} %bitcast.44), channel_id=1, source_target_pairs={{32,0},{64,32},{96,64},{128,96},{160,128},{192,160},{224,192},{0,2... | collective-permute-start | bytes 1572872 | tf_op jit(solution)/shard_map/ppermute | solution.py:40
  50.5 9.3 %collective-permute-start.12 = (f32[32,32,128]{2,1,0:T(8,128)S(1)}, f32[32,32,128]{2,1,0:T(8,128)S(1)}, u32[]{:S(2)}, u32[]{:S(2)}) collective-permute-start(f32[32,32,128]{2,1,0:T(8,128)S(1)} %bitcast.43), channel_id=1, source_target_pairs={{0,32},{32,64},{64,96},{96,128},{128,160},{160,192},{192,224},{224... | collective-permute-start | bytes 1572872 | tf_op jit(solution)/shard_map/ppermute | solution.py:37
  59.7 33.6 %copy-start.1 = (f32[128,128,1]{1,0,2:T(8,128)S(1)}, f32[128,128,1]{1,0,2:T(8,128)}, u32[]{:S(2)}) copy-start(f32[128,128,1]{1,0,2:T(8,128)} %constant.9) | copy-start | bytes 196612
  60.1 27.7 %collective-permute-start.15 = (f32[64,32,128]{2,1,0:T(8,128)S(1)}, f32[64,32,128]{2,1,0:T(8,128)S(1)}, u32[]{:S(2)}, u32[]{:S(2)}) collective-permute-start(f32[64,32,128]{2,1,0:T(8,128)S(1)} %fusion.17), channel_id=1, source_target_pairs={{1,0},{2,1},{3,2},{4,3},{5,4},{6,5},{7,6},{8,7},{9,8},{10,9},{11,1... | collective-permute-start | bytes 3145736 | tf_op jit(solution)/shard_map/ppermute | solution.py:40
  65.5 27.8 %collective-permute-start.14 = (f32[64,32,128]{2,1,0:T(8,128)S(1)}, f32[64,32,128]{2,1,0:T(8,128)S(1)}, u32[]{:S(2)}, u32[]{:S(2)}) collective-permute-start(f32[64,32,128]{2,1,0:T(8,128)S(1)} %fusion.17), channel_id=1, source_target_pairs={{0,1},{1,2},{2,3},{3,4},{4,5},{5,6},{6,7},{7,8},{8,9},{9,10},{10,1... | collective-permute-start | bytes 3145736 | tf_op jit(solution)/shard_map/ppermute | solution.py:37

commit v6 on v3

--- a/solution.py
+++ b/solution.py
@@ -74,10 +74,13 @@
 
 def finish_table(table, planes):
     means = table / jnp.float32(SUB * SUB * planes)
-    second = means[:, 1]
-    third = means[:, 2] / (second + EPSILON) ** 1.5
-    fourth = means[:, 3] / (second + EPSILON) ** 2
-    return jnp.stack([means[:, 0], second, third, fourth], axis=1)
+    second = means[:, 1:2]
+    column = lax.broadcasted_iota(jnp.int32, means.shape, 1)
+    ones = jnp.ones_like(means)
+    scale = jnp.where(
+        column == 2, (second + EPSILON) ** 1.5, jnp.where(column == 3, (second + EPSILON) ** 2, ones)
+    )
+    return means / scale
 
 
 def gather_partials(partial, axes):
@@ -106,10 +109,16 @@
     count_x = lax.axis_size("row") * size_x // SUB
     count_y = lax.axis_size("col") * size_y // SUB
     gathered = gather_partials(partial, ("row", "col"))
-    per_x = SUB // size_x
-    per_y = SUB // size_y
-    grouped = gathered.reshape(count_x, per_x, count_y, per_y, len(SPACINGS), 4)
-    table = jnp.transpose(jnp.sum(grouped, axis=(1, 3)), (2, 3, 0, 1))
+    rows, cols = lax.axis_size("row"), lax.axis_size("col")
+    owner = np.zeros((count_x * count_y, rows * cols), np.float32)
+    for r in range(rows):
+        for c in range(cols):
+            owner[(r * size_x // SUB) * count_y + c * size_y // SUB, r * cols + c] = 1.0
+    summed = jnp.dot(
+        jnp.asarray(owner), gathered, precision=lax.Precision.HIGHEST,
+        preferred_element_type=jnp.float32,
+    )
+    table = jnp.transpose(summed.reshape(count_x, count_y, len(SPACINGS), 4), (2, 3, 0, 1))
     return (current, finish_table(table, planes))
 
 

time: 116 us -> 117 us (level)
  blocking collectives: 18.1 us -> 0 us
  starting transfers between devices: 21.7 us -> 34.7 us
  waiting for transfers between devices: 61.9 us -> 67.2 us
    ppermute x6, waiting for transfers between devices: 31.7 us -> 0.02 us  [padded_1(): lax.ppermute(lax.slice_in_dim(block, 0, width, axis=dim), axis, backward)]
    ppermute x6, waiting for transfers between devices: 30.3 us -> 55 us  [padded_1(): lax.ppermute(lax.slice_in_dim(block, block.shape[dim] - width, None, axis...]
    all_to_all x1 -> x0, blocking collectives: 18.1 us -> none  [gather_partials(): return lax.all_to_all(sent, axes, 0, 0, tiled=True)]
    all_to_all x0 -> x1, waiting for transfers between devices: none -> 12.2 us  [gather_partials(): return lax.all_to_all(sent, axes, 0, 0, tiled=True)]
    all_to_all x0 -> x1, starting transfers between devices: none -> 10.1 us  [gather_partials(): return lax.all_to_all(sent, axes, 0, 0, tiled=True)]
    ppermute x6, starting transfers between devices: 18.6 us -> 22 us  [padded_1(): lax.ppermute(lax.slice_in_dim(block, 0, width, axis=dim), axis, backward)]
  transfers between devices with their start and end apart: 12 -> 13, of which waited for: 9 -> 7; matrix products, arithmetic and copies ran while one was open for 2% -> 2% of each run, Pallas kernels for 0% -> 0%
where the time goes in v6:
time: 117 us; the launch traced here: 115 us
  waiting for transfers between devices  67.2 us (57%)
  starting transfers between devices  34.7 us (30%)
  matrix products  4.28 us (4%)
  local copies, waits for them, and re-layouts  3.78 us (3%)
  other arithmetic  3.73 us (3%)
    ppermute x6, waiting for transfers between devices, padded_1(): lax.ppermute(lax.slice_in_dim(block, block.shape[dim] - width, None, axis...  55 us
    ppermute x6, starting transfers between devices, padded_1(): lax.ppermute(lax.slice_in_dim(block, 0, width, axis=dim), axis, backward)  22 us
    all_to_all x1, waiting for transfers between devices, gather_partials(): return lax.all_to_all(sent, axes, 0, 0, tiled=True)  12.2 us
    all_to_all x1, starting transfers between devices, gather_partials(): return lax.all_to_all(sent, axes, 0, 0, tiled=True)  10.1 us
    dot_general x3, matrix products, depth_pass(): jnp.dot(flat, jnp.asarray(depth_matrix(planes, spacing)), precision=lax.P...  4.1 us
    ppermute x6, starting transfers between devices, padded_1(): lax.ppermute(lax.slice_in_dim(block, block.shape[dim] - width, None, axis...  2.55 us
  transfers between devices with their start and end apart: 13, of which 7 were waited for; matrix products, arithmetic and copies ran while one was open for 2% of the time, Pallas kernels for 0%

profile of v6, /device:TPU:8, one launch (start us, length us, event | category | flops | bytes accessed | tf_op | source)
XLA Modules:
  0.0 114.5 jit_solution(1807618576935925221)
XLA Ops:
  0.6 1.0 fusion.77
  1.6 1.7 %collective-permute-start.1 = (f32[8,32,128]{2,1,0:T(8,128)S(1)}, f32[8,32,128]{2,1,0:T(8,128)S(1)}, u32[]{:S(2)}, u32[]{:S(2)}) collective-permute-start(f32[8,32,128]{2,1,0:T(8,128)S(1)} %get-tuple-element.27), channel_id=1, source_target_pairs={{32,0},{64,32},{96,64},{128,96},{160,128},{192,160},{224,192},{0,2... | collective-permute-start | bytes 393224 | tf_op jit(solution)/shard_map/ppermute | solution.py:28
  3.4 2.6 %collective-permute-done = f32[8,32,128]{2,1,0:T(8,128)S(1)} collective-permute-done((f32[8,32,128]{2,1,0:T(8,128)S(1)}, f32[8,32,128]{2,1,0:T(8,128)S(1)}, u32[]{:S(2)}, u32[]{:S(2)}) %collective-permute-start) | collective-permute-done | bytes 131104 | tf_op jit(solution)/shard_map/ppermute | solution.py:25
  6.1 1.6 %constant_dynamic-update-slice_fusion = (f32[72,32,128]{2,1,0:T(8,128)S(1)}, f32[72,32,128]{2,1,0:T(8,128)S(1)}) fusion(f32[72,32,128]{2,1,0:T(8,128)S(1)} %constant_dynamic-update-slice_fusion.1, f32[64,32,128]{2,1,0:T(8,128)} %param.5), kind=kLoop, calls=%fused_computation.110 | loop fusion | bytes 3145728 | tf_op jit(solution)/shard_map/concatenate | solution.py:29
  7.7 0.4 fusion.58
  8.1 2.0 %collective-permute-start.2 = (f32[64,8,128]{2,1,0:T(8,128)S(1)}, f32[64,8,128]{2,1,0:T(8,128)S(1)}, u32[]{:S(2)}, u32[]{:S(2)}) collective-permute-start(f32[64,8,128]{2,1,0:T(8,128)S(1)} %get-tuple-element.22), channel_id=1, source_target_pairs={{0,1},{1,2},{2,3},{3,4},{4,5},{5,6},{6,7},{7,8},{8,9},{9,10},{10,1... | collective-permute-start | bytes 786440 | tf_op jit(solution)/shard_map/ppermute | solution.py:25
  10.1 6.2 %collective-permute-start.3 = (f32[64,8,128]{2,1,0:T(8,128)S(1)}, f32[64,8,128]{2,1,0:T(8,128)S(1)}, u32[]{:S(2)}, u32[]{:S(2)}) collective-permute-start(f32[64,8,128]{2,1,0:T(8,128)S(1)} %get-tuple-element.23), channel_id=1, source_target_pairs={{1,0},{2,1},{3,2},{4,3},{5,4},{6,5},{7,6},{8,7},{9,8},{10,9},{11,1... | collective-permute-start | bytes 786440 | tf_op jit(solution)/shard_map/ppermute | solution.py:28
  16.3 6.4 %collective-permute-done.2 = f32[64,8,128]{2,1,0:T(8,128)S(1)} collective-permute-done((f32[64,8,128]{2,1,0:T(8,128)S(1)}, f32[64,8,128]{2,1,0:T(8,128)S(1)}, u32[]{:S(2)}, u32[]{:S(2)}) %collective-permute-start.2) | collective-permute-done | bytes 262176 | tf_op jit(solution)/shard_map/ppermute | solution.py:25
  22.8 0.5 fusion.12
  23.3 1.0 fusion.80
  24.4 1.7 %collective-permute-start.5 = (f32[16,32,128]{2,1,0:T(8,128)S(1)}, f32[16,32,128]{2,1,0:T(8,128)S(1)}, u32[]{:S(2)}, u32[]{:S(2)}) collective-permute-start(f32[16,32,128]{2,1,0:T(8,128)S(1)} %bitcast.53), channel_id=1, source_target_pairs={{32,0},{64,32},{96,64},{128,96},{160,128},{192,160},{224,192},{0,2... | collective-permute-start | bytes 786440 | tf_op jit(solution)/shard_map/ppermute | solution.py:28
  26.1 4.1 %collective-permute-done.4 = f32[16,32,128]{2,1,0:T(8,128)S(1)} collective-permute-done((f32[16,32,128]{2,1,0:T(8,128)S(1)}, f32[16,32,128]{2,1,0:T(8,128)S(1)}, u32[]{:S(2)}, u32[]{:S(2)}) %collective-permute-start.4) | collective-permute-done | bytes 262176 | tf_op jit(solution)/shard_map/ppermute | solution.py:25
  30.2 0.4 fusion.72
  30.7 5.3 %collective-permute-start.7 = (f32[64,16,128]{2,1,0:T(8,128)S(1)}, f32[64,16,128]{2,1,0:T(8,128)S(1)}, u32[]{:S(2)}, u32[]{:S(2)}) collective-permute-start(f32[64,16,128]{2,1,0:T(8,128)S(1)} %get-tuple-element.19), channel_id=1, source_target_pairs={{1,0},{2,1},{3,2},{4,3},{5,4},{6,5},{7,6},{8,7},{9,8},{10,9},{11,1... | collective-permute-start | bytes 1572872 | tf_op jit(solution)/shard_map/ppermute | solution.py:28
  36.1 12.2 %collective-permute-done.6 = f32[64,16,128]{2,1,0:T(8,128)S(1)} collective-permute-done((f32[64,16,128]{2,1,0:T(8,128)S(1)}, f32[64,16,128]{2,1,0:T(8,128)S(1)}, u32[]{:S(2)}, u32[]{:S(2)}) %collective-permute-start.6) | collective-permute-done | bytes 524320 | tf_op jit(solution)/shard_map/ppermute | solution.py:25
  48.3 0.4 fusion.34
  48.7 1.0 fusion.79
  49.8 0.4 collective-permute-start.8
  50.1 1.4 %collective-permute-start.9 = (f32[32,32,128]{2,1,0:T(8,128)S(1)}, f32[32,32,128]{2,1,0:T(8,128)S(1)}, u32[]{:S(2)}, u32[]{:S(2)}) collective-permute-start(f32[32,32,128]{2,1,0:T(8,128)S(1)} %bitcast.51), channel_id=1, source_target_pairs={{32,0},{64,32},{96,64},{128,96},{160,128},{192,160},{224,192},{0,2... | collective-permute-start | bytes 1572872 | tf_op jit(solution)/shard_map/ppermute | solution.py:28
  51.5 6.9 %collective-permute-done.8 = f32[32,32,128]{2,1,0:T(8,128)S(1)} collective-permute-done((f32[32,32,128]{2,1,0:T(8,128)S(1)}, f32[32,32,128]{2,1,0:T(8,128)S(1)}, u32[]{:S(2)}, u32[]{:S(2)}) %collective-permute-start.8) | collective-permute-done | bytes 524320 | tf_op jit(solution)/shard_map/ppermute | solution.py:25
  58.4 0.4 fusion.26
  58.9 5.6 %collective-permute-start.11 = (f32[64,32,128]{2,1,0:T(8,128)S(1)}, f32[64,32,128]{2,1,0:T(8,128)S(1)}, u32[]{:S(2)}, u32[]{:S(2)}) collective-permute-start(f32[64,32,128]{2,1,0:T(8,128)S(1)} %fusion.26), channel_id=1, source_target_pairs={{1,0},{2,1},{3,2},{4,3},{5,4},{6,5},{7,6},{8,7},{9,8},{10,9},{11,1... | collective-permute-start | bytes 3145736 | tf_op jit(solution)/shard_map/ppermute | solution.py:28
  64.5 0.3 abs_reduce_fusion.2
  64.8 0.3 abs_reduce_fusion.1
  65.1 22.8 %collective-permute-done.10 = f32[64,32,128]{2,1,0:T(8,128)S(1)} collective-permute-done((f32[64,32,128]{2,1,0:T(8,128)S(1)}, f32[64,32,128]{2,1,0:T(8,128)S(1)}, u32[]{:S(2)}, u32[]{:S(2)}) %collective-permute-start.10) | collective-permute-done | bytes 1048608 | tf_op jit(solution)/shard_map/ppermute | solution.py:25
  87.9 2.1 %fusion.78 = (f32[64,32,128]{2,1,0:T(8,128)S(1)}, f32[64,32,128]{2,1,0:T(8,128)}) fusion(f32[64,32,128]{2,1,0:T(8,128)S(1)} %bitcast.46, f32[128,128,1]{1,0,2:T(8,128)S(1)} %copy-done.1, f32[64,32,128]{2,1,0:T(8,128)S(1)} %collective-permute-done.11, f32[64,32,128]{2,1,0:T(8,128)S(1)} %fusion.26, f32[64,32,128]{2,1,0:T(8,128)S(1)} %collective-permute-done.10), kind=kOutput, calls=%fused_computation.133 | convolution fusion | flops 405798912 | bytes 6356992 | tf_op jit(solution)/shard_map/dot_general | solution.py:54
  90.0 0.3 abs_reduce_fusion
  90.5 0.7 broadcast_in_dim.28
  91.2 10.1 %all-to-all-start = ((f32[256,1,12]{2,1,0:T(1,128)}), f32[256,1,12]{2,1,0:T(1,128)S(1)}, u32[]{:S(2)}, u32[]{:S(2)}) async-start(f32[256,1,12]{2,1,0:T(1,128)} %broadcast_in_dim.28), calls=%async_computation | async-start | bytes 262144 | tf_op jit(solution)/shard_map/all_to_all | solution.py:92
  101.3 12.2 %all-to-all-done = f32[256,1,12]{2,1,0:T(1,128)S(1)} async-done(((f32[256,1,12]{2,1,0:T(1,128)}), f32[256,1,12]{2,1,0:T(1,128)S(1)}, u32[]{:S(2)}, u32[]{:S(2)}) %all-to-all-start) | async-done | bytes 12320 | tf_op jit(solution)/shard_map/all_to_all | solution.py:92
  113.4 0.2 fusion
  113.8 0.7 select_divide_fusion
  (34 shorter events, 0.9 us)
Async XLA Ops:
  1.6 4.4 %collective-permute-start = (f32[8,32,128]{2,1,0:T(8,128)S(1)}, f32[8,32,128]{2,1,0:T(8,128)S(1)}, u32[]{:S(2)}, u32[]{:S(2)}) collective-permute-start(f32[8,32,128]{2,1,0:T(8,128)S(1)} %get-tuple-element.26), channel_id=1, source_target_pairs={{0,32},{32,64},{64,96},{96,128},{128,160},{160,192},{192,224},{224... | collective-permute-start | bytes 393224 | tf_op jit(solution)/shard_map/ppermute | solution.py:25
  1.6 6.0 %collective-permute-start.1 = (f32[8,32,128]{2,1,0:T(8,128)S(1)}, f32[8,32,128]{2,1,0:T(8,128)S(1)}, u32[]{:S(2)}, u32[]{:S(2)}) collective-permute-start(f32[8,32,128]{2,1,0:T(8,128)S(1)} %get-tuple-element.27), channel_id=1, source_target_pairs={{32,0},{64,32},{96,64},{128,96},{160,128},{192,160},{224,192},{0,2... | collective-permute-start | bytes 393224 | tf_op jit(solution)/shard_map/ppermute | solution.py:28
  6.0 1.6 %copy-start = (f32[64,32,128]{2,1,0:T(8,128)S(1)}, f32[64,32,128]{2,1,0:T(8,128)}, u32[]{:S(2)}) copy-start(f32[64,32,128]{2,1,0:T(8,128)} %param.5) | copy-start | bytes 3145732
  8.1 14.7 %collective-permute-start.2 = (f32[64,8,128]{2,1,0:T(8,128)S(1)}, f32[64,8,128]{2,1,0:T(8,128)S(1)}, u32[]{:S(2)}, u32[]{:S(2)}) collective-permute-start(f32[64,8,128]{2,1,0:T(8,128)S(1)} %get-tuple-element.22), channel_id=1, source_target_pairs={{0,1},{1,2},{2,3},{3,4},{4,5},{5,6},{6,7},{7,8},{8,9},{9,10},{10,1... | collective-permute-start | bytes 786440 | tf_op jit(solution)/shard_map/ppermute | solution.py:25
  10.1 13.2 %copy-start.3 = (f32[128,128]{1,0:T(8,128)S(1)}, f32[128,128]{1,0:T(8,128)}, u32[]{:S(2)}) copy-start(f32[128,128]{1,0:T(8,128)} %constant.29.clone) | copy-start | bytes 196612
  10.1 12.7 %collective-permute-start.3 = (f32[64,8,128]{2,1,0:T(8,128)S(1)}, f32[64,8,128]{2,1,0:T(8,128)S(1)}, u32[]{:S(2)}, u32[]{:S(2)}) collective-permute-start(f32[64,8,128]{2,1,0:T(8,128)S(1)} %get-tuple-element.23), channel_id=1, source_target_pairs={{1,0},{2,1},{3,2},{4,3},{5,4},{6,5},{7,6},{8,7},{9,8},{10,9},{11,1... | collective-permute-start | bytes 786440 | tf_op jit(solution)/shard_map/ppermute | solution.py:28
  24.3 5.8 %collective-permute-start.4 = (f32[16,32,128]{2,1,0:T(8,128)S(1)}, f32[16,32,128]{2,1,0:T(8,128)S(1)}, u32[]{:S(2)}, u32[]{:S(2)}) collective-permute-start(f32[16,32,128]{2,1,0:T(8,128)S(1)} %bitcast.54), channel_id=1, source_target_pairs={{0,32},{32,64},{64,96},{96,128},{128,160},{160,192},{192,224},{224... | collective-permute-start | bytes 786440 | tf_op jit(solution)/shard_map/ppermute | solution.py:25
  24.4 5.8 %collective-permute-start.5 = (f32[16,32,128]{2,1,0:T(8,128)S(1)}, f32[16,32,128]{2,1,0:T(8,128)S(1)}, u32[]{:S(2)}, u32[]{:S(2)}) collective-permute-start(f32[16,32,128]{2,1,0:T(8,128)S(1)} %bitcast.53), channel_id=1, source_target_pairs={{32,0},{64,32},{96,64},{128,96},{160,128},{192,160},{224,192},{0,2... | collective-permute-start | bytes 786440 | tf_op jit(solution)/shard_map/ppermute | solution.py:28
  30.6 17.7 %collective-permute-start.6 = (f32[64,16,128]{2,1,0:T(8,128)S(1)}, f32[64,16,128]{2,1,0:T(8,128)S(1)}, u32[]{:S(2)}, u32[]{:S(2)}) collective-permute-start(f32[64,16,128]{2,1,0:T(8,128)S(1)} %get-tuple-element.18), channel_id=1, source_target_pairs={{0,1},{1,2},{2,3},{3,4},{4,5},{5,6},{6,7},{7,8},{8,9},{9,10},{10,1... | collective-permute-start | bytes 1572872 | tf_op jit(solution)/shard_map/ppermute | solution.py:25
  30.7 18.0 %copy-start.2 = (f32[128,128]{1,0:T(8,128)S(1)}, f32[128,128]{1,0:T(8,128)}, u32[]{:S(2)}) copy-start(f32[128,128]{1,0:T(8,128)} %constant.30.clone) | copy-start | bytes 196612
  30.7 17.6 %collective-permute-start.7 = (f32[64,16,128]{2,1,0:T(8,128)S(1)}, f32[64,16,128]{2,1,0:T(8,128)S(1)}, u32[]{:S(2)}, u32[]{:S(2)}) collective-permute-start(f32[64,16,128]{2,1,0:T(8,128)S(1)} %get-tuple-element.19), channel_id=1, source_target_pairs={{1,0},{2,1},{3,2},{4,3},{5,4},{6,5},{7,6},{8,7},{9,8},{10,9},{11,1... | collective-permute-start | bytes 1572872 | tf_op jit(solution)/shard_map/ppermute | solution.py:28
  49.8 8.6 %collective-permute-start.8 = (f32[32,32,128]{2,1,0:T(8,128)S(1)}, f32[32,32,128]{2,1,0:T(8,128)S(1)}, u32[]{:S(2)}, u32[]{:S(2)}) collective-permute-start(f32[32,32,128]{2,1,0:T(8,128)S(1)} %bitcast.52), channel_id=1, source_target_pairs={{0,32},{32,64},{64,96},{96,128},{128,160},{160,192},{192,224},{224... | collective-permute-start | bytes 1572872 | tf_op jit(solution)/shard_map/ppermute | solution.py:25
  50.1 8.3 %collective-permute-start.9 = (f32[32,32,128]{2,1,0:T(8,128)S(1)}, f32[32,32,128]{2,1,0:T(8,128)S(1)}, u32[]{:S(2)}, u32[]{:S(2)}) collective-permute-start(f32[32,32,128]{2,1,0:T(8,128)S(1)} %bitcast.51), channel_id=1, source_target_pairs={{32,0},{64,32},{96,64},{128,96},{160,128},{192,160},{224,192},{0,2... | collective-permute-start | bytes 1572872 | tf_op jit(solution)/shard_map/ppermute | solution.py:28
  58.8 29.1 %copy-start.1 = (f32[128,128,1]{1,0,2:T(8,128)S(1)}, f32[128,128,1]{1,0,2:T(8,128)}, u32[]{:S(2)}) copy-start(f32[128,128,1]{1,0,2:T(8,128)} %constant.33) | copy-start | bytes 196612
  58.8 29.1 %collective-permute-start.10 = (f32[64,32,128]{2,1,0:T(8,128)S(1)}, f32[64,32,128]{2,1,0:T(8,128)S(1)}, u32[]{:S(2)}, u32[]{:S(2)}) collective-permute-start(f32[64,32,128]{2,1,0:T(8,128)S(1)} %fusion.26), channel_id=1, source_target_pairs={{0,1},{1,2},{2,3},{3,4},{4,5},{5,6},{6,7},{7,8},{8,9},{9,10},{10,1... | collective-permute-start | bytes 3145736 | tf_op jit(solution)/shard_map/ppermute | solution.py:25
  58.9 29.0 %collective-permute-start.11 = (f32[64,32,128]{2,1,0:T(8,128)S(1)}, f32[64,32,128]{2,1,0:T(8,128)S(1)}, u32[]{:S(2)}, u32[]{:S(2)}) collective-permute-start(f32[64,32,128]{2,1,0:T(8,128)S(1)} %fusion.26), channel_id=1, source_target_pairs={{1,0},{2,1},{3,2},{4,3},{5,4},{6,5},{7,6},{8,7},{9,8},{10,9},{11,1... | collective-permute-start | bytes 3145736 | tf_op jit(solution)/shard_map/ppermute | solution.py:28
  90.0 23.4 %copy-start.4 = (f32[8,256]{1,0:T(8,128)S(1)}, f32[8,256]{1,0:T(8,128)}, u32[]{:S(2)}) copy-start(f32[8,256]{1,0:T(8,128)} %constant.32.clone) | copy-start | bytes 24580
  91.2 22.3 %all-to-all-start = ((f32[256,1,12]{2,1,0:T(1,128)}), f32[256,1,12]{2,1,0:T(1,128)S(1)}, u32[]{:S(2)}, u32[]{:S(2)}) async-start(f32[256,1,12]{2,1,0:T(1,128)} %broadcast_in_dim.28), calls=%async_computation | async-start | bytes 262144 | tf_op jit(solution)/shard_map/all_to_all | solution.py:92

commit v7 on v6

--- a/solution.py
+++ b/solution.py
@@ -10,6 +10,7 @@
 SPLINE_TAPS = (0.0625, 0.25, 0.375, 0.25, 0.0625)
 SPACINGS = (4, 8, 16)
 EPSILON = 1e-06
+REACH_AHEAD = (1,)
 
 
 def ring_pairs(count):
@@ -97,12 +98,18 @@
     assert SUB % size_x == 0 and SUB % size_y == 0
     sums = []
     current = density
-    for spacing in SPACINGS:
-        padded_x = padded_1(current, "row", 0, 2 * spacing)
-        along_x = holed_pass(padded_x, spacing, 0, size_x)
-        padded_y = padded_1(along_x, "col", 1, 2 * spacing)
+    padded_x = None
+    for scale, spacing in enumerate(SPACINGS):
+        width = 2 * spacing
+        extra = 2 * SPACINGS[scale + 1] if scale + 1 in REACH_AHEAD else 0
+        if padded_x is None:
+            padded_x = padded_1(current, "row", 0, width + extra)
+        along_x = holed_pass(padded_x, spacing, 0, size_x + 2 * extra)
+        padded_y = padded_1(along_x, "col", 1, width)
         along_y = holed_pass(padded_y, spacing, 1, size_y)
         smoother = depth_pass(along_y, spacing)
+        padded_x = smoother if extra else None
+        smoother = lax.slice_in_dim(smoother, extra, extra + size_x, axis=0)
         sums.append(moment_sums(current - smoother))
         current = smoother
     partial = jnp.sum(jnp.stack(sums), axis=-1)

time: 117 us -> 117 us (level)
  waiting for transfers between devices: 67.2 us -> 68.7 us
  local copies, waits for them, and re-layouts: 3.78 us -> 2.57 us
    concatenate x2 -> x1, local copies, waits for them, and re-layouts: 1.57 us -> 0.03 us  [padded_1(): return jnp.concatenate([low, block, high], axis=dim)]
    ppermute x6 -> x5, waiting for transfers between devices: 55 us -> 56.5 us  [padded_1(): lax.ppermute(lax.slice_in_dim(block, block.shape[dim] - width, None, axis...]
    slice x0 -> x1, local copies, waits for them, and re-layouts: none -> 1.25 us  [padded_1(): lax.slice_in_dim(block, 0, width, axis=dim)]
    ppermute x6 -> x5, starting transfers between devices: 22 us -> 20.9 us  [padded_1(): lax.ppermute(lax.slice_in_dim(block, 0, width, axis=dim), axis, backward)]
    ppermute x6 -> x5, starting transfers between devices: 2.55 us -> 2.2 us  [padded_1(): lax.ppermute(lax.slice_in_dim(block, block.shape[dim] - width, None, axis...]
  transfers between devices with their start and end apart: 13 -> 11, of which waited for: 7 -> 6; matrix products, arithmetic and copies ran while one was open for 2% -> 0% of each run, Pallas kernels for 0% -> 0%
where the time goes in v7:
time: 117 us; the launch traced here: 115 us
  waiting for transfers between devices  68.7 us (59%)
  starting transfers between devices  33.9 us (29%)
  matrix products  4.9 us (4%)
  other arithmetic  4.12 us (4%)
  local copies, waits for them, and re-layouts  2.57 us (2%)
    ppermute x5, waiting for transfers between devices, padded_1(): lax.ppermute(lax.slice_in_dim(block, block.shape[dim] - width, None, axis...  56.5 us
    ppermute x5, starting transfers between devices, padded_1(): lax.ppermute(lax.slice_in_dim(block, 0, width, axis=dim), axis, backward)  20.9 us
    all_to_all x1, waiting for transfers between devices, gather_partials(): return lax.all_to_all(sent, axes, 0, 0, tiled=True)  12.2 us
    all_to_all x1, starting transfers between devices, gather_partials(): return lax.all_to_all(sent, axes, 0, 0, tiled=True)  10.8 us
    dot_general x3, matrix products, depth_pass(): jnp.dot(flat, jnp.asarray(depth_matrix(planes, spacing)), precision=lax.P...  4.72 us
  transfers between devices with their start and end apart: 11, of which 6 were waited for; matrix products, arithmetic and copies ran while one was open for 0% of the time, Pallas kernels for 0%

profile of v7, /device:TPU:8, one launch (start us, length us, event | category | flops | bytes accessed | tf_op | source)
XLA Modules:
  0.0 115.0 jit_solution(18416315328083616735)
XLA Ops:
  0.6 1.3 %fusion.68 = (f32[24,32,128]{2,1,0:T(8,128)S(1)}, f32[24,32,128]{2,1,0:T(8,128)S(1)}) fusion(f32[64,32,128]{2,1,0:T(8,128)} %param.5), kind=kLoop, calls=%fused_computation.123 | loop fusion | bytes 1572864 | tf_op jit(solution)/shard_map/slice | solution.py:29
  1.9 1.7 %collective-permute-start.1 = (f32[24,32,128]{2,1,0:T(8,128)S(1)}, f32[24,32,128]{2,1,0:T(8,128)S(1)}, u32[]{:S(2)}, u32[]{:S(2)}) collective-permute-start(f32[24,32,128]{2,1,0:T(8,128)S(1)} %get-tuple-element.26), channel_id=1, source_target_pairs={{32,0},{64,32},{96,64},{128,96},{160,128},{192,160},{224,192},{0,2... | collective-permute-start | bytes 1179656 | tf_op jit(solution)/shard_map/ppermute | solution.py:29
  3.7 5.5 %collective-permute-done = f32[24,32,128]{2,1,0:T(8,128)S(1)} collective-permute-done((f32[24,32,128]{2,1,0:T(8,128)S(1)}, f32[24,32,128]{2,1,0:T(8,128)S(1)}, u32[]{:S(2)}, u32[]{:S(2)}) %collective-permute-start) | collective-permute-done | bytes 393248 | tf_op jit(solution)/shard_map/ppermute | solution.py:26
  9.3 0.4 fusion.10
  9.7 2.0 %collective-permute-start.2 = (f32[96,8,128]{2,1,0:T(8,128)S(1)}, f32[96,8,128]{2,1,0:T(8,128)S(1)}, u32[]{:S(2)}, u32[]{:S(2)}) collective-permute-start(f32[96,8,128]{2,1,0:T(8,128)S(1)} %get-tuple-element.18), channel_id=1, source_target_pairs={{0,1},{1,2},{2,3},{3,4},{4,5},{5,6},{6,7},{7,8},{8,9},{9,10},{10,1... | collective-permute-start | bytes 1179656 | tf_op jit(solution)/shard_map/ppermute | solution.py:26
  11.7 6.2 %collective-permute-start.3 = (f32[96,8,128]{2,1,0:T(8,128)S(1)}, f32[96,8,128]{2,1,0:T(8,128)S(1)}, u32[]{:S(2)}, u32[]{:S(2)}) collective-permute-start(f32[96,8,128]{2,1,0:T(8,128)S(1)} %get-tuple-element.19), channel_id=1, source_target_pairs={{1,0},{2,1},{3,2},{4,3},{5,4},{6,5},{7,6},{8,7},{9,8},{10,9},{11,1... | collective-permute-start | bytes 1179656 | tf_op jit(solution)/shard_map/ppermute | solution.py:29
  17.9 9.0 %collective-permute-done.2 = f32[96,8,128]{2,1,0:T(8,128)S(1)} collective-permute-done((f32[96,8,128]{2,1,0:T(8,128)S(1)}, f32[96,8,128]{2,1,0:T(8,128)S(1)}, u32[]{:S(2)}, u32[]{:S(2)}) %collective-permute-start.2) | collective-permute-done | bytes 393248 | tf_op jit(solution)/shard_map/ppermute | solution.py:26
  26.9 0.7 fusion.3
  27.7 1.4 %fusion.70 = f32[3072,128]{1,0:T(8,128)S(1)} fusion(f32[3072,128]{1,0:T(8,128)S(1)} %bitcast.48, f32[128,128]{1,0:T(8,128)S(1)} %copy-done.3), kind=kOutput, calls=%fused_computation.125 | convolution fusion | flops 603979776 | bytes 3211264 | tf_op jit(solution)/shard_map/dot_general | solution.py:55
  29.1 0.3 fusion.63
  29.4 0.6 fusion.65
  30.2 5.8 %collective-permute-start.5 = (f32[64,16,128]{2,1,0:T(8,128)S(1)}, f32[64,16,128]{2,1,0:T(8,128)S(1)}, u32[]{:S(2)}, u32[]{:S(2)}) collective-permute-start(f32[64,16,128]{2,1,0:T(8,128)S(1)} %get-tuple-element.25), channel_id=1, source_target_pairs={{1,0},{2,1},{3,2},{4,3},{5,4},{6,5},{7,6},{8,7},{9,8},{10,9},{11,1... | collective-permute-start | bytes 1572872 | tf_op jit(solution)/shard_map/ppermute | solution.py:29
  36.0 12.4 %collective-permute-done.4 = f32[64,16,128]{2,1,0:T(8,128)S(1)} collective-permute-done((f32[64,16,128]{2,1,0:T(8,128)S(1)}, f32[64,16,128]{2,1,0:T(8,128)S(1)}, u32[]{:S(2)}, u32[]{:S(2)}) %collective-permute-start.4) | collective-permute-done | bytes 524320 | tf_op jit(solution)/shard_map/ppermute | solution.py:26
  48.4 0.3 fusion.32
  48.7 1.2 %abs_reduce_fusion.1 = (f32[128]{0:T(128)S(1)}, f32[128]{0:T(128)S(1)}, f32[128]{0:T(128)S(1)}, f32[128]{0:T(128)S(1)}, f32[2048,128]{1,0:T(8,128)S(1)}) fusion(f32[2048,128]{1,0:T(8,128)S(1)} %bitcast.53, f32[128,128]{1,0:T(8,128)S(1)} %copy-done.2, f32[3072,128]{1,0:T(8,128)S(1)} %fusion.70), kind=kOutput, calls=%fused_computation.91 | convolution fusion | flops 405011968 | bytes 3213312 | tf_op jit(solution)/shard_map/dot_general | solution.py:55
  50.0 1.7 %collective-permute-start.7 = (f32[32,32,128]{2,1,0:T(8,128)S(1)}, f32[32,32,128]{2,1,0:T(8,128)S(1)}, u32[]{:S(2)}, u32[]{:S(2)}) collective-permute-start(f32[32,32,128]{2,1,0:T(8,128)S(1)} %bitcast.55), channel_id=1, source_target_pairs={{32,0},{64,32},{96,64},{128,96},{160,128},{192,160},{224,192},{0,2... | collective-permute-start | bytes 1572872 | tf_op jit(solution)/shard_map/ppermute | solution.py:29
  51.7 6.9 %collective-permute-done.6 = f32[32,32,128]{2,1,0:T(8,128)S(1)} collective-permute-done((f32[32,32,128]{2,1,0:T(8,128)S(1)}, f32[32,32,128]{2,1,0:T(8,128)S(1)}, u32[]{:S(2)}, u32[]{:S(2)}) %collective-permute-start.6) | collective-permute-done | bytes 524320 | tf_op jit(solution)/shard_map/ppermute | solution.py:26
  58.6 0.4 fusion.24
  59.0 0.1 collective-permute-start.8
  59.1 5.4 %collective-permute-start.9 = (f32[64,32,128]{2,1,0:T(8,128)S(1)}, f32[64,32,128]{2,1,0:T(8,128)S(1)}, u32[]{:S(2)}, u32[]{:S(2)}) collective-permute-start(f32[64,32,128]{2,1,0:T(8,128)S(1)} %fusion.24), channel_id=1, source_target_pairs={{1,0},{2,1},{3,2},{4,3},{5,4},{6,5},{7,6},{8,7},{9,8},{10,9},{11,1... | collective-permute-start | bytes 3145736 | tf_op jit(solution)/shard_map/ppermute | solution.py:29
  64.5 0.3 abs_reduce_fusion.2
  64.8 22.8 %collective-permute-done.8 = f32[64,32,128]{2,1,0:T(8,128)S(1)} collective-permute-done((f32[64,32,128]{2,1,0:T(8,128)S(1)}, f32[64,32,128]{2,1,0:T(8,128)S(1)}, u32[]{:S(2)}, u32[]{:S(2)}) %collective-permute-start.8) | collective-permute-done | bytes 1048608 | tf_op jit(solution)/shard_map/ppermute | solution.py:26
  87.6 2.2 %fusion.69 = (f32[64,32,128]{2,1,0:T(8,128)S(1)}, f32[64,32,128]{2,1,0:T(8,128)}) fusion(f32[64,32,128]{2,1,0:T(8,128)S(1)} %bitcast.47, f32[128,128,1]{1,0,2:T(8,128)S(1)} %copy-done.1, f32[64,32,128]{2,1,0:T(8,128)S(1)} %collective-permute-done.9, f32[64,32,128]{2,1,0:T(8,128)S(1)} %fusion.24, f32[64,32,128]{2,1,0:T(8,128)S(1)} %collective-permute-done.8), kind=kOutput, calls=%fused_computation.124 | convolution fusion | flops 405798912 | bytes 6356992 | tf_op jit(solution)/shard_map/dot_general | solution.py:55
  89.8 0.3 abs_reduce_fusion
  90.1 0.1 maximum_reduce_fusion
  90.1 0.1 broadcast_in_dim.27
  90.2 0.7 broadcast_in_dim.28
  90.9 10.8 %all-to-all-start = ((f32[256,1,12]{2,1,0:T(1,128)}), f32[256,1,12]{2,1,0:T(1,128)S(1)}, u32[]{:S(2)}, u32[]{:S(2)}) async-start(f32[256,1,12]{2,1,0:T(1,128)} %broadcast_in_dim.28), calls=%async_computation | async-start | bytes 262144 | tf_op jit(solution)/shard_map/all_to_all | solution.py:93
  101.7 12.2 %all-to-all-done = f32[256,1,12]{2,1,0:T(1,128)S(1)} async-done(((f32[256,1,12]{2,1,0:T(1,128)}), f32[256,1,12]{2,1,0:T(1,128)S(1)}, u32[]{:S(2)}, u32[]{:S(2)}) %all-to-all-start) | async-done | bytes 12320 | tf_op jit(solution)/shard_map/all_to_all | solution.py:93
  113.9 0.2 fusion.14
  114.1 0.1 copy.8
  114.3 0.7 select_divide_fusion
  (29 shorter events, 0.6 us)
Async XLA Ops:
  0.6 8.5 %copy-start = (f32[64,32,128]{2,1,0:T(8,128)S(1)}, f32[64,32,128]{2,1,0:T(8,128)}, u32[]{:S(2)}) copy-start(f32[64,32,128]{2,1,0:T(8,128)} %param.5) | copy-start | bytes 3145732
  1.9 7.2 %collective-permute-start = (f32[24,32,128]{2,1,0:T(8,128)S(1)}, f32[24,32,128]{2,1,0:T(8,128)S(1)}, u32[]{:S(2)}, u32[]{:S(2)}) collective-permute-start(f32[24,32,128]{2,1,0:T(8,128)S(1)} %get-tuple-element.27), channel_id=1, source_target_pairs={{0,32},{32,64},{64,96},{96,128},{128,160},{160,192},{192,224},{224... | collective-permute-start | bytes 1179656 | tf_op jit(solution)/shard_map/ppermute | solution.py:26
  1.9 7.3 %collective-permute-start.1 = (f32[24,32,128]{2,1,0:T(8,128)S(1)}, f32[24,32,128]{2,1,0:T(8,128)S(1)}, u32[]{:S(2)}, u32[]{:S(2)}) collective-permute-start(f32[24,32,128]{2,1,0:T(8,128)S(1)} %get-tuple-element.26), channel_id=1, source_target_pairs={{32,0},{64,32},{96,64},{128,96},{160,128},{192,160},{224,192},{0,2... | collective-permute-start | bytes 1179656 | tf_op jit(solution)/shard_map/ppermute | solution.py:29
  9.7 17.2 %collective-permute-start.2 = (f32[96,8,128]{2,1,0:T(8,128)S(1)}, f32[96,8,128]{2,1,0:T(8,128)S(1)}, u32[]{:S(2)}, u32[]{:S(2)}) collective-permute-start(f32[96,8,128]{2,1,0:T(8,128)S(1)} %get-tuple-element.18), channel_id=1, source_target_pairs={{0,1},{1,2},{2,3},{3,4},{4,5},{5,6},{6,7},{7,8},{8,9},{9,10},{10,1... | collective-permute-start | bytes 1179656 | tf_op jit(solution)/shard_map/ppermute | solution.py:26
  11.7 16.0 %copy-start.3 = (f32[128,128]{1,0:T(8,128)S(1)}, f32[128,128]{1,0:T(8,128)}, u32[]{:S(2)}) copy-start(f32[128,128]{1,0:T(8,128)} %constant.12.clone) | copy-start | bytes 196612
  11.7 15.2 %collective-permute-start.3 = (f32[96,8,128]{2,1,0:T(8,128)S(1)}, f32[96,8,128]{2,1,0:T(8,128)S(1)}, u32[]{:S(2)}, u32[]{:S(2)}) collective-permute-start(f32[96,8,128]{2,1,0:T(8,128)S(1)} %get-tuple-element.19), channel_id=1, source_target_pairs={{1,0},{2,1},{3,2},{4,3},{5,4},{6,5},{7,6},{8,7},{9,8},{10,9},{11,1... | collective-permute-start | bytes 1179656 | tf_op jit(solution)/shard_map/ppermute | solution.py:29
  30.1 18.3 %collective-permute-start.4 = (f32[64,16,128]{2,1,0:T(8,128)S(1)}, f32[64,16,128]{2,1,0:T(8,128)S(1)}, u32[]{:S(2)}, u32[]{:S(2)}) collective-permute-start(f32[64,16,128]{2,1,0:T(8,128)S(1)} %get-tuple-element.24), channel_id=1, source_target_pairs={{0,1},{1,2},{2,3},{3,4},{4,5},{5,6},{6,7},{7,8},{8,9},{9,10},{10,1... | collective-permute-start | bytes 1572872 | tf_op jit(solution)/shard_map/ppermute | solution.py:26
  30.2 18.5 %copy-start.2 = (f32[128,128]{1,0:T(8,128)S(1)}, f32[128,128]{1,0:T(8,128)}, u32[]{:S(2)}) copy-start(f32[128,128]{1,0:T(8,128)} %constant.13.clone) | copy-start | bytes 196612
  30.2 18.2 %collective-permute-start.5 = (f32[64,16,128]{2,1,0:T(8,128)S(1)}, f32[64,16,128]{2,1,0:T(8,128)S(1)}, u32[]{:S(2)}, u32[]{:S(2)}) collective-permute-start(f32[64,16,128]{2,1,0:T(8,128)S(1)} %get-tuple-element.25), channel_id=1, source_target_pairs={{1,0},{2,1},{3,2},{4,3},{5,4},{6,5},{7,6},{8,7},{9,8},{10,9},{11,1... | collective-permute-start | bytes 1572872 | tf_op jit(solution)/shard_map/ppermute | solution.py:29
  50.0 8.6 %collective-permute-start.6 = (f32[32,32,128]{2,1,0:T(8,128)S(1)}, f32[32,32,128]{2,1,0:T(8,128)S(1)}, u32[]{:S(2)}, u32[]{:S(2)}) collective-permute-start(f32[32,32,128]{2,1,0:T(8,128)S(1)} %bitcast.56), channel_id=1, source_target_pairs={{0,32},{32,64},{64,96},{96,128},{128,160},{160,192},{192,224},{224... | collective-permute-start | bytes 1572872 | tf_op jit(solution)/shard_map/ppermute | solution.py:26
  50.0 8.6 %collective-permute-start.7 = (f32[32,32,128]{2,1,0:T(8,128)S(1)}, f32[32,32,128]{2,1,0:T(8,128)S(1)}, u32[]{:S(2)}, u32[]{:S(2)}) collective-permute-start(f32[32,32,128]{2,1,0:T(8,128)S(1)} %bitcast.55), channel_id=1, source_target_pairs={{32,0},{64,32},{96,64},{128,96},{160,128},{192,160},{224,192},{0,2... | collective-permute-start | bytes 1572872 | tf_op jit(solution)/shard_map/ppermute | solution.py:29
  58.6 29.0 %copy-start.1 = (f32[128,128,1]{1,0,2:T(8,128)S(1)}, f32[128,128,1]{1,0,2:T(8,128)}, u32[]{:S(2)}) copy-start(f32[128,128,1]{1,0,2:T(8,128)} %constant.36) | copy-start | bytes 196612
  59.0 28.6 %collective-permute-start.8 = (f32[64,32,128]{2,1,0:T(8,128)S(1)}, f32[64,32,128]{2,1,0:T(8,128)S(1)}, u32[]{:S(2)}, u32[]{:S(2)}) collective-permute-start(f32[64,32,128]{2,1,0:T(8,128)S(1)} %fusion.24), channel_id=1, source_target_pairs={{0,1},{1,2},{2,3},{3,4},{4,5},{5,6},{6,7},{7,8},{8,9},{9,10},{10,1... | collective-permute-start | bytes 3145736 | tf_op jit(solution)/shard_map/ppermute | solution.py:26
  59.1 28.5 %collective-permute-start.9 = (f32[64,32,128]{2,1,0:T(8,128)S(1)}, f32[64,32,128]{2,1,0:T(8,128)S(1)}, u32[]{:S(2)}, u32[]{:S(2)}) collective-permute-start(f32[64,32,128]{2,1,0:T(8,128)S(1)} %fusion.24), channel_id=1, source_target_pairs={{1,0},{2,1},{3,2},{4,3},{5,4},{6,5},{7,6},{8,7},{9,8},{10,9},{11,1... | collective-permute-start | bytes 3145736 | tf_op jit(solution)/shard_map/ppermute | solution.py:29
  64.8 49.1 %copy-start.4 = (f32[8,256]{1,0:T(8,128)S(1)}, f32[8,256]{1,0:T(8,128)}, u32[]{:S(2)}) copy-start(f32[8,256]{1,0:T(8,128)} %constant.35.clone) | copy-start | bytes 24580
  90.9 23.0 %all-to-all-start = ((f32[256,1,12]{2,1,0:T(1,128)}), f32[256,1,12]{2,1,0:T(1,128)S(1)}, u32[]{:S(2)}, u32[]{:S(2)}) async-start(f32[256,1,12]{2,1,0:T(1,128)} %broadcast_in_dim.28), calls=%async_computation | async-start | bytes 262144 | tf_op jit(solution)/shard_map/all_to_all | solution.py:93

commit v8 on v6

--- a/solution.py
+++ b/solution.py
@@ -97,12 +97,26 @@
     assert SUB % size_x == 0 and SUB % size_y == 0
     sums = []
     current = density
-    for spacing in SPACINGS:
-        padded_x = padded_1(current, "row", 0, 2 * spacing)
-        along_x = holed_pass(padded_x, spacing, 0, size_x)
-        padded_y = padded_1(along_x, "col", 1, 2 * spacing)
-        along_y = holed_pass(padded_y, spacing, 1, size_y)
-        smoother = depth_pass(along_y, spacing)
+    padded_x = None
+    for scale, spacing in enumerate(SPACINGS):
+        width = 2 * spacing
+        if scale == 0:
+            extra = 2 * SPACINGS[1]
+            padded_y = padded_1(current, "col", 1, width)
+            along_y = holed_pass(padded_y, spacing, 1, size_y)
+            padded_x = padded_1(along_y, "row", 0, width + extra)
+            along_x = holed_pass(padded_x, spacing, 0, size_x + 2 * extra)
+            wide = depth_pass(along_x, spacing)
+            padded_x = wide
+            smoother = lax.slice_in_dim(wide, extra, extra + size_x, axis=0)
+        else:
+            if padded_x is None:
+                padded_x = padded_1(current, "row", 0, width)
+            along_x = holed_pass(padded_x, spacing, 0, size_x)
+            padded_x = None
+            padded_y = padded_1(along_x, "col", 1, width)
+            along_y = holed_pass(padded_y, spacing, 1, size_y)
+            smoother = depth_pass(along_y, spacing)
         sums.append(moment_sums(current - smoother))
         current = smoother
     partial = jnp.sum(jnp.stack(sums), axis=-1)

time: 117 us -> 115 us (0.983)
  waiting for transfers between devices: 67.2 us -> 65 us
    ppermute x6 -> x5, waiting for transfers between devices: 55 us -> 52.7 us  [padded_1(): lax.ppermute(lax.slice_in_dim(block, block.shape[dim] - width, None, axis...]
    all_to_all x1, starting transfers between devices: 10.1 us -> 11.8 us  [gather_partials(): return lax.all_to_all(sent, axes, 0, 0, tiled=True)]
    ppermute x6 -> x5, starting transfers between devices: 22 us -> 20.4 us  [padded_1(): lax.ppermute(lax.slice_in_dim(block, 0, width, axis=dim), axis, backward)]
    concatenate x2, local copies, waits for them, and re-layouts: 1.57 us -> 0.16 us  [padded_1(): return jnp.concatenate([low, block, high], axis=dim)]
    ppermute x6 -> x5, starting transfers between devices: 2.55 us -> 2.74 us  [padded_1(): lax.ppermute(lax.slice_in_dim(block, block.shape[dim] - width, None, axis...]
  transfers between devices with their start and end apart: 13 -> 11, of which waited for: 7 -> 7; matrix products, arithmetic and copies ran while one was open for 2% -> 0% of each run, Pallas kernels for 0% -> 0%
where the time goes in v8:
time: 115 us; the launch traced here: 113 us
  waiting for transfers between devices  65 us (57%)
  starting transfers between devices  34.9 us (30%)
  matrix products  4.89 us (4%)
  other arithmetic  4.06 us (4%)
  local copies, waits for them, and re-layouts  2.97 us (3%)
    ppermute x5, waiting for transfers between devices, padded_1(): lax.ppermute(lax.slice_in_dim(block, block.shape[dim] - width, None, axis...  52.7 us
    ppermute x5, starting transfers between devices, padded_1(): lax.ppermute(lax.slice_in_dim(block, 0, width, axis=dim), axis, backward)  20.4 us
    all_to_all x1, waiting for transfers between devices, gather_partials(): return lax.all_to_all(sent, axes, 0, 0, tiled=True)  12.2 us
    all_to_all x1, starting transfers between devices, gather_partials(): return lax.all_to_all(sent, axes, 0, 0, tiled=True)  11.8 us
    dot_general x3, matrix products, depth_pass(): jnp.dot(flat, jnp.asarray(depth_matrix(planes, spacing)), precision=lax.P...  4.71 us
    ppermute x5, starting transfers between devices, padded_1(): lax.ppermute(lax.slice_in_dim(block, block.shape[dim] - width, None, axis...  2.74 us
  transfers between devices with their start and end apart: 11, of which 7 were waited for; matrix products, arithmetic and copies ran while one was open for 0% of the time, Pallas kernels for 0%

profile of v8, /device:TPU:8, one launch (start us, length us, event | category | flops | bytes accessed | tf_op | source)
XLA Modules:
  0.0 112.6 jit_solution(399957792611954854)
XLA Ops:
  0.6 1.2 %fusion.62 = (f32[64,8,128]{2,1,0:T(8,128)S(1)}, f32[64,8,128]{2,1,0:T(8,128)S(1)}) fusion(f32[64,32,128]{2,1,0:T(8,128)} %param.5), kind=kLoop, calls=%fused_computation.117 | loop fusion | bytes 1048576 | tf_op jit(solution)/shard_map/slice | solution.py:26
  1.8 2.0 %collective-permute-start = (f32[64,8,128]{2,1,0:T(8,128)S(1)}, f32[64,8,128]{2,1,0:T(8,128)S(1)}, u32[]{:S(2)}, u32[]{:S(2)}) collective-permute-start(f32[64,8,128]{2,1,0:T(8,128)S(1)} %get-tuple-element.28), channel_id=1, source_target_pairs={{0,1},{1,2},{2,3},{3,4},{4,5},{5,6},{6,7},{7,8},{8,9},{9,10},{10,1... | collective-permute-start | bytes 786440 | tf_op jit(solution)/shard_map/ppermute | solution.py:25
  3.8 6.2 %collective-permute-start.1 = (f32[64,8,128]{2,1,0:T(8,128)S(1)}, f32[64,8,128]{2,1,0:T(8,128)S(1)}, u32[]{:S(2)}, u32[]{:S(2)}) collective-permute-start(f32[64,8,128]{2,1,0:T(8,128)S(1)} %get-tuple-element.29), channel_id=1, source_target_pairs={{1,0},{2,1},{3,2},{4,3},{5,4},{6,5},{7,6},{8,7},{9,8},{10,9},{11,1... | collective-permute-start | bytes 786440 | tf_op jit(solution)/shard_map/ppermute | solution.py:28
  10.0 6.2 %collective-permute-done = f32[64,8,128]{2,1,0:T(8,128)S(1)} collective-permute-done((f32[64,8,128]{2,1,0:T(8,128)S(1)}, f32[64,8,128]{2,1,0:T(8,128)S(1)}, u32[]{:S(2)}, u32[]{:S(2)}) %collective-permute-start) | collective-permute-done | bytes 262176 | tf_op jit(solution)/shard_map/ppermute | solution.py:25
  16.3 0.1 constant_dynamic-update-slice_fusion
  16.4 0.5 fusion.43
  17.0 1.7 %collective-permute-start.3 = (f32[24,32,128]{2,1,0:T(8,128)S(1)}, f32[24,32,128]{2,1,0:T(8,128)S(1)}, u32[]{:S(2)}, u32[]{:S(2)}) collective-permute-start(f32[24,32,128]{2,1,0:T(8,128)S(1)} %get-tuple-element.25), channel_id=1, source_target_pairs={{32,0},{64,32},{96,64},{128,96},{160,128},{192,160},{224,192},{0,2... | collective-permute-start | bytes 1179656 | tf_op jit(solution)/shard_map/ppermute | solution.py:28
  18.8 5.5 %collective-permute-done.2 = f32[24,32,128]{2,1,0:T(8,128)S(1)} collective-permute-done((f32[24,32,128]{2,1,0:T(8,128)S(1)}, f32[24,32,128]{2,1,0:T(8,128)S(1)}, u32[]{:S(2)}, u32[]{:S(2)}) %collective-permute-start.2) | collective-permute-done | bytes 393248 | tf_op jit(solution)/shard_map/ppermute | solution.py:25
  24.2 0.2 pad_maximum_fusion
  24.4 0.4 fusion
  24.8 0.5 copy-done.3
  25.3 1.4 %fusion.64 = f32[3072,128]{1,0:T(8,128)S(1)} fusion(f32[3072,128]{1,0:T(8,128)S(1)} %bitcast.48, f32[128,128]{1,0:T(8,128)S(1)} %copy-done.3), kind=kOutput, calls=%fused_computation.119 | convolution fusion | flops 603979776 | bytes 3211264 | tf_op jit(solution)/shard_map/dot_general | solution.py:54
  26.6 0.3 fusion.57
  26.9 0.6 fusion.58
  27.8 5.3 %collective-permute-start.5 = (f32[64,16,128]{2,1,0:T(8,128)S(1)}, f32[64,16,128]{2,1,0:T(8,128)S(1)}, u32[]{:S(2)}, u32[]{:S(2)}) collective-permute-start(f32[64,16,128]{2,1,0:T(8,128)S(1)} %get-tuple-element.23), channel_id=1, source_target_pairs={{1,0},{2,1},{3,2},{4,3},{5,4},{6,5},{7,6},{8,7},{9,8},{10,9},{11,1... | collective-permute-start | bytes 1572872 | tf_op jit(solution)/shard_map/ppermute | solution.py:28
  33.1 12.0 %collective-permute-done.4 = f32[64,16,128]{2,1,0:T(8,128)S(1)} collective-permute-done((f32[64,16,128]{2,1,0:T(8,128)S(1)}, f32[64,16,128]{2,1,0:T(8,128)S(1)}, u32[]{:S(2)}, u32[]{:S(2)}) %collective-permute-start.4) | collective-permute-done | bytes 524320 | tf_op jit(solution)/shard_map/ppermute | solution.py:25
  45.1 0.3 fusion.22
  45.5 1.2 %abs_reduce_fusion.1 = (f32[128]{0:T(128)S(1)}, f32[128]{0:T(128)S(1)}, f32[128]{0:T(128)S(1)}, f32[128]{0:T(128)S(1)}, f32[2048,128]{1,0:T(8,128)S(1)}) fusion(f32[2048,128]{1,0:T(8,128)S(1)} %bitcast.53, f32[128,128]{1,0:T(8,128)S(1)} %copy-done.2, f32[3072,128]{1,0:T(8,128)S(1)} %fusion.64), kind=kOutput, calls=%fused_computation.84 | convolution fusion | flops 405011968 | bytes 3213312 | tf_op jit(solution)/shard_map/dot_general | solution.py:54
  46.7 0.6 collective-permute-start.6
  47.3 1.2 %collective-permute-start.7 = (f32[32,32,128]{2,1,0:T(8,128)S(1)}, f32[32,32,128]{2,1,0:T(8,128)S(1)}, u32[]{:S(2)}, u32[]{:S(2)}) collective-permute-start(f32[32,32,128]{2,1,0:T(8,128)S(1)} %bitcast.55), channel_id=1, source_target_pairs={{32,0},{64,32},{96,64},{128,96},{160,128},{192,160},{224,192},{0,2... | collective-permute-start | bytes 1572872 | tf_op jit(solution)/shard_map/ppermute | solution.py:28
  48.5 6.9 %collective-permute-done.6 = f32[32,32,128]{2,1,0:T(8,128)S(1)} collective-permute-done((f32[32,32,128]{2,1,0:T(8,128)S(1)}, f32[32,32,128]{2,1,0:T(8,128)S(1)}, u32[]{:S(2)}, u32[]{:S(2)}) %collective-permute-start.6) | collective-permute-done | bytes 524320 | tf_op jit(solution)/shard_map/ppermute | solution.py:25
  55.3 0.4 fusion.14
  55.8 5.9 %collective-permute-start.9 = (f32[64,32,128]{2,1,0:T(8,128)S(1)}, f32[64,32,128]{2,1,0:T(8,128)S(1)}, u32[]{:S(2)}, u32[]{:S(2)}) collective-permute-start(f32[64,32,128]{2,1,0:T(8,128)S(1)} %fusion.14), channel_id=1, source_target_pairs={{1,0},{2,1},{3,2},{4,3},{5,4},{6,5},{7,6},{8,7},{9,8},{10,9},{11,1... | collective-permute-start | bytes 3145736 | tf_op jit(solution)/shard_map/ppermute | solution.py:28
  61.7 0.3 abs_reduce_fusion.2
  62.0 22.1 %collective-permute-done.8 = f32[64,32,128]{2,1,0:T(8,128)S(1)} collective-permute-done((f32[64,32,128]{2,1,0:T(8,128)S(1)}, f32[64,32,128]{2,1,0:T(8,128)S(1)}, u32[]{:S(2)}, u32[]{:S(2)}) %collective-permute-start.8) | collective-permute-done | bytes 1048608 | tf_op jit(solution)/shard_map/ppermute | solution.py:25
  84.2 2.2 %fusion.63 = (f32[64,32,128]{2,1,0:T(8,128)S(1)}, f32[64,32,128]{2,1,0:T(8,128)}) fusion(f32[64,32,128]{2,1,0:T(8,128)S(1)} %bitcast.47, f32[128,128,1]{1,0,2:T(8,128)S(1)} %copy-done.1, f32[64,32,128]{2,1,0:T(8,128)S(1)} %collective-permute-done.9, f32[64,32,128]{2,1,0:T(8,128)S(1)} %fusion.14, f32[64,32,128]{2,1,0:T(8,128)S(1)} %collective-permute-done.8), kind=kOutput, calls=%fused_computation.118 | convolution fusion | flops 405798912 | bytes 6356992 | tf_op jit(solution)/shard_map/dot_general | solution.py:54
  86.4 0.3 abs_reduce_fusion
  86.9 0.7 broadcast_in_dim.28
  87.6 11.8 %all-to-all-start = ((f32[256,1,12]{2,1,0:T(1,128)}), f32[256,1,12]{2,1,0:T(1,128)S(1)}, u32[]{:S(2)}, u32[]{:S(2)}) async-start(f32[256,1,12]{2,1,0:T(1,128)} %broadcast_in_dim.28), calls=%async_computation | async-start | bytes 262144 | tf_op jit(solution)/shard_map/all_to_all | solution.py:92
  99.4 12.2 %all-to-all-done = f32[256,1,12]{2,1,0:T(1,128)S(1)} async-done(((f32[256,1,12]{2,1,0:T(1,128)}), f32[256,1,12]{2,1,0:T(1,128)S(1)}, u32[]{:S(2)}, u32[]{:S(2)}) %all-to-all-start) | async-done | bytes 12320 | tf_op jit(solution)/shard_map/all_to_all | solution.py:92
  111.5 0.2 fusion.4
  111.9 0.7 select_divide_fusion
  (30 shorter events, 0.9 us)
Async XLA Ops:
  0.6 15.6 %copy-start = (f32[64,32,128]{2,1,0:T(8,128)S(1)}, f32[64,32,128]{2,1,0:T(8,128)}, u32[]{:S(2)}) copy-start(f32[64,32,128]{2,1,0:T(8,128)} %param.5) | copy-start | bytes 3145732
  1.8 14.4 %collective-permute-start = (f32[64,8,128]{2,1,0:T(8,128)S(1)}, f32[64,8,128]{2,1,0:T(8,128)S(1)}, u32[]{:S(2)}, u32[]{:S(2)}) collective-permute-start(f32[64,8,128]{2,1,0:T(8,128)S(1)} %get-tuple-element.28), channel_id=1, source_target_pairs={{0,1},{1,2},{2,3},{3,4},{4,5},{5,6},{6,7},{7,8},{8,9},{9,10},{10,1... | collective-permute-start | bytes 786440 | tf_op jit(solution)/shard_map/ppermute | solution.py:25
  3.8 12.6 %collective-permute-start.1 = (f32[64,8,128]{2,1,0:T(8,128)S(1)}, f32[64,8,128]{2,1,0:T(8,128)S(1)}, u32[]{:S(2)}, u32[]{:S(2)}) collective-permute-start(f32[64,8,128]{2,1,0:T(8,128)S(1)} %get-tuple-element.29), channel_id=1, source_target_pairs={{1,0},{2,1},{3,2},{4,3},{5,4},{6,5},{7,6},{8,7},{9,8},{10,9},{11,1... | collective-permute-start | bytes 786440 | tf_op jit(solution)/shard_map/ppermute | solution.py:28
  17.0 7.2 %collective-permute-start.2 = (f32[24,32,128]{2,1,0:T(8,128)S(1)}, f32[24,32,128]{2,1,0:T(8,128)S(1)}, u32[]{:S(2)}, u32[]{:S(2)}) collective-permute-start(f32[24,32,128]{2,1,0:T(8,128)S(1)} %get-tuple-element.24), channel_id=1, source_target_pairs={{0,32},{32,64},{64,96},{96,128},{128,160},{160,192},{192,224},{224... | collective-permute-start | bytes 1179656 | tf_op jit(solution)/shard_map/ppermute | solution.py:25
  17.0 7.2 %collective-permute-start.3 = (f32[24,32,128]{2,1,0:T(8,128)S(1)}, f32[24,32,128]{2,1,0:T(8,128)S(1)}, u32[]{:S(2)}, u32[]{:S(2)}) collective-permute-start(f32[24,32,128]{2,1,0:T(8,128)S(1)} %get-tuple-element.25), channel_id=1, source_target_pairs={{32,0},{64,32},{96,64},{128,96},{160,128},{192,160},{224,192},{0,2... | collective-permute-start | bytes 1179656 | tf_op jit(solution)/shard_map/ppermute | solution.py:28
  24.4 0.8 copy-start.3
  27.7 17.5 %collective-permute-start.4 = (f32[64,16,128]{2,1,0:T(8,128)S(1)}, f32[64,16,128]{2,1,0:T(8,128)S(1)}, u32[]{:S(2)}, u32[]{:S(2)}) collective-permute-start(f32[64,16,128]{2,1,0:T(8,128)S(1)} %get-tuple-element.22), channel_id=1, source_target_pairs={{0,1},{1,2},{2,3},{3,4},{4,5},{5,6},{6,7},{7,8},{8,9},{9,10},{10,1... | collective-permute-start | bytes 1572872 | tf_op jit(solution)/shard_map/ppermute | solution.py:25
  27.8 17.7 %copy-start.2 = (f32[128,128]{1,0:T(8,128)S(1)}, f32[128,128]{1,0:T(8,128)}, u32[]{:S(2)}) copy-start(f32[128,128]{1,0:T(8,128)} %constant.13.clone) | copy-start | bytes 196612
  27.8 17.4 %collective-permute-start.5 = (f32[64,16,128]{2,1,0:T(8,128)S(1)}, f32[64,16,128]{2,1,0:T(8,128)S(1)}, u32[]{:S(2)}, u32[]{:S(2)}) collective-permute-start(f32[64,16,128]{2,1,0:T(8,128)S(1)} %get-tuple-element.23), channel_id=1, source_target_pairs={{1,0},{2,1},{3,2},{4,3},{5,4},{6,5},{7,6},{8,7},{9,8},{10,9},{11,1... | collective-permute-start | bytes 1572872 | tf_op jit(solution)/shard_map/ppermute | solution.py:28
  46.7 8.6 %collective-permute-start.6 = (f32[32,32,128]{2,1,0:T(8,128)S(1)}, f32[32,32,128]{2,1,0:T(8,128)S(1)}, u32[]{:S(2)}, u32[]{:S(2)}) collective-permute-start(f32[32,32,128]{2,1,0:T(8,128)S(1)} %bitcast.56), channel_id=1, source_target_pairs={{0,32},{32,64},{64,96},{96,128},{128,160},{160,192},{192,224},{224... | collective-permute-start | bytes 1572872 | tf_op jit(solution)/shard_map/ppermute | solution.py:25
  47.3 8.1 %collective-permute-start.7 = (f32[32,32,128]{2,1,0:T(8,128)S(1)}, f32[32,32,128]{2,1,0:T(8,128)S(1)}, u32[]{:S(2)}, u32[]{:S(2)}) collective-permute-start(f32[32,32,128]{2,1,0:T(8,128)S(1)} %bitcast.55), channel_id=1, source_target_pairs={{32,0},{64,32},{96,64},{128,96},{160,128},{192,160},{224,192},{0,2... | collective-permute-start | bytes 1572872 | tf_op jit(solution)/shard_map/ppermute | solution.py:28
  55.3 28.9 %copy-start.1 = (f32[128,128,1]{1,0,2:T(8,128)S(1)}, f32[128,128,1]{1,0,2:T(8,128)}, u32[]{:S(2)}) copy-start(f32[128,128,1]{1,0,2:T(8,128)} %constant.36) | copy-start | bytes 196612
  55.7 28.4 %collective-permute-start.8 = (f32[64,32,128]{2,1,0:T(8,128)S(1)}, f32[64,32,128]{2,1,0:T(8,128)S(1)}, u32[]{:S(2)}, u32[]{:S(2)}) collective-permute-start(f32[64,32,128]{2,1,0:T(8,128)S(1)} %fusion.14), channel_id=1, source_target_pairs={{0,1},{1,2},{2,3},{3,4},{4,5},{5,6},{6,7},{7,8},{8,9},{9,10},{10,1... | collective-permute-start | bytes 3145736 | tf_op jit(solution)/shard_map/ppermute | solution.py:25
  55.8 28.4 %collective-permute-start.9 = (f32[64,32,128]{2,1,0:T(8,128)S(1)}, f32[64,32,128]{2,1,0:T(8,128)S(1)}, u32[]{:S(2)}, u32[]{:S(2)}) collective-permute-start(f32[64,32,128]{2,1,0:T(8,128)S(1)} %fusion.14), channel_id=1, source_target_pairs={{1,0},{2,1},{3,2},{4,3},{5,4},{6,5},{7,6},{8,7},{9,8},{10,9},{11,1... | collective-permute-start | bytes 3145736 | tf_op jit(solution)/shard_map/ppermute | solution.py:28
  62.0 49.6 %copy-start.4 = (f32[8,256]{1,0:T(8,128)S(1)}, f32[8,256]{1,0:T(8,128)}, u32[]{:S(2)}) copy-start(f32[8,256]{1,0:T(8,128)} %constant.35.clone) | copy-start | bytes 24580
  87.6 24.0 %all-to-all-start = ((f32[256,1,12]{2,1,0:T(1,128)}), f32[256,1,12]{2,1,0:T(1,128)S(1)}, u32[]{:S(2)}, u32[]{:S(2)}) async-start(f32[256,1,12]{2,1,0:T(1,128)} %broadcast_in_dim.28), calls=%async_computation | async-start | bytes 262144 | tf_op jit(solution)/shard_map/all_to_all | solution.py:92

commit v9 on v8

--- a/solution.py
+++ b/solution.py
@@ -74,13 +74,10 @@
 
 def finish_table(table, planes):
     means = table / jnp.float32(SUB * SUB * planes)
-    second = means[:, 1:2]
-    column = lax.broadcasted_iota(jnp.int32, means.shape, 1)
-    ones = jnp.ones_like(means)
-    scale = jnp.where(
-        column == 2, (second + EPSILON) ** 1.5, jnp.where(column == 3, (second + EPSILON) ** 2, ones)
-    )
-    return means / scale
+    second = means[:, 1]
+    third = means[:, 2] / (second + EPSILON) ** 1.5
+    fourth = means[:, 3] / (second + EPSILON) ** 2
+    return jnp.stack([means[:, 0], second, third, fourth], axis=1)
 
 
 def gather_partials(partial, axes):
@@ -123,16 +120,10 @@
     count_x = lax.axis_size("row") * size_x // SUB
     count_y = lax.axis_size("col") * size_y // SUB
     gathered = gather_partials(partial, ("row", "col"))
-    rows, cols = lax.axis_size("row"), lax.axis_size("col")
-    owner = np.zeros((count_x * count_y, rows * cols), np.float32)
-    for r in range(rows):
-        for c in range(cols):
-            owner[(r * size_x // SUB) * count_y + c * size_y // SUB, r * cols + c] = 1.0
-    summed = jnp.dot(
-        jnp.asarray(owner), gathered, precision=lax.Precision.HIGHEST,
-        preferred_element_type=jnp.float32,
-    )
-    table = jnp.transpose(summed.reshape(count_x, count_y, len(SPACINGS), 4), (2, 3, 0, 1))
+    per_x = SUB // size_x
+    per_y = SUB // size_y
+    grouped = gathered.reshape(count_x, per_x, count_y, per_y, len(SPACINGS), 4)
+    table = jnp.transpose(jnp.sum(grouped, axis=(1, 3)), (2, 3, 0, 1))
     return (current, finish_table(table, planes))
 
 

time: 115 us -> 114 us (level)
  blocking collectives: 0 us -> 18.4 us
  starting transfers between devices: 34.9 us -> 21.4 us
  waiting for transfers between devices: 65 us -> 60.2 us
    ppermute x5, waiting for transfers between devices: 0.1 us -> 29.1 us  [padded_1(): lax.ppermute(lax.slice_in_dim(block, 0, width, axis=dim), axis, backward)]
    ppermute x5, waiting for transfers between devices: 52.7 us -> 31.1 us  [padded_1(): lax.ppermute(lax.slice_in_dim(block, block.shape[dim] - width, None, axis...]
    all_to_all x0 -> x1, blocking collectives: none -> 18.4 us  [gather_partials(): return lax.all_to_all(sent, axes, 0, 0, tiled=True)]
    all_to_all x1 -> x0, waiting for transfers between devices: 12.2 us -> none  [gather_partials(): return lax.all_to_all(sent, axes, 0, 0, tiled=True)]
    all_to_all x1 -> x0, starting transfers between devices: 11.8 us -> none  [gather_partials(): return lax.all_to_all(sent, axes, 0, 0, tiled=True)]
  transfers between devices with their start and end apart: 11 -> 10, of which waited for: 7 -> 7; matrix products, arithmetic and copies ran while one was open for 0% -> 0% of each run, Pallas kernels for 0% -> 0%
where the time goes in v9:
time: 114 us; the launch traced here: 112 us
  waiting for transfers between devices  60.2 us (53%)
  starting transfers between devices  21.4 us (19%)
  blocking collectives  18.4 us (16%)
  matrix products  4.71 us (4%)
  other arithmetic  4.11 us (4%)
  local copies, waits for them, and re-layouts  2.5 us (2%)
    ppermute x5, waiting for transfers between devices, padded_1(): lax.ppermute(lax.slice_in_dim(block, block.shape[dim] - width, None, axis...  31.1 us
    ppermute x5, waiting for transfers between devices, padded_1(): lax.ppermute(lax.slice_in_dim(block, 0, width, axis=dim), axis, backward)  29.1 us
    ppermute x5, starting transfers between devices, padded_1(): lax.ppermute(lax.slice_in_dim(block, 0, width, axis=dim), axis, backward)  19.3 us
    all_to_all x1, blocking collectives, gather_partials(): return lax.all_to_all(sent, axes, 0, 0, tiled=True)  18.4 us
    dot_general x3, matrix products, depth_pass(): jnp.dot(flat, jnp.asarray(depth_matrix(planes, spacing)), precision=lax.P...  4.71 us
  transfers between devices with their start and end apart: 10, of which 7 were waited for; matrix products, arithmetic and copies ran while one was open for 0% of the time, Pallas kernels for 0%

profile of v9, /device:TPU:8, one launch (start us, length us, event | category | flops | bytes accessed | tf_op | source)
XLA Modules:
  0.0 112.2 jit_solution(18131396856938033841)
XLA Ops:
  0.6 1.2 %fusion.61 = (f32[64,8,128]{2,1,0:T(8,128)S(1)}, f32[64,8,128]{2,1,0:T(8,128)S(1)}) fusion(f32[64,32,128]{2,1,0:T(8,128)} %param.4), kind=kLoop, calls=%fused_computation.114 | loop fusion | bytes 1048576 | tf_op jit(solution)/shard_map/slice | solution.py:26
  1.8 2.0 %collective-permute-start = (f32[64,8,128]{2,1,0:T(8,128)S(1)}, f32[64,8,128]{2,1,0:T(8,128)S(1)}, u32[]{:S(2)}, u32[]{:S(2)}) collective-permute-start(f32[64,8,128]{2,1,0:T(8,128)S(1)} %get-tuple-element.28), channel_id=1, source_target_pairs={{0,1},{1,2},{2,3},{3,4},{4,5},{5,6},{6,7},{7,8},{8,9},{9,10},{10,1... | collective-permute-start | bytes 786440 | tf_op jit(solution)/shard_map/ppermute | solution.py:25
  3.8 6.2 %collective-permute-start.1 = (f32[64,8,128]{2,1,0:T(8,128)S(1)}, f32[64,8,128]{2,1,0:T(8,128)S(1)}, u32[]{:S(2)}, u32[]{:S(2)}) collective-permute-start(f32[64,8,128]{2,1,0:T(8,128)S(1)} %get-tuple-element.29), channel_id=1, source_target_pairs={{1,0},{2,1},{3,2},{4,3},{5,4},{6,5},{7,6},{8,7},{9,8},{10,9},{11,1... | collective-permute-start | bytes 786440 | tf_op jit(solution)/shard_map/ppermute | solution.py:28
  10.0 6.2 %collective-permute-done = f32[64,8,128]{2,1,0:T(8,128)S(1)} collective-permute-done((f32[64,8,128]{2,1,0:T(8,128)S(1)}, f32[64,8,128]{2,1,0:T(8,128)S(1)}, u32[]{:S(2)}, u32[]{:S(2)}) %collective-permute-start) | collective-permute-done | bytes 262176 | tf_op jit(solution)/shard_map/ppermute | solution.py:25
  16.3 0.1 constant_dynamic-update-slice_fusion
  16.4 0.5 fusion.42
  17.0 1.7 %collective-permute-start.3 = (f32[24,32,128]{2,1,0:T(8,128)S(1)}, f32[24,32,128]{2,1,0:T(8,128)S(1)}, u32[]{:S(2)}, u32[]{:S(2)}) collective-permute-start(f32[24,32,128]{2,1,0:T(8,128)S(1)} %get-tuple-element.25), channel_id=1, source_target_pairs={{32,0},{64,32},{96,64},{128,96},{160,128},{192,160},{224,192},{0,2... | collective-permute-start | bytes 1179656 | tf_op jit(solution)/shard_map/ppermute | solution.py:28
  18.8 5.5 %collective-permute-done.2 = f32[24,32,128]{2,1,0:T(8,128)S(1)} collective-permute-done((f32[24,32,128]{2,1,0:T(8,128)S(1)}, f32[24,32,128]{2,1,0:T(8,128)S(1)}, u32[]{:S(2)}, u32[]{:S(2)}) %collective-permute-start.2) | collective-permute-done | bytes 393248 | tf_op jit(solution)/shard_map/ppermute | solution.py:25
  24.2 0.2 pad_maximum_fusion
  24.4 0.4 fusion
  24.8 0.5 copy-done.3
  25.3 1.4 %fusion.63 = f32[3072,128]{1,0:T(8,128)S(1)} fusion(f32[3072,128]{1,0:T(8,128)S(1)} %bitcast.39, f32[128,128]{1,0:T(8,128)S(1)} %copy-done.3), kind=kOutput, calls=%fused_computation.116 | convolution fusion | flops 603979776 | bytes 3211264 | tf_op jit(solution)/shard_map/dot_general | solution.py:54
  26.6 0.3 fusion.56
  26.9 0.6 fusion.57
  27.8 5.3 %collective-permute-start.5 = (f32[64,16,128]{2,1,0:T(8,128)S(1)}, f32[64,16,128]{2,1,0:T(8,128)S(1)}, u32[]{:S(2)}, u32[]{:S(2)}) collective-permute-start(f32[64,16,128]{2,1,0:T(8,128)S(1)} %get-tuple-element.23), channel_id=1, source_target_pairs={{1,0},{2,1},{3,2},{4,3},{5,4},{6,5},{7,6},{8,7},{9,8},{10,9},{11,1... | collective-permute-start | bytes 1572872 | tf_op jit(solution)/shard_map/ppermute | solution.py:28
  33.1 12.0 %collective-permute-done.4 = f32[64,16,128]{2,1,0:T(8,128)S(1)} collective-permute-done((f32[64,16,128]{2,1,0:T(8,128)S(1)}, f32[64,16,128]{2,1,0:T(8,128)S(1)}, u32[]{:S(2)}, u32[]{:S(2)}) %collective-permute-start.4) | collective-permute-done | bytes 524320 | tf_op jit(solution)/shard_map/ppermute | solution.py:25
  45.1 0.3 fusion.21
  45.5 1.2 %abs_reduce_fusion.1 = (f32[128]{0:T(128)S(1)}, f32[128]{0:T(128)S(1)}, f32[128]{0:T(128)S(1)}, f32[128]{0:T(128)S(1)}, f32[2048,128]{1,0:T(8,128)S(1)}) fusion(f32[2048,128]{1,0:T(8,128)S(1)} %bitcast.44, f32[128,128]{1,0:T(8,128)S(1)} %copy-done.2, f32[3072,128]{1,0:T(8,128)S(1)} %fusion.63), kind=kOutput, calls=%fused_computation.82 | convolution fusion | flops 405011968 | bytes 3213312 | tf_op jit(solution)/shard_map/dot_general | solution.py:54
  46.7 1.1 %collective-permute-start.7 = (f32[32,32,128]{2,1,0:T(8,128)S(1)}, f32[32,32,128]{2,1,0:T(8,128)S(1)}, u32[]{:S(2)}, u32[]{:S(2)}) collective-permute-start(f32[32,32,128]{2,1,0:T(8,128)S(1)} %bitcast.46), channel_id=1, source_target_pairs={{32,0},{64,32},{96,64},{128,96},{160,128},{192,160},{224,192},{0,2... | collective-permute-start | bytes 1572872 | tf_op jit(solution)/shard_map/ppermute | solution.py:28
  47.8 6.7 %collective-permute-done.7 = f32[32,32,128]{2,1,0:T(8,128)S(1)} collective-permute-done((f32[32,32,128]{2,1,0:T(8,128)S(1)}, f32[32,32,128]{2,1,0:T(8,128)S(1)}, u32[]{:S(2)}, u32[]{:S(2)}) %collective-permute-start.7) | collective-permute-done | bytes 524320 | tf_op jit(solution)/shard_map/ppermute | solution.py:28
  54.5 1.9 %collective-permute-done.6 = f32[32,32,128]{2,1,0:T(8,128)S(1)} collective-permute-done((f32[32,32,128]{2,1,0:T(8,128)S(1)}, f32[32,32,128]{2,1,0:T(8,128)S(1)}, u32[]{:S(2)}, u32[]{:S(2)}) %collective-permute-start.6) | collective-permute-done | bytes 524320 | tf_op jit(solution)/shard_map/ppermute | solution.py:25
  56.4 0.4 fusion.13
  56.8 4.9 %collective-permute-start.9 = (f32[64,32,128]{2,1,0:T(8,128)S(1)}, f32[64,32,128]{2,1,0:T(8,128)S(1)}, u32[]{:S(2)}, u32[]{:S(2)}) collective-permute-start(f32[64,32,128]{2,1,0:T(8,128)S(1)} %fusion.13), channel_id=1, source_target_pairs={{1,0},{2,1},{3,2},{4,3},{5,4},{6,5},{7,6},{8,7},{9,8},{10,9},{11,1... | collective-permute-start | bytes 3145736 | tf_op jit(solution)/shard_map/ppermute | solution.py:28
  61.7 0.3 abs_reduce_fusion.2
  62.0 22.4 %collective-permute-done.9 = f32[64,32,128]{2,1,0:T(8,128)S(1)} collective-permute-done((f32[64,32,128]{2,1,0:T(8,128)S(1)}, f32[64,32,128]{2,1,0:T(8,128)S(1)}, u32[]{:S(2)}, u32[]{:S(2)}) %collective-permute-start.9) | collective-permute-done | bytes 1048608 | tf_op jit(solution)/shard_map/ppermute | solution.py:28
  84.4 5.5 %collective-permute-done.8 = f32[64,32,128]{2,1,0:T(8,128)S(1)} collective-permute-done((f32[64,32,128]{2,1,0:T(8,128)S(1)}, f32[64,32,128]{2,1,0:T(8,128)S(1)}, u32[]{:S(2)}, u32[]{:S(2)}) %collective-permute-start.8) | collective-permute-done | bytes 1048608 | tf_op jit(solution)/shard_map/ppermute | solution.py:25
  89.9 2.2 %fusion.62 = (f32[64,32,128]{2,1,0:T(8,128)S(1)}, f32[64,32,128]{2,1,0:T(8,128)}) fusion(f32[64,32,128]{2,1,0:T(8,128)S(1)} %bitcast.38, f32[128,128,1]{1,0,2:T(8,128)S(1)} %copy-done.1, f32[64,32,128]{2,1,0:T(8,128)S(1)} %collective-permute-done.9, f32[64,32,128]{2,1,0:T(8,128)S(1)} %fusion.13, f32[64,32,128]{2,1,0:T(8,128)S(1)} %collective-permute-done.8), kind=kOutput, calls=%fused_computation.115 | convolution fusion | flops 405798912 | bytes 6356992 | tf_op jit(solution)/shard_map/dot_general | solution.py:54
  92.1 0.3 abs_reduce_fusion
  92.6 18.4 %all_to_all.6 = f32[256,1,12]{2,1,0:T(1,128)S(1)} all-to-all(f32[256,1,12]{2,1,0:T(1,128)S(1)} %broadcast_in_dim.8), channel_id=1, replica_groups=mesh['row'=8,'col'=32] {'row','col'}, dimensions={0} | all-to-all | bytes 24576 | tf_op jit(solution)/shard_map/all_to_all | solution.py:89
  111.1 0.3 reshape.50
  111.4 0.1 reduce_sum.139
  111.6 0.6 pad_maximum_fusion.7
  (28 shorter events, 0.7 us)
Async XLA Ops:
  0.6 15.6 %copy-start = (f32[64,32,128]{2,1,0:T(8,128)S(1)}, f32[64,32,128]{2,1,0:T(8,128)}, u32[]{:S(2)}) copy-start(f32[64,32,128]{2,1,0:T(8,128)} %param.4) | copy-start | bytes 3145732
  1.8 14.4 %collective-permute-start = (f32[64,8,128]{2,1,0:T(8,128)S(1)}, f32[64,8,128]{2,1,0:T(8,128)S(1)}, u32[]{:S(2)}, u32[]{:S(2)}) collective-permute-start(f32[64,8,128]{2,1,0:T(8,128)S(1)} %get-tuple-element.28), channel_id=1, source_target_pairs={{0,1},{1,2},{2,3},{3,4},{4,5},{5,6},{6,7},{7,8},{8,9},{9,10},{10,1... | collective-permute-start | bytes 786440 | tf_op jit(solution)/shard_map/ppermute | solution.py:25
  3.8 12.6 %collective-permute-start.1 = (f32[64,8,128]{2,1,0:T(8,128)S(1)}, f32[64,8,128]{2,1,0:T(8,128)S(1)}, u32[]{:S(2)}, u32[]{:S(2)}) collective-permute-start(f32[64,8,128]{2,1,0:T(8,128)S(1)} %get-tuple-element.29), channel_id=1, source_target_pairs={{1,0},{2,1},{3,2},{4,3},{5,4},{6,5},{7,6},{8,7},{9,8},{10,9},{11,1... | collective-permute-start | bytes 786440 | tf_op jit(solution)/shard_map/ppermute | solution.py:28
  17.0 7.2 %collective-permute-start.2 = (f32[24,32,128]{2,1,0:T(8,128)S(1)}, f32[24,32,128]{2,1,0:T(8,128)S(1)}, u32[]{:S(2)}, u32[]{:S(2)}) collective-permute-start(f32[24,32,128]{2,1,0:T(8,128)S(1)} %get-tuple-element.24), channel_id=1, source_target_pairs={{0,32},{32,64},{64,96},{96,128},{128,160},{160,192},{192,224},{224... | collective-permute-start | bytes 1179656 | tf_op jit(solution)/shard_map/ppermute | solution.py:25
  17.0 7.2 %collective-permute-start.3 = (f32[24,32,128]{2,1,0:T(8,128)S(1)}, f32[24,32,128]{2,1,0:T(8,128)S(1)}, u32[]{:S(2)}, u32[]{:S(2)}) collective-permute-start(f32[24,32,128]{2,1,0:T(8,128)S(1)} %get-tuple-element.25), channel_id=1, source_target_pairs={{32,0},{64,32},{96,64},{128,96},{160,128},{192,160},{224,192},{0,2... | collective-permute-start | bytes 1179656 | tf_op jit(solution)/shard_map/ppermute | solution.py:28
  24.4 0.8 copy-start.3
  27.7 17.5 %collective-permute-start.4 = (f32[64,16,128]{2,1,0:T(8,128)S(1)}, f32[64,16,128]{2,1,0:T(8,128)S(1)}, u32[]{:S(2)}, u32[]{:S(2)}) collective-permute-start(f32[64,16,128]{2,1,0:T(8,128)S(1)} %get-tuple-element.22), channel_id=1, source_target_pairs={{0,1},{1,2},{2,3},{3,4},{4,5},{5,6},{6,7},{7,8},{8,9},{9,10},{10,1... | collective-permute-start | bytes 1572872 | tf_op jit(solution)/shard_map/ppermute | solution.py:25
  27.8 17.7 %copy-start.2 = (f32[128,128]{1,0:T(8,128)S(1)}, f32[128,128]{1,0:T(8,128)}, u32[]{:S(2)}) copy-start(f32[128,128]{1,0:T(8,128)} %constant.26.clone) | copy-start | bytes 196612
  27.8 17.4 %collective-permute-start.5 = (f32[64,16,128]{2,1,0:T(8,128)S(1)}, f32[64,16,128]{2,1,0:T(8,128)S(1)}, u32[]{:S(2)}, u32[]{:S(2)}) collective-permute-start(f32[64,16,128]{2,1,0:T(8,128)S(1)} %get-tuple-element.23), channel_id=1, source_target_pairs={{1,0},{2,1},{3,2},{4,3},{5,4},{6,5},{7,6},{8,7},{9,8},{10,9},{11,1... | collective-permute-start | bytes 1572872 | tf_op jit(solution)/shard_map/ppermute | solution.py:28
  46.7 7.8 %collective-permute-start.7 = (f32[32,32,128]{2,1,0:T(8,128)S(1)}, f32[32,32,128]{2,1,0:T(8,128)S(1)}, u32[]{:S(2)}, u32[]{:S(2)}) collective-permute-start(f32[32,32,128]{2,1,0:T(8,128)S(1)} %bitcast.46), channel_id=1, source_target_pairs={{32,0},{64,32},{96,64},{128,96},{160,128},{192,160},{224,192},{0,2... | collective-permute-start | bytes 1572872 | tf_op jit(solution)/shard_map/ppermute | solution.py:28
  47.8 8.6 %collective-permute-start.6 = (f32[32,32,128]{2,1,0:T(8,128)S(1)}, f32[32,32,128]{2,1,0:T(8,128)S(1)}, u32[]{:S(2)}, u32[]{:S(2)}) collective-permute-start(f32[32,32,128]{2,1,0:T(8,128)S(1)} %bitcast.45), channel_id=1, source_target_pairs={{0,32},{32,64},{64,96},{96,128},{128,160},{160,192},{192,224},{224... | collective-permute-start | bytes 1572872 | tf_op jit(solution)/shard_map/ppermute | solution.py:25
  56.4 33.5 %copy-start.1 = (f32[128,128,1]{1,0,2:T(8,128)S(1)}, f32[128,128,1]{1,0,2:T(8,128)}, u32[]{:S(2)}) copy-start(f32[128,128,1]{1,0,2:T(8,128)} %constant.28) | copy-start | bytes 196612
  56.8 27.6 %collective-permute-start.9 = (f32[64,32,128]{2,1,0:T(8,128)S(1)}, f32[64,32,128]{2,1,0:T(8,128)S(1)}, u32[]{:S(2)}, u32[]{:S(2)}) collective-permute-start(f32[64,32,128]{2,1,0:T(8,128)S(1)} %fusion.13), channel_id=1, source_target_pairs={{1,0},{2,1},{3,2},{4,3},{5,4},{6,5},{7,6},{8,7},{9,8},{10,9},{11,1... | collective-permute-start | bytes 3145736 | tf_op jit(solution)/shard_map/ppermute | solution.py:28
  61.7 28.2 %collective-permute-start.8 = (f32[64,32,128]{2,1,0:T(8,128)S(1)}, f32[64,32,128]{2,1,0:T(8,128)S(1)}, u32[]{:S(2)}, u32[]{:S(2)}) collective-permute-start(f32[64,32,128]{2,1,0:T(8,128)S(1)} %fusion.13), channel_id=1, source_target_pairs={{0,1},{1,2},{2,3},{3,4},{4,5},{5,6},{6,7},{7,8},{8,9},{9,10},{10,1... | collective-permute-start | bytes 3145736 | tf_op jit(solution)/shard_map/ppermute | solution.py:25

commit v10 on v9

--- a/solution.py
+++ b/solution.py
@@ -51,12 +51,14 @@
     rows = values_in.shape[:-1]
     planes = values_in.shape[-1]
     flat = values_in.reshape(-1, planes)
-    summed = jnp.dot(
-        flat,
-        jnp.asarray(depth_matrix(planes, spacing)),
-        precision=lax.Precision.HIGHEST,
-        preferred_element_type=jnp.float32,
-    )
+    high = lax.reduce_precision(flat, exponent_bits=8, mantissa_bits=7)
+    rest = flat - high
+    middle = lax.reduce_precision(rest, exponent_bits=8, mantissa_bits=7)
+    low = rest - middle
+    pieces = jnp.concatenate([high, middle, low], axis=1).astype(jnp.bfloat16)
+    matrix = depth_matrix(planes, spacing)
+    stacked = jnp.asarray(np.concatenate([matrix] * 3, axis=0), dtype=jnp.bfloat16)
+    summed = jnp.dot(pieces, stacked, preferred_element_type=jnp.float32)
     return summed.reshape(*rows, planes)
 
 

time: 114 us -> 116 us (1.018)
  other arithmetic: 4.11 us -> 5.74 us
    dot_general x3 -> x9, matrix products: 4.71 us -> 3.84 us  [depth_pass(): summed = jnp.dot(pieces, stacked, preferred_element_type=jnp.float32)]
where the time goes in v10:
time: 116 us; the launch traced here: 114 us
  waiting for transfers between devices  60.3 us (52%)
  starting transfers between devices  21.4 us (18%)
  blocking collectives  18.4 us (16%)
  other arithmetic  5.74 us (5%)
  matrix products  3.84 us (3%)
  local copies, waits for them, and re-layouts  3.32 us (3%)
    ppermute x5, waiting for transfers between devices, padded_1(): lax.ppermute(lax.slice_in_dim(block, block.shape[dim] - width, None, axis...  31.2 us
    ppermute x5, waiting for transfers between devices, padded_1(): lax.ppermute(lax.slice_in_dim(block, 0, width, axis=dim), axis, backward)  29.1 us
    ppermute x5, starting transfers between devices, padded_1(): lax.ppermute(lax.slice_in_dim(block, 0, width, axis=dim), axis, backward)  19.3 us
    all_to_all x1, blocking collectives, gather_partials(): return lax.all_to_all(sent, axes, 0, 0, tiled=True)  18.4 us
    dot_general x9, matrix products, depth_pass(): summed = jnp.dot(pieces, stacked, preferred_element_type=jnp.float32)  3.84 us
  transfers between devices with their start and end apart: 10, of which 7 were waited for; matrix products, arithmetic and copies ran while one was open for 0% of the time, Pallas kernels for 0%

profile of v10, /device:TPU:8, one launch (start us, length us, event | category | flops | bytes accessed | tf_op | source)
XLA Modules:
  0.0 113.8 jit_solution(1793223745532138260)
XLA Ops:
  0.6 1.2 %fusion.49 = (f32[64,8,128]{2,1,0:T(8,128)S(1)}, f32[64,8,128]{2,1,0:T(8,128)S(1)}) fusion(f32[64,32,128]{2,1,0:T(8,128)} %param.4), kind=kLoop, calls=%fused_computation.122 | loop fusion | bytes 1048576 | tf_op jit(solution)/shard_map/slice | solution.py:26
  1.8 2.0 %collective-permute-start = (f32[64,8,128]{2,1,0:T(8,128)S(1)}, f32[64,8,128]{2,1,0:T(8,128)S(1)}, u32[]{:S(2)}, u32[]{:S(2)}) collective-permute-start(f32[64,8,128]{2,1,0:T(8,128)S(1)} %get-tuple-element.39), channel_id=1, source_target_pairs={{0,1},{1,2},{2,3},{3,4},{4,5},{5,6},{6,7},{7,8},{8,9},{9,10},{10,1... | collective-permute-start | bytes 786440 | tf_op jit(solution)/shard_map/ppermute | solution.py:25
  3.8 6.2 %collective-permute-start.1 = (f32[64,8,128]{2,1,0:T(8,128)S(1)}, f32[64,8,128]{2,1,0:T(8,128)S(1)}, u32[]{:S(2)}, u32[]{:S(2)}) collective-permute-start(f32[64,8,128]{2,1,0:T(8,128)S(1)} %get-tuple-element.40), channel_id=1, source_target_pairs={{1,0},{2,1},{3,2},{4,3},{5,4},{6,5},{7,6},{8,7},{9,8},{10,9},{11,1... | collective-permute-start | bytes 786440 | tf_op jit(solution)/shard_map/ppermute | solution.py:28
  10.0 6.2 %collective-permute-done = f32[64,8,128]{2,1,0:T(8,128)S(1)} collective-permute-done((f32[64,8,128]{2,1,0:T(8,128)S(1)}, f32[64,8,128]{2,1,0:T(8,128)S(1)}, u32[]{:S(2)}, u32[]{:S(2)}) %collective-permute-start) | collective-permute-done | bytes 262176 | tf_op jit(solution)/shard_map/ppermute | solution.py:25
  16.4 0.5 fusion.40
  17.0 1.7 %collective-permute-start.3 = (f32[24,32,128]{2,1,0:T(8,128)S(1)}, f32[24,32,128]{2,1,0:T(8,128)S(1)}, u32[]{:S(2)}, u32[]{:S(2)}) collective-permute-start(f32[24,32,128]{2,1,0:T(8,128)S(1)} %get-tuple-element.36), channel_id=1, source_target_pairs={{32,0},{64,32},{96,64},{128,96},{160,128},{192,160},{224,192},{0,2... | collective-permute-start | bytes 1179656 | tf_op jit(solution)/shard_map/ppermute | solution.py:28
  18.8 5.5 %collective-permute-done.2 = f32[24,32,128]{2,1,0:T(8,128)S(1)} collective-permute-done((f32[24,32,128]{2,1,0:T(8,128)S(1)}, f32[24,32,128]{2,1,0:T(8,128)S(1)}, u32[]{:S(2)}, u32[]{:S(2)}) %collective-permute-start.2) | collective-permute-done | bytes 393248 | tf_op jit(solution)/shard_map/ppermute | solution.py:25
  24.4 0.4 fusion.1
  24.8 0.4 fusion
  25.2 0.3 copy-done.1
  25.6 0.3 fusion.50
  25.9 0.3 convolution_add_fusion.1
  26.3 0.4 convolution_add_fusion
  26.9 0.6 fusion.45
  27.7 5.3 %collective-permute-start.5 = (f32[64,16,128]{2,1,0:T(8,128)S(1)}, f32[64,16,128]{2,1,0:T(8,128)S(1)}, u32[]{:S(2)}, u32[]{:S(2)}) collective-permute-start(f32[64,16,128]{2,1,0:T(8,128)S(1)} %get-tuple-element.34), channel_id=1, source_target_pairs={{1,0},{2,1},{3,2},{4,3},{5,4},{6,5},{7,6},{8,7},{9,8},{10,9},{11,1... | collective-permute-start | bytes 1572872 | tf_op jit(solution)/shard_map/ppermute | solution.py:28
  33.1 12.1 %collective-permute-done.4 = f32[64,16,128]{2,1,0:T(8,128)S(1)} collective-permute-done((f32[64,16,128]{2,1,0:T(8,128)S(1)}, f32[64,16,128]{2,1,0:T(8,128)S(1)}, u32[]{:S(2)}, u32[]{:S(2)}) %collective-permute-start.4) | collective-permute-done | bytes 524320 | tf_op jit(solution)/shard_map/ppermute | solution.py:25
  45.1 0.3 fusion.24
  45.7 0.5 copy-done.3
  47.1 1.1 collective-permute-start.7
  48.3 6.7 %collective-permute-done.7 = f32[32,32,128]{2,1,0:T(8,128)S(1)} collective-permute-done((f32[32,32,128]{2,1,0:T(8,128)S(1)}, f32[32,32,128]{2,1,0:T(8,128)S(1)}, u32[]{:S(2)}, u32[]{:S(2)}) %collective-permute-start.7) | collective-permute-done | bytes 524320 | tf_op jit(solution)/shard_map/ppermute | solution.py:28
  55.0 1.9 %collective-permute-done.6 = f32[32,32,128]{2,1,0:T(8,128)S(1)} collective-permute-done((f32[32,32,128]{2,1,0:T(8,128)S(1)}, f32[32,32,128]{2,1,0:T(8,128)S(1)}, u32[]{:S(2)}, u32[]{:S(2)}) %collective-permute-start.6) | collective-permute-done | bytes 524320 | tf_op jit(solution)/shard_map/ppermute | solution.py:25
  56.9 0.4 fusion.16
  57.2 4.9 %collective-permute-start.9 = (f32[64,32,128]{2,1,0:T(8,128)S(1)}, f32[64,32,128]{2,1,0:T(8,128)S(1)}, u32[]{:S(2)}, u32[]{:S(2)}) collective-permute-start(f32[64,32,128]{2,1,0:T(8,128)S(1)} %fusion.16), channel_id=1, source_target_pairs={{1,0},{2,1},{3,2},{4,3},{5,4},{6,5},{7,6},{8,7},{9,8},{10,9},{11,1... | collective-permute-start | bytes 3145736 | tf_op jit(solution)/shard_map/ppermute | solution.py:28
  62.1 0.3 abs_reduce_fusion.2
  62.4 22.4 %collective-permute-done.9 = f32[64,32,128]{2,1,0:T(8,128)S(1)} collective-permute-done((f32[64,32,128]{2,1,0:T(8,128)S(1)}, f32[64,32,128]{2,1,0:T(8,128)S(1)}, u32[]{:S(2)}, u32[]{:S(2)}) %collective-permute-start.9) | collective-permute-done | bytes 1048608 | tf_op jit(solution)/shard_map/ppermute | solution.py:28
  84.8 5.5 %collective-permute-done.8 = f32[64,32,128]{2,1,0:T(8,128)S(1)} collective-permute-done((f32[64,32,128]{2,1,0:T(8,128)S(1)}, f32[64,32,128]{2,1,0:T(8,128)S(1)}, u32[]{:S(2)}, u32[]{:S(2)}) %collective-permute-start.8) | collective-permute-done | bytes 1048608 | tf_op jit(solution)/shard_map/ppermute | solution.py:25
  90.3 0.4 fusion.31
  91.0 0.5 copy-done.2
  92.1 1.4 %slice_subtract_fusion = (f32[2048,128]{1,0:T(8,128)S(1)}, f32[2048,128]{1,0:T(8,128)S(1)}, f32[2048,128]{1,0:T(8,128)}) fusion(f32[2048,128]{1,0:T(8,128)S(1)} %convolution_add_fusion.4, f32[3072,128]{1,0:T(8,128)S(1)} %convolution_add_fusion, f32[2048,128]{1,0:T(8,128)S(1)} %convolution_add_fusion.3, bf16[2048,128]{1,0:T(8,128)(2,1)S(1)} %get-tuple-element.25, ...), kind=kOutput, calls=%fused_computation.116 | convolution fusion | flops 67895296 | bytes 6848512 | tf_op jit(solution)/shard_map/dot_general | solution.py:61
  93.5 0.6 abs_reduce_fusion
  94.3 18.4 %all_to_all.6 = f32[256,1,12]{2,1,0:T(1,128)S(1)} all-to-all(f32[256,1,12]{2,1,0:T(1,128)S(1)} %broadcast_in_dim.8), channel_id=1, replica_groups=mesh['row'=8,'col'=32] {'row','col'}, dimensions={0} | all-to-all | bytes 24576 | tf_op jit(solution)/shard_map/all_to_all | solution.py:91
  113.2 0.6 pad_maximum_fusion.7
  (39 shorter events, 3.7 us)
Async XLA Ops:
  0.6 15.6 %copy-start = (f32[64,32,128]{2,1,0:T(8,128)S(1)}, f32[64,32,128]{2,1,0:T(8,128)}, u32[]{:S(2)}) copy-start(f32[64,32,128]{2,1,0:T(8,128)} %param.4) | copy-start | bytes 3145732
  1.8 14.4 %collective-permute-start = (f32[64,8,128]{2,1,0:T(8,128)S(1)}, f32[64,8,128]{2,1,0:T(8,128)S(1)}, u32[]{:S(2)}, u32[]{:S(2)}) collective-permute-start(f32[64,8,128]{2,1,0:T(8,128)S(1)} %get-tuple-element.39), channel_id=1, source_target_pairs={{0,1},{1,2},{2,3},{3,4},{4,5},{5,6},{6,7},{7,8},{8,9},{9,10},{10,1... | collective-permute-start | bytes 786440 | tf_op jit(solution)/shard_map/ppermute | solution.py:25
  3.8 12.6 %collective-permute-start.1 = (f32[64,8,128]{2,1,0:T(8,128)S(1)}, f32[64,8,128]{2,1,0:T(8,128)S(1)}, u32[]{:S(2)}, u32[]{:S(2)}) collective-permute-start(f32[64,8,128]{2,1,0:T(8,128)S(1)} %get-tuple-element.40), channel_id=1, source_target_pairs={{1,0},{2,1},{3,2},{4,3},{5,4},{6,5},{7,6},{8,7},{9,8},{10,9},{11,1... | collective-permute-start | bytes 786440 | tf_op jit(solution)/shard_map/ppermute | solution.py:28
  17.0 7.2 %collective-permute-start.2 = (f32[24,32,128]{2,1,0:T(8,128)S(1)}, f32[24,32,128]{2,1,0:T(8,128)S(1)}, u32[]{:S(2)}, u32[]{:S(2)}) collective-permute-start(f32[24,32,128]{2,1,0:T(8,128)S(1)} %get-tuple-element.35), channel_id=1, source_target_pairs={{0,32},{32,64},{64,96},{96,128},{128,160},{160,192},{192,224},{224... | collective-permute-start | bytes 1179656 | tf_op jit(solution)/shard_map/ppermute | solution.py:25
  17.0 7.2 %collective-permute-start.3 = (f32[24,32,128]{2,1,0:T(8,128)S(1)}, f32[24,32,128]{2,1,0:T(8,128)S(1)}, u32[]{:S(2)}, u32[]{:S(2)}) collective-permute-start(f32[24,32,128]{2,1,0:T(8,128)S(1)} %get-tuple-element.36), channel_id=1, source_target_pairs={{32,0},{64,32},{96,64},{128,96},{160,128},{192,160},{224,192},{0,2... | collective-permute-start | bytes 1179656 | tf_op jit(solution)/shard_map/ppermute | solution.py:28
  24.8 0.8 copy-start.1
  27.6 17.5 %collective-permute-start.4 = (f32[64,16,128]{2,1,0:T(8,128)S(1)}, f32[64,16,128]{2,1,0:T(8,128)S(1)}, u32[]{:S(2)}, u32[]{:S(2)}) collective-permute-start(f32[64,16,128]{2,1,0:T(8,128)S(1)} %get-tuple-element.33), channel_id=1, source_target_pairs={{0,1},{1,2},{2,3},{3,4},{4,5},{5,6},{6,7},{7,8},{8,9},{9,10},{10,1... | collective-permute-start | bytes 1572872 | tf_op jit(solution)/shard_map/ppermute | solution.py:25
  27.7 17.4 %collective-permute-start.5 = (f32[64,16,128]{2,1,0:T(8,128)S(1)}, f32[64,16,128]{2,1,0:T(8,128)S(1)}, u32[]{:S(2)}, u32[]{:S(2)}) collective-permute-start(f32[64,16,128]{2,1,0:T(8,128)S(1)} %get-tuple-element.34), channel_id=1, source_target_pairs={{1,0},{2,1},{3,2},{4,3},{5,4},{6,5},{7,6},{8,7},{9,8},{10,9},{11,1... | collective-permute-start | bytes 1572872 | tf_op jit(solution)/shard_map/ppermute | solution.py:28
  45.4 0.8 copy-start.3
  47.1 7.8 %collective-permute-start.7 = (f32[32,32,128]{2,1,0:T(8,128)S(1)}, f32[32,32,128]{2,1,0:T(8,128)S(1)}, u32[]{:S(2)}, u32[]{:S(2)}) collective-permute-start(f32[32,32,128]{2,1,0:T(8,128)S(1)} %bitcast.76), channel_id=1, source_target_pairs={{32,0},{64,32},{96,64},{128,96},{160,128},{192,160},{224,192},{0,2... | collective-permute-start | bytes 1572872 | tf_op jit(solution)/shard_map/ppermute | solution.py:28
  48.3 8.6 %collective-permute-start.6 = (f32[32,32,128]{2,1,0:T(8,128)S(1)}, f32[32,32,128]{2,1,0:T(8,128)S(1)}, u32[]{:S(2)}, u32[]{:S(2)}) collective-permute-start(f32[32,32,128]{2,1,0:T(8,128)S(1)} %bitcast.75), channel_id=1, source_target_pairs={{0,32},{32,64},{64,96},{96,128},{128,160},{160,192},{192,224},{224... | collective-permute-start | bytes 1572872 | tf_op jit(solution)/shard_map/ppermute | solution.py:25
  57.2 27.6 %collective-permute-start.9 = (f32[64,32,128]{2,1,0:T(8,128)S(1)}, f32[64,32,128]{2,1,0:T(8,128)S(1)}, u32[]{:S(2)}, u32[]{:S(2)}) collective-permute-start(f32[64,32,128]{2,1,0:T(8,128)S(1)} %fusion.16), channel_id=1, source_target_pairs={{1,0},{2,1},{3,2},{4,3},{5,4},{6,5},{7,6},{8,7},{9,8},{10,9},{11,1... | collective-permute-start | bytes 3145736 | tf_op jit(solution)/shard_map/ppermute | solution.py:28
  62.1 28.2 %collective-permute-start.8 = (f32[64,32,128]{2,1,0:T(8,128)S(1)}, f32[64,32,128]{2,1,0:T(8,128)S(1)}, u32[]{:S(2)}, u32[]{:S(2)}) collective-permute-start(f32[64,32,128]{2,1,0:T(8,128)S(1)} %fusion.16), channel_id=1, source_target_pairs={{0,1},{1,2},{2,3},{3,4},{4,5},{5,6},{6,7},{7,8},{8,9},{9,10},{10,1... | collective-permute-start | bytes 3145736 | tf_op jit(solution)/shard_map/ppermute | solution.py:25
  90.7 0.8 copy-start.2

commit v11 on v9

--- a/solution.py
+++ b/solution.py
@@ -92,9 +92,10 @@
 def per_device(density):
     size_x, size_y, planes = density.shape
     assert SUB % size_x == 0 and SUB % size_y == 0
-    sums = []
+    pairs = []
     current = density
     padded_x = None
+    last = len(SPACINGS) - 1
     for scale, spacing in enumerate(SPACINGS):
         width = 2 * spacing
         if scale == 0:
@@ -114,8 +115,12 @@
             padded_y = padded_1(along_x, "col", 1, width)
             along_y = holed_pass(padded_y, spacing, 1, size_y)
             smoother = depth_pass(along_y, spacing)
-        sums.append(moment_sums(current - smoother))
+        if scale == last:
+            held = lax.optimization_barrier(pairs)
+            sums = [moment_sums(a - b) for a, b in held]
+        pairs.append((current, smoother))
         current = smoother
+    sums.append(moment_sums(pairs[-1][0] - pairs[-1][1]))
     partial = jnp.sum(jnp.stack(sums), axis=-1)
     count_x = lax.axis_size("row") * size_x // SUB
     count_y = lax.axis_size("col") * size_y // SUB

time: 114 us -> 114 us (level)
  transfers between devices with their start and end apart: 10 -> 10, of which waited for: 7 -> 7; matrix products, arithmetic and copies ran while one was open for 0% -> 1% of each run, Pallas kernels for 0% -> 0%
where the time goes in v11:
time: 114 us; the launch traced here: 112 us
  waiting for transfers between devices  59.9 us (53%)
  starting transfers between devices  21.4 us (19%)
  blocking collectives  18.4 us (16%)
  matrix products  4.52 us (4%)
  other arithmetic  4.34 us (4%)
  local copies, waits for them, and re-layouts  2.51 us (2%)
    ppermute x5, waiting for transfers between devices, padded_1(): lax.ppermute(lax.slice_in_dim(block, block.shape[dim] - width, None, axis...  31.1 us
    ppermute x5, waiting for transfers between devices, padded_1(): lax.ppermute(lax.slice_in_dim(block, 0, width, axis=dim), axis, backward)  28.7 us
    ppermute x5, starting transfers between devices, padded_1(): lax.ppermute(lax.slice_in_dim(block, 0, width, axis=dim), axis, backward)  19.3 us
    all_to_all x1, blocking collectives, gather_partials(): return lax.all_to_all(sent, axes, 0, 0, tiled=True)  18.4 us
    dot_general x3, matrix products, depth_pass(): jnp.dot(flat, jnp.asarray(depth_matrix(planes, spacing)), precision=lax.P...  4.52 us
  transfers between devices with their start and end apart: 10, of which 7 were waited for; matrix products, arithmetic and copies ran while one was open for 1% of the time, Pallas kernels for 0%

profile of v11, /device:TPU:8, one launch (start us, length us, event | category | flops | bytes accessed | tf_op | source)
XLA Modules:
  0.0 111.9 jit_solution(6825472378624836428)
XLA Ops:
  0.6 1.2 %fusion.60 = (f32[64,8,128]{2,1,0:T(8,128)S(1)}, f32[64,8,128]{2,1,0:T(8,128)S(1)}) fusion(f32[64,32,128]{2,1,0:T(8,128)} %param.4), kind=kLoop, calls=%fused_computation.112 | loop fusion | bytes 1048576 | tf_op jit(solution)/shard_map/slice | solution.py:26
  1.8 2.0 %collective-permute-start = (f32[64,8,128]{2,1,0:T(8,128)S(1)}, f32[64,8,128]{2,1,0:T(8,128)S(1)}, u32[]{:S(2)}, u32[]{:S(2)}) collective-permute-start(f32[64,8,128]{2,1,0:T(8,128)S(1)} %get-tuple-element.34), channel_id=1, source_target_pairs={{0,1},{1,2},{2,3},{3,4},{4,5},{5,6},{6,7},{7,8},{8,9},{9,10},{10,1... | collective-permute-start | bytes 786440 | tf_op jit(solution)/shard_map/ppermute | solution.py:25
  3.8 6.2 %collective-permute-start.1 = (f32[64,8,128]{2,1,0:T(8,128)S(1)}, f32[64,8,128]{2,1,0:T(8,128)S(1)}, u32[]{:S(2)}, u32[]{:S(2)}) collective-permute-start(f32[64,8,128]{2,1,0:T(8,128)S(1)} %get-tuple-element.35), channel_id=1, source_target_pairs={{1,0},{2,1},{3,2},{4,3},{5,4},{6,5},{7,6},{8,7},{9,8},{10,9},{11,1... | collective-permute-start | bytes 786440 | tf_op jit(solution)/shard_map/ppermute | solution.py:28
  10.0 6.2 %collective-permute-done = f32[64,8,128]{2,1,0:T(8,128)S(1)} collective-permute-done((f32[64,8,128]{2,1,0:T(8,128)S(1)}, f32[64,8,128]{2,1,0:T(8,128)S(1)}, u32[]{:S(2)}, u32[]{:S(2)}) %collective-permute-start) | collective-permute-done | bytes 262176 | tf_op jit(solution)/shard_map/ppermute | solution.py:25
  16.3 0.1 constant_dynamic-update-slice_fusion
  16.4 0.5 fusion.42
  17.0 1.7 %collective-permute-start.3 = (f32[24,32,128]{2,1,0:T(8,128)S(1)}, f32[24,32,128]{2,1,0:T(8,128)S(1)}, u32[]{:S(2)}, u32[]{:S(2)}) collective-permute-start(f32[24,32,128]{2,1,0:T(8,128)S(1)} %get-tuple-element.31), channel_id=1, source_target_pairs={{32,0},{64,32},{96,64},{128,96},{160,128},{192,160},{224,192},{0,2... | collective-permute-start | bytes 1179656 | tf_op jit(solution)/shard_map/ppermute | solution.py:28
  18.8 5.5 %collective-permute-done.2 = f32[24,32,128]{2,1,0:T(8,128)S(1)} collective-permute-done((f32[24,32,128]{2,1,0:T(8,128)S(1)}, f32[24,32,128]{2,1,0:T(8,128)S(1)}, u32[]{:S(2)}, u32[]{:S(2)}) %collective-permute-start.2) | collective-permute-done | bytes 393248 | tf_op jit(solution)/shard_map/ppermute | solution.py:25
  24.2 0.2 pad_maximum_fusion
  24.4 0.4 fusion
  24.8 0.5 copy-done.3
  25.3 1.4 %fusion.62 = f32[3072,128]{1,0:T(8,128)S(1)} fusion(f32[3072,128]{1,0:T(8,128)S(1)} %bitcast.43, f32[128,128]{1,0:T(8,128)S(1)} %copy-done.3), kind=kOutput, calls=%fused_computation.114 | convolution fusion | flops 603979776 | bytes 3211264 | tf_op jit(solution)/shard_map/dot_general | solution.py:54
  26.6 0.3 fusion.56
  26.9 0.5 add_add_fusion
  27.6 5.3 %collective-permute-start.5 = (f32[64,16,128]{2,1,0:T(8,128)S(1)}, f32[64,16,128]{2,1,0:T(8,128)S(1)}, u32[]{:S(2)}, u32[]{:S(2)}) collective-permute-start(f32[64,16,128]{2,1,0:T(8,128)S(1)} %get-tuple-element.29), channel_id=1, source_target_pairs={{1,0},{2,1},{3,2},{4,3},{5,4},{6,5},{7,6},{8,7},{9,8},{10,9},{11,1... | collective-permute-start | bytes 1572872 | tf_op jit(solution)/shard_map/ppermute | solution.py:28
  33.0 12.0 %collective-permute-done.4 = f32[64,16,128]{2,1,0:T(8,128)S(1)} collective-permute-done((f32[64,16,128]{2,1,0:T(8,128)S(1)}, f32[64,16,128]{2,1,0:T(8,128)S(1)}, u32[]{:S(2)}, u32[]{:S(2)}) %collective-permute-start.4) | collective-permute-done | bytes 524320 | tf_op jit(solution)/shard_map/ppermute | solution.py:25
  45.0 0.3 fusion.21
  45.3 1.0 fusion.63
  46.4 1.1 %collective-permute-start.7 = (f32[32,32,128]{2,1,0:T(8,128)S(1)}, f32[32,32,128]{2,1,0:T(8,128)S(1)}, u32[]{:S(2)}, u32[]{:S(2)}) collective-permute-start(f32[32,32,128]{2,1,0:T(8,128)S(1)} %bitcast.49), channel_id=1, source_target_pairs={{32,0},{64,32},{96,64},{128,96},{160,128},{192,160},{224,192},{0,2... | collective-permute-start | bytes 1572872 | tf_op jit(solution)/shard_map/ppermute | solution.py:28
  47.5 6.7 %collective-permute-done.7 = f32[32,32,128]{2,1,0:T(8,128)S(1)} collective-permute-done((f32[32,32,128]{2,1,0:T(8,128)S(1)}, f32[32,32,128]{2,1,0:T(8,128)S(1)}, u32[]{:S(2)}, u32[]{:S(2)}) %collective-permute-start.7) | collective-permute-done | bytes 524320 | tf_op jit(solution)/shard_map/ppermute | solution.py:28
  54.2 1.9 %collective-permute-done.6 = f32[32,32,128]{2,1,0:T(8,128)S(1)} collective-permute-done((f32[32,32,128]{2,1,0:T(8,128)S(1)}, f32[32,32,128]{2,1,0:T(8,128)S(1)}, u32[]{:S(2)}, u32[]{:S(2)}) %collective-permute-start.6) | collective-permute-done | bytes 524320 | tf_op jit(solution)/shard_map/ppermute | solution.py:25
  56.1 0.4 fusion.13
  56.5 4.9 %collective-permute-start.9 = (f32[64,32,128]{2,1,0:T(8,128)S(1)}, f32[64,32,128]{2,1,0:T(8,128)S(1)}, u32[]{:S(2)}, u32[]{:S(2)}) collective-permute-start(f32[64,32,128]{2,1,0:T(8,128)S(1)} %fusion.13), channel_id=1, source_target_pairs={{1,0},{2,1},{3,2},{4,3},{5,4},{6,5},{7,6},{8,7},{9,8},{10,9},{11,1... | collective-permute-start | bytes 3145736 | tf_op jit(solution)/shard_map/ppermute | solution.py:28
  61.4 0.3 abs_reduce_fusion.2
  61.7 0.3 abs_reduce_fusion.1
  62.0 22.0 %collective-permute-done.9 = f32[64,32,128]{2,1,0:T(8,128)S(1)} collective-permute-done((f32[64,32,128]{2,1,0:T(8,128)S(1)}, f32[64,32,128]{2,1,0:T(8,128)S(1)}, u32[]{:S(2)}, u32[]{:S(2)}) %collective-permute-start.9) | collective-permute-done | bytes 1048608 | tf_op jit(solution)/shard_map/ppermute | solution.py:28
  84.1 5.5 %collective-permute-done.8 = f32[64,32,128]{2,1,0:T(8,128)S(1)} collective-permute-done((f32[64,32,128]{2,1,0:T(8,128)S(1)}, f32[64,32,128]{2,1,0:T(8,128)S(1)}, u32[]{:S(2)}, u32[]{:S(2)}) %collective-permute-start.8) | collective-permute-done | bytes 1048608 | tf_op jit(solution)/shard_map/ppermute | solution.py:25
  89.6 2.2 %fusion.61 = (f32[64,32,128]{2,1,0:T(8,128)S(1)}, f32[64,32,128]{2,1,0:T(8,128)}) fusion(f32[64,32,128]{2,1,0:T(8,128)S(1)} %bitcast.39, f32[128,128,1]{1,0,2:T(8,128)S(1)} %copy-done.1, f32[64,32,128]{2,1,0:T(8,128)S(1)} %collective-permute-done.9, f32[64,32,128]{2,1,0:T(8,128)S(1)} %fusion.13, f32[64,32,128]{2,1,0:T(8,128)S(1)} %collective-permute-done.8), kind=kOutput, calls=%fused_computation.113 | convolution fusion | flops 405798912 | bytes 6356992 | tf_op jit(solution)/shard_map/dot_general | solution.py:54
  91.8 0.3 abs_reduce_fusion
  92.3 18.4 %all_to_all.6 = f32[256,1,12]{2,1,0:T(1,128)S(1)} all-to-all(f32[256,1,12]{2,1,0:T(1,128)S(1)} %broadcast_in_dim.8), channel_id=1, replica_groups=mesh['row'=8,'col'=32] {'row','col'}, dimensions={0} | all-to-all | bytes 24576 | tf_op jit(solution)/shard_map/all_to_all | solution.py:89
  110.8 0.3 reshape.50
  111.3 0.6 pad_maximum_fusion.7
  (29 shorter events, 0.9 us)
Async XLA Ops:
  0.6 15.6 %copy-start = (f32[64,32,128]{2,1,0:T(8,128)S(1)}, f32[64,32,128]{2,1,0:T(8,128)}, u32[]{:S(2)}) copy-start(f32[64,32,128]{2,1,0:T(8,128)} %param.4) | copy-start | bytes 3145732
  1.8 14.4 %collective-permute-start = (f32[64,8,128]{2,1,0:T(8,128)S(1)}, f32[64,8,128]{2,1,0:T(8,128)S(1)}, u32[]{:S(2)}, u32[]{:S(2)}) collective-permute-start(f32[64,8,128]{2,1,0:T(8,128)S(1)} %get-tuple-element.34), channel_id=1, source_target_pairs={{0,1},{1,2},{2,3},{3,4},{4,5},{5,6},{6,7},{7,8},{8,9},{9,10},{10,1... | collective-permute-start | bytes 786440 | tf_op jit(solution)/shard_map/ppermute | solution.py:25
  3.8 12.6 %collective-permute-start.1 = (f32[64,8,128]{2,1,0:T(8,128)S(1)}, f32[64,8,128]{2,1,0:T(8,128)S(1)}, u32[]{:S(2)}, u32[]{:S(2)}) collective-permute-start(f32[64,8,128]{2,1,0:T(8,128)S(1)} %get-tuple-element.35), channel_id=1, source_target_pairs={{1,0},{2,1},{3,2},{4,3},{5,4},{6,5},{7,6},{8,7},{9,8},{10,9},{11,1... | collective-permute-start | bytes 786440 | tf_op jit(solution)/shard_map/ppermute | solution.py:28
  17.0 7.2 %collective-permute-start.2 = (f32[24,32,128]{2,1,0:T(8,128)S(1)}, f32[24,32,128]{2,1,0:T(8,128)S(1)}, u32[]{:S(2)}, u32[]{:S(2)}) collective-permute-start(f32[24,32,128]{2,1,0:T(8,128)S(1)} %get-tuple-element.30), channel_id=1, source_target_pairs={{0,32},{32,64},{64,96},{96,128},{128,160},{160,192},{192,224},{224... | collective-permute-start | bytes 1179656 | tf_op jit(solution)/shard_map/ppermute | solution.py:25
  17.0 7.2 %collective-permute-start.3 = (f32[24,32,128]{2,1,0:T(8,128)S(1)}, f32[24,32,128]{2,1,0:T(8,128)S(1)}, u32[]{:S(2)}, u32[]{:S(2)}) collective-permute-start(f32[24,32,128]{2,1,0:T(8,128)S(1)} %get-tuple-element.31), channel_id=1, source_target_pairs={{32,0},{64,32},{96,64},{128,96},{160,128},{192,160},{224,192},{0,2... | collective-permute-start | bytes 1179656 | tf_op jit(solution)/shard_map/ppermute | solution.py:28
  24.4 0.8 copy-start.3
  27.5 17.5 %collective-permute-start.4 = (f32[64,16,128]{2,1,0:T(8,128)S(1)}, f32[64,16,128]{2,1,0:T(8,128)S(1)}, u32[]{:S(2)}, u32[]{:S(2)}) collective-permute-start(f32[64,16,128]{2,1,0:T(8,128)S(1)} %get-tuple-element.28), channel_id=1, source_target_pairs={{0,1},{1,2},{2,3},{3,4},{4,5},{5,6},{6,7},{7,8},{8,9},{9,10},{10,1... | collective-permute-start | bytes 1572872 | tf_op jit(solution)/shard_map/ppermute | solution.py:25
  27.6 17.7 %copy-start.2 = (f32[128,128]{1,0:T(8,128)S(1)}, f32[128,128]{1,0:T(8,128)}, u32[]{:S(2)}) copy-start(f32[128,128]{1,0:T(8,128)} %constant.26.clone) | copy-start | bytes 196612
  27.6 17.4 %collective-permute-start.5 = (f32[64,16,128]{2,1,0:T(8,128)S(1)}, f32[64,16,128]{2,1,0:T(8,128)S(1)}, u32[]{:S(2)}, u32[]{:S(2)}) collective-permute-start(f32[64,16,128]{2,1,0:T(8,128)S(1)} %get-tuple-element.29), channel_id=1, source_target_pairs={{1,0},{2,1},{3,2},{4,3},{5,4},{6,5},{7,6},{8,7},{9,8},{10,9},{11,1... | collective-permute-start | bytes 1572872 | tf_op jit(solution)/shard_map/ppermute | solution.py:28
  46.4 7.8 %collective-permute-start.7 = (f32[32,32,128]{2,1,0:T(8,128)S(1)}, f32[32,32,128]{2,1,0:T(8,128)S(1)}, u32[]{:S(2)}, u32[]{:S(2)}) collective-permute-start(f32[32,32,128]{2,1,0:T(8,128)S(1)} %bitcast.49), channel_id=1, source_target_pairs={{32,0},{64,32},{96,64},{128,96},{160,128},{192,160},{224,192},{0,2... | collective-permute-start | bytes 1572872 | tf_op jit(solution)/shard_map/ppermute | solution.py:28
  47.5 8.6 %collective-permute-start.6 = (f32[32,32,128]{2,1,0:T(8,128)S(1)}, f32[32,32,128]{2,1,0:T(8,128)S(1)}, u32[]{:S(2)}, u32[]{:S(2)}) collective-permute-start(f32[32,32,128]{2,1,0:T(8,128)S(1)} %bitcast.48), channel_id=1, source_target_pairs={{0,32},{32,64},{64,96},{96,128},{128,160},{160,192},{192,224},{224... | collective-permute-start | bytes 1572872 | tf_op jit(solution)/shard_map/ppermute | solution.py:25
  56.5 27.6 %collective-permute-start.9 = (f32[64,32,128]{2,1,0:T(8,128)S(1)}, f32[64,32,128]{2,1,0:T(8,128)S(1)}, u32[]{:S(2)}, u32[]{:S(2)}) collective-permute-start(f32[64,32,128]{2,1,0:T(8,128)S(1)} %fusion.13), channel_id=1, source_target_pairs={{1,0},{2,1},{3,2},{4,3},{5,4},{6,5},{7,6},{8,7},{9,8},{10,9},{11,1... | collective-permute-start | bytes 3145736 | tf_op jit(solution)/shard_map/ppermute | solution.py:28
  61.4 28.2 %collective-permute-start.8 = (f32[64,32,128]{2,1,0:T(8,128)S(1)}, f32[64,32,128]{2,1,0:T(8,128)S(1)}, u32[]{:S(2)}, u32[]{:S(2)}) collective-permute-start(f32[64,32,128]{2,1,0:T(8,128)S(1)} %fusion.13), channel_id=1, source_target_pairs={{0,1},{1,2},{2,3},{3,4},{4,5},{5,6},{6,7},{7,8},{8,9},{9,10},{10,1... | collective-permute-start | bytes 3145736 | tf_op jit(solution)/shard_map/ppermute | solution.py:25
  61.7 27.9 %copy-start.1 = (f32[128,128,1]{1,0,2:T(8,128)S(1)}, f32[128,128,1]{1,0,2:T(8,128)}, u32[]{:S(2)}) copy-start(f32[128,128,1]{1,0,2:T(8,128)} %constant.28) | copy-start | bytes 196612

commit v12 on v3

--- a/solution.py
+++ b/solution.py
@@ -47,17 +47,17 @@
     return matrix
 
 
-def depth_pass(values_in, spacing):
+def depth_pass(values_in, matrix):
     rows = values_in.shape[:-1]
     planes = values_in.shape[-1]
     flat = values_in.reshape(-1, planes)
     summed = jnp.dot(
         flat,
-        jnp.asarray(depth_matrix(planes, spacing)),
+        jnp.asarray(matrix),
         precision=lax.Precision.HIGHEST,
         preferred_element_type=jnp.float32,
     )
-    return summed.reshape(*rows, planes)
+    return summed.reshape(*rows, matrix.shape[1])
 
 
 def moment_sums(detail):
@@ -92,16 +92,31 @@
 def per_device(density):
     size_x, size_y, planes = density.shape
     assert SUB % size_x == 0 and SUB % size_y == 0
-    sums = []
-    current = density
-    for spacing in SPACINGS:
-        padded_x = padded_1(current, "row", 0, 2 * spacing)
-        along_x = holed_pass(padded_x, spacing, 0, size_x)
-        padded_y = padded_1(along_x, "col", 1, 2 * spacing)
-        along_y = holed_pass(padded_y, spacing, 1, size_y)
-        smoother = depth_pass(along_y, spacing)
-        sums.append(moment_sums(current - smoother))
-        current = smoother
+    assert len(SPACINGS) == 3
+    first, second, third = SPACINGS
+    matrix_1 = depth_matrix(planes, first)
+    matrix_2 = depth_matrix(planes, second)
+    matrix_3 = depth_matrix(planes, third)
+    extra = 2 * second
+    padded_y = padded_1(density, "col", 1, 2 * first)
+    along_y = holed_pass(padded_y, first, 1, size_y)
+    padded_x = padded_1(along_y, "row", 0, 2 * first + extra)
+    along_x = holed_pass(padded_x, first, 0, size_x + 2 * extra)
+    both = depth_pass(along_x, np.concatenate([matrix_1, matrix_1 @ matrix_2], axis=1))
+    smooth_1 = lax.slice_in_dim(both[..., :planes], extra, extra + size_x, axis=0)
+    ahead_2 = both[..., planes:]
+    along_x = holed_pass(ahead_2, second, 0, size_x)
+    padded_y = padded_1(along_x, "col", 1, 2 * second)
+    smooth_2 = holed_pass(padded_y, second, 1, size_y)
+    ahead_3 = depth_pass(smooth_2, matrix_3)
+    padded_x = padded_1(ahead_3, "row", 0, 2 * third)
+    along_x = holed_pass(padded_x, third, 0, size_x)
+    padded_y = padded_1(along_x, "col", 1, 2 * third)
+    smooth_3 = holed_pass(padded_y, third, 1, size_y)
+    current = smooth_3
+    held = lax.optimization_barrier(((density, smooth_1), (smooth_1, smooth_2)))
+    sums = [moment_sums(a - b) for a, b in held]
+    sums.append(moment_sums(smooth_2 - smooth_3))
     partial = jnp.sum(jnp.stack(sums), axis=-1)
     count_x = lax.axis_size("row") * size_x // SUB
     count_y = lax.axis_size("col") * size_y // SUB
@@ -115,10 +130,11 @@
 
 def solution(mesh):
     placed = (P("row", "col", None),)
-    return jax.shard_map(
+    step = jax.shard_map(
         per_device,
         mesh=mesh,
         in_specs=placed,
         out_specs=(P("row", "col", None), P()),
         check_vma=False,
     )
+    return step

time: 116 us -> 113 us (0.974)
  waiting for transfers between devices: 61.9 us -> 59.9 us
  local copies, waits for them, and re-layouts: 3.32 us -> 2.05 us
  other arithmetic: 3.78 us -> 5.01 us
    ppermute x6 -> x5, waiting for transfers between devices: 31.7 us -> 28.7 us  [padded_1(): lax.ppermute(lax.slice_in_dim(block, 0, width, axis=dim), axis, backward)]
    concatenate x2, local copies, waits for them, and re-layouts: 1.57 us -> 0.16 us  [padded_1(): return jnp.concatenate([low, block, high], axis=dim)]
    ppermute x6 -> x5, starting transfers between devices: 3.09 us -> 2.1 us  [padded_1(): lax.ppermute(lax.slice_in_dim(block, block.shape[dim] - width, None, axis...]
    ppermute x6 -> x5, waiting for transfers between devices: 30.3 us -> 31.1 us  [padded_1(): lax.ppermute(lax.slice_in_dim(block, block.shape[dim] - width, None, axis...]
    ppermute x6 -> x5, starting transfers between devices: 18.6 us -> 19.3 us  [padded_1(): lax.ppermute(lax.slice_in_dim(block, 0, width, axis=dim), axis, backward)]
    dot_general x3 -> x2, matrix products: 4.1 us -> 3.57 us  [depth_pass(): jnp.dot(flat, jnp.asarray(matrix), precision=lax.Precision.HIGHEST, prefe...]
  transfers between devices with their start and end apart: 12 -> 10, of which waited for: 9 -> 7; matrix products, arithmetic and copies ran while one was open for 2% -> 1% of each run, Pallas kernels for 0% -> 0%
where the time goes in v12:
time: 113 us; the launch traced here: 111 us
  waiting for transfers between devices  59.9 us (53%)
  starting transfers between devices  21.4 us (19%)
  blocking collectives  18.4 us (16%)
  other arithmetic  5.01 us (4%)
  matrix products  3.57 us (3%)
  local copies, waits for them, and re-layouts  2.05 us (2%)
    ppermute x5, waiting for transfers between devices, padded_1(): lax.ppermute(lax.slice_in_dim(block, block.shape[dim] - width, None, axis...  31.1 us
    ppermute x5, waiting for transfers between devices, padded_1(): lax.ppermute(lax.slice_in_dim(block, 0, width, axis=dim), axis, backward)  28.7 us
    ppermute x5, starting transfers between devices, padded_1(): lax.ppermute(lax.slice_in_dim(block, 0, width, axis=dim), axis, backward)  19.3 us
    all_to_all x1, blocking collectives, gather_partials(): return lax.all_to_all(sent, axes, 0, 0, tiled=True)  18.4 us
    dot_general x2, matrix products, depth_pass(): jnp.dot(flat, jnp.asarray(matrix), precision=lax.Precision.HIGHEST, prefe...  3.57 us
  transfers between devices with their start and end apart: 10, of which 7 were waited for; matrix products, arithmetic and copies ran while one was open for 1% of the time, Pallas kernels for 0%

profile of v12, /device:TPU:8, one launch (start us, length us, event | category | flops | bytes accessed | tf_op | source)
XLA Modules:
  0.0 111.1 jit_solution(10818560969669949851)
XLA Ops:
  0.6 1.2 %fusion.61 = (f32[64,8,128]{2,1,0:T(8,128)S(1)}, f32[64,8,128]{2,1,0:T(8,128)S(1)}) fusion(f32[64,32,128]{2,1,0:T(8,128)} %param.3), kind=kLoop, calls=%fused_computation.110 | loop fusion | bytes 1048576 | tf_op jit(solution)/shard_map/slice | solution.py:26
  1.8 2.0 %collective-permute-start = (f32[64,8,128]{2,1,0:T(8,128)S(1)}, f32[64,8,128]{2,1,0:T(8,128)S(1)}, u32[]{:S(2)}, u32[]{:S(2)}) collective-permute-start(f32[64,8,128]{2,1,0:T(8,128)S(1)} %get-tuple-element.34), channel_id=1, source_target_pairs={{0,1},{1,2},{2,3},{3,4},{4,5},{5,6},{6,7},{7,8},{8,9},{9,10},{10,1... | collective-permute-start | bytes 786440 | tf_op jit(solution)/shard_map/ppermute | solution.py:25
  3.8 6.2 %collective-permute-start.1 = (f32[64,8,128]{2,1,0:T(8,128)S(1)}, f32[64,8,128]{2,1,0:T(8,128)S(1)}, u32[]{:S(2)}, u32[]{:S(2)}) collective-permute-start(f32[64,8,128]{2,1,0:T(8,128)S(1)} %get-tuple-element.35), channel_id=1, source_target_pairs={{1,0},{2,1},{3,2},{4,3},{5,4},{6,5},{7,6},{8,7},{9,8},{10,9},{11,1... | collective-permute-start | bytes 786440 | tf_op jit(solution)/shard_map/ppermute | solution.py:28
  10.0 6.2 %collective-permute-done = f32[64,8,128]{2,1,0:T(8,128)S(1)} collective-permute-done((f32[64,8,128]{2,1,0:T(8,128)S(1)}, f32[64,8,128]{2,1,0:T(8,128)S(1)}, u32[]{:S(2)}, u32[]{:S(2)}) %collective-permute-start) | collective-permute-done | bytes 262176 | tf_op jit(solution)/shard_map/ppermute | solution.py:25
  16.3 0.1 constant_dynamic-update-slice_fusion
  16.4 0.5 fusion.45
  17.1 1.7 %collective-permute-start.3 = (f32[24,32,128]{2,1,0:T(8,128)S(1)}, f32[24,32,128]{2,1,0:T(8,128)S(1)}, u32[]{:S(2)}, u32[]{:S(2)}) collective-permute-start(f32[24,32,128]{2,1,0:T(8,128)S(1)} %get-tuple-element.31), channel_id=1, source_target_pairs={{32,0},{64,32},{96,64},{128,96},{160,128},{192,160},{224,192},{0,2... | collective-permute-start | bytes 1179656 | tf_op jit(solution)/shard_map/ppermute | solution.py:28
  18.8 5.5 %collective-permute-done.2 = f32[24,32,128]{2,1,0:T(8,128)S(1)} collective-permute-done((f32[24,32,128]{2,1,0:T(8,128)S(1)}, f32[24,32,128]{2,1,0:T(8,128)S(1)}, u32[]{:S(2)}, u32[]{:S(2)}) %collective-permute-start.2) | collective-permute-done | bytes 393248 | tf_op jit(solution)/shard_map/ppermute | solution.py:25
  24.2 0.2 pad_maximum_fusion
  24.4 2.6 %fusion.1 = f32[96,32,256]{2,1,0:T(8,128)S(1)} fusion(f32[128,256,1]{1,0,2:T(8,128)S(1)} %copy-done.2, f32[112,32,128]{2,1,0:T(8,128)S(1)} %pad_maximum_fusion), kind=kOutput, calls=%fused_computation.3 | convolution fusion | flops 1211498496 | bytes 11141120 | tf_op jit(solution)/shard_map/dot_general | solution.py:54
  27.0 0.3 fusion.57
  27.6 5.3 %collective-permute-start.5 = (f32[64,16,128]{2,1,0:T(8,128)S(1)}, f32[64,16,128]{2,1,0:T(8,128)S(1)}, u32[]{:S(2)}, u32[]{:S(2)}) collective-permute-start(f32[64,16,128]{2,1,0:T(8,128)S(1)} %get-tuple-element.29), channel_id=1, source_target_pairs={{1,0},{2,1},{3,2},{4,3},{5,4},{6,5},{7,6},{8,7},{9,8},{10,9},{11,1... | collective-permute-start | bytes 1572872 | tf_op jit(solution)/shard_map/ppermute | solution.py:28
  32.9 12.1 %collective-permute-done.4 = f32[64,16,128]{2,1,0:T(8,128)S(1)} collective-permute-done((f32[64,16,128]{2,1,0:T(8,128)S(1)}, f32[64,16,128]{2,1,0:T(8,128)S(1)}, u32[]{:S(2)}, u32[]{:S(2)}) %collective-permute-start.4) | collective-permute-done | bytes 524320 | tf_op jit(solution)/shard_map/ppermute | solution.py:25
  45.0 0.3 fusion.26
  45.3 1.0 fusion.62
  46.3 1.1 %collective-permute-start.7 = (f32[32,32,128]{2,1,0:T(8,128)S(1)}, f32[32,32,128]{2,1,0:T(8,128)S(1)}, u32[]{:S(2)}, u32[]{:S(2)}) collective-permute-start(f32[32,32,128]{2,1,0:T(8,128)S(1)} %bitcast.33), channel_id=1, source_target_pairs={{32,0},{64,32},{96,64},{128,96},{160,128},{192,160},{224,192},{0,2... | collective-permute-start | bytes 1572872 | tf_op jit(solution)/shard_map/ppermute | solution.py:28
  47.5 6.7 %collective-permute-done.7 = f32[32,32,128]{2,1,0:T(8,128)S(1)} collective-permute-done((f32[32,32,128]{2,1,0:T(8,128)S(1)}, f32[32,32,128]{2,1,0:T(8,128)S(1)}, u32[]{:S(2)}, u32[]{:S(2)}) %collective-permute-start.7) | collective-permute-done | bytes 524320 | tf_op jit(solution)/shard_map/ppermute | solution.py:28
  54.2 1.9 %collective-permute-done.6 = f32[32,32,128]{2,1,0:T(8,128)S(1)} collective-permute-done((f32[32,32,128]{2,1,0:T(8,128)S(1)}, f32[32,32,128]{2,1,0:T(8,128)S(1)}, u32[]{:S(2)}, u32[]{:S(2)}) %collective-permute-start.6) | collective-permute-done | bytes 524320 | tf_op jit(solution)/shard_map/ppermute | solution.py:25
  56.1 0.4 fusion.18
  56.5 4.9 %collective-permute-start.9 = (f32[64,32,128]{2,1,0:T(8,128)S(1)}, f32[64,32,128]{2,1,0:T(8,128)S(1)}, u32[]{:S(2)}, u32[]{:S(2)}) collective-permute-start(f32[64,32,128]{2,1,0:T(8,128)S(1)} %fusion.18), channel_id=1, source_target_pairs={{1,0},{2,1},{3,2},{4,3},{5,4},{6,5},{7,6},{8,7},{9,8},{10,9},{11,1... | collective-permute-start | bytes 3145736 | tf_op jit(solution)/shard_map/ppermute | solution.py:28
  61.3 0.3 abs_reduce_fusion.2
  61.6 0.3 abs_reduce_fusion.1
  62.0 22.0 %collective-permute-done.9 = f32[64,32,128]{2,1,0:T(8,128)S(1)} collective-permute-done((f32[64,32,128]{2,1,0:T(8,128)S(1)}, f32[64,32,128]{2,1,0:T(8,128)S(1)}, u32[]{:S(2)}, u32[]{:S(2)}) %collective-permute-start.9) | collective-permute-done | bytes 1048608 | tf_op jit(solution)/shard_map/ppermute | solution.py:28
  84.0 5.5 %collective-permute-done.8 = f32[64,32,128]{2,1,0:T(8,128)S(1)} collective-permute-done((f32[64,32,128]{2,1,0:T(8,128)S(1)}, f32[64,32,128]{2,1,0:T(8,128)S(1)}, u32[]{:S(2)}, u32[]{:S(2)}) %collective-permute-start.8) | collective-permute-done | bytes 1048608 | tf_op jit(solution)/shard_map/ppermute | solution.py:25
  89.5 1.5 %fusion.55 = (f32[64,32,128]{2,1,0:T(8,128)S(1)}, f32[64,32,128]{2,1,0:T(8,128)}) fusion(f32[64,32,128]{2,1,0:T(8,128)S(1)} %fusion.26, f32[64,32,128]{2,1,0:T(8,128)S(1)} %collective-permute-done.9, f32[64,32,128]{2,1,0:T(8,128)S(1)} %fusion.18, f32[64,32,128]{2,1,0:T(8,128)S(1)} %collective-permute-done.8), kind=kLoop, calls=%fused_computation.105 | loop fusion | flops 3145728 | bytes 6291456 | tf_op jit(solution)/shard_map/sub | solution.py:119
  91.0 0.3 abs_reduce_fusion
  91.3 0.1 maximum_reduce_fusion
  91.4 0.1 broadcast_in_dim.7
  91.6 18.4 %all_to_all.6 = f32[256,1,12]{2,1,0:T(1,128)S(1)} all-to-all(f32[256,1,12]{2,1,0:T(1,128)S(1)} %broadcast_in_dim.8), channel_id=1, replica_groups=mesh['row'=8,'col'=32] {'row','col'}, dimensions={0} | all-to-all | bytes 24576 | tf_op jit(solution)/shard_map/all_to_all | solution.py:89
  110.1 0.3 reshape.31
  110.4 0.1 reduce_sum.139
  110.5 0.6 pad_maximum_fusion.7
  (25 shorter events, 0.6 us)
Async XLA Ops:
  0.6 15.6 %copy-start = (f32[64,32,128]{2,1,0:T(8,128)S(1)}, f32[64,32,128]{2,1,0:T(8,128)}, u32[]{:S(2)}) copy-start(f32[64,32,128]{2,1,0:T(8,128)} %param.3) | copy-start | bytes 3145732
  1.8 14.4 %collective-permute-start = (f32[64,8,128]{2,1,0:T(8,128)S(1)}, f32[64,8,128]{2,1,0:T(8,128)S(1)}, u32[]{:S(2)}, u32[]{:S(2)}) collective-permute-start(f32[64,8,128]{2,1,0:T(8,128)S(1)} %get-tuple-element.34), channel_id=1, source_target_pairs={{0,1},{1,2},{2,3},{3,4},{4,5},{5,6},{6,7},{7,8},{8,9},{9,10},{10,1... | collective-permute-start | bytes 786440 | tf_op jit(solution)/shard_map/ppermute | solution.py:25
  3.8 12.6 %collective-permute-start.1 = (f32[64,8,128]{2,1,0:T(8,128)S(1)}, f32[64,8,128]{2,1,0:T(8,128)S(1)}, u32[]{:S(2)}, u32[]{:S(2)}) collective-permute-start(f32[64,8,128]{2,1,0:T(8,128)S(1)} %get-tuple-element.35), channel_id=1, source_target_pairs={{1,0},{2,1},{3,2},{4,3},{5,4},{6,5},{7,6},{8,7},{9,8},{10,9},{11,1... | collective-permute-start | bytes 786440 | tf_op jit(solution)/shard_map/ppermute | solution.py:28
  17.0 7.2 %collective-permute-start.2 = (f32[24,32,128]{2,1,0:T(8,128)S(1)}, f32[24,32,128]{2,1,0:T(8,128)S(1)}, u32[]{:S(2)}, u32[]{:S(2)}) collective-permute-start(f32[24,32,128]{2,1,0:T(8,128)S(1)} %get-tuple-element.30), channel_id=1, source_target_pairs={{0,32},{32,64},{64,96},{96,128},{128,160},{160,192},{192,224},{224... | collective-permute-start | bytes 1179656 | tf_op jit(solution)/shard_map/ppermute | solution.py:25
  17.0 7.4 %copy-start.2 = (f32[128,256,1]{1,0,2:T(8,128)S(1)}, f32[128,256,1]{1,0,2:T(8,128)}, u32[]{:S(2)}) copy-start(f32[128,256,1]{1,0,2:T(8,128)} %constant.25) | copy-start | bytes 393220
  17.1 7.2 %collective-permute-start.3 = (f32[24,32,128]{2,1,0:T(8,128)S(1)}, f32[24,32,128]{2,1,0:T(8,128)S(1)}, u32[]{:S(2)}, u32[]{:S(2)}) collective-permute-start(f32[24,32,128]{2,1,0:T(8,128)S(1)} %get-tuple-element.31), channel_id=1, source_target_pairs={{32,0},{64,32},{96,64},{128,96},{160,128},{192,160},{224,192},{0,2... | collective-permute-start | bytes 1179656 | tf_op jit(solution)/shard_map/ppermute | solution.py:28
  27.5 17.5 %collective-permute-start.4 = (f32[64,16,128]{2,1,0:T(8,128)S(1)}, f32[64,16,128]{2,1,0:T(8,128)S(1)}, u32[]{:S(2)}, u32[]{:S(2)}) collective-permute-start(f32[64,16,128]{2,1,0:T(8,128)S(1)} %get-tuple-element.28), channel_id=1, source_target_pairs={{0,1},{1,2},{2,3},{3,4},{4,5},{5,6},{6,7},{7,8},{8,9},{9,10},{10,1... | collective-permute-start | bytes 1572872 | tf_op jit(solution)/shard_map/ppermute | solution.py:25
  27.6 17.7 %copy-start.1 = (f32[128,128]{1,0:T(8,128)S(1)}, f32[128,128]{1,0:T(8,128)}, u32[]{:S(2)}) copy-start(f32[128,128]{1,0:T(8,128)} %constant.24.clone) | copy-start | bytes 196612
  27.6 17.4 %collective-permute-start.5 = (f32[64,16,128]{2,1,0:T(8,128)S(1)}, f32[64,16,128]{2,1,0:T(8,128)S(1)}, u32[]{:S(2)}, u32[]{:S(2)}) collective-permute-start(f32[64,16,128]{2,1,0:T(8,128)S(1)} %get-tuple-element.29), channel_id=1, source_target_pairs={{1,0},{2,1},{3,2},{4,3},{5,4},{6,5},{7,6},{8,7},{9,8},{10,9},{11,1... | collective-permute-start | bytes 1572872 | tf_op jit(solution)/shard_map/ppermute | solution.py:28
  46.3 7.8 %collective-permute-start.7 = (f32[32,32,128]{2,1,0:T(8,128)S(1)}, f32[32,32,128]{2,1,0:T(8,128)S(1)}, u32[]{:S(2)}, u32[]{:S(2)}) collective-permute-start(f32[32,32,128]{2,1,0:T(8,128)S(1)} %bitcast.33), channel_id=1, source_target_pairs={{32,0},{64,32},{96,64},{128,96},{160,128},{192,160},{224,192},{0,2... | collective-permute-start | bytes 1572872 | tf_op jit(solution)/shard_map/ppermute | solution.py:28
  47.5 8.6 %collective-permute-start.6 = (f32[32,32,128]{2,1,0:T(8,128)S(1)}, f32[32,32,128]{2,1,0:T(8,128)S(1)}, u32[]{:S(2)}, u32[]{:S(2)}) collective-permute-start(f32[32,32,128]{2,1,0:T(8,128)S(1)} %bitcast.32), channel_id=1, source_target_pairs={{0,32},{32,64},{64,96},{96,128},{128,160},{160,192},{192,224},{224... | collective-permute-start | bytes 1572872 | tf_op jit(solution)/shard_map/ppermute | solution.py:25
  56.5 27.6 %collective-permute-start.9 = (f32[64,32,128]{2,1,0:T(8,128)S(1)}, f32[64,32,128]{2,1,0:T(8,128)S(1)}, u32[]{:S(2)}, u32[]{:S(2)}) collective-permute-start(f32[64,32,128]{2,1,0:T(8,128)S(1)} %fusion.18), channel_id=1, source_target_pairs={{1,0},{2,1},{3,2},{4,3},{5,4},{6,5},{7,6},{8,7},{9,8},{10,9},{11,1... | collective-permute-start | bytes 3145736 | tf_op jit(solution)/shard_map/ppermute | solution.py:28
  61.3 28.2 %collective-permute-start.8 = (f32[64,32,128]{2,1,0:T(8,128)S(1)}, f32[64,32,128]{2,1,0:T(8,128)S(1)}, u32[]{:S(2)}, u32[]{:S(2)}) collective-permute-start(f32[64,32,128]{2,1,0:T(8,128)S(1)} %fusion.18), channel_id=1, source_target_pairs={{0,1},{1,2},{2,3},{3,4},{4,5},{5,6},{6,7},{7,8},{8,9},{9,10},{10,1... | collective-permute-start | bytes 3145736 | tf_op jit(solution)/shard_map/ppermute | solution.py:25

commit v13 on v12

--- a/solution.py
+++ b/solution.py
@@ -102,9 +102,8 @@
     along_y = holed_pass(padded_y, first, 1, size_y)
     padded_x = padded_1(along_y, "row", 0, 2 * first + extra)
     along_x = holed_pass(padded_x, first, 0, size_x + 2 * extra)
-    both = depth_pass(along_x, np.concatenate([matrix_1, matrix_1 @ matrix_2], axis=1))
-    smooth_1 = lax.slice_in_dim(both[..., :planes], extra, extra + size_x, axis=0)
-    ahead_2 = both[..., planes:]
+    ahead_2 = depth_pass(along_x, matrix_1 @ matrix_2)
+    smooth_1 = depth_pass(lax.slice_in_dim(along_x, extra, extra + size_x, axis=0), matrix_1)
     along_x = holed_pass(ahead_2, second, 0, size_x)
     padded_y = padded_1(along_x, "col", 1, 2 * second)
     smooth_2 = holed_pass(padded_y, second, 1, size_y)

time: 113 us -> 113 us (level)
    dot_general x2 -> x3, matrix products: 3.57 us -> 3.34 us  [depth_pass(): jnp.dot(flat, jnp.asarray(matrix), precision=lax.Precision.HIGHEST, prefe...]
  transfers between devices with their start and end apart: 10 -> 10, of which waited for: 7 -> 7; matrix products, arithmetic and copies ran while one was open for 1% -> 2% of each run, Pallas kernels for 0% -> 0%
where the time goes in v13:
time: 113 us; the launch traced here: 111 us
  waiting for transfers between devices  58.9 us (52%)
  starting transfers between devices  21.4 us (19%)
  blocking collectives  18.4 us (16%)
  other arithmetic  5.38 us (5%)
  matrix products  3.34 us (3%)
  local copies, waits for them, and re-layouts  2.51 us (2%)
    ppermute x5, waiting for transfers between devices, padded_1(): lax.ppermute(lax.slice_in_dim(block, block.shape[dim] - width, None, axis...  31.1 us
    ppermute x5, waiting for transfers between devices, padded_1(): lax.ppermute(lax.slice_in_dim(block, 0, width, axis=dim), axis, backward)  27.8 us
    ppermute x5, starting transfers between devices, padded_1(): lax.ppermute(lax.slice_in_dim(block, 0, width, axis=dim), axis, backward)  19.3 us
    all_to_all x1, blocking collectives, gather_partials(): return lax.all_to_all(sent, axes, 0, 0, tiled=True)  18.4 us
    dot_general x3, matrix products, depth_pass(): jnp.dot(flat, jnp.asarray(matrix), precision=lax.Precision.HIGHEST, prefe...  3.34 us
  transfers between devices with their start and end apart: 10, of which 7 were waited for; matrix products, arithmetic and copies ran while one was open for 2% of the time, Pallas kernels for 0%

profile of v13, /device:TPU:8, one launch (start us, length us, event | category | flops | bytes accessed | tf_op | source)
XLA Modules:
  0.0 110.8 jit_solution(3319995703830089097)
XLA Ops:
  0.6 1.2 %fusion.49 = (f32[64,8,128]{2,1,0:T(8,128)S(1)}, f32[64,8,128]{2,1,0:T(8,128)S(1)}) fusion(f32[64,32,128]{2,1,0:T(8,128)} %param.4), kind=kLoop, calls=%fused_computation.102 | loop fusion | bytes 1048576 | tf_op jit(solution)/shard_map/slice | solution.py:26
  1.8 2.0 %collective-permute-start = (f32[64,8,128]{2,1,0:T(8,128)S(1)}, f32[64,8,128]{2,1,0:T(8,128)S(1)}, u32[]{:S(2)}, u32[]{:S(2)}) collective-permute-start(f32[64,8,128]{2,1,0:T(8,128)S(1)} %get-tuple-element.32), channel_id=1, source_target_pairs={{0,1},{1,2},{2,3},{3,4},{4,5},{5,6},{6,7},{7,8},{8,9},{9,10},{10,1... | collective-permute-start | bytes 786440 | tf_op jit(solution)/shard_map/ppermute | solution.py:25
  3.8 6.2 %collective-permute-start.1 = (f32[64,8,128]{2,1,0:T(8,128)S(1)}, f32[64,8,128]{2,1,0:T(8,128)S(1)}, u32[]{:S(2)}, u32[]{:S(2)}) collective-permute-start(f32[64,8,128]{2,1,0:T(8,128)S(1)} %get-tuple-element.33), channel_id=1, source_target_pairs={{1,0},{2,1},{3,2},{4,3},{5,4},{6,5},{7,6},{8,7},{9,8},{10,9},{11,1... | collective-permute-start | bytes 786440 | tf_op jit(solution)/shard_map/ppermute | solution.py:28
  10.0 6.2 %collective-permute-done = f32[64,8,128]{2,1,0:T(8,128)S(1)} collective-permute-done((f32[64,8,128]{2,1,0:T(8,128)S(1)}, f32[64,8,128]{2,1,0:T(8,128)S(1)}, u32[]{:S(2)}, u32[]{:S(2)}) %collective-permute-start) | collective-permute-done | bytes 262176 | tf_op jit(solution)/shard_map/ppermute | solution.py:25
  16.3 0.1 constant_dynamic-update-slice_fusion
  16.4 0.5 fusion.40
  17.0 1.7 %collective-permute-start.3 = (f32[24,32,128]{2,1,0:T(8,128)S(1)}, f32[24,32,128]{2,1,0:T(8,128)S(1)}, u32[]{:S(2)}, u32[]{:S(2)}) collective-permute-start(f32[24,32,128]{2,1,0:T(8,128)S(1)} %get-tuple-element.29), channel_id=1, source_target_pairs={{32,0},{64,32},{96,64},{128,96},{160,128},{192,160},{224,192},{0,2... | collective-permute-start | bytes 1179656 | tf_op jit(solution)/shard_map/ppermute | solution.py:28
  18.8 5.5 %collective-permute-done.2 = f32[24,32,128]{2,1,0:T(8,128)S(1)} collective-permute-done((f32[24,32,128]{2,1,0:T(8,128)S(1)}, f32[24,32,128]{2,1,0:T(8,128)S(1)}, u32[]{:S(2)}, u32[]{:S(2)}) %collective-permute-start.2) | collective-permute-done | bytes 393248 | tf_op jit(solution)/shard_map/ppermute | solution.py:25
  24.2 0.2 pad_maximum_fusion
  24.4 0.4 fusion
  24.8 0.5 copy-done.3
  25.3 1.4 %fusion.50 = f32[3072,128]{1,0:T(8,128)S(1)} fusion(f32[3072,128]{1,0:T(8,128)S(1)} %bitcast.36, f32[128,128]{1,0:T(8,128)S(1)} %copy-done.3), kind=kOutput, calls=%fused_computation.103 | convolution fusion | flops 603979776 | bytes 3211264 | tf_op jit(solution)/shard_map/dot_general | solution.py:54
  26.7 0.3 fusion.36
  27.2 5.3 %collective-permute-start.5 = (f32[64,16,128]{2,1,0:T(8,128)S(1)}, f32[64,16,128]{2,1,0:T(8,128)S(1)}, u32[]{:S(2)}, u32[]{:S(2)}) collective-permute-start(f32[64,16,128]{2,1,0:T(8,128)S(1)} %get-tuple-element.27), channel_id=1, source_target_pairs={{1,0},{2,1},{3,2},{4,3},{5,4},{6,5},{7,6},{8,7},{9,8},{10,9},{11,1... | collective-permute-start | bytes 1572872 | tf_op jit(solution)/shard_map/ppermute | solution.py:28
  32.5 12.0 %collective-permute-done.4 = f32[64,16,128]{2,1,0:T(8,128)S(1)} collective-permute-done((f32[64,16,128]{2,1,0:T(8,128)S(1)}, f32[64,16,128]{2,1,0:T(8,128)S(1)}, u32[]{:S(2)}, u32[]{:S(2)}) %collective-permute-start.4) | collective-permute-done | bytes 524320 | tf_op jit(solution)/shard_map/ppermute | solution.py:25
  44.6 0.3 fusion.21
  44.9 1.0 fusion.51
  45.9 1.1 %collective-permute-start.7 = (f32[32,32,128]{2,1,0:T(8,128)S(1)}, f32[32,32,128]{2,1,0:T(8,128)S(1)}, u32[]{:S(2)}, u32[]{:S(2)}) collective-permute-start(f32[32,32,128]{2,1,0:T(8,128)S(1)} %bitcast.41), channel_id=1, source_target_pairs={{32,0},{64,32},{96,64},{128,96},{160,128},{192,160},{224,192},{0,2... | collective-permute-start | bytes 1572872 | tf_op jit(solution)/shard_map/ppermute | solution.py:28
  47.1 6.7 %collective-permute-done.7 = f32[32,32,128]{2,1,0:T(8,128)S(1)} collective-permute-done((f32[32,32,128]{2,1,0:T(8,128)S(1)}, f32[32,32,128]{2,1,0:T(8,128)S(1)}, u32[]{:S(2)}, u32[]{:S(2)}) %collective-permute-start.7) | collective-permute-done | bytes 524320 | tf_op jit(solution)/shard_map/ppermute | solution.py:28
  53.8 1.9 %collective-permute-done.6 = f32[32,32,128]{2,1,0:T(8,128)S(1)} collective-permute-done((f32[32,32,128]{2,1,0:T(8,128)S(1)}, f32[32,32,128]{2,1,0:T(8,128)S(1)}, u32[]{:S(2)}, u32[]{:S(2)}) %collective-permute-start.6) | collective-permute-done | bytes 524320 | tf_op jit(solution)/shard_map/ppermute | solution.py:25
  55.7 0.4 fusion.13
  56.1 4.9 %collective-permute-start.9 = (f32[64,32,128]{2,1,0:T(8,128)S(1)}, f32[64,32,128]{2,1,0:T(8,128)S(1)}, u32[]{:S(2)}, u32[]{:S(2)}) collective-permute-start(f32[64,32,128]{2,1,0:T(8,128)S(1)} %fusion.13), channel_id=1, source_target_pairs={{1,0},{2,1},{3,2},{4,3},{5,4},{6,5},{7,6},{8,7},{9,8},{10,9},{11,1... | collective-permute-start | bytes 3145736 | tf_op jit(solution)/shard_map/ppermute | solution.py:28
  60.9 1.0 fusion.52
  61.9 0.3 abs_reduce_fusion.2
  62.2 0.3 abs_reduce_fusion.1
  62.6 21.1 %collective-permute-done.9 = f32[64,32,128]{2,1,0:T(8,128)S(1)} collective-permute-done((f32[64,32,128]{2,1,0:T(8,128)S(1)}, f32[64,32,128]{2,1,0:T(8,128)S(1)}, u32[]{:S(2)}, u32[]{:S(2)}) %collective-permute-start.9) | collective-permute-done | bytes 1048608 | tf_op jit(solution)/shard_map/ppermute | solution.py:28
  83.6 5.5 %collective-permute-done.8 = f32[64,32,128]{2,1,0:T(8,128)S(1)} collective-permute-done((f32[64,32,128]{2,1,0:T(8,128)S(1)}, f32[64,32,128]{2,1,0:T(8,128)S(1)}, u32[]{:S(2)}, u32[]{:S(2)}) %collective-permute-start.8) | collective-permute-done | bytes 1048608 | tf_op jit(solution)/shard_map/ppermute | solution.py:25
  89.1 1.5 %fusion.44 = (f32[64,32,128]{2,1,0:T(8,128)S(1)}, f32[64,32,128]{2,1,0:T(8,128)}) fusion(f32[64,32,128]{2,1,0:T(8,128)S(1)} %fusion.21, f32[64,32,128]{2,1,0:T(8,128)S(1)} %collective-permute-done.9, f32[64,32,128]{2,1,0:T(8,128)S(1)} %fusion.13, f32[64,32,128]{2,1,0:T(8,128)S(1)} %collective-permute-done.8), kind=kLoop, calls=%fused_computation.98 | loop fusion | flops 3145728 | bytes 6291456 | tf_op jit(solution)/shard_map/sub | solution.py:118
  90.6 0.3 abs_reduce_fusion
  91.2 18.4 %all_to_all.6 = f32[256,1,12]{2,1,0:T(1,128)S(1)} all-to-all(f32[256,1,12]{2,1,0:T(1,128)S(1)} %broadcast_in_dim.8), channel_id=1, replica_groups=mesh['row'=8,'col'=32] {'row','col'}, dimensions={0} | all-to-all | bytes 24576 | tf_op jit(solution)/shard_map/all_to_all | solution.py:89
  109.7 0.3 reshape.54
  110.2 0.6 pad_maximum_fusion.7
  (29 shorter events, 0.9 us)
Async XLA Ops:
  0.6 15.6 %copy-start = (f32[64,32,128]{2,1,0:T(8,128)S(1)}, f32[64,32,128]{2,1,0:T(8,128)}, u32[]{:S(2)}) copy-start(f32[64,32,128]{2,1,0:T(8,128)} %param.4) | copy-start | bytes 3145732
  1.8 14.4 %collective-permute-start = (f32[64,8,128]{2,1,0:T(8,128)S(1)}, f32[64,8,128]{2,1,0:T(8,128)S(1)}, u32[]{:S(2)}, u32[]{:S(2)}) collective-permute-start(f32[64,8,128]{2,1,0:T(8,128)S(1)} %get-tuple-element.32), channel_id=1, source_target_pairs={{0,1},{1,2},{2,3},{3,4},{4,5},{5,6},{6,7},{7,8},{8,9},{9,10},{10,1... | collective-permute-start | bytes 786440 | tf_op jit(solution)/shard_map/ppermute | solution.py:25
  3.8 12.6 %collective-permute-start.1 = (f32[64,8,128]{2,1,0:T(8,128)S(1)}, f32[64,8,128]{2,1,0:T(8,128)S(1)}, u32[]{:S(2)}, u32[]{:S(2)}) collective-permute-start(f32[64,8,128]{2,1,0:T(8,128)S(1)} %get-tuple-element.33), channel_id=1, source_target_pairs={{1,0},{2,1},{3,2},{4,3},{5,4},{6,5},{7,6},{8,7},{9,8},{10,9},{11,1... | collective-permute-start | bytes 786440 | tf_op jit(solution)/shard_map/ppermute | solution.py:28
  17.0 7.2 %collective-permute-start.2 = (f32[24,32,128]{2,1,0:T(8,128)S(1)}, f32[24,32,128]{2,1,0:T(8,128)S(1)}, u32[]{:S(2)}, u32[]{:S(2)}) collective-permute-start(f32[24,32,128]{2,1,0:T(8,128)S(1)} %get-tuple-element.28), channel_id=1, source_target_pairs={{0,32},{32,64},{64,96},{96,128},{128,160},{160,192},{192,224},{224... | collective-permute-start | bytes 1179656 | tf_op jit(solution)/shard_map/ppermute | solution.py:25
  17.0 7.2 %collective-permute-start.3 = (f32[24,32,128]{2,1,0:T(8,128)S(1)}, f32[24,32,128]{2,1,0:T(8,128)S(1)}, u32[]{:S(2)}, u32[]{:S(2)}) collective-permute-start(f32[24,32,128]{2,1,0:T(8,128)S(1)} %get-tuple-element.29), channel_id=1, source_target_pairs={{32,0},{64,32},{96,64},{128,96},{160,128},{192,160},{224,192},{0,2... | collective-permute-start | bytes 1179656 | tf_op jit(solution)/shard_map/ppermute | solution.py:28
  24.4 0.8 copy-start.3
  27.1 17.5 %collective-permute-start.4 = (f32[64,16,128]{2,1,0:T(8,128)S(1)}, f32[64,16,128]{2,1,0:T(8,128)S(1)}, u32[]{:S(2)}, u32[]{:S(2)}) collective-permute-start(f32[64,16,128]{2,1,0:T(8,128)S(1)} %get-tuple-element.26), channel_id=1, source_target_pairs={{0,1},{1,2},{2,3},{3,4},{4,5},{5,6},{6,7},{7,8},{8,9},{9,10},{10,1... | collective-permute-start | bytes 1572872 | tf_op jit(solution)/shard_map/ppermute | solution.py:25
  27.2 17.7 %copy-start.2 = (f32[128,128]{1,0:T(8,128)S(1)}, f32[128,128]{1,0:T(8,128)}, u32[]{:S(2)}) copy-start(f32[128,128]{1,0:T(8,128)} %constant.27.clone) | copy-start | bytes 196612
  27.2 17.4 %collective-permute-start.5 = (f32[64,16,128]{2,1,0:T(8,128)S(1)}, f32[64,16,128]{2,1,0:T(8,128)S(1)}, u32[]{:S(2)}, u32[]{:S(2)}) collective-permute-start(f32[64,16,128]{2,1,0:T(8,128)S(1)} %get-tuple-element.27), channel_id=1, source_target_pairs={{1,0},{2,1},{3,2},{4,3},{5,4},{6,5},{7,6},{8,7},{9,8},{10,9},{11,1... | collective-permute-start | bytes 1572872 | tf_op jit(solution)/shard_map/ppermute | solution.py:28
  45.9 7.8 %collective-permute-start.7 = (f32[32,32,128]{2,1,0:T(8,128)S(1)}, f32[32,32,128]{2,1,0:T(8,128)S(1)}, u32[]{:S(2)}, u32[]{:S(2)}) collective-permute-start(f32[32,32,128]{2,1,0:T(8,128)S(1)} %bitcast.41), channel_id=1, source_target_pairs={{32,0},{64,32},{96,64},{128,96},{160,128},{192,160},{224,192},{0,2... | collective-permute-start | bytes 1572872 | tf_op jit(solution)/shard_map/ppermute | solution.py:28
  47.1 8.6 %collective-permute-start.6 = (f32[32,32,128]{2,1,0:T(8,128)S(1)}, f32[32,32,128]{2,1,0:T(8,128)S(1)}, u32[]{:S(2)}, u32[]{:S(2)}) collective-permute-start(f32[32,32,128]{2,1,0:T(8,128)S(1)} %bitcast.40), channel_id=1, source_target_pairs={{0,32},{32,64},{64,96},{96,128},{128,160},{160,192},{192,224},{224... | collective-permute-start | bytes 1572872 | tf_op jit(solution)/shard_map/ppermute | solution.py:25
  55.7 5.3 %copy-start.1 = (f32[128,128,1]{1,0,2:T(8,128)S(1)}, f32[128,128,1]{1,0,2:T(8,128)}, u32[]{:S(2)}) copy-start(f32[128,128,1]{1,0,2:T(8,128)} %constant.28) | copy-start | bytes 196612
  56.1 27.6 %collective-permute-start.9 = (f32[64,32,128]{2,1,0:T(8,128)S(1)}, f32[64,32,128]{2,1,0:T(8,128)S(1)}, u32[]{:S(2)}, u32[]{:S(2)}) collective-permute-start(f32[64,32,128]{2,1,0:T(8,128)S(1)} %fusion.13), channel_id=1, source_target_pairs={{1,0},{2,1},{3,2},{4,3},{5,4},{6,5},{7,6},{8,7},{9,8},{10,9},{11,1... | collective-permute-start | bytes 3145736 | tf_op jit(solution)/shard_map/ppermute | solution.py:28
  60.9 28.2 %collective-permute-start.8 = (f32[64,32,128]{2,1,0:T(8,128)S(1)}, f32[64,32,128]{2,1,0:T(8,128)S(1)}, u32[]{:S(2)}, u32[]{:S(2)}) collective-permute-start(f32[64,32,128]{2,1,0:T(8,128)S(1)} %fusion.13), channel_id=1, source_target_pairs={{0,1},{1,2},{2,3},{3,4},{4,5},{5,6},{6,7},{7,8},{8,9},{9,10},{10,1... | collective-permute-start | bytes 3145736 | tf_op jit(solution)/shard_map/ppermute | solution.py:25

commit v14 on v13

--- a/solution.py
+++ b/solution.py
@@ -47,13 +47,27 @@
     return matrix
 
 
+def composed_matrix(planes, spacing_a, spacing_b):
+    source = lax.broadcasted_iota(jnp.int32, (planes, planes), 0)
+    target = lax.broadcasted_iota(jnp.int32, (planes, planes), 1)
+    zero = lax.convert_element_type(lax.axis_index("row"), jnp.float32) * 0.0
+    matrix = jnp.zeros((planes, planes), jnp.float32) + zero
+    for tap_a in range(5):
+        for tap_b in range(5):
+            shift = (tap_a - 2) * spacing_a + (tap_b - 2) * spacing_b
+            weight = jnp.float32(SPLINE_TAPS[tap_a] * SPLINE_TAPS[tap_b])
+            hit = (source - target - shift) % planes == 0
+            matrix = matrix + jnp.where(hit, weight, jnp.float32(0.0))
+    return matrix
+
+
 def depth_pass(values_in, matrix):
     rows = values_in.shape[:-1]
     planes = values_in.shape[-1]
     flat = values_in.reshape(-1, planes)
     summed = jnp.dot(
         flat,
-        jnp.asarray(matrix),
+        matrix if isinstance(matrix, jax.Array) else jnp.asarray(matrix),
         precision=lax.Precision.HIGHEST,
         preferred_element_type=jnp.float32,
     )
@@ -102,7 +116,7 @@
     along_y = holed_pass(padded_y, first, 1, size_y)
     padded_x = padded_1(along_y, "row", 0, 2 * first + extra)
     along_x = holed_pass(padded_x, first, 0, size_x + 2 * extra)
-    ahead_2 = depth_pass(along_x, matrix_1 @ matrix_2)
+    ahead_2 = depth_pass(along_x, composed_matrix(planes, first, second))
     smooth_1 = depth_pass(lax.slice_in_dim(along_x, extra, extra + size_x, axis=0), matrix_1)
     along_x = holed_pass(ahead_2, second, 0, size_x)
     padded_y = padded_1(along_x, "col", 1, 2 * second)

time: 113 us -> 114 us (level)
  no operation moved by 1% of the time
where the time goes in v14:
time: 114 us; the launch traced here: 112 us
  waiting for transfers between devices  59.3 us (52%)
  starting transfers between devices  21.1 us (19%)
  blocking collectives  18.7 us (16%)
  other arithmetic  5.34 us (5%)
  matrix products  3.8 us (3%)
  local copies, waits for them, and re-layouts  2.8 us (2%)
    ppermute x5, waiting for transfers between devices, padded_1(): lax.ppermute(lax.slice_in_dim(block, block.shape[dim] - width, None, axis...  31.6 us
    ppermute x5, waiting for transfers between devices, padded_1(): lax.ppermute(lax.slice_in_dim(block, 0, width, axis=dim), axis, backward)  27.7 us
    ppermute x5, starting transfers between devices, padded_1(): lax.ppermute(lax.slice_in_dim(block, 0, width, axis=dim), axis, backward)  19 us
    all_to_all x1, blocking collectives, gather_partials(): return lax.all_to_all(sent, axes, 0, 0, tiled=True)  18.7 us
    dot_general x3, matrix products, depth_pass(): jnp.dot(flat, matrix if isinstance(matrix, jax.Array) else jnp.asarray(ma...  3.8 us
  transfers between devices with their start and end apart: 10, of which 7 were waited for; matrix products, arithmetic and copies ran while one was open for 2% of the time, Pallas kernels for 0%

profile of v14, /device:TPU:8, one launch (start us, length us, event | category | flops | bytes accessed | tf_op | source)
XLA Modules:
  0.0 111.9 jit_solution(15302699229901116983)
XLA Ops:
  0.6 1.2 %fusion.222 = (f32[64,8,128]{2,1,0:T(8,128)S(1)}, f32[64,8,128]{2,1,0:T(8,128)S(1)}) fusion(f32[64,32,128]{2,1,0:T(8,128)} %param.3), kind=kLoop, calls=%fused_computation.301 | loop fusion | bytes 1048576 | tf_op jit(solution)/shard_map/slice | solution.py:26
  1.8 2.0 %collective-permute-start = (f32[64,8,128]{2,1,0:T(8,128)S(1)}, f32[64,8,128]{2,1,0:T(8,128)S(1)}, u32[]{:S(2)}, u32[]{:S(2)}) collective-permute-start(f32[64,8,128]{2,1,0:T(8,128)S(1)} %get-tuple-element.32), channel_id=1, source_target_pairs={{0,1},{1,2},{2,3},{3,4},{4,5},{5,6},{6,7},{7,8},{8,9},{9,10},{10,1... | collective-permute-start | bytes 786440 | tf_op jit(solution)/shard_map/ppermute | solution.py:25
  3.8 6.2 %collective-permute-start.1 = (f32[64,8,128]{2,1,0:T(8,128)S(1)}, f32[64,8,128]{2,1,0:T(8,128)S(1)}, u32[]{:S(2)}, u32[]{:S(2)}) collective-permute-start(f32[64,8,128]{2,1,0:T(8,128)S(1)} %get-tuple-element.33), channel_id=1, source_target_pairs={{1,0},{2,1},{3,2},{4,3},{5,4},{6,5},{7,6},{8,7},{9,8},{10,9},{11,1... | collective-permute-start | bytes 786440 | tf_op jit(solution)/shard_map/ppermute | solution.py:28
  10.0 6.2 %collective-permute-done = f32[64,8,128]{2,1,0:T(8,128)S(1)} collective-permute-done((f32[64,8,128]{2,1,0:T(8,128)S(1)}, f32[64,8,128]{2,1,0:T(8,128)S(1)}, u32[]{:S(2)}, u32[]{:S(2)}) %collective-permute-start) | collective-permute-done | bytes 262176 | tf_op jit(solution)/shard_map/ppermute | solution.py:25
  16.3 0.1 constant_dynamic-update-slice_fusion
  16.4 0.5 fusion.40
  17.0 0.8 fusion.221
  17.8 1.7 %collective-permute-start.3 = (f32[24,32,128]{2,1,0:T(8,128)S(1)}, f32[24,32,128]{2,1,0:T(8,128)S(1)}, u32[]{:S(2)}, u32[]{:S(2)}) collective-permute-start(f32[24,32,128]{2,1,0:T(8,128)S(1)} %get-tuple-element.29), channel_id=1, source_target_pairs={{32,0},{64,32},{96,64},{128,96},{160,128},{192,160},{224,192},{0,2... | collective-permute-start | bytes 1179656 | tf_op jit(solution)/shard_map/ppermute | solution.py:28
  19.5 5.7 %collective-permute-done.2 = f32[24,32,128]{2,1,0:T(8,128)S(1)} collective-permute-done((f32[24,32,128]{2,1,0:T(8,128)}, f32[24,32,128]{2,1,0:T(8,128)S(1)}, u32[]{:S(2)}, u32[]{:S(2)}) %collective-permute-start.2) | collective-permute-done | bytes 393248 | tf_op jit(solution)/shard_map/ppermute | solution.py:25
  25.2 0.1 pad_maximum_fusion
  25.3 0.4 fusion
  25.7 1.9 %fusion.64 = f32[3072,128]{1,0:T(8,128)S(1)} fusion(f32[3072,128]{1,0:T(8,128)S(1)} %bitcast.38, f32[]{:T(128)S(6)} %mul.141), kind=kOutput, calls=%fused_computation.146 | convolution fusion | flops 607551488 | bytes 3145732 | tf_op jit(solution)/shard_map/dot_general | solution.py:68
  27.6 0.3 fusion.36
  28.1 5.3 %collective-permute-start.5 = (f32[64,16,128]{2,1,0:T(8,128)S(1)}, f32[64,16,128]{2,1,0:T(8,128)S(1)}, u32[]{:S(2)}, u32[]{:S(2)}) collective-permute-start(f32[64,16,128]{2,1,0:T(8,128)S(1)} %get-tuple-element.27), channel_id=1, source_target_pairs={{1,0},{2,1},{3,2},{4,3},{5,4},{6,5},{7,6},{8,7},{9,8},{10,9},{11,1... | collective-permute-start | bytes 1572872 | tf_op jit(solution)/shard_map/ppermute | solution.py:28
  33.4 12.3 %collective-permute-done.4 = f32[64,16,128]{2,1,0:T(8,128)S(1)} collective-permute-done((f32[64,16,128]{2,1,0:T(8,128)S(1)}, f32[64,16,128]{2,1,0:T(8,128)S(1)}, u32[]{:S(2)}, u32[]{:S(2)}) %collective-permute-start.4) | collective-permute-done | bytes 524320 | tf_op jit(solution)/shard_map/ppermute | solution.py:25
  45.7 0.3 fusion.21
  46.0 1.0 fusion.223
  47.1 0.5 collective-permute-start.7
  47.6 6.7 %collective-permute-done.7 = f32[32,32,128]{2,1,0:T(8,128)S(1)} collective-permute-done((f32[32,32,128]{2,1,0:T(8,128)S(1)}, f32[32,32,128]{2,1,0:T(8,128)S(1)}, u32[]{:S(2)}, u32[]{:S(2)}) %collective-permute-start.7) | collective-permute-done | bytes 524320 | tf_op jit(solution)/shard_map/ppermute | solution.py:28
  54.2 1.9 %collective-permute-done.6 = f32[32,32,128]{2,1,0:T(8,128)S(1)} collective-permute-done((f32[32,32,128]{2,1,0:T(8,128)S(1)}, f32[32,32,128]{2,1,0:T(8,128)S(1)}, u32[]{:S(2)}, u32[]{:S(2)}) %collective-permute-start.6) | collective-permute-done | bytes 524320 | tf_op jit(solution)/shard_map/ppermute | solution.py:25
  56.2 0.4 fusion.13
  56.5 5.2 %collective-permute-start.9 = (f32[64,32,128]{2,1,0:T(8,128)S(1)}, f32[64,32,128]{2,1,0:T(8,128)S(1)}, u32[]{:S(2)}, u32[]{:S(2)}) collective-permute-start(f32[64,32,128]{2,1,0:T(8,128)S(1)} %fusion.13), channel_id=1, source_target_pairs={{1,0},{2,1},{3,2},{4,3},{5,4},{6,5},{7,6},{8,7},{9,8},{10,9},{11,1... | collective-permute-start | bytes 3145736 | tf_op jit(solution)/shard_map/ppermute | solution.py:28
  61.8 1.0 fusion.224
  62.8 0.3 abs_reduce_fusion.2
  63.1 0.3 abs_reduce_fusion.1
  63.4 21.1 %collective-permute-done.9 = f32[64,32,128]{2,1,0:T(8,128)S(1)} collective-permute-done((f32[64,32,128]{2,1,0:T(8,128)S(1)}, f32[64,32,128]{2,1,0:T(8,128)S(1)}, u32[]{:S(2)}, u32[]{:S(2)}) %collective-permute-start.9) | collective-permute-done | bytes 1048608 | tf_op jit(solution)/shard_map/ppermute | solution.py:28
  84.5 5.5 %collective-permute-done.8 = f32[64,32,128]{2,1,0:T(8,128)S(1)} collective-permute-done((f32[64,32,128]{2,1,0:T(8,128)S(1)}, f32[64,32,128]{2,1,0:T(8,128)S(1)}, u32[]{:S(2)}, u32[]{:S(2)}) %collective-permute-start.8) | collective-permute-done | bytes 1048608 | tf_op jit(solution)/shard_map/ppermute | solution.py:25
  90.0 1.5 %fusion.217 = (f32[64,32,128]{2,1,0:T(8,128)S(1)}, f32[64,32,128]{2,1,0:T(8,128)}) fusion(f32[64,32,128]{2,1,0:T(8,128)S(1)} %fusion.21, f32[64,32,128]{2,1,0:T(8,128)S(1)} %collective-permute-done.9, f32[64,32,128]{2,1,0:T(8,128)S(1)} %fusion.13, f32[64,32,128]{2,1,0:T(8,128)S(1)} %collective-permute-done.8), kind=kLoop, calls=%fused_computation.297 | loop fusion | flops 3145728 | bytes 6291456 | tf_op jit(solution)/shard_map/sub | solution.py:132
  91.5 0.3 abs_reduce_fusion
  92.0 18.7 %all_to_all.6 = f32[256,1,12]{2,1,0:T(1,128)S(1)} all-to-all(f32[256,1,12]{2,1,0:T(1,128)S(1)} %broadcast_in_dim.81), channel_id=1, replica_groups=mesh['row'=8,'col'=32] {'row','col'}, dimensions={0} | all-to-all | bytes 24576 | tf_op jit(solution)/shard_map/all_to_all | solution.py:103
  110.8 0.3 reshape.54
  111.3 0.6 pad_maximum_fusion.7
  (27 shorter events, 0.8 us)
Async XLA Ops:
  0.6 15.6 %copy-start = (f32[64,32,128]{2,1,0:T(8,128)S(1)}, f32[64,32,128]{2,1,0:T(8,128)}, u32[]{:S(2)}) copy-start(f32[64,32,128]{2,1,0:T(8,128)} %param.3) | copy-start | bytes 3145732
  1.8 14.4 %collective-permute-start = (f32[64,8,128]{2,1,0:T(8,128)S(1)}, f32[64,8,128]{2,1,0:T(8,128)S(1)}, u32[]{:S(2)}, u32[]{:S(2)}) collective-permute-start(f32[64,8,128]{2,1,0:T(8,128)S(1)} %get-tuple-element.32), channel_id=1, source_target_pairs={{0,1},{1,2},{2,3},{3,4},{4,5},{5,6},{6,7},{7,8},{8,9},{9,10},{10,1... | collective-permute-start | bytes 786440 | tf_op jit(solution)/shard_map/ppermute | solution.py:25
  3.8 12.6 %collective-permute-start.1 = (f32[64,8,128]{2,1,0:T(8,128)S(1)}, f32[64,8,128]{2,1,0:T(8,128)S(1)}, u32[]{:S(2)}, u32[]{:S(2)}) collective-permute-start(f32[64,8,128]{2,1,0:T(8,128)S(1)} %get-tuple-element.33), channel_id=1, source_target_pairs={{1,0},{2,1},{3,2},{4,3},{5,4},{6,5},{7,6},{8,7},{9,8},{10,9},{11,1... | collective-permute-start | bytes 786440 | tf_op jit(solution)/shard_map/ppermute | solution.py:28
  17.8 7.4 %collective-permute-start.2 = (f32[24,32,128]{2,1,0:T(8,128)}, f32[24,32,128]{2,1,0:T(8,128)S(1)}, u32[]{:S(2)}, u32[]{:S(2)}) collective-permute-start(f32[24,32,128]{2,1,0:T(8,128)} %get-tuple-element.28), channel_id=1, source_target_pairs={{0,32},{32,64},{64,96},{96,128},{128,160},{160,192},{192,224},{224... | collective-permute-start | bytes 1179656 | tf_op jit(solution)/shard_map/ppermute | solution.py:25
  17.8 7.4 %collective-permute-start.3 = (f32[24,32,128]{2,1,0:T(8,128)S(1)}, f32[24,32,128]{2,1,0:T(8,128)S(1)}, u32[]{:S(2)}, u32[]{:S(2)}) collective-permute-start(f32[24,32,128]{2,1,0:T(8,128)S(1)} %get-tuple-element.29), channel_id=1, source_target_pairs={{32,0},{64,32},{96,64},{128,96},{160,128},{192,160},{224,192},{0,2... | collective-permute-start | bytes 1179656 | tf_op jit(solution)/shard_map/ppermute | solution.py:28
  28.0 17.7 %collective-permute-start.4 = (f32[64,16,128]{2,1,0:T(8,128)S(1)}, f32[64,16,128]{2,1,0:T(8,128)S(1)}, u32[]{:S(2)}, u32[]{:S(2)}) collective-permute-start(f32[64,16,128]{2,1,0:T(8,128)S(1)} %get-tuple-element.26), channel_id=1, source_target_pairs={{0,1},{1,2},{2,3},{3,4},{4,5},{5,6},{6,7},{7,8},{8,9},{9,10},{10,1... | collective-permute-start | bytes 1572872 | tf_op jit(solution)/shard_map/ppermute | solution.py:25
  28.1 17.9 %copy-start.2 = (f32[128,128]{1,0:T(8,128)S(1)}, f32[128,128]{1,0:T(8,128)}, u32[]{:S(2)}) copy-start(f32[128,128]{1,0:T(8,128)} %constant.189.clone) | copy-start | bytes 196612
  28.1 17.6 %collective-permute-start.5 = (f32[64,16,128]{2,1,0:T(8,128)S(1)}, f32[64,16,128]{2,1,0:T(8,128)S(1)}, u32[]{:S(2)}, u32[]{:S(2)}) collective-permute-start(f32[64,16,128]{2,1,0:T(8,128)S(1)} %get-tuple-element.27), channel_id=1, source_target_pairs={{1,0},{2,1},{3,2},{4,3},{5,4},{6,5},{7,6},{8,7},{9,8},{10,9},{11,1... | collective-permute-start | bytes 1572872 | tf_op jit(solution)/shard_map/ppermute | solution.py:28
  47.1 7.2 %collective-permute-start.7 = (f32[32,32,128]{2,1,0:T(8,128)S(1)}, f32[32,32,128]{2,1,0:T(8,128)S(1)}, u32[]{:S(2)}, u32[]{:S(2)}) collective-permute-start(f32[32,32,128]{2,1,0:T(8,128)S(1)} %bitcast.40), channel_id=1, source_target_pairs={{32,0},{64,32},{96,64},{128,96},{160,128},{192,160},{224,192},{0,2... | collective-permute-start | bytes 1572872 | tf_op jit(solution)/shard_map/ppermute | solution.py:28
  47.5 8.6 %collective-permute-start.6 = (f32[32,32,128]{2,1,0:T(8,128)S(1)}, f32[32,32,128]{2,1,0:T(8,128)S(1)}, u32[]{:S(2)}, u32[]{:S(2)}) collective-permute-start(f32[32,32,128]{2,1,0:T(8,128)S(1)} %bitcast.39), channel_id=1, source_target_pairs={{0,32},{32,64},{64,96},{96,128},{128,160},{160,192},{192,224},{224... | collective-permute-start | bytes 1572872 | tf_op jit(solution)/shard_map/ppermute | solution.py:25
  56.2 5.6 %copy-start.1 = (f32[128,128,1]{1,0,2:T(8,128)S(1)}, f32[128,128,1]{1,0,2:T(8,128)}, u32[]{:S(2)}) copy-start(f32[128,128,1]{1,0,2:T(8,128)} %constant.190) | copy-start | bytes 196612
  56.5 27.9 %collective-permute-start.9 = (f32[64,32,128]{2,1,0:T(8,128)S(1)}, f32[64,32,128]{2,1,0:T(8,128)S(1)}, u32[]{:S(2)}, u32[]{:S(2)}) collective-permute-start(f32[64,32,128]{2,1,0:T(8,128)S(1)} %fusion.13), channel_id=1, source_target_pairs={{1,0},{2,1},{3,2},{4,3},{5,4},{6,5},{7,6},{8,7},{9,8},{10,9},{11,1... | collective-permute-start | bytes 3145736 | tf_op jit(solution)/shard_map/ppermute | solution.py:28
  61.8 28.2 %collective-permute-start.8 = (f32[64,32,128]{2,1,0:T(8,128)S(1)}, f32[64,32,128]{2,1,0:T(8,128)S(1)}, u32[]{:S(2)}, u32[]{:S(2)}) collective-permute-start(f32[64,32,128]{2,1,0:T(8,128)S(1)} %fusion.13), channel_id=1, source_target_pairs={{0,1},{1,2},{2,3},{3,4},{4,5},{5,6},{6,7},{7,8},{8,9},{9,10},{10,1... | collective-permute-start | bytes 3145736 | tf_op jit(solution)/shard_map/ppermute | solution.py:25

commit v15 on v13

--- a/solution.py
+++ b/solution.py
@@ -105,9 +105,14 @@
     ahead_2 = depth_pass(along_x, matrix_1 @ matrix_2)
     smooth_1 = depth_pass(lax.slice_in_dim(along_x, extra, extra + size_x, axis=0), matrix_1)
     along_x = holed_pass(ahead_2, second, 0, size_x)
-    padded_y = padded_1(along_x, "col", 1, 2 * second)
-    smooth_2 = holed_pass(padded_y, second, 1, size_y)
-    ahead_3 = depth_pass(smooth_2, matrix_3)
+    width = 2 * second
+    assert width <= size_y
+    forward, backward = ring_pairs(lax.axis_size("col"))
+    low = lax.ppermute(along_x[:, size_y - width :], "col", forward)
+    high = lax.ppermute(along_x[:, :width], "col", backward)
+    smooth_2 = holed_pass(jnp.concatenate([low, along_x, high], axis=1), second, 1, size_y)
+    ahead_pieces = [depth_pass(piece, matrix_3) for piece in (low, along_x, high)]
+    ahead_3 = holed_pass(jnp.concatenate(ahead_pieces, axis=1), second, 1, size_y)
     padded_x = padded_1(ahead_3, "row", 0, 2 * third)
     along_x = holed_pass(padded_x, third, 0, size_x)
     padded_y = padded_1(along_x, "col", 1, 2 * third)

time: 113 us -> 114 us (level)
  waiting for transfers between devices: 58.9 us -> 57.2 us
    ppermute x0 -> x2, waiting for transfers between devices: none -> 11.1 us  [the longest x1 11.1 us: per_device(): low = lax.ppermute(along_x[:, size_y - width:], 'col', forward)]
    ppermute x5 -> x4, waiting for transfers between devices: 31.1 us -> 24.6 us  [padded_1(): lax.ppermute(lax.slice_in_dim(block, block.shape[dim] - width, None, axis...]
    ppermute x5 -> x4, waiting for transfers between devices: 27.8 us -> 21.6 us  [padded_1(): lax.ppermute(lax.slice_in_dim(block, 0, width, axis=dim), axis, backward)]
    ppermute x0 -> x2, starting transfers between devices: none -> 5.42 us  [the longest x1 5.33 us: per_device(): high = lax.ppermute(along_x[:, :width], 'col', backward)]
    ppermute x5 -> x4, starting transfers between devices: 19.3 us -> 14.3 us  [padded_1(): lax.ppermute(lax.slice_in_dim(block, 0, width, axis=dim), axis, backward)]
    dot_general x3 -> x5, matrix products: 3.34 us -> 4.45 us  [depth_pass(): jnp.dot(flat, jnp.asarray(matrix), precision=lax.Precision.HIGHEST, prefe...]
    ppermute x5 -> x4, starting transfers between devices: 2.1 us -> 2.58 us  [padded_1(): lax.ppermute(lax.slice_in_dim(block, block.shape[dim] - width, None, axis...]
  transfers between devices with their start and end apart: 10 -> 10, of which waited for: 7 -> 6; matrix products, arithmetic and copies ran while one was open for 2% -> 2% of each run, Pallas kernels for 0% -> 0%
where the time goes in v15:
time: 114 us; the launch traced here: 112 us
  waiting for transfers between devices  57.2 us (50%)
  starting transfers between devices  22.3 us (20%)
  blocking collectives  19 us (17%)
  other arithmetic  5.89 us (5%)
  matrix products  4.45 us (4%)
  local copies, waits for them, and re-layouts  2.51 us (2%)
    ppermute x4, waiting for transfers between devices, padded_1(): lax.ppermute(lax.slice_in_dim(block, block.shape[dim] - width, None, axis...  24.6 us
    ppermute x4, waiting for transfers between devices, padded_1(): lax.ppermute(lax.slice_in_dim(block, 0, width, axis=dim), axis, backward)  21.6 us
    all_to_all x1, blocking collectives, gather_partials(): return lax.all_to_all(sent, axes, 0, 0, tiled=True)  19 us
    ppermute x4, starting transfers between devices, padded_1(): lax.ppermute(lax.slice_in_dim(block, 0, width, axis=dim), axis, backward)  14.3 us
    ppermute x1, waiting for transfers between devices, per_device(): low = lax.ppermute(along_x[:, size_y - width:], 'col', forward)  11.1 us
    ppermute x1, starting transfers between devices, per_device(): high = lax.ppermute(along_x[:, :width], 'col', backward)  5.33 us
    dot_general x5, matrix products, depth_pass(): jnp.dot(flat, jnp.asarray(matrix), precision=lax.Precision.HIGHEST, prefe...  4.45 us
    ppermute x4, starting transfers between devices, padded_1(): lax.ppermute(lax.slice_in_dim(block, block.shape[dim] - width, None, axis...  2.58 us
  transfers between devices with their start and end apart: 10, of which 6 were waited for; matrix products, arithmetic and copies ran while one was open for 2% of the time, Pallas kernels for 0%

profile of v15, /device:TPU:8, one launch (start us, length us, event | category | flops | bytes accessed | tf_op | source)
XLA Modules:
  0.0 112.2 jit_solution(12127918347362533496)
XLA Ops:
  0.6 1.2 %fusion.60 = (f32[64,8,128]{2,1,0:T(8,128)S(1)}, f32[64,8,128]{2,1,0:T(8,128)S(1)}) fusion(f32[64,32,128]{2,1,0:T(8,128)} %param.4), kind=kLoop, calls=%fused_computation.118 | loop fusion | bytes 1048576 | tf_op jit(solution)/shard_map/slice | solution.py:26
  1.8 2.0 %collective-permute-start = (f32[64,8,128]{2,1,0:T(8,128)S(1)}, f32[64,8,128]{2,1,0:T(8,128)S(1)}, u32[]{:S(2)}, u32[]{:S(2)}) collective-permute-start(f32[64,8,128]{2,1,0:T(8,128)S(1)} %get-tuple-element.33), channel_id=1, source_target_pairs={{0,1},{1,2},{2,3},{3,4},{4,5},{5,6},{6,7},{7,8},{8,9},{9,10},{10,1... | collective-permute-start | bytes 786440 | tf_op jit(solution)/shard_map/ppermute | solution.py:25
  3.8 6.2 %collective-permute-start.1 = (f32[64,8,128]{2,1,0:T(8,128)S(1)}, f32[64,8,128]{2,1,0:T(8,128)S(1)}, u32[]{:S(2)}, u32[]{:S(2)}) collective-permute-start(f32[64,8,128]{2,1,0:T(8,128)S(1)} %get-tuple-element.34), channel_id=1, source_target_pairs={{1,0},{2,1},{3,2},{4,3},{5,4},{6,5},{7,6},{8,7},{9,8},{10,9},{11,1... | collective-permute-start | bytes 786440 | tf_op jit(solution)/shard_map/ppermute | solution.py:28
  10.0 6.2 %collective-permute-done = f32[64,8,128]{2,1,0:T(8,128)S(1)} collective-permute-done((f32[64,8,128]{2,1,0:T(8,128)S(1)}, f32[64,8,128]{2,1,0:T(8,128)S(1)}, u32[]{:S(2)}, u32[]{:S(2)}) %collective-permute-start) | collective-permute-done | bytes 262176 | tf_op jit(solution)/shard_map/ppermute | solution.py:25
  16.4 0.5 fusion.50
  17.0 1.7 %collective-permute-start.3 = (f32[24,32,128]{2,1,0:T(8,128)S(1)}, f32[24,32,128]{2,1,0:T(8,128)S(1)}, u32[]{:S(2)}, u32[]{:S(2)}) collective-permute-start(f32[24,32,128]{2,1,0:T(8,128)S(1)} %get-tuple-element.30), channel_id=1, source_target_pairs={{32,0},{64,32},{96,64},{128,96},{160,128},{192,160},{224,192},{0,2... | collective-permute-start | bytes 1179656 | tf_op jit(solution)/shard_map/ppermute | solution.py:28
  18.8 5.5 %collective-permute-done.2 = f32[24,32,128]{2,1,0:T(8,128)S(1)} collective-permute-done((f32[24,32,128]{2,1,0:T(8,128)S(1)}, f32[24,32,128]{2,1,0:T(8,128)S(1)}, u32[]{:S(2)}, u32[]{:S(2)}) %collective-permute-start.2) | collective-permute-done | bytes 393248 | tf_op jit(solution)/shard_map/ppermute | solution.py:25
  24.4 0.4 fusion
  24.8 0.5 copy-done.3
  25.3 1.4 %fusion.61 = f32[3072,128]{1,0:T(8,128)S(1)} fusion(f32[3072,128]{1,0:T(8,128)S(1)} %bitcast.39, f32[128,128]{1,0:T(8,128)S(1)} %copy-done.3), kind=kOutput, calls=%fused_computation.119 | convolution fusion | flops 603979776 | bytes 3211264 | tf_op jit(solution)/shard_map/dot_general | solution.py:54
  26.7 0.3 fusion.46
  27.2 5.3 %collective-permute-start.5 = (f32[64,16,128]{2,1,0:T(8,128)S(1)}, f32[64,16,128]{2,1,0:T(8,128)S(1)}, u32[]{:S(2)}, u32[]{:S(2)}) collective-permute-start(f32[64,16,128]{2,1,0:T(8,128)S(1)} %get-tuple-element.28), channel_id=1, source_target_pairs={{1,0},{2,1},{3,2},{4,3},{5,4},{6,5},{7,6},{8,7},{9,8},{10,9},{11,1... | collective-permute-start | bytes 1572872 | tf_op jit(solution)/shard_map/ppermute | solution.py:112
  32.5 1.0 fusion.63
  33.5 11.1 %collective-permute-done.4 = f32[64,16,128]{2,1,0:T(8,128)S(1)} collective-permute-done((f32[64,16,128]{2,1,0:T(8,128)S(1)}, f32[64,16,128]{2,1,0:T(8,128)S(1)}, u32[]{:S(2)}, u32[]{:S(2)}) %collective-permute-start.4) | collective-permute-done | bytes 524320 | tf_op jit(solution)/shard_map/ppermute | solution.py:111
  44.6 0.6 fusion.62
  45.2 0.6 fusion.64
  45.7 0.3 fusion.29
  46.1 0.6 collective-permute-start.6
  46.7 1.2 %collective-permute-start.7 = (f32[32,32,128]{2,1,0:T(8,128)S(1)}, f32[32,32,128]{2,1,0:T(8,128)S(1)}, u32[]{:S(2)}, u32[]{:S(2)}) collective-permute-start(f32[32,32,128]{2,1,0:T(8,128)S(1)} %get-tuple-element.26), channel_id=1, source_target_pairs={{32,0},{64,32},{96,64},{128,96},{160,128},{192,160},{224,192},{0,2... | collective-permute-start | bytes 1572872 | tf_op jit(solution)/shard_map/ppermute | solution.py:28
  47.9 6.9 %collective-permute-done.6 = f32[32,32,128]{2,1,0:T(8,128)S(1)} collective-permute-done((f32[32,32,128]{2,1,0:T(8,128)S(1)}, f32[32,32,128]{2,1,0:T(8,128)S(1)}, u32[]{:S(2)}, u32[]{:S(2)}) %collective-permute-start.6) | collective-permute-done | bytes 524320 | tf_op jit(solution)/shard_map/ppermute | solution.py:25
  54.7 0.4 fusion.21
  55.1 5.1 %collective-permute-start.9 = (f32[64,32,128]{2,1,0:T(8,128)S(1)}, f32[64,32,128]{2,1,0:T(8,128)S(1)}, u32[]{:S(2)}, u32[]{:S(2)}) collective-permute-start(f32[64,32,128]{2,1,0:T(8,128)S(1)} %fusion.21), channel_id=1, source_target_pairs={{1,0},{2,1},{3,2},{4,3},{5,4},{6,5},{7,6},{8,7},{9,8},{10,9},{11,1... | collective-permute-start | bytes 3145736 | tf_op jit(solution)/shard_map/ppermute | solution.py:28
  60.3 1.0 fusion.65
  61.2 21.5 %collective-permute-done.9 = f32[64,32,128]{2,1,0:T(8,128)S(1)} collective-permute-done((f32[64,32,128]{2,1,0:T(8,128)S(1)}, f32[64,32,128]{2,1,0:T(8,128)S(1)}, u32[]{:S(2)}, u32[]{:S(2)}) %collective-permute-start.9) | collective-permute-done | bytes 1048608 | tf_op jit(solution)/shard_map/ppermute | solution.py:28
  82.8 6.1 %collective-permute-done.8 = f32[64,32,128]{2,1,0:T(8,128)S(1)} collective-permute-done((f32[64,32,128]{2,1,0:T(8,128)S(1)}, f32[64,32,128]{2,1,0:T(8,128)S(1)}, u32[]{:S(2)}, u32[]{:S(2)}) %collective-permute-start.8) | collective-permute-done | bytes 1048608 | tf_op jit(solution)/shard_map/ppermute | solution.py:25
  88.9 2.0 %fusion.54 = (f32[64,32,128]{2,1,0:T(8,128)S(1)}, f32[64,32,128]{2,1,0:T(8,128)S(1)}, f32[64,32,128]{2,1,0:T(8,128)}) fusion(f32[64,16,128]{2,1,0:T(8,128)S(1)} %collective-permute-done.5, f32[64,32,128]{2,1,0:T(8,128)S(1)} %bitcast.38, f32[64,16,128]{2,1,0:T(8,128)S(1)} %collective-permute-done.4, f32[64,32,128]{2,1,0:T(8,128)S(1)} %collective-permute-done.9, ...), kind=kLoop, calls=%fused_computation.114 | loop fusion | flops 6553600 | bytes 8388608 | tf_op jit(solution)/shard_map/sub | solution.py:123
  90.9 0.3 abs_reduce_fusion
  91.2 0.3 abs_reduce_fusion.2
  91.5 0.3 abs_reduce_fusion.1
  92.1 19.0 %all_to_all.6 = f32[256,1,12]{2,1,0:T(1,128)S(1)} all-to-all(f32[256,1,12]{2,1,0:T(1,128)S(1)} %broadcast_in_dim.8), channel_id=1, replica_groups=mesh['row'=8,'col'=32] {'row','col'}, dimensions={0} | all-to-all | bytes 24576 | tf_op jit(solution)/shard_map/all_to_all | solution.py:89
  111.1 0.3 reshape.55
  111.6 0.6 pad_maximum_fusion.9
  (31 shorter events, 1.2 us)
Async XLA Ops:
  0.6 15.6 %copy-start = (f32[64,32,128]{2,1,0:T(8,128)S(1)}, f32[64,32,128]{2,1,0:T(8,128)}, u32[]{:S(2)}) copy-start(f32[64,32,128]{2,1,0:T(8,128)} %param.4) | copy-start | bytes 3145732
  1.8 14.4 %collective-permute-start = (f32[64,8,128]{2,1,0:T(8,128)S(1)}, f32[64,8,128]{2,1,0:T(8,128)S(1)}, u32[]{:S(2)}, u32[]{:S(2)}) collective-permute-start(f32[64,8,128]{2,1,0:T(8,128)S(1)} %get-tuple-element.33), channel_id=1, source_target_pairs={{0,1},{1,2},{2,3},{3,4},{4,5},{5,6},{6,7},{7,8},{8,9},{9,10},{10,1... | collective-permute-start | bytes 786440 | tf_op jit(solution)/shard_map/ppermute | solution.py:25
  3.8 12.6 %collective-permute-start.1 = (f32[64,8,128]{2,1,0:T(8,128)S(1)}, f32[64,8,128]{2,1,0:T(8,128)S(1)}, u32[]{:S(2)}, u32[]{:S(2)}) collective-permute-start(f32[64,8,128]{2,1,0:T(8,128)S(1)} %get-tuple-element.34), channel_id=1, source_target_pairs={{1,0},{2,1},{3,2},{4,3},{5,4},{6,5},{7,6},{8,7},{9,8},{10,9},{11,1... | collective-permute-start | bytes 786440 | tf_op jit(solution)/shard_map/ppermute | solution.py:28
  17.0 7.2 %collective-permute-start.2 = (f32[24,32,128]{2,1,0:T(8,128)S(1)}, f32[24,32,128]{2,1,0:T(8,128)S(1)}, u32[]{:S(2)}, u32[]{:S(2)}) collective-permute-start(f32[24,32,128]{2,1,0:T(8,128)S(1)} %get-tuple-element.29), channel_id=1, source_target_pairs={{0,32},{32,64},{64,96},{96,128},{128,160},{160,192},{192,224},{224... | collective-permute-start | bytes 1179656 | tf_op jit(solution)/shard_map/ppermute | solution.py:25
  17.0 7.2 %collective-permute-start.3 = (f32[24,32,128]{2,1,0:T(8,128)S(1)}, f32[24,32,128]{2,1,0:T(8,128)S(1)}, u32[]{:S(2)}, u32[]{:S(2)}) collective-permute-start(f32[24,32,128]{2,1,0:T(8,128)S(1)} %get-tuple-element.30), channel_id=1, source_target_pairs={{32,0},{64,32},{96,64},{128,96},{160,128},{192,160},{224,192},{0,2... | collective-permute-start | bytes 1179656 | tf_op jit(solution)/shard_map/ppermute | solution.py:28
  24.4 0.8 copy-start.3
  27.0 5.5 %copy-start.1 = (f32[128,128,1]{1,0,2:T(8,128)S(1)}, f32[128,128,1]{1,0,2:T(8,128)}, u32[]{:S(2)}) copy-start(f32[128,128,1]{1,0,2:T(8,128)} %constant.28) | copy-start | bytes 196612
  27.1 17.5 %collective-permute-start.4 = (f32[64,16,128]{2,1,0:T(8,128)S(1)}, f32[64,16,128]{2,1,0:T(8,128)S(1)}, u32[]{:S(2)}, u32[]{:S(2)}) collective-permute-start(f32[64,16,128]{2,1,0:T(8,128)S(1)} %get-tuple-element.27), channel_id=1, source_target_pairs={{0,1},{1,2},{2,3},{3,4},{4,5},{5,6},{6,7},{7,8},{8,9},{9,10},{10,1... | collective-permute-start | bytes 1572872 | tf_op jit(solution)/shard_map/ppermute | solution.py:111
  27.2 18.0 %collective-permute-start.5 = (f32[64,16,128]{2,1,0:T(8,128)S(1)}, f32[64,16,128]{2,1,0:T(8,128)S(1)}, u32[]{:S(2)}, u32[]{:S(2)}) collective-permute-start(f32[64,16,128]{2,1,0:T(8,128)S(1)} %get-tuple-element.28), channel_id=1, source_target_pairs={{1,0},{2,1},{3,2},{4,3},{5,4},{6,5},{7,6},{8,7},{9,8},{10,9},{11,1... | collective-permute-start | bytes 1572872 | tf_op jit(solution)/shard_map/ppermute | solution.py:112
  46.1 8.6 %collective-permute-start.6 = (f32[32,32,128]{2,1,0:T(8,128)S(1)}, f32[32,32,128]{2,1,0:T(8,128)S(1)}, u32[]{:S(2)}, u32[]{:S(2)}) collective-permute-start(f32[32,32,128]{2,1,0:T(8,128)S(1)} %get-tuple-element.25), channel_id=1, source_target_pairs={{0,32},{32,64},{64,96},{96,128},{128,160},{160,192},{192,224},{224... | collective-permute-start | bytes 1572872 | tf_op jit(solution)/shard_map/ppermute | solution.py:25
  46.7 13.6 %copy-start.2 = (f32[128,128,1]{1,0,2:T(8,128)S(1)}, f32[128,128,1]{1,0,2:T(8,128)}, u32[]{:S(2)}) copy-start(f32[128,128,1]{1,0,2:T(8,128)} %constant.29) | copy-start | bytes 196612
  46.7 8.1 %collective-permute-start.7 = (f32[32,32,128]{2,1,0:T(8,128)S(1)}, f32[32,32,128]{2,1,0:T(8,128)S(1)}, u32[]{:S(2)}, u32[]{:S(2)}) collective-permute-start(f32[32,32,128]{2,1,0:T(8,128)S(1)} %get-tuple-element.26), channel_id=1, source_target_pairs={{32,0},{64,32},{96,64},{128,96},{160,128},{192,160},{224,192},{0,2... | collective-permute-start | bytes 1572872 | tf_op jit(solution)/shard_map/ppermute | solution.py:28
  55.1 27.7 %collective-permute-start.9 = (f32[64,32,128]{2,1,0:T(8,128)S(1)}, f32[64,32,128]{2,1,0:T(8,128)S(1)}, u32[]{:S(2)}, u32[]{:S(2)}) collective-permute-start(f32[64,32,128]{2,1,0:T(8,128)S(1)} %fusion.21), channel_id=1, source_target_pairs={{1,0},{2,1},{3,2},{4,3},{5,4},{6,5},{7,6},{8,7},{9,8},{10,9},{11,1... | collective-permute-start | bytes 3145736 | tf_op jit(solution)/shard_map/ppermute | solution.py:28
  60.2 28.6 %collective-permute-start.8 = (f32[64,32,128]{2,1,0:T(8,128)S(1)}, f32[64,32,128]{2,1,0:T(8,128)S(1)}, u32[]{:S(2)}, u32[]{:S(2)}) collective-permute-start(f32[64,32,128]{2,1,0:T(8,128)S(1)} %fusion.21), channel_id=1, source_target_pairs={{0,1},{1,2},{2,3},{3,4},{4,5},{5,6},{6,7},{7,8},{8,9},{9,10},{10,1... | collective-permute-start | bytes 3145736 | tf_op jit(solution)/shard_map/ppermute | solution.py:25

commit v16 on v13

--- a/solution.py
+++ b/solution.py
@@ -102,9 +102,8 @@
     along_y = holed_pass(padded_y, first, 1, size_y)
     padded_x = padded_1(along_y, "row", 0, 2 * first + extra)
     along_x = holed_pass(padded_x, first, 0, size_x + 2 * extra)
-    ahead_2 = depth_pass(along_x, matrix_1 @ matrix_2)
     smooth_1 = depth_pass(lax.slice_in_dim(along_x, extra, extra + size_x, axis=0), matrix_1)
-    along_x = holed_pass(ahead_2, second, 0, size_x)
+    along_x = depth_pass(holed_pass(along_x, second, 0, size_x), matrix_1 @ matrix_2)
     padded_y = padded_1(along_x, "col", 1, 2 * second)
     smooth_2 = holed_pass(padded_y, second, 1, size_y)
     ahead_3 = depth_pass(smooth_2, matrix_3)

time: 113 us -> 112 us (level)
  no operation moved by 1% of the time
where the time goes in v16:
time: 112 us; the launch traced here: 110 us
  waiting for transfers between devices  58.9 us (53%)
  starting transfers between devices  21.4 us (19%)
  blocking collectives  18.4 us (16%)
  other arithmetic  5.05 us (5%)
  matrix products  3.09 us (3%)
  local copies, waits for them, and re-layouts  2.51 us (2%)
    ppermute x5, waiting for transfers between devices, padded_1(): lax.ppermute(lax.slice_in_dim(block, block.shape[dim] - width, None, axis...  31.1 us
    ppermute x5, waiting for transfers between devices, padded_1(): lax.ppermute(lax.slice_in_dim(block, 0, width, axis=dim), axis, backward)  27.8 us
    ppermute x5, starting transfers between devices, padded_1(): lax.ppermute(lax.slice_in_dim(block, 0, width, axis=dim), axis, backward)  19.3 us
    all_to_all x1, blocking collectives, gather_partials(): return lax.all_to_all(sent, axes, 0, 0, tiled=True)  18.4 us
    dot_general x3, matrix products, depth_pass(): jnp.dot(flat, jnp.asarray(matrix), precision=lax.Precision.HIGHEST, prefe...  3.09 us
  transfers between devices with their start and end apart: 10, of which 7 were waited for; matrix products, arithmetic and copies ran while one was open for 2% of the time, Pallas kernels for 0%

profile of v16, /device:TPU:8, one launch (start us, length us, event | category | flops | bytes accessed | tf_op | source)
XLA Modules:
  0.0 110.2 jit_solution(1925478550314435984)
XLA Ops:
  0.6 1.2 %fusion.60 = (f32[64,8,128]{2,1,0:T(8,128)S(1)}, f32[64,8,128]{2,1,0:T(8,128)S(1)}) fusion(f32[64,32,128]{2,1,0:T(8,128)} %param.4), kind=kLoop, calls=%fused_computation.109 | loop fusion | bytes 1048576 | tf_op jit(solution)/shard_map/slice | solution.py:26
  1.8 2.0 %collective-permute-start = (f32[64,8,128]{2,1,0:T(8,128)S(1)}, f32[64,8,128]{2,1,0:T(8,128)S(1)}, u32[]{:S(2)}, u32[]{:S(2)}) collective-permute-start(f32[64,8,128]{2,1,0:T(8,128)S(1)} %get-tuple-element.32), channel_id=1, source_target_pairs={{0,1},{1,2},{2,3},{3,4},{4,5},{5,6},{6,7},{7,8},{8,9},{9,10},{10,1... | collective-permute-start | bytes 786440 | tf_op jit(solution)/shard_map/ppermute | solution.py:25
  3.8 6.2 %collective-permute-start.1 = (f32[64,8,128]{2,1,0:T(8,128)S(1)}, f32[64,8,128]{2,1,0:T(8,128)S(1)}, u32[]{:S(2)}, u32[]{:S(2)}) collective-permute-start(f32[64,8,128]{2,1,0:T(8,128)S(1)} %get-tuple-element.33), channel_id=1, source_target_pairs={{1,0},{2,1},{3,2},{4,3},{5,4},{6,5},{7,6},{8,7},{9,8},{10,9},{11,1... | collective-permute-start | bytes 786440 | tf_op jit(solution)/shard_map/ppermute | solution.py:28
  10.0 6.2 %collective-permute-done = f32[64,8,128]{2,1,0:T(8,128)S(1)} collective-permute-done((f32[64,8,128]{2,1,0:T(8,128)S(1)}, f32[64,8,128]{2,1,0:T(8,128)S(1)}, u32[]{:S(2)}, u32[]{:S(2)}) %collective-permute-start) | collective-permute-done | bytes 262176 | tf_op jit(solution)/shard_map/ppermute | solution.py:25
  16.3 0.1 constant_dynamic-update-slice_fusion
  16.4 0.5 fusion.45
  17.0 1.7 %collective-permute-start.3 = (f32[24,32,128]{2,1,0:T(8,128)S(1)}, f32[24,32,128]{2,1,0:T(8,128)S(1)}, u32[]{:S(2)}, u32[]{:S(2)}) collective-permute-start(f32[24,32,128]{2,1,0:T(8,128)S(1)} %get-tuple-element.29), channel_id=1, source_target_pairs={{32,0},{64,32},{96,64},{128,96},{160,128},{192,160},{224,192},{0,2... | collective-permute-start | bytes 1179656 | tf_op jit(solution)/shard_map/ppermute | solution.py:28
  18.8 5.5 %collective-permute-done.2 = f32[24,32,128]{2,1,0:T(8,128)S(1)} collective-permute-done((f32[24,32,128]{2,1,0:T(8,128)S(1)}, f32[24,32,128]{2,1,0:T(8,128)S(1)}, u32[]{:S(2)}, u32[]{:S(2)}) %collective-permute-start.2) | collective-permute-done | bytes 393248 | tf_op jit(solution)/shard_map/ppermute | solution.py:25
  24.2 0.2 pad_maximum_fusion
  24.4 0.4 fusion
  24.8 0.5 copy-done.3
  25.3 1.2 %fusion.37 = f32[64,32,128]{2,1,0:T(8,128)S(1)} fusion(f32[128,128,1]{1,0,2:T(8,128)S(1)} %copy-done.3, f32[96,32,128]{2,1,0:T(8,128)S(1)} %fusion), kind=kOutput, calls=%fused_computation.67 | convolution fusion | flops 405012480 | bytes 6356992 | tf_op jit(solution)/shard_map/dot_general | solution.py:54
  26.6 5.3 %collective-permute-start.5 = (f32[64,16,128]{2,1,0:T(8,128)S(1)}, f32[64,16,128]{2,1,0:T(8,128)S(1)}, u32[]{:S(2)}, u32[]{:S(2)}) collective-permute-start(f32[64,16,128]{2,1,0:T(8,128)S(1)} %get-tuple-element.27), channel_id=1, source_target_pairs={{1,0},{2,1},{3,2},{4,3},{5,4},{6,5},{7,6},{8,7},{9,8},{10,9},{11,1... | collective-permute-start | bytes 1572872 | tf_op jit(solution)/shard_map/ppermute | solution.py:28
  31.9 12.1 %collective-permute-done.4 = f32[64,16,128]{2,1,0:T(8,128)S(1)} collective-permute-done((f32[64,16,128]{2,1,0:T(8,128)S(1)}, f32[64,16,128]{2,1,0:T(8,128)S(1)}, u32[]{:S(2)}, u32[]{:S(2)}) %collective-permute-start.4) | collective-permute-done | bytes 524320 | tf_op jit(solution)/shard_map/ppermute | solution.py:25
  44.0 0.3 fusion.21
  44.3 1.0 fusion.61
  45.4 1.1 %collective-permute-start.7 = (f32[32,32,128]{2,1,0:T(8,128)S(1)}, f32[32,32,128]{2,1,0:T(8,128)S(1)}, u32[]{:S(2)}, u32[]{:S(2)}) collective-permute-start(f32[32,32,128]{2,1,0:T(8,128)S(1)} %bitcast.36), channel_id=1, source_target_pairs={{32,0},{64,32},{96,64},{128,96},{160,128},{192,160},{224,192},{0,2... | collective-permute-start | bytes 1572872 | tf_op jit(solution)/shard_map/ppermute | solution.py:28
  46.5 6.7 %collective-permute-done.7 = f32[32,32,128]{2,1,0:T(8,128)S(1)} collective-permute-done((f32[32,32,128]{2,1,0:T(8,128)S(1)}, f32[32,32,128]{2,1,0:T(8,128)S(1)}, u32[]{:S(2)}, u32[]{:S(2)}) %collective-permute-start.7) | collective-permute-done | bytes 524320 | tf_op jit(solution)/shard_map/ppermute | solution.py:28
  53.2 1.9 %collective-permute-done.6 = f32[32,32,128]{2,1,0:T(8,128)S(1)} collective-permute-done((f32[32,32,128]{2,1,0:T(8,128)S(1)}, f32[32,32,128]{2,1,0:T(8,128)S(1)}, u32[]{:S(2)}, u32[]{:S(2)}) %collective-permute-start.6) | collective-permute-done | bytes 524320 | tf_op jit(solution)/shard_map/ppermute | solution.py:25
  55.1 0.4 fusion.13
  55.5 4.9 %collective-permute-start.9 = (f32[64,32,128]{2,1,0:T(8,128)S(1)}, f32[64,32,128]{2,1,0:T(8,128)S(1)}, u32[]{:S(2)}, u32[]{:S(2)}) collective-permute-start(f32[64,32,128]{2,1,0:T(8,128)S(1)} %fusion.13), channel_id=1, source_target_pairs={{1,0},{2,1},{3,2},{4,3},{5,4},{6,5},{7,6},{8,7},{9,8},{10,9},{11,1... | collective-permute-start | bytes 3145736 | tf_op jit(solution)/shard_map/ppermute | solution.py:28
  60.4 1.0 fusion.62
  61.3 0.3 abs_reduce_fusion.2
  61.7 0.3 abs_reduce_fusion.1
  62.0 21.1 %collective-permute-done.9 = f32[64,32,128]{2,1,0:T(8,128)S(1)} collective-permute-done((f32[64,32,128]{2,1,0:T(8,128)S(1)}, f32[64,32,128]{2,1,0:T(8,128)S(1)}, u32[]{:S(2)}, u32[]{:S(2)}) %collective-permute-start.9) | collective-permute-done | bytes 1048608 | tf_op jit(solution)/shard_map/ppermute | solution.py:28
  83.1 5.5 %collective-permute-done.8 = f32[64,32,128]{2,1,0:T(8,128)S(1)} collective-permute-done((f32[64,32,128]{2,1,0:T(8,128)S(1)}, f32[64,32,128]{2,1,0:T(8,128)S(1)}, u32[]{:S(2)}, u32[]{:S(2)}) %collective-permute-start.8) | collective-permute-done | bytes 1048608 | tf_op jit(solution)/shard_map/ppermute | solution.py:25
  88.6 1.5 %fusion.55 = (f32[64,32,128]{2,1,0:T(8,128)S(1)}, f32[64,32,128]{2,1,0:T(8,128)}) fusion(f32[64,32,128]{2,1,0:T(8,128)S(1)} %fusion.21, f32[64,32,128]{2,1,0:T(8,128)S(1)} %collective-permute-done.9, f32[64,32,128]{2,1,0:T(8,128)S(1)} %fusion.13, f32[64,32,128]{2,1,0:T(8,128)S(1)} %collective-permute-done.8), kind=kLoop, calls=%fused_computation.105 | loop fusion | flops 3145728 | bytes 6291456 | tf_op jit(solution)/shard_map/sub | solution.py:117
  90.1 0.3 abs_reduce_fusion
  90.6 18.4 %all_to_all.6 = f32[256,1,12]{2,1,0:T(1,128)S(1)} all-to-all(f32[256,1,12]{2,1,0:T(1,128)S(1)} %broadcast_in_dim.8), channel_id=1, replica_groups=mesh['row'=8,'col'=32] {'row','col'}, dimensions={0} | all-to-all | bytes 24576 | tf_op jit(solution)/shard_map/all_to_all | solution.py:89
  109.1 0.3 reshape.35
  109.4 0.1 reduce_sum.139
  109.6 0.6 pad_maximum_fusion.7
  (28 shorter events, 0.7 us)
Async XLA Ops:
  0.6 15.6 %copy-start = (f32[64,32,128]{2,1,0:T(8,128)S(1)}, f32[64,32,128]{2,1,0:T(8,128)}, u32[]{:S(2)}) copy-start(f32[64,32,128]{2,1,0:T(8,128)} %param.4) | copy-start | bytes 3145732
  1.8 14.4 %collective-permute-start = (f32[64,8,128]{2,1,0:T(8,128)S(1)}, f32[64,8,128]{2,1,0:T(8,128)S(1)}, u32[]{:S(2)}, u32[]{:S(2)}) collective-permute-start(f32[64,8,128]{2,1,0:T(8,128)S(1)} %get-tuple-element.32), channel_id=1, source_target_pairs={{0,1},{1,2},{2,3},{3,4},{4,5},{5,6},{6,7},{7,8},{8,9},{9,10},{10,1... | collective-permute-start | bytes 786440 | tf_op jit(solution)/shard_map/ppermute | solution.py:25
  3.8 12.6 %collective-permute-start.1 = (f32[64,8,128]{2,1,0:T(8,128)S(1)}, f32[64,8,128]{2,1,0:T(8,128)S(1)}, u32[]{:S(2)}, u32[]{:S(2)}) collective-permute-start(f32[64,8,128]{2,1,0:T(8,128)S(1)} %get-tuple-element.33), channel_id=1, source_target_pairs={{1,0},{2,1},{3,2},{4,3},{5,4},{6,5},{7,6},{8,7},{9,8},{10,9},{11,1... | collective-permute-start | bytes 786440 | tf_op jit(solution)/shard_map/ppermute | solution.py:28
  17.0 7.2 %collective-permute-start.2 = (f32[24,32,128]{2,1,0:T(8,128)S(1)}, f32[24,32,128]{2,1,0:T(8,128)S(1)}, u32[]{:S(2)}, u32[]{:S(2)}) collective-permute-start(f32[24,32,128]{2,1,0:T(8,128)S(1)} %get-tuple-element.28), channel_id=1, source_target_pairs={{0,32},{32,64},{64,96},{96,128},{128,160},{160,192},{192,224},{224... | collective-permute-start | bytes 1179656 | tf_op jit(solution)/shard_map/ppermute | solution.py:25
  17.0 7.2 %collective-permute-start.3 = (f32[24,32,128]{2,1,0:T(8,128)S(1)}, f32[24,32,128]{2,1,0:T(8,128)S(1)}, u32[]{:S(2)}, u32[]{:S(2)}) collective-permute-start(f32[24,32,128]{2,1,0:T(8,128)S(1)} %get-tuple-element.29), channel_id=1, source_target_pairs={{32,0},{64,32},{96,64},{128,96},{160,128},{192,160},{224,192},{0,2... | collective-permute-start | bytes 1179656 | tf_op jit(solution)/shard_map/ppermute | solution.py:28
  24.4 0.8 copy-start.3
  26.5 17.5 %collective-permute-start.4 = (f32[64,16,128]{2,1,0:T(8,128)S(1)}, f32[64,16,128]{2,1,0:T(8,128)S(1)}, u32[]{:S(2)}, u32[]{:S(2)}) collective-permute-start(f32[64,16,128]{2,1,0:T(8,128)S(1)} %get-tuple-element.26), channel_id=1, source_target_pairs={{0,1},{1,2},{2,3},{3,4},{4,5},{5,6},{6,7},{7,8},{8,9},{9,10},{10,1... | collective-permute-start | bytes 1572872 | tf_op jit(solution)/shard_map/ppermute | solution.py:25
  26.6 17.7 %copy-start.2 = (f32[128,128]{1,0:T(8,128)S(1)}, f32[128,128]{1,0:T(8,128)}, u32[]{:S(2)}) copy-start(f32[128,128]{1,0:T(8,128)} %constant.27.clone) | copy-start | bytes 196612
  26.6 17.4 %collective-permute-start.5 = (f32[64,16,128]{2,1,0:T(8,128)S(1)}, f32[64,16,128]{2,1,0:T(8,128)S(1)}, u32[]{:S(2)}, u32[]{:S(2)}) collective-permute-start(f32[64,16,128]{2,1,0:T(8,128)S(1)} %get-tuple-element.27), channel_id=1, source_target_pairs={{1,0},{2,1},{3,2},{4,3},{5,4},{6,5},{7,6},{8,7},{9,8},{10,9},{11,1... | collective-permute-start | bytes 1572872 | tf_op jit(solution)/shard_map/ppermute | solution.py:28
  45.4 7.8 %collective-permute-start.7 = (f32[32,32,128]{2,1,0:T(8,128)S(1)}, f32[32,32,128]{2,1,0:T(8,128)S(1)}, u32[]{:S(2)}, u32[]{:S(2)}) collective-permute-start(f32[32,32,128]{2,1,0:T(8,128)S(1)} %bitcast.36), channel_id=1, source_target_pairs={{32,0},{64,32},{96,64},{128,96},{160,128},{192,160},{224,192},{0,2... | collective-permute-start | bytes 1572872 | tf_op jit(solution)/shard_map/ppermute | solution.py:28
  46.5 8.6 %collective-permute-start.6 = (f32[32,32,128]{2,1,0:T(8,128)S(1)}, f32[32,32,128]{2,1,0:T(8,128)S(1)}, u32[]{:S(2)}, u32[]{:S(2)}) collective-permute-start(f32[32,32,128]{2,1,0:T(8,128)S(1)} %bitcast.35), channel_id=1, source_target_pairs={{0,32},{32,64},{64,96},{96,128},{128,160},{160,192},{192,224},{224... | collective-permute-start | bytes 1572872 | tf_op jit(solution)/shard_map/ppermute | solution.py:25
  55.1 5.2 %copy-start.1 = (f32[128,128,1]{1,0,2:T(8,128)S(1)}, f32[128,128,1]{1,0,2:T(8,128)}, u32[]{:S(2)}) copy-start(f32[128,128,1]{1,0,2:T(8,128)} %constant.29) | copy-start | bytes 196612
  55.5 27.6 %collective-permute-start.9 = (f32[64,32,128]{2,1,0:T(8,128)S(1)}, f32[64,32,128]{2,1,0:T(8,128)S(1)}, u32[]{:S(2)}, u32[]{:S(2)}) collective-permute-start(f32[64,32,128]{2,1,0:T(8,128)S(1)} %fusion.13), channel_id=1, source_target_pairs={{1,0},{2,1},{3,2},{4,3},{5,4},{6,5},{7,6},{8,7},{9,8},{10,9},{11,1... | collective-permute-start | bytes 3145736 | tf_op jit(solution)/shard_map/ppermute | solution.py:28
  60.3 28.2 %collective-permute-start.8 = (f32[64,32,128]{2,1,0:T(8,128)S(1)}, f32[64,32,128]{2,1,0:T(8,128)S(1)}, u32[]{:S(2)}, u32[]{:S(2)}) collective-permute-start(f32[64,32,128]{2,1,0:T(8,128)S(1)} %fusion.13), channel_id=1, source_target_pairs={{0,1},{1,2},{2,3},{3,4},{4,5},{5,6},{6,7},{7,8},{8,9},{9,10},{10,1... | collective-permute-start | bytes 3145736 | tf_op jit(solution)/shard_map/ppermute | solution.py:25

commit v17 on v16

--- a/solution.py
+++ b/solution.py
@@ -54,7 +54,7 @@
     summed = jnp.dot(
         flat,
         jnp.asarray(matrix),
-        precision=lax.Precision.HIGHEST,
+        precision=lax.Precision.HIGH,
         preferred_element_type=jnp.float32,
     )
     return summed.reshape(*rows, matrix.shape[1])

time: 112 us -> 111 us (level)
  matrix products: 3.09 us -> 1.92 us
    dot_general x3, matrix products: 3.09 us -> 1.92 us  [depth_pass(): jnp.dot(flat, jnp.asarray(matrix), precision=lax.Precision.HIGH, preferre...]
  transfers between devices with their start and end apart: 10 -> 10, of which waited for: 7 -> 7; matrix products, arithmetic and copies ran while one was open for 2% -> 1% of each run, Pallas kernels for 0% -> 0%
where the time goes in v17:
time: 111 us; the launch traced here: 109 us
  waiting for transfers between devices  59.3 us (53%)
  starting transfers between devices  21.4 us (19%)
  blocking collectives  18.4 us (17%)
  other arithmetic  5.05 us (5%)
  local copies, waits for them, and re-layouts  2.51 us (2%)
  matrix products  1.92 us (2%)
    ppermute x5, waiting for transfers between devices, padded_1(): lax.ppermute(lax.slice_in_dim(block, block.shape[dim] - width, None, axis...  31.1 us
    ppermute x5, waiting for transfers between devices, padded_1(): lax.ppermute(lax.slice_in_dim(block, 0, width, axis=dim), axis, backward)  28.2 us
    ppermute x5, starting transfers between devices, padded_1(): lax.ppermute(lax.slice_in_dim(block, 0, width, axis=dim), axis, backward)  19.3 us
    all_to_all x1, blocking collectives, gather_partials(): return lax.all_to_all(sent, axes, 0, 0, tiled=True)  18.4 us
  transfers between devices with their start and end apart: 10, of which 7 were waited for; matrix products, arithmetic and copies ran while one was open for 1% of the time, Pallas kernels for 0%

profile of v17, /device:TPU:8, one launch (start us, length us, event | category | flops | bytes accessed | tf_op | source)
XLA Modules:
  0.0 109.4 jit_solution(4105224806278456046)
XLA Ops:
  0.6 1.2 %fusion.60 = (f32[64,8,128]{2,1,0:T(8,128)S(1)}, f32[64,8,128]{2,1,0:T(8,128)S(1)}) fusion(f32[64,32,128]{2,1,0:T(8,128)} %param.4), kind=kLoop, calls=%fused_computation.109 | loop fusion | bytes 1048576 | tf_op jit(solution)/shard_map/slice | solution.py:26
  1.8 2.0 %collective-permute-start = (f32[64,8,128]{2,1,0:T(8,128)S(1)}, f32[64,8,128]{2,1,0:T(8,128)S(1)}, u32[]{:S(2)}, u32[]{:S(2)}) collective-permute-start(f32[64,8,128]{2,1,0:T(8,128)S(1)} %get-tuple-element.32), channel_id=1, source_target_pairs={{0,1},{1,2},{2,3},{3,4},{4,5},{5,6},{6,7},{7,8},{8,9},{9,10},{10,1... | collective-permute-start | bytes 786440 | tf_op jit(solution)/shard_map/ppermute | solution.py:25
  3.8 6.2 %collective-permute-start.1 = (f32[64,8,128]{2,1,0:T(8,128)S(1)}, f32[64,8,128]{2,1,0:T(8,128)S(1)}, u32[]{:S(2)}, u32[]{:S(2)}) collective-permute-start(f32[64,8,128]{2,1,0:T(8,128)S(1)} %get-tuple-element.33), channel_id=1, source_target_pairs={{1,0},{2,1},{3,2},{4,3},{5,4},{6,5},{7,6},{8,7},{9,8},{10,9},{11,1... | collective-permute-start | bytes 786440 | tf_op jit(solution)/shard_map/ppermute | solution.py:28
  10.0 6.2 %collective-permute-done = f32[64,8,128]{2,1,0:T(8,128)S(1)} collective-permute-done((f32[64,8,128]{2,1,0:T(8,128)S(1)}, f32[64,8,128]{2,1,0:T(8,128)S(1)}, u32[]{:S(2)}, u32[]{:S(2)}) %collective-permute-start) | collective-permute-done | bytes 262176 | tf_op jit(solution)/shard_map/ppermute | solution.py:25
  16.3 0.1 constant_dynamic-update-slice_fusion
  16.4 0.5 fusion.45
  17.0 1.7 %collective-permute-start.3 = (f32[24,32,128]{2,1,0:T(8,128)S(1)}, f32[24,32,128]{2,1,0:T(8,128)S(1)}, u32[]{:S(2)}, u32[]{:S(2)}) collective-permute-start(f32[24,32,128]{2,1,0:T(8,128)S(1)} %get-tuple-element.29), channel_id=1, source_target_pairs={{32,0},{64,32},{96,64},{128,96},{160,128},{192,160},{224,192},{0,2... | collective-permute-start | bytes 1179656 | tf_op jit(solution)/shard_map/ppermute | solution.py:28
  18.8 5.5 %collective-permute-done.2 = f32[24,32,128]{2,1,0:T(8,128)S(1)} collective-permute-done((f32[24,32,128]{2,1,0:T(8,128)S(1)}, f32[24,32,128]{2,1,0:T(8,128)S(1)}, u32[]{:S(2)}, u32[]{:S(2)}) %collective-permute-start.2) | collective-permute-done | bytes 393248 | tf_op jit(solution)/shard_map/ppermute | solution.py:25
  24.2 0.2 pad_maximum_fusion
  24.4 0.4 fusion
  24.8 0.5 copy-done.3
  25.3 0.8 fusion.37
  26.2 5.3 %collective-permute-start.5 = (f32[64,16,128]{2,1,0:T(8,128)S(1)}, f32[64,16,128]{2,1,0:T(8,128)S(1)}, u32[]{:S(2)}, u32[]{:S(2)}) collective-permute-start(f32[64,16,128]{2,1,0:T(8,128)S(1)} %get-tuple-element.27), channel_id=1, source_target_pairs={{1,0},{2,1},{3,2},{4,3},{5,4},{6,5},{7,6},{8,7},{9,8},{10,9},{11,1... | collective-permute-start | bytes 1572872 | tf_op jit(solution)/shard_map/ppermute | solution.py:28
  31.6 12.1 %collective-permute-done.4 = f32[64,16,128]{2,1,0:T(8,128)S(1)} collective-permute-done((f32[64,16,128]{2,1,0:T(8,128)S(1)}, f32[64,16,128]{2,1,0:T(8,128)S(1)}, u32[]{:S(2)}, u32[]{:S(2)}) %collective-permute-start.4) | collective-permute-done | bytes 524320 | tf_op jit(solution)/shard_map/ppermute | solution.py:25
  43.6 0.3 fusion.21
  43.9 0.6 fusion.61
  44.6 1.1 %collective-permute-start.7 = (f32[32,32,128]{2,1,0:T(8,128)S(1)}, f32[32,32,128]{2,1,0:T(8,128)S(1)}, u32[]{:S(2)}, u32[]{:S(2)}) collective-permute-start(f32[32,32,128]{2,1,0:T(8,128)S(1)} %bitcast.36), channel_id=1, source_target_pairs={{32,0},{64,32},{96,64},{128,96},{160,128},{192,160},{224,192},{0,2... | collective-permute-start | bytes 1572872 | tf_op jit(solution)/shard_map/ppermute | solution.py:28
  45.7 6.7 %collective-permute-done.7 = f32[32,32,128]{2,1,0:T(8,128)S(1)} collective-permute-done((f32[32,32,128]{2,1,0:T(8,128)S(1)}, f32[32,32,128]{2,1,0:T(8,128)S(1)}, u32[]{:S(2)}, u32[]{:S(2)}) %collective-permute-start.7) | collective-permute-done | bytes 524320 | tf_op jit(solution)/shard_map/ppermute | solution.py:28
  52.4 1.9 %collective-permute-done.6 = f32[32,32,128]{2,1,0:T(8,128)S(1)} collective-permute-done((f32[32,32,128]{2,1,0:T(8,128)S(1)}, f32[32,32,128]{2,1,0:T(8,128)S(1)}, u32[]{:S(2)}, u32[]{:S(2)}) %collective-permute-start.6) | collective-permute-done | bytes 524320 | tf_op jit(solution)/shard_map/ppermute | solution.py:25
  54.3 0.4 fusion.13
  54.7 4.9 %collective-permute-start.9 = (f32[64,32,128]{2,1,0:T(8,128)S(1)}, f32[64,32,128]{2,1,0:T(8,128)S(1)}, u32[]{:S(2)}, u32[]{:S(2)}) collective-permute-start(f32[64,32,128]{2,1,0:T(8,128)S(1)} %fusion.13), channel_id=1, source_target_pairs={{1,0},{2,1},{3,2},{4,3},{5,4},{6,5},{7,6},{8,7},{9,8},{10,9},{11,1... | collective-permute-start | bytes 3145736 | tf_op jit(solution)/shard_map/ppermute | solution.py:28
  59.6 0.6 fusion.62
  60.2 0.3 abs_reduce_fusion.2
  60.5 0.3 abs_reduce_fusion.1
  60.8 21.5 %collective-permute-done.9 = f32[64,32,128]{2,1,0:T(8,128)S(1)} collective-permute-done((f32[64,32,128]{2,1,0:T(8,128)S(1)}, f32[64,32,128]{2,1,0:T(8,128)S(1)}, u32[]{:S(2)}, u32[]{:S(2)}) %collective-permute-start.9) | collective-permute-done | bytes 1048608 | tf_op jit(solution)/shard_map/ppermute | solution.py:28
  82.3 5.5 %collective-permute-done.8 = f32[64,32,128]{2,1,0:T(8,128)S(1)} collective-permute-done((f32[64,32,128]{2,1,0:T(8,128)S(1)}, f32[64,32,128]{2,1,0:T(8,128)S(1)}, u32[]{:S(2)}, u32[]{:S(2)}) %collective-permute-start.8) | collective-permute-done | bytes 1048608 | tf_op jit(solution)/shard_map/ppermute | solution.py:25
  87.8 1.5 %fusion.55 = (f32[64,32,128]{2,1,0:T(8,128)S(1)}, f32[64,32,128]{2,1,0:T(8,128)}) fusion(f32[64,32,128]{2,1,0:T(8,128)S(1)} %fusion.21, f32[64,32,128]{2,1,0:T(8,128)S(1)} %collective-permute-done.9, f32[64,32,128]{2,1,0:T(8,128)S(1)} %fusion.13, f32[64,32,128]{2,1,0:T(8,128)S(1)} %collective-permute-done.8), kind=kLoop, calls=%fused_computation.105 | loop fusion | flops 3145728 | bytes 6291456 | tf_op jit(solution)/shard_map/sub | solution.py:117
  89.3 0.3 abs_reduce_fusion
  89.8 18.4 %all_to_all.6 = f32[256,1,12]{2,1,0:T(1,128)S(1)} all-to-all(f32[256,1,12]{2,1,0:T(1,128)S(1)} %broadcast_in_dim.8), channel_id=1, replica_groups=mesh['row'=8,'col'=32] {'row','col'}, dimensions={0} | all-to-all | bytes 24576 | tf_op jit(solution)/shard_map/all_to_all | solution.py:89
  108.3 0.3 reshape.35
  108.6 0.1 reduce_sum.139
  108.8 0.6 pad_maximum_fusion.7
  (28 shorter events, 0.7 us)
Async XLA Ops:
  0.6 15.6 %copy-start = (f32[64,32,128]{2,1,0:T(8,128)S(1)}, f32[64,32,128]{2,1,0:T(8,128)}, u32[]{:S(2)}) copy-start(f32[64,32,128]{2,1,0:T(8,128)} %param.4) | copy-start | bytes 3145732
  1.8 14.4 %collective-permute-start = (f32[64,8,128]{2,1,0:T(8,128)S(1)}, f32[64,8,128]{2,1,0:T(8,128)S(1)}, u32[]{:S(2)}, u32[]{:S(2)}) collective-permute-start(f32[64,8,128]{2,1,0:T(8,128)S(1)} %get-tuple-element.32), channel_id=1, source_target_pairs={{0,1},{1,2},{2,3},{3,4},{4,5},{5,6},{6,7},{7,8},{8,9},{9,10},{10,1... | collective-permute-start | bytes 786440 | tf_op jit(solution)/shard_map/ppermute | solution.py:25
  3.8 12.6 %collective-permute-start.1 = (f32[64,8,128]{2,1,0:T(8,128)S(1)}, f32[64,8,128]{2,1,0:T(8,128)S(1)}, u32[]{:S(2)}, u32[]{:S(2)}) collective-permute-start(f32[64,8,128]{2,1,0:T(8,128)S(1)} %get-tuple-element.33), channel_id=1, source_target_pairs={{1,0},{2,1},{3,2},{4,3},{5,4},{6,5},{7,6},{8,7},{9,8},{10,9},{11,1... | collective-permute-start | bytes 786440 | tf_op jit(solution)/shard_map/ppermute | solution.py:28
  17.0 7.2 %collective-permute-start.2 = (f32[24,32,128]{2,1,0:T(8,128)S(1)}, f32[24,32,128]{2,1,0:T(8,128)S(1)}, u32[]{:S(2)}, u32[]{:S(2)}) collective-permute-start(f32[24,32,128]{2,1,0:T(8,128)S(1)} %get-tuple-element.28), channel_id=1, source_target_pairs={{0,32},{32,64},{64,96},{96,128},{128,160},{160,192},{192,224},{224... | collective-permute-start | bytes 1179656 | tf_op jit(solution)/shard_map/ppermute | solution.py:25
  17.0 7.2 %collective-permute-start.3 = (f32[24,32,128]{2,1,0:T(8,128)S(1)}, f32[24,32,128]{2,1,0:T(8,128)S(1)}, u32[]{:S(2)}, u32[]{:S(2)}) collective-permute-start(f32[24,32,128]{2,1,0:T(8,128)S(1)} %get-tuple-element.29), channel_id=1, source_target_pairs={{32,0},{64,32},{96,64},{128,96},{160,128},{192,160},{224,192},{0,2... | collective-permute-start | bytes 1179656 | tf_op jit(solution)/shard_map/ppermute | solution.py:28
  24.4 0.8 copy-start.3
  26.1 17.5 %collective-permute-start.4 = (f32[64,16,128]{2,1,0:T(8,128)S(1)}, f32[64,16,128]{2,1,0:T(8,128)S(1)}, u32[]{:S(2)}, u32[]{:S(2)}) collective-permute-start(f32[64,16,128]{2,1,0:T(8,128)S(1)} %get-tuple-element.26), channel_id=1, source_target_pairs={{0,1},{1,2},{2,3},{3,4},{4,5},{5,6},{6,7},{7,8},{8,9},{9,10},{10,1... | collective-permute-start | bytes 1572872 | tf_op jit(solution)/shard_map/ppermute | solution.py:25
  26.2 17.7 %copy-start.2 = (f32[128,128]{1,0:T(8,128)S(1)}, f32[128,128]{1,0:T(8,128)}, u32[]{:S(2)}) copy-start(f32[128,128]{1,0:T(8,128)} %constant.27.clone) | copy-start | bytes 196612
  26.2 17.4 %collective-permute-start.5 = (f32[64,16,128]{2,1,0:T(8,128)S(1)}, f32[64,16,128]{2,1,0:T(8,128)S(1)}, u32[]{:S(2)}, u32[]{:S(2)}) collective-permute-start(f32[64,16,128]{2,1,0:T(8,128)S(1)} %get-tuple-element.27), channel_id=1, source_target_pairs={{1,0},{2,1},{3,2},{4,3},{5,4},{6,5},{7,6},{8,7},{9,8},{10,9},{11,1... | collective-permute-start | bytes 1572872 | tf_op jit(solution)/shard_map/ppermute | solution.py:28
  44.6 7.8 %collective-permute-start.7 = (f32[32,32,128]{2,1,0:T(8,128)S(1)}, f32[32,32,128]{2,1,0:T(8,128)S(1)}, u32[]{:S(2)}, u32[]{:S(2)}) collective-permute-start(f32[32,32,128]{2,1,0:T(8,128)S(1)} %bitcast.36), channel_id=1, source_target_pairs={{32,0},{64,32},{96,64},{128,96},{160,128},{192,160},{224,192},{0,2... | collective-permute-start | bytes 1572872 | tf_op jit(solution)/shard_map/ppermute | solution.py:28
  45.7 8.6 %collective-permute-start.6 = (f32[32,32,128]{2,1,0:T(8,128)S(1)}, f32[32,32,128]{2,1,0:T(8,128)S(1)}, u32[]{:S(2)}, u32[]{:S(2)}) collective-permute-start(f32[32,32,128]{2,1,0:T(8,128)S(1)} %bitcast.35), channel_id=1, source_target_pairs={{0,32},{32,64},{64,96},{96,128},{128,160},{160,192},{192,224},{224... | collective-permute-start | bytes 1572872 | tf_op jit(solution)/shard_map/ppermute | solution.py:25
  54.3 5.2 %copy-start.1 = (f32[128,128,1]{1,0,2:T(8,128)S(1)}, f32[128,128,1]{1,0,2:T(8,128)}, u32[]{:S(2)}) copy-start(f32[128,128,1]{1,0,2:T(8,128)} %constant.29) | copy-start | bytes 196612
  54.7 27.6 %collective-permute-start.9 = (f32[64,32,128]{2,1,0:T(8,128)S(1)}, f32[64,32,128]{2,1,0:T(8,128)S(1)}, u32[]{:S(2)}, u32[]{:S(2)}) collective-permute-start(f32[64,32,128]{2,1,0:T(8,128)S(1)} %fusion.13), channel_id=1, source_target_pairs={{1,0},{2,1},{3,2},{4,3},{5,4},{6,5},{7,6},{8,7},{9,8},{10,9},{11,1... | collective-permute-start | bytes 3145736 | tf_op jit(solution)/shard_map/ppermute | solution.py:28
  59.6 28.2 %collective-permute-start.8 = (f32[64,32,128]{2,1,0:T(8,128)S(1)}, f32[64,32,128]{2,1,0:T(8,128)S(1)}, u32[]{:S(2)}, u32[]{:S(2)}) collective-permute-start(f32[64,32,128]{2,1,0:T(8,128)S(1)} %fusion.13), channel_id=1, source_target_pairs={{0,1},{1,2},{2,3},{3,4},{4,5},{5,6},{6,7},{7,8},{8,9},{9,10},{10,1... | collective-permute-start | bytes 3145736 | tf_op jit(solution)/shard_map/ppermute | solution.py:25

commit v18 on v16

--- a/solution.py
+++ b/solution.py
@@ -107,10 +107,10 @@
     padded_y = padded_1(along_x, "col", 1, 2 * second)
     smooth_2 = holed_pass(padded_y, second, 1, size_y)
     ahead_3 = depth_pass(smooth_2, matrix_3)
-    padded_x = padded_1(ahead_3, "row", 0, 2 * third)
-    along_x = holed_pass(padded_x, third, 0, size_x)
-    padded_y = padded_1(along_x, "col", 1, 2 * third)
-    smooth_3 = holed_pass(padded_y, third, 1, size_y)
+    padded_y = padded_1(ahead_3, "col", 1, 2 * third)
+    along_y = holed_pass(padded_y, third, 1, size_y)
+    padded_x = padded_1(along_y, "row", 0, 2 * third)
+    smooth_3 = holed_pass(padded_x, third, 0, size_x)
     current = smooth_3
     held = lax.optimization_barrier(((density, smooth_1), (smooth_1, smooth_2)))
     sums = [moment_sums(a - b) for a, b in held]

time: 112 us -> 112 us (level)
  waiting for transfers between devices: 58.9 us -> 57.3 us
  starting transfers between devices: 21.4 us -> 22.8 us
    ppermute x5, waiting for transfers between devices: 27.8 us -> 21.9 us  [padded_1(): lax.ppermute(lax.slice_in_dim(block, 0, width, axis=dim), axis, backward)]
    ppermute x5, waiting for transfers between devices: 31.1 us -> 35.4 us  [padded_1(): lax.ppermute(lax.slice_in_dim(block, block.shape[dim] - width, None, axis...]
    ppermute x5, starting transfers between devices: 19.3 us -> 20.7 us  [padded_1(): lax.ppermute(lax.slice_in_dim(block, 0, width, axis=dim), axis, backward)]
  transfers between devices with their start and end apart: 10 -> 10, of which waited for: 7 -> 6; matrix products, arithmetic and copies ran while one was open for 2% -> 2% of each run, Pallas kernels for 0% -> 0%
where the time goes in v18:
time: 112 us; the launch traced here: 110 us
  waiting for transfers between devices  57.3 us (51%)
  starting transfers between devices  22.8 us (20%)
  blocking collectives  18.7 us (17%)
  other arithmetic  5.06 us (5%)
  matrix products  3.11 us (3%)
  local copies, waits for them, and re-layouts  2.51 us (2%)
    ppermute x5, waiting for transfers between devices, padded_1(): lax.ppermute(lax.slice_in_dim(block, block.shape[dim] - width, None, axis...  35.4 us
    ppermute x5, waiting for transfers between devices, padded_1(): lax.ppermute(lax.slice_in_dim(block, 0, width, axis=dim), axis, backward)  21.9 us
    ppermute x5, starting transfers between devices, padded_1(): lax.ppermute(lax.slice_in_dim(block, 0, width, axis=dim), axis, backward)  20.7 us
    all_to_all x1, blocking collectives, gather_partials(): return lax.all_to_all(sent, axes, 0, 0, tiled=True)  18.7 us
    dot_general x3, matrix products, depth_pass(): jnp.dot(flat, jnp.asarray(matrix), precision=lax.Precision.HIGHEST, prefe...  3.11 us
  transfers between devices with their start and end apart: 10, of which 6 were waited for; matrix products, arithmetic and copies ran while one was open for 2% of the time, Pallas kernels for 0%

profile of v18, /device:TPU:8, one launch (start us, length us, event | category | flops | bytes accessed | tf_op | source)
XLA Modules:
  0.0 110.3 jit_solution(3687415415804662814)
XLA Ops:
  0.6 1.2 %fusion.60 = (f32[64,8,128]{2,1,0:T(8,128)S(1)}, f32[64,8,128]{2,1,0:T(8,128)S(1)}) fusion(f32[64,32,128]{2,1,0:T(8,128)} %param.4), kind=kLoop, calls=%fused_computation.109 | loop fusion | bytes 1048576 | tf_op jit(solution)/shard_map/slice | solution.py:26
  1.8 2.0 %collective-permute-start = (f32[64,8,128]{2,1,0:T(8,128)S(1)}, f32[64,8,128]{2,1,0:T(8,128)S(1)}, u32[]{:S(2)}, u32[]{:S(2)}) collective-permute-start(f32[64,8,128]{2,1,0:T(8,128)S(1)} %get-tuple-element.32), channel_id=1, source_target_pairs={{0,1},{1,2},{2,3},{3,4},{4,5},{5,6},{6,7},{7,8},{8,9},{9,10},{10,1... | collective-permute-start | bytes 786440 | tf_op jit(solution)/shard_map/ppermute | solution.py:25
  3.8 6.2 %collective-permute-start.1 = (f32[64,8,128]{2,1,0:T(8,128)S(1)}, f32[64,8,128]{2,1,0:T(8,128)S(1)}, u32[]{:S(2)}, u32[]{:S(2)}) collective-permute-start(f32[64,8,128]{2,1,0:T(8,128)S(1)} %get-tuple-element.33), channel_id=1, source_target_pairs={{1,0},{2,1},{3,2},{4,3},{5,4},{6,5},{7,6},{8,7},{9,8},{10,9},{11,1... | collective-permute-start | bytes 786440 | tf_op jit(solution)/shard_map/ppermute | solution.py:28
  10.0 6.2 %collective-permute-done = f32[64,8,128]{2,1,0:T(8,128)S(1)} collective-permute-done((f32[64,8,128]{2,1,0:T(8,128)S(1)}, f32[64,8,128]{2,1,0:T(8,128)S(1)}, u32[]{:S(2)}, u32[]{:S(2)}) %collective-permute-start) | collective-permute-done | bytes 262176 | tf_op jit(solution)/shard_map/ppermute | solution.py:25
  16.3 0.1 constant_dynamic-update-slice_fusion
  16.4 0.5 fusion.45
  17.0 1.7 %collective-permute-start.3 = (f32[24,32,128]{2,1,0:T(8,128)S(1)}, f32[24,32,128]{2,1,0:T(8,128)S(1)}, u32[]{:S(2)}, u32[]{:S(2)}) collective-permute-start(f32[24,32,128]{2,1,0:T(8,128)S(1)} %get-tuple-element.29), channel_id=1, source_target_pairs={{32,0},{64,32},{96,64},{128,96},{160,128},{192,160},{224,192},{0,2... | collective-permute-start | bytes 1179656 | tf_op jit(solution)/shard_map/ppermute | solution.py:28
  18.8 5.5 %collective-permute-done.2 = f32[24,32,128]{2,1,0:T(8,128)S(1)} collective-permute-done((f32[24,32,128]{2,1,0:T(8,128)S(1)}, f32[24,32,128]{2,1,0:T(8,128)S(1)}, u32[]{:S(2)}, u32[]{:S(2)}) %collective-permute-start.2) | collective-permute-done | bytes 393248 | tf_op jit(solution)/shard_map/ppermute | solution.py:25
  24.2 0.2 pad_maximum_fusion
  24.4 0.4 fusion
  24.8 0.5 copy-done.3
  25.3 1.2 %fusion.37 = f32[64,32,128]{2,1,0:T(8,128)S(1)} fusion(f32[128,128,1]{1,0,2:T(8,128)S(1)} %copy-done.3, f32[96,32,128]{2,1,0:T(8,128)S(1)} %fusion), kind=kOutput, calls=%fused_computation.67 | convolution fusion | flops 405012480 | bytes 6356992 | tf_op jit(solution)/shard_map/dot_general | solution.py:54
  26.6 5.3 %collective-permute-start.5 = (f32[64,16,128]{2,1,0:T(8,128)S(1)}, f32[64,16,128]{2,1,0:T(8,128)S(1)}, u32[]{:S(2)}, u32[]{:S(2)}) collective-permute-start(f32[64,16,128]{2,1,0:T(8,128)S(1)} %get-tuple-element.27), channel_id=1, source_target_pairs={{1,0},{2,1},{3,2},{4,3},{5,4},{6,5},{7,6},{8,7},{9,8},{10,9},{11,1... | collective-permute-start | bytes 1572872 | tf_op jit(solution)/shard_map/ppermute | solution.py:28
  31.9 12.1 %collective-permute-done.4 = f32[64,16,128]{2,1,0:T(8,128)S(1)} collective-permute-done((f32[64,16,128]{2,1,0:T(8,128)S(1)}, f32[64,16,128]{2,1,0:T(8,128)S(1)}, u32[]{:S(2)}, u32[]{:S(2)}) %collective-permute-start.4) | collective-permute-done | bytes 524320 | tf_op jit(solution)/shard_map/ppermute | solution.py:25
  44.0 0.3 fusion.21
  44.3 1.0 fusion.61
  45.3 5.7 %collective-permute-start.7 = (f32[64,32,128]{2,1,0:T(8,128)S(1)}, f32[64,32,128]{2,1,0:T(8,128)S(1)}, u32[]{:S(2)}, u32[]{:S(2)}) collective-permute-start(f32[64,32,128]{2,1,0:T(8,128)S(1)} %fusion.61), channel_id=1, source_target_pairs={{1,0},{2,1},{3,2},{4,3},{5,4},{6,5},{7,6},{8,7},{9,8},{10,9},{11,1... | collective-permute-start | bytes 3145736 | tf_op jit(solution)/shard_map/ppermute | solution.py:28
  51.0 1.0 fusion.62
  52.0 21.9 %collective-permute-done.7 = f32[64,32,128]{2,1,0:T(8,128)S(1)} collective-permute-done((f32[64,32,128]{2,1,0:T(8,128)S(1)}, f32[64,32,128]{2,1,0:T(8,128)S(1)}, u32[]{:S(2)}, u32[]{:S(2)}) %collective-permute-start.7) | collective-permute-done | bytes 1048608 | tf_op jit(solution)/shard_map/ppermute | solution.py:28
  73.9 5.5 %collective-permute-done.6 = f32[64,32,128]{2,1,0:T(8,128)S(1)} collective-permute-done((f32[64,32,128]{2,1,0:T(8,128)S(1)}, f32[64,32,128]{2,1,0:T(8,128)S(1)}, u32[]{:S(2)}, u32[]{:S(2)}) %collective-permute-start.6) | collective-permute-done | bytes 1048608 | tf_op jit(solution)/shard_map/ppermute | solution.py:25
  79.4 0.4 fusion.30
  79.9 1.7 %collective-permute-start.9 = (f32[32,32,128]{2,1,0:T(8,128)S(1)}, f32[32,32,128]{2,1,0:T(8,128)S(1)}, u32[]{:S(2)}, u32[]{:S(2)}) collective-permute-start(f32[32,32,128]{2,1,0:T(8,128)S(1)} %get-tuple-element.25), channel_id=1, source_target_pairs={{32,0},{64,32},{96,64},{128,96},{160,128},{192,160},{224,192},{0,2... | collective-permute-start | bytes 1572872 | tf_op jit(solution)/shard_map/ppermute | solution.py:28
  81.6 0.3 abs_reduce_fusion.2
  81.9 0.3 abs_reduce_fusion.1
  82.3 6.2 %collective-permute-done.8 = f32[32,32,128]{2,1,0:T(8,128)S(1)} collective-permute-done((f32[32,32,128]{2,1,0:T(8,128)S(1)}, f32[32,32,128]{2,1,0:T(8,128)S(1)}, u32[]{:S(2)}, u32[]{:S(2)}) %collective-permute-start.8) | collective-permute-done | bytes 524320 | tf_op jit(solution)/shard_map/ppermute | solution.py:25
  88.5 1.5 %fusion.55 = (f32[64,32,128]{2,1,0:T(8,128)S(1)}, f32[64,32,128]{2,1,0:T(8,128)}) fusion(f32[64,32,128]{2,1,0:T(8,128)S(1)} %fusion.21, f32[32,32,128]{2,1,0:T(8,128)S(1)} %collective-permute-done.9, f32[64,32,128]{2,1,0:T(8,128)S(1)} %fusion.30, f32[32,32,128]{2,1,0:T(8,128)S(1)} %collective-permute-done.8), kind=kLoop, calls=%fused_computation.105 | loop fusion | flops 3670016 | bytes 5242880 | tf_op jit(solution)/shard_map/sub | solution.py:117
  90.0 0.3 abs_reduce_fusion
  90.3 0.1 maximum_reduce_fusion
  90.5 18.7 %all_to_all.6 = f32[256,1,12]{2,1,0:T(1,128)S(1)} all-to-all(f32[256,1,12]{2,1,0:T(1,128)S(1)} %broadcast_in_dim.8), channel_id=1, replica_groups=mesh['row'=8,'col'=32] {'row','col'}, dimensions={0} | all-to-all | bytes 24576 | tf_op jit(solution)/shard_map/all_to_all | solution.py:89
  109.3 0.3 reshape.29
  109.5 0.1 reduce_sum.139
  109.7 0.6 pad_maximum_fusion.7
  (28 shorter events, 0.7 us)
Async XLA Ops:
  0.6 15.6 %copy-start = (f32[64,32,128]{2,1,0:T(8,128)S(1)}, f32[64,32,128]{2,1,0:T(8,128)}, u32[]{:S(2)}) copy-start(f32[64,32,128]{2,1,0:T(8,128)} %param.4) | copy-start | bytes 3145732
  1.8 14.4 %collective-permute-start = (f32[64,8,128]{2,1,0:T(8,128)S(1)}, f32[64,8,128]{2,1,0:T(8,128)S(1)}, u32[]{:S(2)}, u32[]{:S(2)}) collective-permute-start(f32[64,8,128]{2,1,0:T(8,128)S(1)} %get-tuple-element.32), channel_id=1, source_target_pairs={{0,1},{1,2},{2,3},{3,4},{4,5},{5,6},{6,7},{7,8},{8,9},{9,10},{10,1... | collective-permute-start | bytes 786440 | tf_op jit(solution)/shard_map/ppermute | solution.py:25
  3.8 12.6 %collective-permute-start.1 = (f32[64,8,128]{2,1,0:T(8,128)S(1)}, f32[64,8,128]{2,1,0:T(8,128)S(1)}, u32[]{:S(2)}, u32[]{:S(2)}) collective-permute-start(f32[64,8,128]{2,1,0:T(8,128)S(1)} %get-tuple-element.33), channel_id=1, source_target_pairs={{1,0},{2,1},{3,2},{4,3},{5,4},{6,5},{7,6},{8,7},{9,8},{10,9},{11,1... | collective-permute-start | bytes 786440 | tf_op jit(solution)/shard_map/ppermute | solution.py:28
  17.0 7.2 %collective-permute-start.2 = (f32[24,32,128]{2,1,0:T(8,128)S(1)}, f32[24,32,128]{2,1,0:T(8,128)S(1)}, u32[]{:S(2)}, u32[]{:S(2)}) collective-permute-start(f32[24,32,128]{2,1,0:T(8,128)S(1)} %get-tuple-element.28), channel_id=1, source_target_pairs={{0,32},{32,64},{64,96},{96,128},{128,160},{160,192},{192,224},{224... | collective-permute-start | bytes 1179656 | tf_op jit(solution)/shard_map/ppermute | solution.py:25
  17.0 7.2 %collective-permute-start.3 = (f32[24,32,128]{2,1,0:T(8,128)S(1)}, f32[24,32,128]{2,1,0:T(8,128)S(1)}, u32[]{:S(2)}, u32[]{:S(2)}) collective-permute-start(f32[24,32,128]{2,1,0:T(8,128)S(1)} %get-tuple-element.29), channel_id=1, source_target_pairs={{32,0},{64,32},{96,64},{128,96},{160,128},{192,160},{224,192},{0,2... | collective-permute-start | bytes 1179656 | tf_op jit(solution)/shard_map/ppermute | solution.py:28
  24.4 0.8 copy-start.3
  26.5 17.5 %collective-permute-start.4 = (f32[64,16,128]{2,1,0:T(8,128)S(1)}, f32[64,16,128]{2,1,0:T(8,128)S(1)}, u32[]{:S(2)}, u32[]{:S(2)}) collective-permute-start(f32[64,16,128]{2,1,0:T(8,128)S(1)} %get-tuple-element.26), channel_id=1, source_target_pairs={{0,1},{1,2},{2,3},{3,4},{4,5},{5,6},{6,7},{7,8},{8,9},{9,10},{10,1... | collective-permute-start | bytes 1572872 | tf_op jit(solution)/shard_map/ppermute | solution.py:25
  26.6 17.7 %copy-start.2 = (f32[128,128,1]{1,0,2:T(8,128)S(1)}, f32[128,128,1]{1,0,2:T(8,128)}, u32[]{:S(2)}) copy-start(f32[128,128,1]{1,0,2:T(8,128)} %constant.29) | copy-start | bytes 196612
  26.6 17.4 %collective-permute-start.5 = (f32[64,16,128]{2,1,0:T(8,128)S(1)}, f32[64,16,128]{2,1,0:T(8,128)S(1)}, u32[]{:S(2)}, u32[]{:S(2)}) collective-permute-start(f32[64,16,128]{2,1,0:T(8,128)S(1)} %get-tuple-element.27), channel_id=1, source_target_pairs={{1,0},{2,1},{3,2},{4,3},{5,4},{6,5},{7,6},{8,7},{9,8},{10,9},{11,1... | collective-permute-start | bytes 1572872 | tf_op jit(solution)/shard_map/ppermute | solution.py:28
  44.3 6.7 %copy-start.1 = (f32[128,128,1]{1,0,2:T(8,128)S(1)}, f32[128,128,1]{1,0,2:T(8,128)}, u32[]{:S(2)}) copy-start(f32[128,128,1]{1,0,2:T(8,128)} %constant.30) | copy-start | bytes 196612
  45.3 28.5 %collective-permute-start.7 = (f32[64,32,128]{2,1,0:T(8,128)S(1)}, f32[64,32,128]{2,1,0:T(8,128)S(1)}, u32[]{:S(2)}, u32[]{:S(2)}) collective-permute-start(f32[64,32,128]{2,1,0:T(8,128)S(1)} %fusion.61), channel_id=1, source_target_pairs={{1,0},{2,1},{3,2},{4,3},{5,4},{6,5},{7,6},{8,7},{9,8},{10,9},{11,1... | collective-permute-start | bytes 3145736 | tf_op jit(solution)/shard_map/ppermute | solution.py:28
  51.0 28.4 %collective-permute-start.6 = (f32[64,32,128]{2,1,0:T(8,128)S(1)}, f32[64,32,128]{2,1,0:T(8,128)S(1)}, u32[]{:S(2)}, u32[]{:S(2)}) collective-permute-start(f32[64,32,128]{2,1,0:T(8,128)S(1)} %fusion.61), channel_id=1, source_target_pairs={{0,1},{1,2},{2,3},{3,4},{4,5},{5,6},{6,7},{7,8},{8,9},{9,10},{10,1... | collective-permute-start | bytes 3145736 | tf_op jit(solution)/shard_map/ppermute | solution.py:25
  79.9 8.6 %collective-permute-start.8 = (f32[32,32,128]{2,1,0:T(8,128)S(1)}, f32[32,32,128]{2,1,0:T(8,128)S(1)}, u32[]{:S(2)}, u32[]{:S(2)}) collective-permute-start(f32[32,32,128]{2,1,0:T(8,128)S(1)} %get-tuple-element.24), channel_id=1, source_target_pairs={{0,32},{32,64},{64,96},{96,128},{128,160},{160,192},{192,224},{224... | collective-permute-start | bytes 1572872 | tf_op jit(solution)/shard_map/ppermute | solution.py:25
  79.9 8.6 %collective-permute-start.9 = (f32[32,32,128]{2,1,0:T(8,128)S(1)}, f32[32,32,128]{2,1,0:T(8,128)S(1)}, u32[]{:S(2)}, u32[]{:S(2)}) collective-permute-start(f32[32,32,128]{2,1,0:T(8,128)S(1)} %get-tuple-element.25), channel_id=1, source_target_pairs={{32,0},{64,32},{96,64},{128,96},{160,128},{192,160},{224,192},{0,2... | collective-permute-start | bytes 1572872 | tf_op jit(solution)/shard_map/ppermute | solution.py:28

commit v19 on v18

--- a/solution.py
+++ b/solution.py
@@ -53,7 +53,7 @@
     flat = values_in.reshape(-1, planes)
     summed = jnp.dot(
         flat,
-        jnp.asarray(matrix),
+        jnp.asarray(matrix) if isinstance(matrix, np.ndarray) else matrix,
         precision=lax.Precision.HIGHEST,
         preferred_element_type=jnp.float32,
     )
@@ -98,12 +98,13 @@
     matrix_2 = depth_matrix(planes, second)
     matrix_3 = depth_matrix(planes, third)
     extra = 2 * second
+    density, composed = lax.optimization_barrier((density, jnp.asarray(matrix_1 @ matrix_2)))
     padded_y = padded_1(density, "col", 1, 2 * first)
     along_y = holed_pass(padded_y, first, 1, size_y)
     padded_x = padded_1(along_y, "row", 0, 2 * first + extra)
     along_x = holed_pass(padded_x, first, 0, size_x + 2 * extra)
     smooth_1 = depth_pass(lax.slice_in_dim(along_x, extra, extra + size_x, axis=0), matrix_1)
-    along_x = depth_pass(holed_pass(along_x, second, 0, size_x), matrix_1 @ matrix_2)
+    along_x = depth_pass(holed_pass(along_x, second, 0, size_x), composed)
     padded_y = padded_1(along_x, "col", 1, 2 * second)
     smooth_2 = holed_pass(padded_y, second, 1, size_y)
     ahead_3 = depth_pass(smooth_2, matrix_3)

time: 112 us -> 112 us (level)
  no operation moved by 1% of the time
where the time goes in v19:
time: 112 us; the launch traced here: 110 us
  waiting for transfers between devices  57.3 us (51%)
  starting transfers between devices  22.8 us (20%)
  blocking collectives  18.7 us (17%)
  other arithmetic  5.06 us (5%)
  matrix products  3.11 us (3%)
  local copies, waits for them, and re-layouts  2.51 us (2%)
    ppermute x5, waiting for transfers between devices, padded_1(): lax.ppermute(lax.slice_in_dim(block, block.shape[dim] - width, None, axis...  35.4 us
    ppermute x5, waiting for transfers between devices, padded_1(): lax.ppermute(lax.slice_in_dim(block, 0, width, axis=dim), axis, backward)  21.9 us
    ppermute x5, starting transfers between devices, padded_1(): lax.ppermute(lax.slice_in_dim(block, 0, width, axis=dim), axis, backward)  20.7 us
    all_to_all x1, blocking collectives, gather_partials(): return lax.all_to_all(sent, axes, 0, 0, tiled=True)  18.7 us
    dot_general x3, matrix products, depth_pass(): jnp.dot(flat, jnp.asarray(matrix) if isinstance(matrix, np.ndarray) else...  3.11 us
  transfers between devices with their start and end apart: 10, of which 6 were waited for; matrix products, arithmetic and copies ran while one was open for 2% of the time, Pallas kernels for 0%

profile of v19, /device:TPU:8, one launch (start us, length us, event | category | flops | bytes accessed | tf_op | source)
XLA Modules:
  0.0 110.3 jit_solution(7330928160233558025)
XLA Ops:
  0.6 1.2 %fusion.61 = (f32[64,8,128]{2,1,0:T(8,128)S(1)}, f32[64,8,128]{2,1,0:T(8,128)S(1)}) fusion(f32[64,32,128]{2,1,0:T(8,128)} %param.4), kind=kLoop, calls=%fused_computation.110 | loop fusion | bytes 1048576 | tf_op jit(solution)/shard_map/slice | solution.py:26
  1.8 2.0 %collective-permute-start = (f32[64,8,128]{2,1,0:T(8,128)S(1)}, f32[64,8,128]{2,1,0:T(8,128)S(1)}, u32[]{:S(2)}, u32[]{:S(2)}) collective-permute-start(f32[64,8,128]{2,1,0:T(8,128)S(1)} %get-tuple-element.36), channel_id=1, source_target_pairs={{0,1},{1,2},{2,3},{3,4},{4,5},{5,6},{6,7},{7,8},{8,9},{9,10},{10,1... | collective-permute-start | bytes 786440 | tf_op jit(solution)/shard_map/ppermute | solution.py:25
  3.8 6.2 %collective-permute-start.1 = (f32[64,8,128]{2,1,0:T(8,128)S(1)}, f32[64,8,128]{2,1,0:T(8,128)S(1)}, u32[]{:S(2)}, u32[]{:S(2)}) collective-permute-start(f32[64,8,128]{2,1,0:T(8,128)S(1)} %get-tuple-element.37), channel_id=1, source_target_pairs={{1,0},{2,1},{3,2},{4,3},{5,4},{6,5},{7,6},{8,7},{9,8},{10,9},{11,1... | collective-permute-start | bytes 786440 | tf_op jit(solution)/shard_map/ppermute | solution.py:28
  10.0 6.2 %collective-permute-done = f32[64,8,128]{2,1,0:T(8,128)S(1)} collective-permute-done((f32[64,8,128]{2,1,0:T(8,128)S(1)}, f32[64,8,128]{2,1,0:T(8,128)S(1)}, u32[]{:S(2)}, u32[]{:S(2)}) %collective-permute-start) | collective-permute-done | bytes 262176 | tf_op jit(solution)/shard_map/ppermute | solution.py:25
  16.3 0.1 constant_dynamic-update-slice_fusion
  16.4 0.5 fusion.45
  17.0 1.7 %collective-permute-start.3 = (f32[24,32,128]{2,1,0:T(8,128)S(1)}, f32[24,32,128]{2,1,0:T(8,128)S(1)}, u32[]{:S(2)}, u32[]{:S(2)}) collective-permute-start(f32[24,32,128]{2,1,0:T(8,128)S(1)} %get-tuple-element.33), channel_id=1, source_target_pairs={{32,0},{64,32},{96,64},{128,96},{160,128},{192,160},{224,192},{0,2... | collective-permute-start | bytes 1179656 | tf_op jit(solution)/shard_map/ppermute | solution.py:28
  18.8 5.5 %collective-permute-done.2 = f32[24,32,128]{2,1,0:T(8,128)S(1)} collective-permute-done((f32[24,32,128]{2,1,0:T(8,128)S(1)}, f32[24,32,128]{2,1,0:T(8,128)S(1)}, u32[]{:S(2)}, u32[]{:S(2)}) %collective-permute-start.2) | collective-permute-done | bytes 393248 | tf_op jit(solution)/shard_map/ppermute | solution.py:25
  24.2 0.2 pad_maximum_fusion
  24.4 0.4 fusion
  24.8 0.5 copy-done.3
  25.3 1.2 %fusion.37 = f32[64,32,128]{2,1,0:T(8,128)S(1)} fusion(f32[96,32,128]{2,1,0:T(8,128)S(1)} %fusion, f32[128,128]{1,0:T(8,128)S(1)} %copy-done.3), kind=kOutput, calls=%fused_computation.67 | convolution fusion | flops 405012480 | bytes 6356992 | tf_op jit(solution)/shard_map/dot_general | solution.py:54
  26.6 5.3 %collective-permute-start.5 = (f32[64,16,128]{2,1,0:T(8,128)S(1)}, f32[64,16,128]{2,1,0:T(8,128)S(1)}, u32[]{:S(2)}, u32[]{:S(2)}) collective-permute-start(f32[64,16,128]{2,1,0:T(8,128)S(1)} %get-tuple-element.31), channel_id=1, source_target_pairs={{1,0},{2,1},{3,2},{4,3},{5,4},{6,5},{7,6},{8,7},{9,8},{10,9},{11,1... | collective-permute-start | bytes 1572872 | tf_op jit(solution)/shard_map/ppermute | solution.py:28
  31.9 12.1 %collective-permute-done.4 = f32[64,16,128]{2,1,0:T(8,128)S(1)} collective-permute-done((f32[64,16,128]{2,1,0:T(8,128)S(1)}, f32[64,16,128]{2,1,0:T(8,128)S(1)}, u32[]{:S(2)}, u32[]{:S(2)}) %collective-permute-start.4) | collective-permute-done | bytes 524320 | tf_op jit(solution)/shard_map/ppermute | solution.py:25
  44.0 0.3 fusion.21
  44.3 1.0 fusion.62
  45.3 5.7 %collective-permute-start.7 = (f32[64,32,128]{2,1,0:T(8,128)S(1)}, f32[64,32,128]{2,1,0:T(8,128)S(1)}, u32[]{:S(2)}, u32[]{:S(2)}) collective-permute-start(f32[64,32,128]{2,1,0:T(8,128)S(1)} %fusion.62), channel_id=1, source_target_pairs={{1,0},{2,1},{3,2},{4,3},{5,4},{6,5},{7,6},{8,7},{9,8},{10,9},{11,1... | collective-permute-start | bytes 3145736 | tf_op jit(solution)/shard_map/ppermute | solution.py:28
  51.0 1.0 fusion.63
  52.0 21.9 %collective-permute-done.7 = f32[64,32,128]{2,1,0:T(8,128)S(1)} collective-permute-done((f32[64,32,128]{2,1,0:T(8,128)S(1)}, f32[64,32,128]{2,1,0:T(8,128)S(1)}, u32[]{:S(2)}, u32[]{:S(2)}) %collective-permute-start.7) | collective-permute-done | bytes 1048608 | tf_op jit(solution)/shard_map/ppermute | solution.py:28
  73.9 5.5 %collective-permute-done.6 = f32[64,32,128]{2,1,0:T(8,128)S(1)} collective-permute-done((f32[64,32,128]{2,1,0:T(8,128)S(1)}, f32[64,32,128]{2,1,0:T(8,128)S(1)}, u32[]{:S(2)}, u32[]{:S(2)}) %collective-permute-start.6) | collective-permute-done | bytes 1048608 | tf_op jit(solution)/shard_map/ppermute | solution.py:25
  79.4 0.4 fusion.30
  79.9 1.7 %collective-permute-start.9 = (f32[32,32,128]{2,1,0:T(8,128)S(1)}, f32[32,32,128]{2,1,0:T(8,128)S(1)}, u32[]{:S(2)}, u32[]{:S(2)}) collective-permute-start(f32[32,32,128]{2,1,0:T(8,128)S(1)} %get-tuple-element.29), channel_id=1, source_target_pairs={{32,0},{64,32},{96,64},{128,96},{160,128},{192,160},{224,192},{0,2... | collective-permute-start | bytes 1572872 | tf_op jit(solution)/shard_map/ppermute | solution.py:28
  81.6 0.3 abs_reduce_fusion.2
  81.9 0.3 abs_reduce_fusion.1
  82.3 6.2 %collective-permute-done.8 = f32[32,32,128]{2,1,0:T(8,128)S(1)} collective-permute-done((f32[32,32,128]{2,1,0:T(8,128)S(1)}, f32[32,32,128]{2,1,0:T(8,128)S(1)}, u32[]{:S(2)}, u32[]{:S(2)}) %collective-permute-start.8) | collective-permute-done | bytes 524320 | tf_op jit(solution)/shard_map/ppermute | solution.py:25
  88.5 1.5 %fusion.56 = (f32[64,32,128]{2,1,0:T(8,128)S(1)}, f32[64,32,128]{2,1,0:T(8,128)}) fusion(f32[64,32,128]{2,1,0:T(8,128)S(1)} %fusion.21, f32[32,32,128]{2,1,0:T(8,128)S(1)} %collective-permute-done.9, f32[64,32,128]{2,1,0:T(8,128)S(1)} %fusion.30, f32[32,32,128]{2,1,0:T(8,128)S(1)} %collective-permute-done.8), kind=kLoop, calls=%fused_computation.106 | loop fusion | flops 3670016 | bytes 5242880 | tf_op jit(solution)/shard_map/sub | solution.py:118
  90.0 0.3 abs_reduce_fusion
  90.3 0.1 maximum_reduce_fusion
  90.5 18.7 %all_to_all.6 = f32[256,1,12]{2,1,0:T(1,128)S(1)} all-to-all(f32[256,1,12]{2,1,0:T(1,128)S(1)} %broadcast_in_dim.8), channel_id=1, replica_groups=mesh['row'=8,'col'=32] {'row','col'}, dimensions={0} | all-to-all | bytes 24576 | tf_op jit(solution)/shard_map/all_to_all | solution.py:89
  109.3 0.3 reshape.29
  109.5 0.1 reduce_sum.139
  109.7 0.6 pad_maximum_fusion.7
  (28 shorter events, 0.7 us)
Async XLA Ops:
  0.6 15.6 %copy-start = (f32[64,32,128]{2,1,0:T(8,128)S(1)}, f32[64,32,128]{2,1,0:T(8,128)}, u32[]{:S(2)}) copy-start(f32[64,32,128]{2,1,0:T(8,128)} %param.4) | copy-start | bytes 3145732
  1.8 14.4 %collective-permute-start = (f32[64,8,128]{2,1,0:T(8,128)S(1)}, f32[64,8,128]{2,1,0:T(8,128)S(1)}, u32[]{:S(2)}, u32[]{:S(2)}) collective-permute-start(f32[64,8,128]{2,1,0:T(8,128)S(1)} %get-tuple-element.36), channel_id=1, source_target_pairs={{0,1},{1,2},{2,3},{3,4},{4,5},{5,6},{6,7},{7,8},{8,9},{9,10},{10,1... | collective-permute-start | bytes 786440 | tf_op jit(solution)/shard_map/ppermute | solution.py:25
  3.8 12.6 %collective-permute-start.1 = (f32[64,8,128]{2,1,0:T(8,128)S(1)}, f32[64,8,128]{2,1,0:T(8,128)S(1)}, u32[]{:S(2)}, u32[]{:S(2)}) collective-permute-start(f32[64,8,128]{2,1,0:T(8,128)S(1)} %get-tuple-element.37), channel_id=1, source_target_pairs={{1,0},{2,1},{3,2},{4,3},{5,4},{6,5},{7,6},{8,7},{9,8},{10,9},{11,1... | collective-permute-start | bytes 786440 | tf_op jit(solution)/shard_map/ppermute | solution.py:28
  17.0 7.2 %collective-permute-start.2 = (f32[24,32,128]{2,1,0:T(8,128)S(1)}, f32[24,32,128]{2,1,0:T(8,128)S(1)}, u32[]{:S(2)}, u32[]{:S(2)}) collective-permute-start(f32[24,32,128]{2,1,0:T(8,128)S(1)} %get-tuple-element.32), channel_id=1, source_target_pairs={{0,32},{32,64},{64,96},{96,128},{128,160},{160,192},{192,224},{224... | collective-permute-start | bytes 1179656 | tf_op jit(solution)/shard_map/ppermute | solution.py:25
  17.0 7.2 %collective-permute-start.3 = (f32[24,32,128]{2,1,0:T(8,128)S(1)}, f32[24,32,128]{2,1,0:T(8,128)S(1)}, u32[]{:S(2)}, u32[]{:S(2)}) collective-permute-start(f32[24,32,128]{2,1,0:T(8,128)S(1)} %get-tuple-element.33), channel_id=1, source_target_pairs={{32,0},{64,32},{96,64},{128,96},{160,128},{192,160},{224,192},{0,2... | collective-permute-start | bytes 1179656 | tf_op jit(solution)/shard_map/ppermute | solution.py:28
  24.4 0.8 copy-start.3
  26.5 17.5 %collective-permute-start.4 = (f32[64,16,128]{2,1,0:T(8,128)S(1)}, f32[64,16,128]{2,1,0:T(8,128)S(1)}, u32[]{:S(2)}, u32[]{:S(2)}) collective-permute-start(f32[64,16,128]{2,1,0:T(8,128)S(1)} %get-tuple-element.30), channel_id=1, source_target_pairs={{0,1},{1,2},{2,3},{3,4},{4,5},{5,6},{6,7},{7,8},{8,9},{9,10},{10,1... | collective-permute-start | bytes 1572872 | tf_op jit(solution)/shard_map/ppermute | solution.py:25
  26.6 17.7 %copy-start.2 = (f32[128,128,1]{1,0,2:T(8,128)S(1)}, f32[128,128,1]{1,0,2:T(8,128)}, u32[]{:S(2)}) copy-start(f32[128,128,1]{1,0,2:T(8,128)} %constant.28) | copy-start | bytes 196612
  26.6 17.4 %collective-permute-start.5 = (f32[64,16,128]{2,1,0:T(8,128)S(1)}, f32[64,16,128]{2,1,0:T(8,128)S(1)}, u32[]{:S(2)}, u32[]{:S(2)}) collective-permute-start(f32[64,16,128]{2,1,0:T(8,128)S(1)} %get-tuple-element.31), channel_id=1, source_target_pairs={{1,0},{2,1},{3,2},{4,3},{5,4},{6,5},{7,6},{8,7},{9,8},{10,9},{11,1... | collective-permute-start | bytes 1572872 | tf_op jit(solution)/shard_map/ppermute | solution.py:28
  44.3 6.7 %copy-start.1 = (f32[128,128,1]{1,0,2:T(8,128)S(1)}, f32[128,128,1]{1,0,2:T(8,128)}, u32[]{:S(2)}) copy-start(f32[128,128,1]{1,0,2:T(8,128)} %constant.29) | copy-start | bytes 196612
  45.3 28.5 %collective-permute-start.7 = (f32[64,32,128]{2,1,0:T(8,128)S(1)}, f32[64,32,128]{2,1,0:T(8,128)S(1)}, u32[]{:S(2)}, u32[]{:S(2)}) collective-permute-start(f32[64,32,128]{2,1,0:T(8,128)S(1)} %fusion.62), channel_id=1, source_target_pairs={{1,0},{2,1},{3,2},{4,3},{5,4},{6,5},{7,6},{8,7},{9,8},{10,9},{11,1... | collective-permute-start | bytes 3145736 | tf_op jit(solution)/shard_map/ppermute | solution.py:28
  51.0 28.4 %collective-permute-start.6 = (f32[64,32,128]{2,1,0:T(8,128)S(1)}, f32[64,32,128]{2,1,0:T(8,128)S(1)}, u32[]{:S(2)}, u32[]{:S(2)}) collective-permute-start(f32[64,32,128]{2,1,0:T(8,128)S(1)} %fusion.62), channel_id=1, source_target_pairs={{0,1},{1,2},{2,3},{3,4},{4,5},{5,6},{6,7},{7,8},{8,9},{9,10},{10,1... | collective-permute-start | bytes 3145736 | tf_op jit(solution)/shard_map/ppermute | solution.py:25
  79.9 8.6 %collective-permute-start.8 = (f32[32,32,128]{2,1,0:T(8,128)S(1)}, f32[32,32,128]{2,1,0:T(8,128)S(1)}, u32[]{:S(2)}, u32[]{:S(2)}) collective-permute-start(f32[32,32,128]{2,1,0:T(8,128)S(1)} %get-tuple-element.28), channel_id=1, source_target_pairs={{0,32},{32,64},{64,96},{96,128},{128,160},{160,192},{192,224},{224... | collective-permute-start | bytes 1572872 | tf_op jit(solution)/shard_map/ppermute | solution.py:25
  79.9 8.6 %collective-permute-start.9 = (f32[32,32,128]{2,1,0:T(8,128)S(1)}, f32[32,32,128]{2,1,0:T(8,128)S(1)}, u32[]{:S(2)}, u32[]{:S(2)}) collective-permute-start(f32[32,32,128]{2,1,0:T(8,128)S(1)} %get-tuple-element.29), channel_id=1, source_target_pairs={{32,0},{64,32},{96,64},{128,96},{160,128},{192,160},{224,192},{0,2... | collective-permute-start | bytes 1572872 | tf_op jit(solution)/shard_map/ppermute | solution.py:28
